TPU v7x, 32 devices: a whole 2x2x4 slice. The times are simulated.
32 devices in a mesh: occ: 4 (over z), aux: 4 (over x, core), vir: 2 (over y).
Axes of the slice: x: 2, y: 2, z: 4, core: 2. Of those that a mesh axis runs over, the one named last changes fastest.
Arguments:
- integrals: bfloat16 [4, 2048, 4096], P('occ', 'vir', 'aux'), may hold values from -0.65625 to 0.65625
- occ_energy: float32 [4], replicated, may hold values from -2 to -0.5
- vir_energy: float32 [2048], replicated, may hold values from 0.25 to 3
Outputs:
- lagrangian: bfloat16 [4, 2048, 4096], P('occ', 'vir', 'aux')
All inputs are finite; a program needn't handle non-finite values.
Results may differ from a plain program's by a relative error of at most 0.0039.
Values may be sent and summed in bfloat16 or wider, within the bound.
No kernel may reach another device: no remote copies, remote signals or barrier semaphores. Data moves between devices by JAX's collectives and lax.ppermute only.
A program may use at most 64 MiB of HBM per device.

v0:
```python
import jax
import jax.numpy as jnp
from jax import lax
from jax.sharding import PartitionSpec as P


def shifted_2(value, axis, by):
    count = lax.axis_size(axis)
    return lax.ppermute(value, axis, [(i, (i + by) % count) for i in range(count)])


def on_device(integrals, occ_energy, vir_energy):
    row_count = integrals.shape[0]
    vir_width = integrals.shape[1]
    cycle_size = lax.axis_size("occ")
    position = lax.axis_index("occ")
    own_level = lax.dynamic_slice_in_dim(occ_energy, position * row_count, row_count)
    partner_level = lax.dynamic_slice_in_dim(
        occ_energy, (position - 2) % cycle_size * row_count, row_count
    )
    local_vir = lax.dynamic_slice_in_dim(vir_energy, lax.axis_index("vir") * vir_width, vir_width)
    shifted = shifted_2(integrals, "occ", 2)
    partner = lax.all_gather(shifted, "vir", axis=1, tiled=True)
    virtuals = partner.shape[1]
    pair_level = own_level + partner_level
    share_rows = virtuals // lax.axis_size("aux")
    partner_cols = partner
    partial_value = lax.psum_scatter(
        jnp.einsum("nbq,naq->bna", partner_cols, integrals, preferred_element_type=jnp.float32),
        "aux",
        scatter_dimension=0,
        tiled=True,
    )
    first_row = lax.axis_index("aux") * share_rows
    vir_rows = lax.dynamic_slice_in_dim(vir_energy, first_row, share_rows)
    amplitudes = (
        partial_value
        / (pair_level[None, :, None] - vir_rows[:, None, None] - local_vir[None, None, :])
    ).astype(jnp.bfloat16)
    portion = lax.all_gather(amplitudes, "aux", axis=0, tiled=True)
    partner_cols = partner
    own_part = jnp.einsum("bna,nbq->naq", portion, partner_cols, preferred_element_type=jnp.float32)
    rows_back = jnp.einsum("bna,naq->nbq", portion, integrals, preferred_element_type=jnp.float32)
    own_part, second_part = (own_part, rows_back)
    owned = lax.psum_scatter(second_part, "vir", scatter_dimension=1, tiled=True)
    returned = shifted_2(owned, "occ", -2)
    return (own_part + returned).astype(jnp.bfloat16)


def solution(mesh):
    placed = (P("occ", "vir", "aux"), P(), P())
    return jax.shard_map(
        on_device, mesh=mesh, in_specs=placed, out_specs=P("occ", "vir", "aux"), check_vma=False
    )
```

profile of v0, /device:TPU:1, one launch (start us, length us, event | category | flops | bytes accessed | tf_op | source)
XLA Modules:
  0.0 587.2 jit_solution(6917923964808509090)
XLA Ops:
  6.5 0.0 all-gather.3.cloned.1.call-start
  6.5 3.1 collective-permute-start
  9.7 90.5 %collective-permute-done = bf16[1,1024,1024]{2,1,0:T(8,128)(2,1)S(1)} collective-permute-done((bf16[1,1024,1024]{2,1,0:T(8,128)(2,1)}, bf16[1,1024,1024]{2,1,0:T(8,128)(2,1)S(1)}, u32[]{:S(2)}, u32[]{:S(2)}) %collective-permute-start) | collective-permute-done | bytes 2097184 | tf_op jit(solution)/shard_map/ppermute | solution.py:9
  100.2 0.0 copy-start
  100.2 1.3 copy-done
  101.5 0.0 all-gather.3.cloned.1.call-update
  101.5 0.0 reduce-scatter.3.cloned.1.call-start
  101.6 58.6 %all-gather.3.cloned.1.call-done = bf16[1,2048,1024]{2,1,0:T(8,128)(2,1)} async-done(((bf16[1,1024,1024]{2,1,0:T(8,128)(2,1)}), bf16[1,2048,1024]{2,1,0:T(8,128)(2,1)}) %all-gather.3.cloned.1.call-update) | async-done | bytes 4194320 | tf_op jit(solution)/shard_map/all_gather | solution.py:23
  160.2 10.6 %convolution_bitcast_fusion.1 = f32[2048,1,1024]{0,2,1:T(8,128)} fusion(bf16[1,2048,1024]{2,1,0:T(8,128)(2,1)} %all-gather.3.cloned.1.call-done, bf16[1,1024,1024]{2,1,0:T(8,128)(2,1)} %param.3), kind=kOutput, calls=%fused_computation.1 | convolution fusion | flops 4294967296 | bytes 14680064 | tf_op jit(solution)/shard_map/nbq,naq->bna/dot_general | solution.py:29
  170.8 0.0 copy-start.2
  170.8 0.0 copy-start.1
  170.8 0.0 reduce-scatter.3.cloned.1.call-update
  170.8 0.0 copy-start.3
  170.8 0.0 all-gather.5.cloned.1.call-start
  170.9 0.5 copy-done.2
  171.4 0.7 fusion.12
  173.3 0.0 copy-done.1
  173.4 0.1 dynamic-slice_subtract_fusion
  173.5 69.2 %reduce-scatter.3.cloned.1.call-done = f32[512,1,1024]{0,2,1:T(8,128)} async-done(((f32[2048,1,1024]{0,2,1:T(8,128)}), f32[512,1,1024]{0,2,1:T(8,128)}) %reduce-scatter.3.cloned.1.call-update) | async-done | bytes 2097168 | tf_op jit(solution)/shard_map/reduce_scatter | solution.py:28
  242.7 2.9 divide_convert_fusion
  245.6 0.0 all-gather.5.cloned.1.call-update
  245.6 0.0 reduce-scatter.5.cloned.1.call-start
  245.7 35.0 %all-gather.5.cloned.1.call-done = bf16[2048,1,1024]{0,2,1:T(8,128)(2,1)} async-done(((bf16[512,1,1024]{0,2,1:T(8,128)(2,1)}), bf16[2048,1,1024]{0,2,1:T(8,128)(2,1)}) %all-gather.5.cloned.1.call-update) | async-done | bytes 4194320 | tf_op jit(solution)/shard_map/all_gather | solution.py:40
  280.7 0.0 copy-done.3
  280.7 9.1 %convolution_bitcast_fusion = f32[1,2048,1024]{2,1,0:T(8,128)} fusion(bf16[2048,1,1024]{0,2,1:T(8,128)(2,1)} %all-gather.5.cloned.1.call-done, bf16[1,1024,1024]{2,1,0:T(8,128)(2,1)S(1)} %copy-done.3), kind=kOutput, calls=%fused_computation | convolution fusion | flops 4294967296 | bytes 14680064 | tf_op jit(solution)/shard_map/bna,naq->nbq/dot_general | solution.py:43
  289.7 0.0 reduce-scatter.5.cloned.1.call-update
  289.8 99.0 %reduce-scatter.5.cloned.1.call-done = f32[1,1024,1024]{2,1,0:T(8,128)} async-done(((f32[1,2048,1024]{2,1,0:T(8,128)}), f32[1,1024,1024]{2,1,0:T(8,128)}) %reduce-scatter.5.cloned.1.call-update) | async-done | bytes 4194320 | tf_op jit(solution)/shard_map/reduce_scatter | solution.py:45
  388.8 2.1 collective-permute-start.1
  390.9 180.4 %collective-permute-done.1 = f32[1,1024,1024]{2,1,0:T(8,128)S(1)} collective-permute-done((f32[1,1024,1024]{2,1,0:T(8,128)}, f32[1,1024,1024]{2,1,0:T(8,128)S(1)}, u32[]{:S(2)}, u32[]{:S(2)}) %collective-permute-start.1) | collective-permute-done | bytes 4194336 | tf_op jit(solution)/shard_map/ppermute | solution.py:9
  571.3 9.3 %fusion = bf16[1,1024,1024]{2,1,0:T(8,128)(2,1)} fusion(f32[1,1024,1024]{2,1,0:T(8,128)S(1)} %collective-permute-done.1, bf16[1,2048,1024]{2,1,0:T(8,128)(2,1)} %all-gather.3.cloned.1.call-done, bf16[2048,1,1024]{0,2,1:T(8,128)(2,1)} %all-gather.5.cloned.1.call-done), kind=kOutput, calls=%fused_computation.3 | convolution fusion | flops 4297064448 | bytes 14680064 | tf_op jit(solution)/shard_map/bna,nbq->naq/dot_general | solution.py:42
  (1 shorter events, 0.0 us)
Async XLA Ops:
  6.5 153.6 %all-gather.3.cloned.1.call-start = ((), (), s32[]{:S(2)}) async-start(), calls=%async_computation.2 | async-start | bytes 6291456 | tf_op jit(solution)/shard_map/all_gather | solution.py:23
  6.5 93.6 %collective-permute-start = (bf16[1,1024,1024]{2,1,0:T(8,128)(2,1)}, bf16[1,1024,1024]{2,1,0:T(8,128)(2,1)S(1)}, u32[]{:S(2)}, u32[]{:S(2)}) collective-permute-start(bf16[1,1024,1024]{2,1,0:T(8,128)(2,1)} %param.3), channel_id=1, source_target_pairs={{0,16},{8,24},{16,0},{24,8},{1,17},{9,25},{17,1},{25,9},{2,18},{10... | collective-permute-start | bytes 6291464 | tf_op jit(solution)/shard_map/ppermute | solution.py:9
  100.2 1.3 copy-start
  101.5 141.2 %reduce-scatter.3.cloned.1.call-start = ((), (), s32[]{:S(2)}) async-start(), calls=%async_computation.3 | async-start | bytes 10485760 | tf_op jit(solution)/shard_map/reduce_scatter | solution.py:28
  170.8 0.7 copy-start.2
  170.8 2.6 copy-start.1
  170.8 109.9 %copy-start.3 = (bf16[1,1024,1024]{2,1,0:T(8,128)(2,1)S(1)}, bf16[1,1024,1024]{2,1,0:T(8,128)(2,1)}, u32[]{:S(2)}) copy-start(bf16[1,1024,1024]{2,1,0:T(8,128)(2,1)} %param.3) | copy-start | bytes 6291460
  170.8 109.9 %all-gather.5.cloned.1.call-start = ((), (), s32[]{:S(2)}) async-start(), calls=%async_computation.4 | async-start | bytes 5242880 | tf_op jit(solution)/shard_map/all_gather | solution.py:40
  245.6 143.1 %reduce-scatter.5.cloned.1.call-start = ((), (), s32[]{:S(2)}) async-start(), calls=%async_computation.5 | async-start | bytes 12582912 | tf_op jit(solution)/shard_map/reduce_scatter | solution.py:45
  388.8 182.5 %collective-permute-start.1 = (f32[1,1024,1024]{2,1,0:T(8,128)}, f32[1,1024,1024]{2,1,0:T(8,128)S(1)}, u32[]{:S(2)}, u32[]{:S(2)}) collective-permute-start(f32[1,1024,1024]{2,1,0:T(8,128)} %reduce-scatter.5.cloned.1.call-done), channel_id=1, source_target_pairs={{0,16},{8,24},{16,0},{24,8},{1,17},{9,25},{17,1},{25,9},{2,18},{10... | collective-permute-start | bytes 12582920 | tf_op jit(solution)/shard_map/ppermute | solution.py:9
Sparse Core Ops, SparseCore 0:
  101.6 58.4 all-gather.2
  170.9 71.7 reduce-scatter.2
  245.7 34.8 all-gather.4
  289.9 98.8 reduce-scatter.4
where the time goes:
time: 589 us; the launch traced here: 587 us
  waiting for transfers between devices  533 us (90%)
  matrix products  29 us (5%)
  between operations  14.5 us (2%)
    ppermute x2, waiting for transfers between devices, shifted_2(): lax.ppermute(value, axis, [(i, (i + by) % count) for i in range(count)])  271 us
    reduce_scatter x1, waiting for transfers between devices, on_device(): lax.psum_scatter(second_part, 'vir', scatter_dimension=1, tiled=True)  99 us
    reduce_scatter x1, waiting for transfers between devices, on_device(): lax.psum_scatter(jnp.einsum('nbq,naq->bna', partner_cols, integrals, pref...  69.2 us
    all_gather x1, waiting for transfers between devices, on_device(): partner = lax.all_gather(shifted, 'vir', axis=1, tiled=True)  58.6 us
    all_gather x1, waiting for transfers between devices, on_device(): portion = lax.all_gather(amplitudes, 'aux', axis=0, tiled=True)  35 us
  transfers between devices with their start and end apart: 6, of which 6 were waited for; matrix products, arithmetic and copies ran while one was open for 0% of the time, Pallas kernels for 0%

commit v1 on v0

--- a/solution.py
+++ b/solution.py
@@ -2,6 +2,9 @@
 import jax.numpy as jnp
 from jax import lax
 from jax.sharding import PartitionSpec as P
+
+CHUNKS = 4
+AUX_BY_PERMUTE = True
 
 
 def shifted_2(value, axis, by):
@@ -9,7 +12,7 @@
     return lax.ppermute(value, axis, [(i, (i + by) % count) for i in range(count)])
 
 
-def on_device(integrals, occ_energy, vir_energy):
+def general_plan(integrals, occ_energy, vir_energy):
     row_count = integrals.shape[0]
     vir_width = integrals.shape[1]
     cycle_size = lax.axis_size("occ")
@@ -24,9 +27,8 @@
     virtuals = partner.shape[1]
     pair_level = own_level + partner_level
     share_rows = virtuals // lax.axis_size("aux")
-    partner_cols = partner
     partial_value = lax.psum_scatter(
-        jnp.einsum("nbq,naq->bna", partner_cols, integrals, preferred_element_type=jnp.float32),
+        jnp.einsum("nbq,naq->bna", partner, integrals, preferred_element_type=jnp.float32),
         "aux",
         scatter_dimension=0,
         tiled=True,
@@ -38,13 +40,104 @@
         / (pair_level[None, :, None] - vir_rows[:, None, None] - local_vir[None, None, :])
     ).astype(jnp.bfloat16)
     portion = lax.all_gather(amplitudes, "aux", axis=0, tiled=True)
-    partner_cols = partner
-    own_part = jnp.einsum("bna,nbq->naq", portion, partner_cols, preferred_element_type=jnp.float32)
+    own_part = jnp.einsum("bna,nbq->naq", portion, partner, preferred_element_type=jnp.float32)
     rows_back = jnp.einsum("bna,naq->nbq", portion, integrals, preferred_element_type=jnp.float32)
-    own_part, second_part = (own_part, rows_back)
-    owned = lax.psum_scatter(second_part, "vir", scatter_dimension=1, tiled=True)
+    owned = lax.psum_scatter(rows_back, "vir", scatter_dimension=1, tiled=True)
     returned = shifted_2(owned, "occ", -2)
     return (own_part + returned).astype(jnp.bfloat16)
+
+
+def xor_pairs(count, step):
+    return [(j, j ^ step) for j in range(count)]
+
+
+def aux_reduce_scatter(x):
+    count = lax.axis_size("aux")
+    k = lax.axis_index("aux")
+    first = 0
+    step = 1
+    while step < count:
+        half = x.shape[0] // 2
+        bit = (k // step) % 2
+        keep = lax.dynamic_slice_in_dim(x, bit * half, half, 0)
+        send = lax.dynamic_slice_in_dim(x, (1 - bit) * half, half, 0)
+        x = keep + lax.ppermute(send, "aux", xor_pairs(count, step))
+        first = first + bit * half
+        step *= 2
+    return x, first
+
+
+def aux_all_gather(x):
+    count = lax.axis_size("aux")
+    k = lax.axis_index("aux")
+    step = count // 2
+    while step >= 1:
+        bit = (k // step) % 2
+        other = lax.ppermute(x, "aux", xor_pairs(count, step))
+        x = jnp.where(bit == 0, jnp.concatenate([x, other]), jnp.concatenate([other, x]))
+        step //= 2
+    return x
+
+
+def paired_plan(integrals, occ_energy, vir_energy):
+    own = integrals[0]
+    vir_rows, _ = own.shape
+    cycle_size = lax.axis_size("occ")
+    position = lax.axis_index("occ")
+    pair_level = occ_energy[position] + occ_energy[(position - 2) % cycle_size]
+    vir_pos = lax.axis_index("vir")
+    vir_count = lax.axis_size("vir")
+    aux_count = lax.axis_size("aux")
+    share = vir_rows // aux_count
+    width = vir_rows // CHUNKS
+
+    if not AUX_BY_PERMUTE:
+        first_row = lax.axis_index("aux") * share
+
+    total = None
+    previous = None
+    for c in range(CHUNKS):
+        piece = own[c * width:(c + 1) * width]
+        if previous is not None:
+            piece, _ = lax.optimization_barrier((piece, previous))
+        arrived = shifted_2(piece, "occ", 2)
+        previous = arrived
+        if vir_count == 2:
+            mate = shifted_2(arrived, "vir", 1)
+            block = jnp.concatenate([arrived, mate])
+            cols = [vir_pos, 1 - vir_pos]
+        else:
+            block = lax.all_gather(arrived, "vir", axis=0, tiled=True)
+            cols = list(range(vir_count))
+        col_level = jnp.concatenate(
+            [lax.dynamic_slice_in_dim(vir_energy, w * vir_rows + c * width, width) for w in cols]
+        )
+        partial = jnp.einsum("aq,bq->ab", own, block, preferred_element_type=jnp.float32)
+        if AUX_BY_PERMUTE:
+            summed, first = aux_reduce_scatter(partial)
+        else:
+            summed = lax.psum_scatter(partial, "aux", scatter_dimension=0, tiled=True)
+            first = first_row
+        row_level = lax.dynamic_slice_in_dim(vir_energy, vir_pos * vir_rows + first, share)
+        amplitudes = (summed / (pair_level - row_level[:, None] - col_level[None, :])).astype(
+            jnp.bfloat16
+        )
+        if AUX_BY_PERMUTE:
+            rows = aux_all_gather(amplitudes)
+        else:
+            rows = lax.all_gather(amplitudes, "aux", axis=0, tiled=True)
+        term = jnp.dot(rows, block, preferred_element_type=jnp.float32)
+        total = term if total is None else total + term
+    gamma_own = total
+    gamma_back = total
+    return (gamma_own + gamma_back).astype(jnp.bfloat16)[None]
+
+
+def on_device(integrals, occ_energy, vir_energy):
+    cycle_size = lax.axis_size("occ")
+    if integrals.shape[0] == 1 and 4 % cycle_size == 0 and integrals.shape[1] % (CHUNKS * 8) == 0:
+        return paired_plan(integrals, occ_energy, vir_energy)
+    return general_plan(integrals, occ_energy, vir_energy)
 
 
 def solution(mesh):

time: 589 us -> 206 us (0.35)
  waiting for transfers between devices: 533 us -> 148 us
  starting transfers between devices: 5.4 us -> 25.2 us
  matrix products: 29 us -> 13.7 us
  between operations: 14.5 us -> 1.61 us
  local copies, waits for them, and re-layouts: 2.53 us -> 11.5 us
    ppermute x2 -> x8, waiting for transfers between devices: 271 us -> 95.8 us  [shifted_2(): lax.ppermute(value, axis, [(i, (i + by) % count) for i in range(count)])]
    reduce_scatter x2 -> x0, waiting for transfers between devices: 168 us -> none  [the longest x1 99 us: on_device(): lax.psum_scatter(second_part, 'vir', scatter_dimension=1, tiled=True)]
    all_gather x2 -> x0, waiting for transfers between devices: 93.6 us -> none  [the longest x1 58.6 us: on_device(): partner = lax.all_gather(shifted, 'vir', axis=1, tiled=True)]
    ppermute x0 -> x16, waiting for transfers between devices: none -> 51.9 us  [the longest x8 38.2 us: aux_reduce_scatter(): x = keep + lax.ppermute(send, 'aux', xor_pairs(count, step))]
    ppermute x0 -> x16, starting transfers between devices: none -> 19.3 us  [the longest x8 9.98 us: aux_all_gather(): other = lax.ppermute(x, 'aux', xor_pairs(count, step))]
    dot_general x3 -> x8, matrix products: 29 us -> 13.7 us  [the longest x4 8.54 us: paired_plan(): term = jnp.dot(rows, block, preferred_element_type=jnp.float32)]
  transfers between devices with their start and end apart: 6 -> 24, of which waited for: 6 -> 12; matrix products, arithmetic and copies ran while one was open for 0% -> 10% of each run, Pallas kernels for 0% -> 0%
where the time goes in v1:
time: 206 us
  waiting for transfers between devices  148 us (72%)
  starting transfers between devices  25.2 us (12%)
  matrix products  13.7 us (7%)
  local copies, waits for them, and re-layouts  11.5 us (6%)
  other arithmetic  6.45 us (3%)
    ppermute x8, waiting for transfers between devices, shifted_2(): lax.ppermute(value, axis, [(i, (i + by) % count) for i in range(count)])  95.8 us
    ppermute x8, waiting for transfers between devices, aux_reduce_scatter(): x = keep + lax.ppermute(send, 'aux', xor_pairs(count, step))  38.2 us
    ppermute x8, waiting for transfers between devices, aux_all_gather(): other = lax.ppermute(x, 'aux', xor_pairs(count, step))  13.6 us
    ppermute x8, starting transfers between devices, aux_all_gather(): other = lax.ppermute(x, 'aux', xor_pairs(count, step))  9.98 us
    ppermute x8, starting transfers between devices, aux_reduce_scatter(): x = keep + lax.ppermute(send, 'aux', xor_pairs(count, step))  9.35 us
    dot_general x4, matrix products, paired_plan(): term = jnp.dot(rows, block, preferred_element_type=jnp.float32)  8.54 us
    ppermute x8, starting transfers between devices, shifted_2(): lax.ppermute(value, axis, [(i, (i + by) % count) for i in range(count)])  5.88 us
    dot_general x4, matrix products, paired_plan(): jnp.einsum('aq,bq->ab', own, block, preferred_element_type=jnp.float32)  5.14 us
  transfers between devices with their start and end apart: 24, of which 12 were waited for; matrix products, arithmetic and copies ran while one was open for 10% of the time, Pallas kernels for 0%

profile of v1, /device:TPU:1, one launch (start us, length us, event | category | flops | bytes accessed | tf_op | source)
XLA Modules:
  0.0 206.2 jit_solution(9769264171996043639)
XLA Ops:
  0.0 2.7 %slice_bitcast_fusion = (bf16[256,1024]{1,0:T(8,128)(2,1)}, bf16[256,1024]{1,0:T(8,128)(2,1)}, bf16[256,1024]{1,0:T(8,128)(2,1)S(1)}, bf16[256,1024]{1,0:T(8,128)(2,1)}) fusion(bf16[1,1024,1024]{2,1,0:T(8,128)(2,1)} %param.3), kind=kLoop, calls=%fused_computation.55 | loop fusion | bytes 4194304 | tf_op jit(solution)/shard_map/slice | solution.py:100
  2.7 3.1 %collective-permute-start = (bf16[256,1024]{1,0:T(8,128)(2,1)S(1)}, bf16[256,1024]{1,0:T(8,128)(2,1)S(1)}, u32[]{:S(2)}, u32[]{:S(2)}) collective-permute-start(bf16[256,1024]{1,0:T(8,128)(2,1)S(1)} %get-tuple-element.13), channel_id=1, source_target_pairs={{0,16},{8,24},{16,0},{24,8},{1,17},{9,25},{17,1},{25,9},{2,18},{10... | collective-permute-start | bytes 1572872 | tf_op jit(solution)/shard_map/ppermute | solution.py:12
  5.8 22.9 %collective-permute-done = bf16[256,1024]{1,0:T(8,128)(2,1)S(1)} collective-permute-done((bf16[256,1024]{1,0:T(8,128)(2,1)S(1)}, bf16[256,1024]{1,0:T(8,128)(2,1)S(1)}, u32[]{:S(2)}, u32[]{:S(2)}) %collective-permute-start) | collective-permute-done | bytes 524320 | tf_op jit(solution)/shard_map/ppermute | solution.py:12
  29.8 23.5 %collective-permute-done.6 = bf16[256,1024]{1,0:T(8,128)(2,1)S(1)} collective-permute-done((bf16[256,1024]{1,0:T(8,128)(2,1)}, bf16[256,1024]{1,0:T(8,128)(2,1)S(1)}, u32[]{:S(2)}, u32[]{:S(2)}) %collective-permute-start.6) | collective-permute-done | bytes 524320 | tf_op jit(solution)/shard_map/ppermute | solution.py:12
  54.0 1.1 constant_dynamic-update-slice_fusion
  56.0 1.3 fusion.7
  57.5 2.8 %collective-permute-start.2 = (f32[512,512]{0,1:T(8,128)S(1)}, f32[512,512]{0,1:T(8,128)S(1)}, u32[]{:S(2)}, u32[]{:S(2)}) collective-permute-start(f32[512,512]{0,1:T(8,128)S(1)} %dynamic-slice_bitcast_fusion.3), channel_id=1, source_target_pairs={{0,2},{2,0},{4,6},{6,4},{1,3},{3,1},{5,7},{7,5},{8,10},{10,8},{12,... | collective-permute-start | bytes 3145736 | tf_op jit(solution)/shard_map/ppermute | solution.py:64
  60.3 19.0 %collective-permute-done.12 = bf16[256,1024]{1,0:T(8,128)(2,1)S(1)} collective-permute-done((bf16[256,1024]{1,0:T(8,128)(2,1)}, bf16[256,1024]{1,0:T(8,128)(2,1)S(1)}, u32[]{:S(2)}, u32[]{:S(2)}) %collective-permute-start.12) | collective-permute-done | bytes 524320 | tf_op jit(solution)/shard_map/ppermute | solution.py:12
  80.6 1.3 fusion.5
  82.0 1.4 collective-permute-start.8
  83.5 20.5 %collective-permute-done.18 = bf16[256,1024]{1,0:T(8,128)(2,1)S(1)} collective-permute-done((bf16[256,1024]{1,0:T(8,128)(2,1)S(1)}, bf16[256,1024]{1,0:T(8,128)(2,1)S(1)}, u32[]{:S(2)}, u32[]{:S(2)}) %collective-permute-start.18) | collective-permute-done | bytes 524320 | tf_op jit(solution)/shard_map/ppermute | solution.py:12
  104.7 1.3 fusion.3
  107.0 10.0 %collective-permute-done.19 = bf16[256,1024]{1,0:T(8,128)(2,1)S(1)} collective-permute-done((bf16[256,1024]{1,0:T(8,128)(2,1)S(1)}, bf16[256,1024]{1,0:T(8,128)(2,1)S(1)}, u32[]{:S(2)}, u32[]{:S(2)}) %collective-permute-start.19) | collective-permute-done | bytes 524320 | tf_op jit(solution)/shard_map/ppermute | solution.py:12
  117.0 1.3 fusion.1
  118.4 1.4 collective-permute-start.20
  130.2 4.5 %collective-permute-done.3 = f32[256,512]{0,1:T(8,128)} collective-permute-done((f32[256,512]{0,1:T(8,128)}, f32[256,512]{0,1:T(8,128)}, u32[]{:S(2)}, u32[]{:S(2)}) %collective-permute-start.3) | collective-permute-done | bytes 524320 | tf_op jit(solution)/shard_map/ppermute | solution.py:64
  134.7 11.2 %collective-permute-done.9 = f32[256,512]{0,1:T(8,128)} collective-permute-done((f32[256,512]{0,1:T(8,128)}, f32[256,512]{0,1:T(8,128)}, u32[]{:S(2)}, u32[]{:S(2)}) %collective-permute-start.9) | collective-permute-done | bytes 524320 | tf_op jit(solution)/shard_map/ppermute | solution.py:64
  146.0 11.2 %collective-permute-done.15 = f32[256,512]{0,1:T(8,128)} collective-permute-done((f32[256,512]{0,1:T(8,128)}, f32[256,512]{0,1:T(8,128)}, u32[]{:S(2)}, u32[]{:S(2)}) %collective-permute-start.15) | collective-permute-done | bytes 524320 | tf_op jit(solution)/shard_map/ppermute | solution.py:64
  157.2 11.2 %collective-permute-done.21 = f32[256,512]{0,1:T(8,128)} collective-permute-done((f32[256,512]{0,1:T(8,128)}, f32[256,512]{0,1:T(8,128)}, u32[]{:S(2)}, u32[]{:S(2)}) %collective-permute-start.21) | collective-permute-done | bytes 524320 | tf_op jit(solution)/shard_map/ppermute | solution.py:64
  168.4 2.9 %divide_convert_fusion = (bf16[256,512]{0,1:T(8,128)(2,1)S(1)}, bf16[256,512]{0,1:T(8,128)(2,1)}, bf16[256,512]{0,1:T(8,128)(2,1)}, bf16[256,512]{0,1:T(8,128)(2,1)}) fusion(f32[256,512]{0,1:T(8,128)} %collective-permute-done.21, f32[512,512]{0,1:T(8,128)} %copy-done, s32[]{:T(128)S(6)} %select_n.169, f32[512]{0:T(512)S(1)} %get-tuple-element.33, ...), kind=kLoop, calls=%fused_computation.54 | loop fusion | flops 2097152 | bytes 5252100 | tf_op jit(solution)/shard_map/convert_element_type | solution.py:122
  172.8 5.8 %collective-permute-done.16 = bf16[256,512]{0,1:T(8,128)(2,1)S(1)} collective-permute-done((bf16[256,512]{0,1:T(8,128)(2,1)}, bf16[256,512]{0,1:T(8,128)(2,1)S(1)}, u32[]{:S(2)}, u32[]{:S(2)}) %collective-permute-start.16) | collective-permute-done | bytes 262176 | tf_op jit(solution)/shard_map/ppermute | solution.py:76
  178.6 1.2 maximum_select_fusion.12
  179.7 3.1 %collective-permute-start.17 = (bf16[512,512]{0,1:T(8,128)(2,1)S(1)}, bf16[512,512]{0,1:T(8,128)(2,1)}, u32[]{:S(2)}, u32[]{:S(2)}) collective-permute-start(bf16[512,512]{0,1:T(8,128)(2,1)S(1)} %maximum_select_fusion.12), channel_id=1, source_target_pairs={{0,2},{2,0},{4,6},{6,4},{1,3},{3,1},{5,7},{7,5},{8,10},{10,8},{12,... | collective-permute-start | bytes 1572872 | tf_op jit(solution)/shard_map/ppermute | solution.py:76
  184.3 1.2 maximum_select_fusion.11
  185.5 1.7 collective-permute-start.11
  187.1 3.7 %collective-permute-done.4 = bf16[256,512]{0,1:T(8,128)(2,1)S(1)} collective-permute-done((bf16[256,512]{0,1:T(8,128)(2,1)}, bf16[256,512]{0,1:T(8,128)(2,1)S(1)}, u32[]{:S(2)}, u32[]{:S(2)}) %collective-permute-start.4) | collective-permute-done | bytes 262176 | tf_op jit(solution)/shard_map/ppermute | solution.py:76
  191.0 1.4 collective-permute-start.5
  192.4 4.1 %collective-permute-done.22 = bf16[256,512]{0,1:T(8,128)(2,1)S(1)} collective-permute-done((bf16[256,512]{0,1:T(8,128)(2,1)S(1)}, bf16[256,512]{0,1:T(8,128)(2,1)S(1)}, u32[]{:S(2)}, u32[]{:S(2)}) %collective-permute-start.22) | collective-permute-done | bytes 262176 | tf_op jit(solution)/shard_map/ppermute | solution.py:76
  197.6 2.8 %fusion.21 = f32[1024,1024]{1,0:T(8,128)S(1)} fusion(bf16[512,1024]{1,0:T(8,128)(2,1)} %copy-done.10, bf16[512,512]{0,1:T(8,128)(2,1)} %collective-permute-done.17, bf16[512,512]{0,1:T(8,128)(2,1)S(1)} %maximum_select_fusion.12, pred[]{:T(512)S(6)} %eq.30), kind=kOutput, calls=%fused_computation.25 | convolution fusion | flops 1078460416 | bytes 6291457 | tf_op jit(solution)/shard_map/dot_general | solution.py:129
  200.4 1.3 fusion.15
  201.8 1.3 fusion.9
  203.1 3.1 %fusion = bf16[1,1024,1024]{2,1,0:T(8,128)(2,1)} fusion(f32[1024,1024]{1,0:T(8,128)S(1)} %fusion.21, f32[1024,1024]{1,0:T(8,128)S(1)} %fusion.9, f32[1024,1024]{1,0:T(8,128)S(1)} %fusion.15, bf16[512,1024]{1,0:T(8,128)(2,1)S(1)} %copy-done.2, bf16[512,512]{0,1:T(8,128)(2,1)S(1)} %collective-permute-done.23, bf16[512,512]{0,1:T(8,128)(2,1)S(1)} %maximum_select_fusion.13, ...), kind=kOutput, calls=%fused_computation.1 | convolution fusion | flops 1083703296 | bytes 16777216 | tf_op jit(solution)/shard_map/dot_general | solution.py:129
  (80 shorter events, 19.4 us)
Async XLA Ops:
  2.7 53.4 %copy-start.3 = (bf16[1,1024,1024]{2,1,0:T(8,128)(2,1)S(1)}, bf16[1,1024,1024]{2,1,0:T(8,128)(2,1)}, u32[]{:S(2)}) copy-start(bf16[1,1024,1024]{2,1,0:T(8,128)(2,1)} %param.3) | copy-start | bytes 6291460
  2.7 26.0 %collective-permute-start = (bf16[256,1024]{1,0:T(8,128)(2,1)S(1)}, bf16[256,1024]{1,0:T(8,128)(2,1)S(1)}, u32[]{:S(2)}, u32[]{:S(2)}) collective-permute-start(bf16[256,1024]{1,0:T(8,128)(2,1)S(1)} %get-tuple-element.13), channel_id=1, source_target_pairs={{0,16},{8,24},{16,0},{24,8},{1,17},{9,25},{17,1},{25,9},{2,18},{10... | collective-permute-start | bytes 1572872 | tf_op jit(solution)/shard_map/ppermute | solution.py:12
  28.7 24.5 %collective-permute-start.6 = (bf16[256,1024]{1,0:T(8,128)(2,1)}, bf16[256,1024]{1,0:T(8,128)(2,1)S(1)}, u32[]{:S(2)}, u32[]{:S(2)}) collective-permute-start(bf16[256,1024]{1,0:T(8,128)(2,1)} %get-tuple-element.8), channel_id=1, source_target_pairs={{0,16},{8,24},{16,0},{24,8},{1,17},{9,25},{17,1},{25,9},{2,18},{10... | collective-permute-start | bytes 1572872 | tf_op jit(solution)/shard_map/ppermute | solution.py:12
  28.7 25.2 %collective-permute-start.1 = (bf16[256,1024]{1,0:T(8,128)(2,1)S(1)}, bf16[256,1024]{1,0:T(8,128)(2,1)}, u32[]{:S(2)}, u32[]{:S(2)}) collective-permute-start(bf16[256,1024]{1,0:T(8,128)(2,1)S(1)} %collective-permute-done), channel_id=1, source_target_pairs={{0,1},{1,0},{2,3},{3,2},{4,5},{5,4},{6,7},{7,6},{8,9},{9,8},{10,11... | collective-permute-start | bytes 1572872 | tf_op jit(solution)/shard_map/ppermute | solution.py:12
  53.3 26.0 %collective-permute-start.12 = (bf16[256,1024]{1,0:T(8,128)(2,1)}, bf16[256,1024]{1,0:T(8,128)(2,1)S(1)}, u32[]{:S(2)}, u32[]{:S(2)}) collective-permute-start(bf16[256,1024]{1,0:T(8,128)(2,1)} %get-tuple-element.9), channel_id=1, source_target_pairs={{0,16},{8,24},{16,0},{24,8},{1,17},{9,25},{17,1},{25,9},{2,18},{10... | collective-permute-start | bytes 1572872 | tf_op jit(solution)/shard_map/ppermute | solution.py:12
  53.3 26.3 %collective-permute-start.7 = (bf16[256,1024]{1,0:T(8,128)(2,1)S(1)}, bf16[256,1024]{1,0:T(8,128)(2,1)S(1)}, u32[]{:S(2)}, u32[]{:S(2)}) collective-permute-start(bf16[256,1024]{1,0:T(8,128)(2,1)S(1)} %collective-permute-done.6), channel_id=1, source_target_pairs={{0,1},{1,0},{2,3},{3,2},{4,5},{5,4},{6,7},{7,6},{8,9},{9,8},{10,11... | collective-permute-start | bytes 1572872 | tf_op jit(solution)/shard_map/ppermute | solution.py:12
  57.3 21.9 %copy-start.5 = (bf16[256,1024]{1,0:T(8,128)(2,1)S(1)}, bf16[256,1024]{1,0:T(8,128)(2,1)}, u32[]{:S(2)}) copy-start(bf16[256,1024]{1,0:T(8,128)(2,1)} %get-tuple-element.10) | copy-start | bytes 1572868
  57.5 62.4 %collective-permute-start.2 = (f32[512,512]{0,1:T(8,128)S(1)}, f32[512,512]{0,1:T(8,128)S(1)}, u32[]{:S(2)}, u32[]{:S(2)}) collective-permute-start(f32[512,512]{0,1:T(8,128)S(1)} %dynamic-slice_bitcast_fusion.3), channel_id=1, source_target_pairs={{0,2},{2,0},{4,6},{6,4},{1,3},{3,1},{5,7},{7,5},{8,10},{10,8},{12,... | collective-permute-start | bytes 3145736 | tf_op jit(solution)/shard_map/ppermute | solution.py:64
  79.3 24.7 %collective-permute-start.18 = (bf16[256,1024]{1,0:T(8,128)(2,1)S(1)}, bf16[256,1024]{1,0:T(8,128)(2,1)S(1)}, u32[]{:S(2)}, u32[]{:S(2)}) collective-permute-start(bf16[256,1024]{1,0:T(8,128)(2,1)S(1)} %copy-done.5), channel_id=1, source_target_pairs={{0,16},{8,24},{16,0},{24,8},{1,17},{9,25},{17,1},{25,9},{2,18},{10... | collective-permute-start | bytes 1572872 | tf_op jit(solution)/shard_map/ppermute | solution.py:12
  79.3 25.4 %collective-permute-start.13 = (bf16[256,1024]{1,0:T(8,128)(2,1)S(1)}, bf16[256,1024]{1,0:T(8,128)(2,1)S(1)}, u32[]{:S(2)}, u32[]{:S(2)}) collective-permute-start(bf16[256,1024]{1,0:T(8,128)(2,1)S(1)} %collective-permute-done.12), channel_id=1, source_target_pairs={{0,1},{1,0},{2,3},{3,2},{4,5},{5,4},{6,7},{7,6},{8,9},{9,8},{10,11... | collective-permute-start | bytes 1572872 | tf_op jit(solution)/shard_map/ppermute | solution.py:12
  82.0 39.5 %collective-permute-start.8 = (f32[512,512]{0,1:T(8,128)S(1)}, f32[512,512]{0,1:T(8,128)S(1)}, u32[]{:S(2)}, u32[]{:S(2)}) collective-permute-start(f32[512,512]{0,1:T(8,128)S(1)} %dynamic-slice_bitcast_fusion.2), channel_id=1, source_target_pairs={{0,2},{2,0},{4,6},{6,4},{1,3},{3,1},{5,7},{7,5},{8,10},{10,8},{12,... | collective-permute-start | bytes 3145736 | tf_op jit(solution)/shard_map/ppermute | solution.py:64
  104.0 13.0 %collective-permute-start.19 = (bf16[256,1024]{1,0:T(8,128)(2,1)S(1)}, bf16[256,1024]{1,0:T(8,128)(2,1)S(1)}, u32[]{:S(2)}, u32[]{:S(2)}) collective-permute-start(bf16[256,1024]{1,0:T(8,128)(2,1)S(1)} %collective-permute-done.18), channel_id=1, source_target_pairs={{0,1},{1,0},{2,3},{3,2},{4,5},{5,4},{6,7},{7,6},{8,9},{9,8},{10,11... | collective-permute-start | bytes 1572872 | tf_op jit(solution)/shard_map/ppermute | solution.py:12
  106.1 17.3 %collective-permute-start.14 = (f32[512,512]{0,1:T(8,128)S(1)}, f32[512,512]{0,1:T(8,128)S(1)}, u32[]{:S(2)}, u32[]{:S(2)}) collective-permute-start(f32[512,512]{0,1:T(8,128)S(1)} %dynamic-slice_bitcast_fusion.1), channel_id=1, source_target_pairs={{0,2},{2,0},{4,6},{6,4},{1,3},{3,1},{5,7},{7,5},{8,10},{10,8},{12,... | collective-permute-start | bytes 3145736 | tf_op jit(solution)/shard_map/ppermute | solution.py:64
  118.4 6.8 %collective-permute-start.20 = (f32[512,512]{0,1:T(8,128)S(1)}, f32[512,512]{0,1:T(8,128)S(1)}, u32[]{:S(2)}, u32[]{:S(2)}) collective-permute-start(f32[512,512]{0,1:T(8,128)S(1)} %dynamic-slice_bitcast_fusion), channel_id=1, source_target_pairs={{0,2},{2,0},{4,6},{6,4},{1,3},{3,1},{5,7},{7,5},{8,10},{10,8},{12,... | collective-permute-start | bytes 3145736 | tf_op jit(solution)/shard_map/ppermute | solution.py:64
  120.9 13.8 %collective-permute-start.3 = (f32[256,512]{0,1:T(8,128)}, f32[256,512]{0,1:T(8,128)}, u32[]{:S(2)}, u32[]{:S(2)}) collective-permute-start(f32[256,512]{0,1:T(8,128)} %constant_dynamic-slice_fusion.3), channel_id=1, source_target_pairs={{0,4},{2,6},{4,0},{6,2},{1,5},{3,7},{5,1},{7,3},{8,12},{10,14},{12... | collective-permute-start | bytes 1572872 | tf_op jit(solution)/shard_map/ppermute | solution.py:64
  122.6 23.3 %collective-permute-start.9 = (f32[256,512]{0,1:T(8,128)}, f32[256,512]{0,1:T(8,128)}, u32[]{:S(2)}, u32[]{:S(2)}) collective-permute-start(f32[256,512]{0,1:T(8,128)} %constant_dynamic-slice_fusion.2), channel_id=1, source_target_pairs={{0,4},{2,6},{4,0},{6,2},{1,5},{3,7},{5,1},{7,3},{8,12},{10,14},{12... | collective-permute-start | bytes 1572872 | tf_op jit(solution)/shard_map/ppermute | solution.py:64
  124.5 3.6 %copy-start.12 = (f32[4]{0:T(128)S(1)}, f32[4]{0:T(128)}, u32[]{:S(2)}) copy-start(f32[4]{0:T(128)} %param.4) | copy-start | bytes 52
  124.5 5.5 %copy-start.11 = (f32[2048]{0:T(1024)S(1)}, f32[2048]{0:T(1024)}, u32[]{:S(2)}) copy-start(f32[2048]{0:T(1024)} %param.5) | copy-start | bytes 24580
  124.5 32.7 %collective-permute-start.15 = (f32[256,512]{0,1:T(8,128)}, f32[256,512]{0,1:T(8,128)}, u32[]{:S(2)}, u32[]{:S(2)}) collective-permute-start(f32[256,512]{0,1:T(8,128)} %constant_dynamic-slice_fusion.1), channel_id=1, source_target_pairs={{0,4},{2,6},{4,0},{6,2},{1,5},{3,7},{5,1},{7,3},{8,12},{10,14},{12... | collective-permute-start | bytes 1572872 | tf_op jit(solution)/shard_map/ppermute | solution.py:64
  127.3 41.1 %collective-permute-start.21 = (f32[256,512]{0,1:T(8,128)}, f32[256,512]{0,1:T(8,128)}, u32[]{:S(2)}, u32[]{:S(2)}) collective-permute-start(f32[256,512]{0,1:T(8,128)} %constant_dynamic-slice_fusion), channel_id=1, source_target_pairs={{0,4},{2,6},{4,0},{6,2},{1,5},{3,7},{5,1},{7,3},{8,12},{10,14},{12... | collective-permute-start | bytes 1572872 | tf_op jit(solution)/shard_map/ppermute | solution.py:64
  171.3 19.6 %copy-start.4 = (bf16[256,512]{0,1:T(8,128)(2,1)S(1)}, bf16[256,512]{0,1:T(8,128)(2,1)}, u32[]{:S(2)}) copy-start(bf16[256,512]{0,1:T(8,128)(2,1)} %get-tuple-element.27) | copy-start | bytes 786436
  171.3 7.2 %collective-permute-start.16 = (bf16[256,512]{0,1:T(8,128)(2,1)}, bf16[256,512]{0,1:T(8,128)(2,1)S(1)}, u32[]{:S(2)}, u32[]{:S(2)}) collective-permute-start(bf16[256,512]{0,1:T(8,128)(2,1)} %get-tuple-element.25), channel_id=1, source_target_pairs={{0,4},{2,6},{4,0},{6,2},{1,5},{3,7},{5,1},{7,3},{8,12},{10,14},{12... | collective-permute-start | bytes 786440 | tf_op jit(solution)/shard_map/ppermute | solution.py:76
  172.1 12.2 %collective-permute-start.10 = (bf16[256,512]{0,1:T(8,128)(2,1)}, bf16[256,512]{0,1:T(8,128)(2,1)S(1)}, u32[]{:S(2)}, u32[]{:S(2)}) collective-permute-start(bf16[256,512]{0,1:T(8,128)(2,1)} %get-tuple-element.26), channel_id=1, source_target_pairs={{0,4},{2,6},{4,0},{6,2},{1,5},{3,7},{5,1},{7,3},{8,12},{10,14},{12... | collective-permute-start | bytes 786440 | tf_op jit(solution)/shard_map/ppermute | solution.py:76
  179.7 17.8 %collective-permute-start.17 = (bf16[512,512]{0,1:T(8,128)(2,1)S(1)}, bf16[512,512]{0,1:T(8,128)(2,1)}, u32[]{:S(2)}, u32[]{:S(2)}) collective-permute-start(bf16[512,512]{0,1:T(8,128)(2,1)S(1)} %maximum_select_fusion.12), channel_id=1, source_target_pairs={{0,2},{2,0},{4,6},{6,4},{1,3},{3,1},{5,7},{7,5},{8,10},{10,8},{12,... | collective-permute-start | bytes 1572872 | tf_op jit(solution)/shard_map/ppermute | solution.py:76
  182.8 8.1 %collective-permute-start.4 = (bf16[256,512]{0,1:T(8,128)(2,1)}, bf16[256,512]{0,1:T(8,128)(2,1)S(1)}, u32[]{:S(2)}, u32[]{:S(2)}) collective-permute-start(bf16[256,512]{0,1:T(8,128)(2,1)} %get-tuple-element.27), channel_id=1, source_target_pairs={{0,4},{2,6},{4,0},{6,2},{1,5},{3,7},{5,1},{7,3},{8,12},{10,14},{12... | collective-permute-start | bytes 786440 | tf_op jit(solution)/shard_map/ppermute | solution.py:76
  183.5 13.0 %collective-permute-start.22 = (bf16[256,512]{0,1:T(8,128)(2,1)S(1)}, bf16[256,512]{0,1:T(8,128)(2,1)S(1)}, u32[]{:S(2)}, u32[]{:S(2)}) collective-permute-start(bf16[256,512]{0,1:T(8,128)(2,1)S(1)} %get-tuple-element.24), channel_id=1, source_target_pairs={{0,4},{2,6},{4,0},{6,2},{1,5},{3,7},{5,1},{7,3},{8,12},{10,14},{12... | collective-permute-start | bytes 786440 | tf_op jit(solution)/shard_map/ppermute | solution.py:76
  185.5 14.9 %collective-permute-start.11 = (bf16[512,512]{0,1:T(8,128)(2,1)S(1)}, bf16[512,512]{0,1:T(8,128)(2,1)S(1)}, u32[]{:S(2)}, u32[]{:S(2)}) collective-permute-start(bf16[512,512]{0,1:T(8,128)(2,1)S(1)} %maximum_select_fusion.11), channel_id=1, source_target_pairs={{0,2},{2,0},{4,6},{6,4},{1,3},{3,1},{5,7},{7,5},{8,10},{10,8},{12,... | collective-permute-start | bytes 1572872 | tf_op jit(solution)/shard_map/ppermute | solution.py:76
  191.0 10.7 %collective-permute-start.5 = (bf16[512,512]{0,1:T(8,128)(2,1)S(1)}, bf16[512,512]{0,1:T(8,128)(2,1)S(1)}, u32[]{:S(2)}, u32[]{:S(2)}) collective-permute-start(bf16[512,512]{0,1:T(8,128)(2,1)S(1)} %maximum_select_fusion.10), channel_id=1, source_target_pairs={{0,2},{2,0},{4,6},{6,4},{1,3},{3,1},{5,7},{7,5},{8,10},{10,8},{12,... | collective-permute-start | bytes 1572872 | tf_op jit(solution)/shard_map/ppermute | solution.py:76
  196.6 3.8 %copy-start.7 = (bf16[512,1024]{1,0:T(8,128)(2,1)S(1)}, bf16[512,1024]{1,0:T(8,128)(2,1)}, u32[]{:S(2)}) copy-start(bf16[512,1024]{1,0:T(8,128)(2,1)} %copy-done.6) | copy-start | bytes 3145732
  196.6 6.4 %collective-permute-start.23 = (bf16[512,512]{0,1:T(8,128)(2,1)S(1)}, bf16[512,512]{0,1:T(8,128)(2,1)S(1)}, u32[]{:S(2)}, u32[]{:S(2)}) collective-permute-start(bf16[512,512]{0,1:T(8,128)(2,1)S(1)} %maximum_select_fusion.13), channel_id=1, source_target_pairs={{0,2},{2,0},{4,6},{6,4},{1,3},{3,1},{5,7},{7,5},{8,10},{10,8},{12,... | collective-permute-start | bytes 1572872 | tf_op jit(solution)/shard_map/ppermute | solution.py:76
  200.4 1.3 copy-start.9
  201.7 1.3 copy-start.2
  (5 other events, 5.6 us)

commit v2 on v1

--- a/solution.py
+++ b/solution.py
@@ -90,18 +90,10 @@
     aux_count = lax.axis_size("aux")
     share = vir_rows // aux_count
     width = vir_rows // CHUNKS
-
     if not AUX_BY_PERMUTE:
         first_row = lax.axis_index("aux") * share
 
-    total = None
-    previous = None
-    for c in range(CHUNKS):
-        piece = own[c * width:(c + 1) * width]
-        if previous is not None:
-            piece, _ = lax.optimization_barrier((piece, previous))
-        arrived = shifted_2(piece, "occ", 2)
-        previous = arrived
+    def forward(c, arrived):
         if vir_count == 2:
             mate = shifted_2(arrived, "vir", 1)
             block = jnp.concatenate([arrived, mate])
@@ -112,22 +104,68 @@
         col_level = jnp.concatenate(
             [lax.dynamic_slice_in_dim(vir_energy, w * vir_rows + c * width, width) for w in cols]
         )
+        return block, col_level
+
+    def reduce(block):
         partial = jnp.einsum("aq,bq->ab", own, block, preferred_element_type=jnp.float32)
         if AUX_BY_PERMUTE:
-            summed, first = aux_reduce_scatter(partial)
-        else:
-            summed = lax.psum_scatter(partial, "aux", scatter_dimension=0, tiled=True)
-            first = first_row
+            return aux_reduce_scatter(partial)
+        return lax.psum_scatter(partial, "aux", scatter_dimension=0, tiled=True), first_row
+
+    def amplitudes_of(summed, first, col_level):
         row_level = lax.dynamic_slice_in_dim(vir_energy, vir_pos * vir_rows + first, share)
         amplitudes = (summed / (pair_level - row_level[:, None] - col_level[None, :])).astype(
             jnp.bfloat16
         )
         if AUX_BY_PERMUTE:
-            rows = aux_all_gather(amplitudes)
-        else:
-            rows = lax.all_gather(amplitudes, "aux", axis=0, tiled=True)
-        term = jnp.dot(rows, block, preferred_element_type=jnp.float32)
-        total = term if total is None else total + term
+            return aux_all_gather(amplitudes)
+        return lax.all_gather(amplitudes, "aux", axis=0, tiled=True)
+
+    arrived = [None] * CHUNKS
+    blocks = [None] * CHUNKS
+    levels = [None] * CHUNKS
+    summed = [None] * CHUNKS
+    firsts = [None] * CHUNKS
+    gathered = [None] * CHUNKS
+    total = None
+    for t in range(CHUNKS + 4):
+        piece = own[t * width:(t + 1) * width] if t < CHUNKS else None
+        if 0 < t < CHUNKS:
+            gate = {"piece": piece, "arrived": arrived[t - 1]}
+            if t >= 2:
+                gate["block"] = blocks[t - 2]
+            if t >= 3:
+                gate["summed"] = summed[t - 3]
+            if t >= 4:
+                gate["gathered"] = gathered[t - 4]
+            if total is not None:
+                gate["total"] = total
+            gate = lax.optimization_barrier(gate)
+            piece = gate["piece"]
+            arrived[t - 1] = gate["arrived"]
+            if t >= 2:
+                blocks[t - 2] = gate["block"]
+            if t >= 3:
+                summed[t - 3] = gate["summed"]
+            if t >= 4:
+                gathered[t - 4] = gate["gathered"]
+            if total is not None:
+                total = gate["total"]
+        if t < CHUNKS:
+            arrived[t] = shifted_2(piece, "occ", 2)
+        c = t - 1
+        if 0 <= c < CHUNKS:
+            blocks[c], levels[c] = forward(c, arrived[c])
+        c = t - 2
+        if 0 <= c < CHUNKS:
+            summed[c], firsts[c] = reduce(blocks[c])
+        c = t - 3
+        if 0 <= c < CHUNKS:
+            gathered[c] = amplitudes_of(summed[c], firsts[c], levels[c])
+        c = t - 4
+        if 0 <= c < CHUNKS:
+            term = jnp.dot(gathered[c], blocks[c], preferred_element_type=jnp.float32)
+            total = term if total is None else total + term
     gamma_own = total
     gamma_back = total
     return (gamma_own + gamma_back).astype(jnp.bfloat16)[None]

time: 206 us -> 209 us (1.015)
  other arithmetic: 6.45 us -> 12.8 us
  local copies, waits for them, and re-layouts: 11.5 us -> 9.16 us
    add x4 -> x5, other arithmetic: 0.83 us -> 3.98 us  [aux_reduce_scatter(): x = keep + lax.ppermute(send, 'aux', xor_pairs(count, step))]
    ppermute x8, waiting for transfers between devices: 38.2 us -> 35.5 us  [aux_reduce_scatter(): x = keep + lax.ppermute(send, 'aux', xor_pairs(count, step))]
    ppermute x8, waiting for transfers between devices: 95.8 us -> 98.2 us  [shifted_2(): lax.ppermute(value, axis, [(i, (i + by) % count) for i in range(count)])]
  transfers between devices with their start and end apart: 24 -> 24, of which waited for: 12 -> 15; matrix products, arithmetic and copies ran while one was open for 10% -> 12% of each run, Pallas kernels for 0% -> 0%
where the time goes in v2:
time: 209 us
  waiting for transfers between devices  146 us (70%)
  starting transfers between devices  23.5 us (11%)
  matrix products  15.1 us (7%)
  other arithmetic  12.8 us (6%)
  local copies, waits for them, and re-layouts  9.16 us (4%)
    ppermute x8, waiting for transfers between devices, shifted_2(): lax.ppermute(value, axis, [(i, (i + by) % count) for i in range(count)])  98.2 us
    ppermute x8, waiting for transfers between devices, aux_reduce_scatter(): x = keep + lax.ppermute(send, 'aux', xor_pairs(count, step))  35.5 us
    ppermute x8, waiting for transfers between devices, aux_all_gather(): other = lax.ppermute(x, 'aux', xor_pairs(count, step))  12.8 us
    ppermute x8, starting transfers between devices, aux_all_gather(): other = lax.ppermute(x, 'aux', xor_pairs(count, step))  9.93 us
    ppermute x8, starting transfers between devices, aux_reduce_scatter(): x = keep + lax.ppermute(send, 'aux', xor_pairs(count, step))  8.51 us
    dot_general x4, matrix products, paired_plan(): term = jnp.dot(gathered[c], blocks[c], preferred_element_type=jnp.float32)  8.41 us
    dot_general x4, matrix products, reduce(): jnp.einsum('aq,bq->ab', own, block, preferred_element_type=jnp.float32)  6.73 us
    ppermute x8, starting transfers between devices, shifted_2(): lax.ppermute(value, axis, [(i, (i + by) % count) for i in range(count)])  5.07 us
  transfers between devices with their start and end apart: 24, of which 15 were waited for; matrix products, arithmetic and copies ran while one was open for 12% of the time, Pallas kernels for 0%

profile of v2, /device:TPU:1, one launch (start us, length us, event | category | flops | bytes accessed | tf_op | source)
XLA Modules:
  0.0 208.7 jit_solution(11705342774479265642)
XLA Ops:
  0.0 2.7 %slice_bitcast_fusion = (bf16[256,1024]{1,0:T(8,128)(2,1)}, bf16[256,1024]{1,0:T(8,128)(2,1)}, bf16[256,1024]{1,0:T(8,128)(2,1)S(1)}, bf16[256,1024]{1,0:T(8,128)(2,1)S(1)}) fusion(bf16[1,1024,1024]{2,1,0:T(8,128)(2,1)} %param.3), kind=kLoop, calls=%fused_computation.60 | loop fusion | bytes 4194304 | tf_op jit(solution)/shard_map/slice | solution.py:132
  2.7 3.1 %collective-permute-start = (bf16[256,1024]{1,0:T(8,128)(2,1)S(1)}, bf16[256,1024]{1,0:T(8,128)(2,1)S(1)}, u32[]{:S(2)}, u32[]{:S(2)}) collective-permute-start(bf16[256,1024]{1,0:T(8,128)(2,1)S(1)} %get-tuple-element.26), channel_id=1, source_target_pairs={{0,16},{8,24},{16,0},{24,8},{1,17},{9,25},{17,1},{25,9},{2,18},{10... | collective-permute-start | bytes 1572872 | tf_op jit(solution)/shard_map/ppermute | solution.py:12
  5.9 22.9 %collective-permute-done = bf16[256,1024]{1,0:T(8,128)(2,1)S(1)} collective-permute-done((bf16[256,1024]{1,0:T(8,128)(2,1)S(1)}, bf16[256,1024]{1,0:T(8,128)(2,1)S(1)}, u32[]{:S(2)}, u32[]{:S(2)}) %collective-permute-start) | collective-permute-done | bytes 524320 | tf_op jit(solution)/shard_map/ppermute | solution.py:12
  29.8 11.2 %collective-permute-done.2 = bf16[256,1024]{1,0:T(8,128)(2,1)S(1)} collective-permute-done((bf16[256,1024]{1,0:T(8,128)(2,1)S(1)}, bf16[256,1024]{1,0:T(8,128)(2,1)S(1)}, u32[]{:S(2)}, u32[]{:S(2)}) %collective-permute-start.2) | collective-permute-done | bytes 524320 | tf_op jit(solution)/shard_map/ppermute | solution.py:12
  41.0 12.8 %collective-permute-done.1 = bf16[256,1024]{1,0:T(8,128)(2,1)S(1)} collective-permute-done((bf16[256,1024]{1,0:T(8,128)(2,1)S(1)}, bf16[256,1024]{1,0:T(8,128)(2,1)S(1)}, u32[]{:S(2)}, u32[]{:S(2)}) %collective-permute-start.1) | collective-permute-done | bytes 524320 | tf_op jit(solution)/shard_map/ppermute | solution.py:12
  54.6 2.9 %fusion.6 = f32[512,1024]{1,0:T(8,128)S(1)} fusion(bf16[512,1024]{1,0:T(8,128)(2,1)S(1)} %pad_maximum_fusion, bf16[1,1024,1024]{2,1,0:T(8,128)(2,1)} %param.3), kind=kOutput, calls=%fused_computation.7 | convolution fusion | flops 1073741824 | bytes 5242880 | tf_op jit(solution)/shard_map/aq,bq->ab/dot_general | solution.py:110
  57.6 2.5 %collective-permute-start.5 = (f32[512,512]{0,1:T(8,128)S(1)}, f32[512,512]{0,1:T(8,128)}, u32[]{:S(2)}, u32[]{:S(2)}) collective-permute-start(f32[512,512]{0,1:T(8,128)S(1)} %dynamic-slice_bitcast_fusion.3), channel_id=1, source_target_pairs={{0,2},{2,0},{4,6},{6,4},{1,3},{3,1},{5,7},{7,5},{8,10},{10,8},{12,... | collective-permute-start | bytes 3145736 | tf_op jit(solution)/shard_map/ppermute | solution.py:64
  60.6 1.9 collective-permute-done.5
  62.5 1.4 bitcast_add_fusion.3
  66.0 7.8 %collective-permute-done.4 = bf16[256,1024]{1,0:T(8,128)(2,1)} collective-permute-done((bf16[256,1024]{1,0:T(8,128)(2,1)}, bf16[256,1024]{1,0:T(8,128)(2,1)}, u32[]{:S(2)}, u32[]{:S(2)}) %collective-permute-start.4) | collective-permute-done | bytes 524320 | tf_op jit(solution)/shard_map/ppermute | solution.py:12
  75.1 3.2 %collective-permute-done.6 = f32[256,512]{0,1:T(8,128)} collective-permute-done((f32[256,512]{0,1:T(8,128)}, f32[256,512]{0,1:T(8,128)}, u32[]{:S(2)}, u32[]{:S(2)}) %collective-permute-start.6) | collective-permute-done | bytes 524320 | tf_op jit(solution)/shard_map/ppermute | solution.py:64
  78.2 1.9 dynamic-slice_add_fusion
  80.2 10.7 %collective-permute-done.3 = bf16[256,1024]{1,0:T(8,128)(2,1)} collective-permute-done((bf16[256,1024]{1,0:T(8,128)(2,1)}, bf16[256,1024]{1,0:T(8,128)(2,1)}, u32[]{:S(2)}, u32[]{:S(2)}) %collective-permute-start.3) | collective-permute-done | bytes 524320 | tf_op jit(solution)/shard_map/ppermute | solution.py:12
  94.4 22.4 %collective-permute-done.18 = bf16[256,1024]{1,0:T(8,128)(2,1)S(1)} collective-permute-done((bf16[256,1024]{1,0:T(8,128)(2,1)S(1)}, bf16[256,1024]{1,0:T(8,128)(2,1)S(1)}, u32[]{:S(2)}, u32[]{:S(2)}) %collective-permute-start.18) | collective-permute-done | bytes 524320 | tf_op jit(solution)/shard_map/ppermute | solution.py:12
  117.1 1.3 fusion.2
  119.4 10.4 %collective-permute-done.19 = bf16[256,1024]{1,0:T(8,128)(2,1)S(1)} collective-permute-done((bf16[256,1024]{1,0:T(8,128)(2,1)S(1)}, bf16[256,1024]{1,0:T(8,128)(2,1)S(1)}, u32[]{:S(2)}, u32[]{:S(2)}) %collective-permute-start.19) | collective-permute-done | bytes 524320 | tf_op jit(solution)/shard_map/ppermute | solution.py:12
  129.9 1.3 fusion
  131.3 1.4 collective-permute-start.20
  139.6 8.0 %collective-permute-done.10 = f32[256,512]{0,1:T(8,128)} collective-permute-done((f32[256,512]{0,1:T(8,128)}, f32[256,512]{0,1:T(8,128)}, u32[]{:S(2)}, u32[]{:S(2)}) %collective-permute-start.10) | collective-permute-done | bytes 524320 | tf_op jit(solution)/shard_map/ppermute | solution.py:64
  147.6 11.2 %collective-permute-done.15 = f32[256,512]{0,1:T(8,128)} collective-permute-done((f32[256,512]{0,1:T(8,128)}, f32[256,512]{0,1:T(8,128)}, u32[]{:S(2)}, u32[]{:S(2)}) %collective-permute-start.15) | collective-permute-done | bytes 524320 | tf_op jit(solution)/shard_map/ppermute | solution.py:64
  158.8 11.2 %collective-permute-done.21 = f32[256,512]{0,1:T(8,128)} collective-permute-done((f32[256,512]{0,1:T(8,128)}, f32[256,512]{0,1:T(8,128)}, u32[]{:S(2)}, u32[]{:S(2)}) %collective-permute-start.21) | collective-permute-done | bytes 524320 | tf_op jit(solution)/shard_map/ppermute | solution.py:64
  170.0 2.7 %divide_convert_fusion = (bf16[256,512]{0,1:T(8,128)(2,1)S(1)}, bf16[256,512]{0,1:T(8,128)(2,1)}, bf16[256,512]{0,1:T(8,128)(2,1)}, bf16[256,512]{0,1:T(8,128)(2,1)}) fusion(f32[256,512]{0,1:T(8,128)} %collective-permute-done.21, f32[512,512]{0,1:T(8,128)S(1)} %bitcast_add_fusion, s32[]{:T(128)S(6)} %select_n.169, f32[512]{0:T(512)S(1)} %get-tuple-element.45, ...), kind=kLoop, calls=%fused_computation.55 | loop fusion | flops 1966080 | bytes 4727812 | tf_op jit(solution)/shard_map/convert_element_type | solution.py:117
  174.2 5.8 %collective-permute-done.7 = bf16[256,512]{0,1:T(8,128)(2,1)S(1)} collective-permute-done((bf16[256,512]{0,1:T(8,128)(2,1)}, bf16[256,512]{0,1:T(8,128)(2,1)S(1)}, u32[]{:S(2)}, u32[]{:S(2)}) %collective-permute-start.7) | collective-permute-done | bytes 262176 | tf_op jit(solution)/shard_map/ppermute | solution.py:76
  181.2 3.1 %collective-permute-start.8 = (bf16[512,512]{0,1:T(8,128)(2,1)S(1)}, bf16[512,512]{0,1:T(8,128)(2,1)}, u32[]{:S(2)}, u32[]{:S(2)}) collective-permute-start(bf16[512,512]{0,1:T(8,128)(2,1)S(1)} %maximum_select_fusion.8), channel_id=1, source_target_pairs={{0,2},{2,0},{4,6},{6,4},{1,3},{3,1},{5,7},{7,5},{8,10},{10,8},{12,... | collective-permute-start | bytes 1572872 | tf_op jit(solution)/shard_map/ppermute | solution.py:76
  186.9 1.6 collective-permute-start.17
  188.5 3.9 %collective-permute-done.11 = bf16[256,512]{0,1:T(8,128)(2,1)} collective-permute-done((bf16[256,512]{0,1:T(8,128)(2,1)}, bf16[256,512]{0,1:T(8,128)(2,1)}, u32[]{:S(2)}, u32[]{:S(2)}) %collective-permute-start.11) | collective-permute-done | bytes 262176 | tf_op jit(solution)/shard_map/ppermute | solution.py:76
  193.6 1.4 collective-permute-start.12
  195.0 3.1 %collective-permute-done.22 = bf16[256,512]{0,1:T(8,128)(2,1)} collective-permute-done((bf16[256,512]{0,1:T(8,128)(2,1)S(1)}, bf16[256,512]{0,1:T(8,128)(2,1)}, u32[]{:S(2)}, u32[]{:S(2)}) %collective-permute-start.22) | collective-permute-done | bytes 262176 | tf_op jit(solution)/shard_map/ppermute | solution.py:76
  200.2 2.5 %fusion.9 = f32[1024,1024]{1,0:T(8,128)S(1)} fusion(bf16[512,1024]{1,0:T(8,128)(2,1)S(1)} %copy-done.4, bf16[512,512]{0,1:T(8,128)(2,1)} %collective-permute-done.8, bf16[512,512]{0,1:T(8,128)(2,1)S(1)} %maximum_select_fusion.8, pred[]{:T(512)S(6)} %eq.30), kind=kOutput, calls=%fused_computation.13 | convolution fusion | flops 1078460416 | bytes 6291457 | tf_op jit(solution)/shard_map/dot_general | solution.py:167
  202.7 1.3 fusion.21
  204.1 1.5 fusion.15
  205.6 3.1 %fusion.8 = bf16[1,1024,1024]{2,1,0:T(8,128)(2,1)} fusion(bf16[512,1024]{1,0:T(8,128)(2,1)S(1)} %copy-done.1, f32[1024,1024]{1,0:T(8,128)S(1)} %fusion.21, f32[1024,1024]{1,0:T(8,128)S(1)} %fusion.9, f32[1024,1024]{1,0:T(8,128)S(1)} %fusion.15, bf16[512,512]{0,1:T(8,128)(2,1)S(1)} %collective-permute-done.23, ...), kind=kOutput, calls=%fused_computation.9 | convolution fusion | flops 1083703296 | bytes 16777216 | tf_op jit(solution)/shard_map/dot_general | solution.py:167
  (81 shorter events, 24.9 us)
Async XLA Ops:
  2.7 26.0 %collective-permute-start = (bf16[256,1024]{1,0:T(8,128)(2,1)S(1)}, bf16[256,1024]{1,0:T(8,128)(2,1)S(1)}, u32[]{:S(2)}, u32[]{:S(2)}) collective-permute-start(bf16[256,1024]{1,0:T(8,128)(2,1)S(1)} %get-tuple-element.26), channel_id=1, source_target_pairs={{0,16},{8,24},{16,0},{24,8},{1,17},{9,25},{17,1},{25,9},{2,18},{10... | collective-permute-start | bytes 1572872 | tf_op jit(solution)/shard_map/ppermute | solution.py:12
  28.8 12.2 %collective-permute-start.2 = (bf16[256,1024]{1,0:T(8,128)(2,1)S(1)}, bf16[256,1024]{1,0:T(8,128)(2,1)S(1)}, u32[]{:S(2)}, u32[]{:S(2)}) collective-permute-start(bf16[256,1024]{1,0:T(8,128)(2,1)S(1)} %collective-permute-done), channel_id=1, source_target_pairs={{0,1},{1,0},{2,3},{3,2},{4,5},{5,4},{6,7},{7,6},{8,9},{9,8},{10,11... | collective-permute-start | bytes 1572872 | tf_op jit(solution)/shard_map/ppermute | solution.py:12
  29.8 24.0 %collective-permute-start.1 = (bf16[256,1024]{1,0:T(8,128)(2,1)S(1)}, bf16[256,1024]{1,0:T(8,128)(2,1)S(1)}, u32[]{:S(2)}, u32[]{:S(2)}) collective-permute-start(bf16[256,1024]{1,0:T(8,128)(2,1)S(1)} %get-tuple-element.14), channel_id=1, source_target_pairs={{0,16},{8,24},{16,0},{24,8},{1,17},{9,25},{17,1},{25,9},{2,18},{10... | collective-permute-start | bytes 1572872 | tf_op jit(solution)/shard_map/ppermute | solution.py:12
  41.0 16.4 %copy-start.3 = (bf16[512,1024]{1,0:T(8,128)(2,1)}, bf16[512,1024]{1,0:T(8,128)(2,1)S(1)}, u32[]{:S(2)}) copy-start(bf16[512,1024]{1,0:T(8,128)(2,1)S(1)} %pad_maximum_fusion) | copy-start | bytes 3145732
  57.6 4.9 %collective-permute-start.5 = (f32[512,512]{0,1:T(8,128)S(1)}, f32[512,512]{0,1:T(8,128)}, u32[]{:S(2)}, u32[]{:S(2)}) collective-permute-start(f32[512,512]{0,1:T(8,128)S(1)} %dynamic-slice_bitcast_fusion.3), channel_id=1, source_target_pairs={{0,2},{2,0},{4,6},{6,4},{1,3},{3,1},{5,7},{7,5},{8,10},{10,8},{12,... | collective-permute-start | bytes 3145736 | tf_op jit(solution)/shard_map/ppermute | solution.py:64
  60.1 13.7 %collective-permute-start.4 = (bf16[256,1024]{1,0:T(8,128)(2,1)}, bf16[256,1024]{1,0:T(8,128)(2,1)}, u32[]{:S(2)}, u32[]{:S(2)}) collective-permute-start(bf16[256,1024]{1,0:T(8,128)(2,1)} %copy-done.8), channel_id=1, source_target_pairs={{0,1},{1,0},{2,3},{3,2},{4,5},{5,4},{6,7},{7,6},{8,9},{9,8},{10,11... | collective-permute-start | bytes 1572872 | tf_op jit(solution)/shard_map/ppermute | solution.py:12
  64.8 26.3 %copy-start.2 = (bf16[1,1024,1024]{2,1,0:T(8,128)(2,1)S(1)}, bf16[1,1024,1024]{2,1,0:T(8,128)(2,1)}, u32[]{:S(2)}) copy-start(bf16[1,1024,1024]{2,1,0:T(8,128)(2,1)} %param.3) | copy-start | bytes 6291460
  64.8 13.5 %collective-permute-start.6 = (f32[256,512]{0,1:T(8,128)}, f32[256,512]{0,1:T(8,128)}, u32[]{:S(2)}, u32[]{:S(2)}) collective-permute-start(f32[256,512]{0,1:T(8,128)} %constant_dynamic-slice_fusion.3), channel_id=1, source_target_pairs={{0,4},{2,6},{4,0},{6,2},{1,5},{3,7},{5,1},{7,3},{8,12},{10,14},{12... | collective-permute-start | bytes 1572872 | tf_op jit(solution)/shard_map/ppermute | solution.py:64
  66.0 24.8 %collective-permute-start.3 = (bf16[256,1024]{1,0:T(8,128)(2,1)}, bf16[256,1024]{1,0:T(8,128)(2,1)}, u32[]{:S(2)}, u32[]{:S(2)}) collective-permute-start(bf16[256,1024]{1,0:T(8,128)(2,1)} %get-tuple-element.16), channel_id=1, source_target_pairs={{0,16},{8,24},{16,0},{24,8},{1,17},{9,25},{17,1},{25,9},{2,18},{10... | collective-permute-start | bytes 1572872 | tf_op jit(solution)/shard_map/ppermute | solution.py:12
  66.0 24.8 %copy-start.9 = (bf16[256,1024]{1,0:T(8,128)(2,1)S(1)}, bf16[256,1024]{1,0:T(8,128)(2,1)}, u32[]{:S(2)}) copy-start(bf16[256,1024]{1,0:T(8,128)(2,1)} %get-tuple-element.22) | copy-start | bytes 1572868
  75.1 17.3 %copy-start.5 = (bf16[512,1024]{1,0:T(8,128)(2,1)}, bf16[512,1024]{1,0:T(8,128)(2,1)S(1)}, u32[]{:S(2)}) copy-start(bf16[512,1024]{1,0:T(8,128)(2,1)S(1)} %pad_maximum_fusion.1) | copy-start | bytes 3145732
  90.8 26.0 %collective-permute-start.18 = (bf16[256,1024]{1,0:T(8,128)(2,1)S(1)}, bf16[256,1024]{1,0:T(8,128)(2,1)S(1)}, u32[]{:S(2)}, u32[]{:S(2)}) collective-permute-start(bf16[256,1024]{1,0:T(8,128)(2,1)S(1)} %copy-done.9), channel_id=1, source_target_pairs={{0,16},{8,24},{16,0},{24,8},{1,17},{9,25},{17,1},{25,9},{2,18},{10... | collective-permute-start | bytes 1572872 | tf_op jit(solution)/shard_map/ppermute | solution.py:12
  90.8 26.2 %collective-permute-start.13 = (bf16[256,1024]{1,0:T(8,128)(2,1)}, bf16[256,1024]{1,0:T(8,128)(2,1)S(1)}, u32[]{:S(2)}, u32[]{:S(2)}) collective-permute-start(bf16[256,1024]{1,0:T(8,128)(2,1)} %collective-permute-done.3), channel_id=1, source_target_pairs={{0,1},{1,0},{2,3},{3,2},{4,5},{5,4},{6,7},{7,6},{8,9},{9,8},{10,11... | collective-permute-start | bytes 1572872 | tf_op jit(solution)/shard_map/ppermute | solution.py:12
  92.5 40.2 %collective-permute-start.9 = (f32[512,512]{0,1:T(8,128)S(1)}, f32[512,512]{0,1:T(8,128)S(1)}, u32[]{:S(2)}, u32[]{:S(2)}) collective-permute-start(f32[512,512]{0,1:T(8,128)S(1)} %dynamic-slice_bitcast_fusion.2), channel_id=1, source_target_pairs={{0,2},{2,0},{4,6},{6,4},{1,3},{3,1},{5,7},{7,5},{8,10},{10,8},{12,... | collective-permute-start | bytes 3145736 | tf_op jit(solution)/shard_map/ppermute | solution.py:64
  116.8 13.0 %collective-permute-start.19 = (bf16[256,1024]{1,0:T(8,128)(2,1)S(1)}, bf16[256,1024]{1,0:T(8,128)(2,1)S(1)}, u32[]{:S(2)}, u32[]{:S(2)}) collective-permute-start(bf16[256,1024]{1,0:T(8,128)(2,1)S(1)} %collective-permute-done.18), channel_id=1, source_target_pairs={{0,1},{1,0},{2,3},{3,2},{4,5},{5,4},{6,7},{7,6},{8,9},{9,8},{10,11... | collective-permute-start | bytes 1572872 | tf_op jit(solution)/shard_map/ppermute | solution.py:12
  118.5 15.5 %collective-permute-start.14 = (f32[512,512]{0,1:T(8,128)S(1)}, f32[512,512]{0,1:T(8,128)S(1)}, u32[]{:S(2)}, u32[]{:S(2)}) collective-permute-start(f32[512,512]{0,1:T(8,128)S(1)} %dynamic-slice_bitcast_fusion.1), channel_id=1, source_target_pairs={{0,2},{2,0},{4,6},{6,4},{1,3},{3,1},{5,7},{7,5},{8,10},{10,8},{12,... | collective-permute-start | bytes 3145736 | tf_op jit(solution)/shard_map/ppermute | solution.py:64
  131.3 5.0 %collective-permute-start.20 = (f32[512,512]{0,1:T(8,128)S(1)}, f32[512,512]{0,1:T(8,128)S(1)}, u32[]{:S(2)}, u32[]{:S(2)}) collective-permute-start(f32[512,512]{0,1:T(8,128)S(1)} %dynamic-slice_bitcast_fusion), channel_id=1, source_target_pairs={{0,2},{2,0},{4,6},{6,4},{1,3},{3,1},{5,7},{7,5},{8,10},{10,8},{12,... | collective-permute-start | bytes 3145736 | tf_op jit(solution)/shard_map/ppermute | solution.py:64
  133.7 13.8 %collective-permute-start.10 = (f32[256,512]{0,1:T(8,128)}, f32[256,512]{0,1:T(8,128)}, u32[]{:S(2)}, u32[]{:S(2)}) collective-permute-start(f32[256,512]{0,1:T(8,128)} %constant_dynamic-slice_fusion.2), channel_id=1, source_target_pairs={{0,4},{2,6},{4,0},{6,2},{1,5},{3,7},{5,1},{7,3},{8,12},{10,14},{12... | collective-permute-start | bytes 1572872 | tf_op jit(solution)/shard_map/ppermute | solution.py:64
  135.0 4.4 %copy-start.12 = (f32[2048]{0:T(1024)S(1)}, f32[2048]{0:T(1024)}, u32[]{:S(2)}) copy-start(f32[2048]{0:T(1024)} %param.5) | copy-start | bytes 24580
  135.0 23.7 %collective-permute-start.15 = (f32[256,512]{0,1:T(8,128)}, f32[256,512]{0,1:T(8,128)}, u32[]{:S(2)}, u32[]{:S(2)}) collective-permute-start(f32[256,512]{0,1:T(8,128)} %constant_dynamic-slice_fusion.1), channel_id=1, source_target_pairs={{0,4},{2,6},{4,0},{6,2},{1,5},{3,7},{5,1},{7,3},{8,12},{10,14},{12... | collective-permute-start | bytes 1572872 | tf_op jit(solution)/shard_map/ppermute | solution.py:64
  137.3 32.7 %collective-permute-start.21 = (f32[256,512]{0,1:T(8,128)}, f32[256,512]{0,1:T(8,128)}, u32[]{:S(2)}, u32[]{:S(2)}) collective-permute-start(f32[256,512]{0,1:T(8,128)} %constant_dynamic-slice_fusion), channel_id=1, source_target_pairs={{0,4},{2,6},{4,0},{6,2},{1,5},{3,7},{5,1},{7,3},{8,12},{10,14},{12... | collective-permute-start | bytes 1572872 | tf_op jit(solution)/shard_map/ppermute | solution.py:64
  172.8 19.7 %copy-start.7 = (bf16[256,512]{0,1:T(8,128)(2,1)S(1)}, bf16[256,512]{0,1:T(8,128)(2,1)}, u32[]{:S(2)}) copy-start(bf16[256,512]{0,1:T(8,128)(2,1)} %get-tuple-element.39) | copy-start | bytes 786436
  172.8 7.2 %collective-permute-start.7 = (bf16[256,512]{0,1:T(8,128)(2,1)}, bf16[256,512]{0,1:T(8,128)(2,1)S(1)}, u32[]{:S(2)}, u32[]{:S(2)}) collective-permute-start(bf16[256,512]{0,1:T(8,128)(2,1)} %get-tuple-element.37), channel_id=1, source_target_pairs={{0,4},{2,6},{4,0},{6,2},{1,5},{3,7},{5,1},{7,3},{8,12},{10,14},{12... | collective-permute-start | bytes 786440 | tf_op jit(solution)/shard_map/ppermute | solution.py:76
  173.1 27.1 %copy-start.4 = (bf16[512,1024]{1,0:T(8,128)(2,1)S(1)}, bf16[512,1024]{1,0:T(8,128)(2,1)}, u32[]{:S(2)}) copy-start(bf16[512,1024]{1,0:T(8,128)(2,1)} %copy-done.3) | copy-start | bytes 3145732
  173.1 12.7 %collective-permute-start.16 = (bf16[256,512]{0,1:T(8,128)(2,1)}, bf16[256,512]{0,1:T(8,128)(2,1)S(1)}, u32[]{:S(2)}, u32[]{:S(2)}) collective-permute-start(bf16[256,512]{0,1:T(8,128)(2,1)} %get-tuple-element.38), channel_id=1, source_target_pairs={{0,4},{2,6},{4,0},{6,2},{1,5},{3,7},{5,1},{7,3},{8,12},{10,14},{12... | collective-permute-start | bytes 786440 | tf_op jit(solution)/shard_map/ppermute | solution.py:76
  181.2 19.0 %collective-permute-start.8 = (bf16[512,512]{0,1:T(8,128)(2,1)S(1)}, bf16[512,512]{0,1:T(8,128)(2,1)}, u32[]{:S(2)}, u32[]{:S(2)}) collective-permute-start(bf16[512,512]{0,1:T(8,128)(2,1)S(1)} %maximum_select_fusion.8), channel_id=1, source_target_pairs={{0,2},{2,0},{4,6},{6,4},{1,3},{3,1},{5,7},{7,5},{8,10},{10,8},{12,... | collective-permute-start | bytes 1572872 | tf_op jit(solution)/shard_map/ppermute | solution.py:76
  184.3 8.2 %collective-permute-start.11 = (bf16[256,512]{0,1:T(8,128)(2,1)}, bf16[256,512]{0,1:T(8,128)(2,1)}, u32[]{:S(2)}, u32[]{:S(2)}) collective-permute-start(bf16[256,512]{0,1:T(8,128)(2,1)} %get-tuple-element.39), channel_id=1, source_target_pairs={{0,4},{2,6},{4,0},{6,2},{1,5},{3,7},{5,1},{7,3},{8,12},{10,14},{12... | collective-permute-start | bytes 786440 | tf_op jit(solution)/shard_map/ppermute | solution.py:76
  184.6 13.5 %collective-permute-start.22 = (bf16[256,512]{0,1:T(8,128)(2,1)S(1)}, bf16[256,512]{0,1:T(8,128)(2,1)}, u32[]{:S(2)}, u32[]{:S(2)}) collective-permute-start(bf16[256,512]{0,1:T(8,128)(2,1)S(1)} %get-tuple-element.36), channel_id=1, source_target_pairs={{0,4},{2,6},{4,0},{6,2},{1,5},{3,7},{5,1},{7,3},{8,12},{10,14},{12... | collective-permute-start | bytes 786440 | tf_op jit(solution)/shard_map/ppermute | solution.py:76
  186.9 15.8 %collective-permute-start.17 = (bf16[512,512]{0,1:T(8,128)(2,1)S(1)}, bf16[512,512]{0,1:T(8,128)(2,1)S(1)}, u32[]{:S(2)}, u32[]{:S(2)}) collective-permute-start(bf16[512,512]{0,1:T(8,128)(2,1)S(1)} %maximum_select_fusion.10), channel_id=1, source_target_pairs={{0,2},{2,0},{4,6},{6,4},{1,3},{3,1},{5,7},{7,5},{8,10},{10,8},{12,... | collective-permute-start | bytes 1572872 | tf_op jit(solution)/shard_map/ppermute | solution.py:76
  193.6 10.4 %collective-permute-start.12 = (bf16[512,512]{0,1:T(8,128)(2,1)S(1)}, bf16[512,512]{0,1:T(8,128)(2,1)S(1)}, u32[]{:S(2)}, u32[]{:S(2)}) collective-permute-start(bf16[512,512]{0,1:T(8,128)(2,1)S(1)} %maximum_select_fusion.9), channel_id=1, source_target_pairs={{0,2},{2,0},{4,6},{6,4},{1,3},{3,1},{5,7},{7,5},{8,10},{10,8},{12,... | collective-permute-start | bytes 1572872 | tf_op jit(solution)/shard_map/ppermute | solution.py:76
  199.2 3.5 %copy-start.11 = (bf16[512,1024]{1,0:T(8,128)(2,1)S(1)}, bf16[512,1024]{1,0:T(8,128)(2,1)}, u32[]{:S(2)}) copy-start(bf16[512,1024]{1,0:T(8,128)(2,1)} %copy-done.10) | copy-start | bytes 3145732
  199.2 6.3 %collective-permute-start.23 = (bf16[512,512]{0,1:T(8,128)(2,1)S(1)}, bf16[512,512]{0,1:T(8,128)(2,1)S(1)}, u32[]{:S(2)}, u32[]{:S(2)}) collective-permute-start(bf16[512,512]{0,1:T(8,128)(2,1)S(1)} %maximum_select_fusion.11), channel_id=1, source_target_pairs={{0,2},{2,0},{4,6},{6,4},{1,3},{3,1},{5,7},{7,5},{8,10},{10,8},{12,... | collective-permute-start | bytes 1572872 | tf_op jit(solution)/shard_map/ppermute | solution.py:76
  (6 other events, 8.8 us)

commit v3 on v2

--- a/solution.py
+++ b/solution.py
@@ -5,6 +5,7 @@
 
 CHUNKS = 4
 AUX_BY_PERMUTE = True
+Z_GATED = False
 
 
 def shifted_2(value, axis, by):
@@ -128,30 +129,36 @@
     firsts = [None] * CHUNKS
     gathered = [None] * CHUNKS
     total = None
+    for c in range(CHUNKS if not Z_GATED else 0):
+        arrived[c] = shifted_2(own[c * width:(c + 1) * width], "occ", 2)
     for t in range(CHUNKS + 4):
-        piece = own[t * width:(t + 1) * width] if t < CHUNKS else None
-        if 0 < t < CHUNKS:
-            gate = {"piece": piece, "arrived": arrived[t - 1]}
-            if t >= 2:
+        piece = own[t * width:(t + 1) * width] if (Z_GATED and t < CHUNKS) else None
+        if t > 0:
+            gate = {"arrived": arrived[t - 1] if t - 1 < CHUNKS else None}
+            if piece is not None:
+                gate["piece"] = piece
+            if 0 <= t - 2 < CHUNKS:
                 gate["block"] = blocks[t - 2]
-            if t >= 3:
+            if 0 <= t - 3 < CHUNKS:
                 gate["summed"] = summed[t - 3]
-            if t >= 4:
+            if 0 <= t - 4 < CHUNKS:
                 gate["gathered"] = gathered[t - 4]
             if total is not None:
                 gate["total"] = total
             gate = lax.optimization_barrier(gate)
-            piece = gate["piece"]
-            arrived[t - 1] = gate["arrived"]
-            if t >= 2:
+            if piece is not None:
+                piece = gate["piece"]
+            if t - 1 < CHUNKS:
+                arrived[t - 1] = gate["arrived"]
+            if 0 <= t - 2 < CHUNKS:
                 blocks[t - 2] = gate["block"]
-            if t >= 3:
+            if 0 <= t - 3 < CHUNKS:
                 summed[t - 3] = gate["summed"]
-            if t >= 4:
+            if 0 <= t - 4 < CHUNKS:
                 gathered[t - 4] = gate["gathered"]
             if total is not None:
                 total = gate["total"]
-        if t < CHUNKS:
+        if piece is not None:
             arrived[t] = shifted_2(piece, "occ", 2)
         c = t - 1
         if 0 <= c < CHUNKS:

time: 209 us -> 203 us (0.971)
  waiting for transfers between devices: 146 us -> 137 us
  other arithmetic: 12.8 us -> 18.5 us
    ppermute x8, waiting for transfers between devices: 98.2 us -> 80.8 us  [shifted_2(): lax.ppermute(value, axis, [(i, (i + by) % count) for i in range(count)])]
    ppermute x8, waiting for transfers between devices: 12.8 us -> 26.2 us  [aux_all_gather(): other = lax.ppermute(x, 'aux', xor_pairs(count, step))]
    ppermute x8, waiting for transfers between devices: 35.5 us -> 30.3 us  [aux_reduce_scatter(): x = keep + lax.ppermute(send, 'aux', xor_pairs(count, step))]
    add x5 -> x8, other arithmetic: 3.98 us -> 7.14 us  [aux_reduce_scatter(): x = keep + lax.ppermute(send, 'aux', xor_pairs(count, step))]
    add x0 -> x2, other arithmetic: none -> 2.72 us  [paired_plan(): total = term if total is None else total + term]
    concatenate x2 -> x4, other arithmetic: 1.34 us -> 3.72 us  [forward(): block = jnp.concatenate([arrived, mate])]
    convert_element_type x1 -> x4, other arithmetic: 2.74 us -> 0.57 us  [amplitudes_of(): (summed / (pair_level - row_level[:, None] - col_level[None, :])).astype(...]
    select_n x4 -> x8, other arithmetic: 4.65 us -> 4.2 us  [aux_all_gather(): jnp.where(bit == 0, jnp.concatenate([x, other]), jnp.concatenate([other,...]
  transfers between devices with their start and end apart: 24 -> 24, of which waited for: 15 -> 17; matrix products, arithmetic and copies ran while one was open for 12% -> 12% of each run, Pallas kernels for 0% -> 0%
where the time goes in v3:
time: 203 us; the launch traced here: 202 us
  waiting for transfers between devices  137 us (67%)
  starting transfers between devices  22.2 us (11%)
  other arithmetic  18.5 us (9%)
  matrix products  13.5 us (7%)
  local copies, waits for them, and re-layouts  9.14 us (5%)
    ppermute x8, waiting for transfers between devices, shifted_2(): lax.ppermute(value, axis, [(i, (i + by) % count) for i in range(count)])  80.8 us
    ppermute x8, waiting for transfers between devices, aux_reduce_scatter(): x = keep + lax.ppermute(send, 'aux', xor_pairs(count, step))  30.3 us
    ppermute x8, waiting for transfers between devices, aux_all_gather(): other = lax.ppermute(x, 'aux', xor_pairs(count, step))  26.2 us
    ppermute x8, starting transfers between devices, aux_reduce_scatter(): x = keep + lax.ppermute(send, 'aux', xor_pairs(count, step))  8.47 us
    ppermute x8, starting transfers between devices, aux_all_gather(): other = lax.ppermute(x, 'aux', xor_pairs(count, step))  8.45 us
    add x8, other arithmetic, aux_reduce_scatter(): x = keep + lax.ppermute(send, 'aux', xor_pairs(count, step))  7.14 us
    dot_general x4, matrix products, paired_plan(): term = jnp.dot(gathered[c], blocks[c], preferred_element_type=jnp.float32)  6.81 us
    dot_general x4, matrix products, reduce(): jnp.einsum('aq,bq->ab', own, block, preferred_element_type=jnp.float32)  6.73 us
  transfers between devices with their start and end apart: 24, of which 17 were waited for; matrix products, arithmetic and copies ran while one was open for 12% of the time, Pallas kernels for 0%

profile of v3, /device:TPU:1, one launch (start us, length us, event | category | flops | bytes accessed | tf_op | source)
XLA Modules:
  0.0 202.2 jit_solution(16121786891905251682)
XLA Ops:
  0.0 2.8 %slice_bitcast_fusion = (bf16[256,1024]{1,0:T(8,128)(2,1)S(1)}, bf16[256,1024]{1,0:T(8,128)(2,1)S(1)}, bf16[256,1024]{1,0:T(8,128)(2,1)}, bf16[256,1024]{1,0:T(8,128)(2,1)}) fusion(bf16[1,1024,1024]{2,1,0:T(8,128)(2,1)} %param.3), kind=kLoop, calls=%fused_computation.38 | loop fusion | bytes 4194304 | tf_op jit(solution)/shard_map/slice | solution.py:133
  2.8 3.1 %collective-permute-start.3 = (bf16[256,1024]{1,0:T(8,128)(2,1)S(1)}, bf16[256,1024]{1,0:T(8,128)(2,1)S(1)}, u32[]{:S(2)}, u32[]{:S(2)}) collective-permute-start(bf16[256,1024]{1,0:T(8,128)(2,1)S(1)} %get-tuple-element.41), channel_id=1, source_target_pairs={{0,16},{8,24},{16,0},{24,8},{1,17},{9,25},{17,1},{25,9},{2,18},{10... | collective-permute-start | bytes 1572872 | tf_op jit(solution)/shard_map/ppermute | solution.py:13
  5.9 22.9 %collective-permute-done.3 = bf16[256,1024]{1,0:T(8,128)(2,1)S(1)} collective-permute-done((bf16[256,1024]{1,0:T(8,128)(2,1)S(1)}, bf16[256,1024]{1,0:T(8,128)(2,1)S(1)}, u32[]{:S(2)}, u32[]{:S(2)}) %collective-permute-start.3) | collective-permute-done | bytes 524320 | tf_op jit(solution)/shard_map/ppermute | solution.py:13
  29.8 11.2 %collective-permute-done.4 = bf16[256,1024]{1,0:T(8,128)(2,1)S(1)} collective-permute-done((bf16[256,1024]{1,0:T(8,128)(2,1)S(1)}, bf16[256,1024]{1,0:T(8,128)(2,1)S(1)}, u32[]{:S(2)}, u32[]{:S(2)}) %collective-permute-start.4) | collective-permute-done | bytes 524320 | tf_op jit(solution)/shard_map/ppermute | solution.py:13
  41.1 12.9 %collective-permute-done.2 = bf16[256,1024]{1,0:T(8,128)(2,1)} collective-permute-done((bf16[256,1024]{1,0:T(8,128)(2,1)S(1)}, bf16[256,1024]{1,0:T(8,128)(2,1)}, u32[]{:S(2)}, u32[]{:S(2)}) %collective-permute-start.2) | collective-permute-done | bytes 524320 | tf_op jit(solution)/shard_map/ppermute | solution.py:13
  53.9 2.9 %fusion.6 = f32[512,1024]{1,0:T(8,128)S(1)} fusion(bf16[512,1024]{1,0:T(8,128)(2,1)S(1)} %pad_maximum_fusion, bf16[1,1024,1024]{2,1,0:T(8,128)(2,1)} %param.3), kind=kOutput, calls=%fused_computation.7 | convolution fusion | flops 1073741824 | bytes 5242880 | tf_op jit(solution)/shard_map/aq,bq->ab/dot_general | solution.py:111
  56.8 1.3 copy-done.1
  58.2 2.5 %collective-permute-start.6 = (f32[512,512]{0,1:T(8,128)S(1)}, f32[512,512]{0,1:T(8,128)}, u32[]{:S(2)}, u32[]{:S(2)}) collective-permute-start(f32[512,512]{0,1:T(8,128)S(1)} %dynamic-slice_bitcast_fusion.3), channel_id=1, source_target_pairs={{0,2},{2,0},{4,6},{6,4},{1,3},{3,1},{5,7},{7,5},{8,10},{10,8},{12,... | collective-permute-start | bytes 3145736 | tf_op jit(solution)/shard_map/ppermute | solution.py:65
  61.2 1.9 collective-permute-done.6
  63.1 1.7 bitcast_add_fusion.3
  66.9 7.5 %collective-permute-done.5 = bf16[256,1024]{1,0:T(8,128)(2,1)} collective-permute-done((bf16[256,1024]{1,0:T(8,128)(2,1)}, bf16[256,1024]{1,0:T(8,128)(2,1)}, u32[]{:S(2)}, u32[]{:S(2)}) %collective-permute-start.5) | collective-permute-done | bytes 524320 | tf_op jit(solution)/shard_map/ppermute | solution.py:13
  75.7 3.5 %collective-permute-done.7 = f32[256,512]{0,1:T(8,128)} collective-permute-done((f32[256,512]{0,1:T(8,128)}, f32[256,512]{0,1:T(8,128)}, u32[]{:S(2)}, u32[]{:S(2)}) %collective-permute-start.7) | collective-permute-done | bytes 524320 | tf_op jit(solution)/shard_map/ppermute | solution.py:65
  79.2 1.9 dynamic-slice_add_fusion.3
  81.1 10.7 %collective-permute-done.1 = bf16[256,1024]{1,0:T(8,128)(2,1)} collective-permute-done((bf16[256,1024]{1,0:T(8,128)(2,1)}, bf16[256,1024]{1,0:T(8,128)(2,1)}, u32[]{:S(2)}, u32[]{:S(2)}) %collective-permute-start.1) | collective-permute-done | bytes 524320 | tf_op jit(solution)/shard_map/ppermute | solution.py:13
  93.1 1.3 copy-done
  98.9 7.3 %collective-permute-done.9 = bf16[256,512]{0,1:T(8,128)(2,1)S(1)} collective-permute-done((bf16[256,512]{0,1:T(8,128)(2,1)S(1)}, bf16[256,512]{0,1:T(8,128)(2,1)S(1)}, u32[]{:S(2)}, u32[]{:S(2)}) %collective-permute-start.9) | collective-permute-done | bytes 262176 | tf_op jit(solution)/shard_map/ppermute | solution.py:77
  107.9 1.7 bitcast_add_fusion.2
  113.3 2.0 maximum_select_fusion
  115.3 9.0 %collective-permute-done.12 = f32[256,512]{0,1:T(8,128)} collective-permute-done((f32[256,512]{0,1:T(8,128)}, f32[256,512]{0,1:T(8,128)}, u32[]{:S(2)}, u32[]{:S(2)}) %collective-permute-start.12) | collective-permute-done | bytes 524320 | tf_op jit(solution)/shard_map/ppermute | solution.py:65
  125.5 11.6 %collective-permute-done = bf16[256,1024]{1,0:T(8,128)(2,1)} collective-permute-done((bf16[256,1024]{1,0:T(8,128)(2,1)}, bf16[256,1024]{1,0:T(8,128)(2,1)}, u32[]{:S(2)}, u32[]{:S(2)}) %collective-permute-start) | collective-permute-done | bytes 524320 | tf_op jit(solution)/shard_map/ppermute | solution.py:13
  140.6 6.5 %collective-permute-done.14 = bf16[256,512]{0,1:T(8,128)(2,1)S(1)} collective-permute-done((bf16[256,512]{0,1:T(8,128)(2,1)S(1)}, bf16[256,512]{0,1:T(8,128)(2,1)S(1)}, u32[]{:S(2)}, u32[]{:S(2)}) %collective-permute-start.14) | collective-permute-done | bytes 262176 | tf_op jit(solution)/shard_map/ppermute | solution.py:77
  150.9 2.9 %collective-permute-done.13 = bf16[256,1024]{1,0:T(8,128)(2,1)S(1)} collective-permute-done((bf16[256,1024]{1,0:T(8,128)(2,1)}, bf16[256,1024]{1,0:T(8,128)(2,1)S(1)}, u32[]{:S(2)}, u32[]{:S(2)}) %collective-permute-start.13) | collective-permute-done | bytes 524320 | tf_op jit(solution)/shard_map/ppermute | solution.py:13
  155.2 6.7 %collective-permute-done.17 = f32[256,512]{0,1:T(8,128)S(1)} collective-permute-done((f32[256,512]{0,1:T(8,128)S(1)}, f32[256,512]{0,1:T(8,128)S(1)}, u32[]{:S(2)}, u32[]{:S(2)}) %collective-permute-start.17) | collective-permute-done | bytes 524320 | tf_op jit(solution)/shard_map/ppermute | solution.py:65
  165.8 6.7 %collective-permute-done.18 = bf16[256,512]{0,1:T(8,128)(2,1)S(1)} collective-permute-done((bf16[256,512]{0,1:T(8,128)(2,1)S(1)}, bf16[256,512]{0,1:T(8,128)(2,1)S(1)}, u32[]{:S(2)}, u32[]{:S(2)}) %collective-permute-start.18) | collective-permute-done | bytes 262176 | tf_op jit(solution)/shard_map/ppermute | solution.py:77
  175.0 1.5 fusion.12
  176.5 1.4 add.203
  178.2 9.1 %collective-permute-done.21 = f32[256,512]{0,1:T(8,128)S(1)} collective-permute-done((f32[256,512]{0,1:T(8,128)S(1)}, f32[256,512]{0,1:T(8,128)S(1)}, u32[]{:S(2)}, u32[]{:S(2)}) %collective-permute-start.21) | collective-permute-done | bytes 524320 | tf_op jit(solution)/shard_map/ppermute | solution.py:65
  187.5 1.3 collective-permute-start.22
  188.9 5.8 %collective-permute-done.22 = bf16[256,512]{0,1:T(8,128)(2,1)S(1)} collective-permute-done((bf16[256,512]{0,1:T(8,128)(2,1)S(1)}, bf16[256,512]{0,1:T(8,128)(2,1)S(1)}, u32[]{:S(2)}, u32[]{:S(2)}) %collective-permute-start.22) | collective-permute-done | bytes 262176 | tf_op jit(solution)/shard_map/ppermute | solution.py:77
  194.8 1.8 collective-permute-start.23
  197.8 1.4 add.208
  199.5 2.7 %fusion.8 = bf16[1,1024,1024]{2,1,0:T(8,128)(2,1)} fusion(f32[1024,1024]{1,0:T(8,128)S(1)} %add.208, bf16[1024,512]{0,1:T(8,128)(2,1)S(1)} %maximum_select_fusion.3, bf16[512,1024]{1,0:T(8,128)(2,1)S(1)} %pad_maximum_fusion.3), kind=kOutput, calls=%fused_computation.9 | convolution fusion | flops 1076887552 | bytes 8388608 | tf_op jit(solution)/shard_map/dot_general | solution.py:174
  (79 shorter events, 33.3 us)
Async XLA Ops:
  2.8 26.0 %collective-permute-start.3 = (bf16[256,1024]{1,0:T(8,128)(2,1)S(1)}, bf16[256,1024]{1,0:T(8,128)(2,1)S(1)}, u32[]{:S(2)}, u32[]{:S(2)}) collective-permute-start(bf16[256,1024]{1,0:T(8,128)(2,1)S(1)} %get-tuple-element.41), channel_id=1, source_target_pairs={{0,16},{8,24},{16,0},{24,8},{1,17},{9,25},{17,1},{25,9},{2,18},{10... | collective-permute-start | bytes 1572872 | tf_op jit(solution)/shard_map/ppermute | solution.py:13
  28.8 12.2 %collective-permute-start.4 = (bf16[256,1024]{1,0:T(8,128)(2,1)S(1)}, bf16[256,1024]{1,0:T(8,128)(2,1)S(1)}, u32[]{:S(2)}, u32[]{:S(2)}) collective-permute-start(bf16[256,1024]{1,0:T(8,128)(2,1)S(1)} %collective-permute-done.3), channel_id=1, source_target_pairs={{0,1},{1,0},{2,3},{3,2},{4,5},{5,4},{6,7},{7,6},{8,9},{9,8},{10,11... | collective-permute-start | bytes 1572872 | tf_op jit(solution)/shard_map/ppermute | solution.py:13
  29.8 24.1 %collective-permute-start.2 = (bf16[256,1024]{1,0:T(8,128)(2,1)S(1)}, bf16[256,1024]{1,0:T(8,128)(2,1)}, u32[]{:S(2)}, u32[]{:S(2)}) collective-permute-start(bf16[256,1024]{1,0:T(8,128)(2,1)S(1)} %get-tuple-element.42), channel_id=1, source_target_pairs={{0,16},{8,24},{16,0},{24,8},{1,17},{9,25},{17,1},{25,9},{2,18},{10... | collective-permute-start | bytes 1572872 | tf_op jit(solution)/shard_map/ppermute | solution.py:13
  56.8 1.3 copy-start.1
  58.2 4.9 %collective-permute-start.6 = (f32[512,512]{0,1:T(8,128)S(1)}, f32[512,512]{0,1:T(8,128)}, u32[]{:S(2)}, u32[]{:S(2)}) collective-permute-start(f32[512,512]{0,1:T(8,128)S(1)} %dynamic-slice_bitcast_fusion.3), channel_id=1, source_target_pairs={{0,2},{2,0},{4,6},{6,4},{1,3},{3,1},{5,7},{7,5},{8,10},{10,8},{12,... | collective-permute-start | bytes 3145736 | tf_op jit(solution)/shard_map/ppermute | solution.py:65
  60.7 13.7 %collective-permute-start.5 = (bf16[256,1024]{1,0:T(8,128)(2,1)}, bf16[256,1024]{1,0:T(8,128)(2,1)}, u32[]{:S(2)}, u32[]{:S(2)}) collective-permute-start(bf16[256,1024]{1,0:T(8,128)(2,1)} %collective-permute-done.2), channel_id=1, source_target_pairs={{0,1},{1,0},{2,3},{3,2},{4,5},{5,4},{6,7},{7,6},{8,9},{9,8},{10,11... | collective-permute-start | bytes 1572872 | tf_op jit(solution)/shard_map/ppermute | solution.py:13
  65.7 13.5 %collective-permute-start.7 = (f32[256,512]{0,1:T(8,128)}, f32[256,512]{0,1:T(8,128)}, u32[]{:S(2)}, u32[]{:S(2)}) collective-permute-start(f32[256,512]{0,1:T(8,128)} %constant_dynamic-slice_fusion.3), channel_id=1, source_target_pairs={{0,4},{2,6},{4,0},{6,2},{1,5},{3,7},{5,1},{7,3},{8,12},{10,14},{12... | collective-permute-start | bytes 1572872 | tf_op jit(solution)/shard_map/ppermute | solution.py:65
  66.9 24.8 %collective-permute-start.1 = (bf16[256,1024]{1,0:T(8,128)(2,1)}, bf16[256,1024]{1,0:T(8,128)(2,1)}, u32[]{:S(2)}, u32[]{:S(2)}) collective-permute-start(bf16[256,1024]{1,0:T(8,128)(2,1)} %get-tuple-element.43), channel_id=1, source_target_pairs={{0,16},{8,24},{16,0},{24,8},{1,17},{9,25},{17,1},{25,9},{2,18},{10... | collective-permute-start | bytes 1572872 | tf_op jit(solution)/shard_map/ppermute | solution.py:13
  66.9 24.8 %copy-start.2 = (bf16[1,1024,1024]{2,1,0:T(8,128)(2,1)S(1)}, bf16[1,1024,1024]{2,1,0:T(8,128)(2,1)}, u32[]{:S(2)}) copy-start(bf16[1,1024,1024]{2,1,0:T(8,128)(2,1)} %param.3) | copy-start | bytes 6291460
  93.1 1.3 copy-start
  94.4 1.5 copy-start.6
  94.4 3.5 %copy-start.5 = (f32[2048]{0:T(1024)S(1)}, f32[2048]{0:T(1024)}, u32[]{:S(2)}) copy-start(f32[2048]{0:T(1024)} %param.5) | copy-start | bytes 24580
  94.4 3.6 %copy-start.4 = (f32[256,512]{0,1:T(8,128)S(1)}, f32[256,512]{0,1:T(8,128)}, u32[]{:S(2)}) copy-start(f32[256,512]{0,1:T(8,128)} %dynamic-slice_add_fusion.3) | copy-start | bytes 1572868
  95.4 12.4 %collective-permute-start.11 = (f32[512,512]{0,1:T(8,128)}, f32[512,512]{0,1:T(8,128)}, u32[]{:S(2)}, u32[]{:S(2)}) collective-permute-start(f32[512,512]{0,1:T(8,128)} %dynamic-slice_bitcast_fusion.2), channel_id=1, source_target_pairs={{0,2},{2,0},{4,6},{6,4},{1,3},{3,1},{5,7},{7,5},{8,10},{10,8},{12,... | collective-permute-start | bytes 3145736 | tf_op jit(solution)/shard_map/ppermute | solution.py:65
  98.1 8.1 %collective-permute-start.9 = (bf16[256,512]{0,1:T(8,128)(2,1)S(1)}, bf16[256,512]{0,1:T(8,128)(2,1)S(1)}, u32[]{:S(2)}, u32[]{:S(2)}) collective-permute-start(bf16[256,512]{0,1:T(8,128)(2,1)S(1)} %divide_convert_fusion.3), channel_id=1, source_target_pairs={{0,4},{2,6},{4,0},{6,2},{1,5},{3,7},{5,1},{7,3},{8,12},{10,14},{12... | collective-permute-start | bytes 786440 | tf_op jit(solution)/shard_map/ppermute | solution.py:77
  98.5 13.5 %collective-permute-start.8 = (bf16[256,1024]{1,0:T(8,128)(2,1)}, bf16[256,1024]{1,0:T(8,128)(2,1)}, u32[]{:S(2)}, u32[]{:S(2)}) collective-permute-start(bf16[256,1024]{1,0:T(8,128)(2,1)} %collective-permute-done.1), channel_id=1, source_target_pairs={{0,1},{1,0},{2,3},{3,2},{4,5},{5,4},{6,7},{7,6},{8,9},{9,8},{10,11... | collective-permute-start | bytes 1572872 | tf_op jit(solution)/shard_map/ppermute | solution.py:13
  107.2 6.1 %collective-permute-start.10 = (bf16[512,512]{0,1:T(8,128)(2,1)}, bf16[512,512]{0,1:T(8,128)(2,1)}, u32[]{:S(2)}, u32[]{:S(2)}) collective-permute-start(bf16[512,512]{0,1:T(8,128)(2,1)} %maximum_select_fusion.4), channel_id=1, source_target_pairs={{0,2},{2,0},{4,6},{6,4},{1,3},{3,1},{5,7},{7,5},{8,10},{10,8},{12,... | collective-permute-start | bytes 1572872 | tf_op jit(solution)/shard_map/ppermute | solution.py:77
  110.4 13.9 %collective-permute-start.12 = (f32[256,512]{0,1:T(8,128)}, f32[256,512]{0,1:T(8,128)}, u32[]{:S(2)}, u32[]{:S(2)}) collective-permute-start(f32[256,512]{0,1:T(8,128)} %constant_dynamic-slice_fusion.2), channel_id=1, source_target_pairs={{0,4},{2,6},{4,0},{6,2},{1,5},{3,7},{5,1},{7,3},{8,12},{10,14},{12... | collective-permute-start | bytes 1572872 | tf_op jit(solution)/shard_map/ppermute | solution.py:65
  110.7 26.3 %collective-permute-start = (bf16[256,1024]{1,0:T(8,128)(2,1)}, bf16[256,1024]{1,0:T(8,128)(2,1)}, u32[]{:S(2)}, u32[]{:S(2)}) collective-permute-start(bf16[256,1024]{1,0:T(8,128)(2,1)} %get-tuple-element.44), channel_id=1, source_target_pairs={{0,16},{8,24},{16,0},{24,8},{1,17},{9,25},{17,1},{25,9},{2,18},{10... | collective-permute-start | bytes 1572872 | tf_op jit(solution)/shard_map/ppermute | solution.py:13
  113.3 23.7 %copy-start.3 = (bf16[1,1024,1024]{2,1,0:T(8,128)(2,1)S(1)}, bf16[1,1024,1024]{2,1,0:T(8,128)(2,1)}, u32[]{:S(2)}) copy-start(bf16[1,1024,1024]{2,1,0:T(8,128)(2,1)} %param.3) | copy-start | bytes 6291460
  138.4 9.7 %collective-permute-start.16 = (f32[512,512]{0,1:T(8,128)S(1)}, f32[512,512]{0,1:T(8,128)S(1)}, u32[]{:S(2)}, u32[]{:S(2)}) collective-permute-start(f32[512,512]{0,1:T(8,128)S(1)} %dynamic-slice_bitcast_fusion.1), channel_id=1, source_target_pairs={{0,2},{2,0},{4,6},{6,4},{1,3},{3,1},{5,7},{7,5},{8,10},{10,8},{12,... | collective-permute-start | bytes 3145736 | tf_op jit(solution)/shard_map/ppermute | solution.py:65
  139.1 8.0 %collective-permute-start.14 = (bf16[256,512]{0,1:T(8,128)(2,1)S(1)}, bf16[256,512]{0,1:T(8,128)(2,1)S(1)}, u32[]{:S(2)}, u32[]{:S(2)}) collective-permute-start(bf16[256,512]{0,1:T(8,128)(2,1)S(1)} %divide_convert_fusion.2), channel_id=1, source_target_pairs={{0,4},{2,6},{4,0},{6,2},{1,5},{3,7},{5,1},{7,3},{8,12},{10,14},{12... | collective-permute-start | bytes 786440 | tf_op jit(solution)/shard_map/ppermute | solution.py:77
  140.4 13.4 %collective-permute-start.13 = (bf16[256,1024]{1,0:T(8,128)(2,1)}, bf16[256,1024]{1,0:T(8,128)(2,1)S(1)}, u32[]{:S(2)}, u32[]{:S(2)}) collective-permute-start(bf16[256,1024]{1,0:T(8,128)(2,1)} %collective-permute-done), channel_id=1, source_target_pairs={{0,1},{1,0},{2,3},{3,2},{4,5},{5,4},{6,7},{7,6},{8,9},{9,8},{10,11... | collective-permute-start | bytes 1572872 | tf_op jit(solution)/shard_map/ppermute | solution.py:13
  147.2 7.7 %collective-permute-start.15 = (bf16[512,512]{0,1:T(8,128)(2,1)S(1)}, bf16[512,512]{0,1:T(8,128)(2,1)S(1)}, u32[]{:S(2)}, u32[]{:S(2)}) collective-permute-start(bf16[512,512]{0,1:T(8,128)(2,1)S(1)} %maximum_select_fusion.5), channel_id=1, source_target_pairs={{0,2},{2,0},{4,6},{6,4},{1,3},{3,1},{5,7},{7,5},{8,10},{10,8},{12,... | collective-permute-start | bytes 1572872 | tf_op jit(solution)/shard_map/ppermute | solution.py:77
  148.4 13.6 %collective-permute-start.17 = (f32[256,512]{0,1:T(8,128)S(1)}, f32[256,512]{0,1:T(8,128)S(1)}, u32[]{:S(2)}, u32[]{:S(2)}) collective-permute-start(f32[256,512]{0,1:T(8,128)S(1)} %constant_dynamic-slice_fusion.1), channel_id=1, source_target_pairs={{0,4},{2,6},{4,0},{6,2},{1,5},{3,7},{5,1},{7,3},{8,12},{10,14},{12... | collective-permute-start | bytes 1572872 | tf_op jit(solution)/shard_map/ppermute | solution.py:65
  163.4 10.0 %collective-permute-start.20 = (f32[512,512]{0,1:T(8,128)S(1)}, f32[512,512]{0,1:T(8,128)S(1)}, u32[]{:S(2)}, u32[]{:S(2)}) collective-permute-start(f32[512,512]{0,1:T(8,128)S(1)} %dynamic-slice_bitcast_fusion), channel_id=1, source_target_pairs={{0,2},{2,0},{4,6},{6,4},{1,3},{3,1},{5,7},{7,5},{8,10},{10,8},{12,... | collective-permute-start | bytes 3145736 | tf_op jit(solution)/shard_map/ppermute | solution.py:65
  164.5 8.0 %collective-permute-start.18 = (bf16[256,512]{0,1:T(8,128)(2,1)S(1)}, bf16[256,512]{0,1:T(8,128)(2,1)S(1)}, u32[]{:S(2)}, u32[]{:S(2)}) collective-permute-start(bf16[256,512]{0,1:T(8,128)(2,1)S(1)} %divide_convert_fusion.1), channel_id=1, source_target_pairs={{0,4},{2,6},{4,0},{6,2},{1,5},{3,7},{5,1},{7,3},{8,12},{10,14},{12... | collective-permute-start | bytes 786440 | tf_op jit(solution)/shard_map/ppermute | solution.py:77
  172.6 5.3 %collective-permute-start.19 = (bf16[512,512]{0,1:T(8,128)(2,1)S(1)}, bf16[512,512]{0,1:T(8,128)(2,1)S(1)}, u32[]{:S(2)}, u32[]{:S(2)}) collective-permute-start(bf16[512,512]{0,1:T(8,128)(2,1)S(1)} %maximum_select_fusion.6), channel_id=1, source_target_pairs={{0,2},{2,0},{4,6},{6,4},{1,3},{3,1},{5,7},{7,5},{8,10},{10,8},{12,... | collective-permute-start | bytes 1572872 | tf_op jit(solution)/shard_map/ppermute | solution.py:77
  173.7 13.6 %collective-permute-start.21 = (f32[256,512]{0,1:T(8,128)S(1)}, f32[256,512]{0,1:T(8,128)S(1)}, u32[]{:S(2)}, u32[]{:S(2)}) collective-permute-start(f32[256,512]{0,1:T(8,128)S(1)} %constant_dynamic-slice_fusion), channel_id=1, source_target_pairs={{0,4},{2,6},{4,0},{6,2},{1,5},{3,7},{5,1},{7,3},{8,12},{10,14},{12... | collective-permute-start | bytes 1572872 | tf_op jit(solution)/shard_map/ppermute | solution.py:65
  187.5 7.1 %collective-permute-start.22 = (bf16[256,512]{0,1:T(8,128)(2,1)S(1)}, bf16[256,512]{0,1:T(8,128)(2,1)S(1)}, u32[]{:S(2)}, u32[]{:S(2)}) collective-permute-start(bf16[256,512]{0,1:T(8,128)(2,1)S(1)} %divide_convert_fusion), channel_id=1, source_target_pairs={{0,4},{2,6},{4,0},{6,2},{1,5},{3,7},{5,1},{7,3},{8,12},{10,14},{12... | collective-permute-start | bytes 786440 | tf_op jit(solution)/shard_map/ppermute | solution.py:77
  194.8 4.4 %collective-permute-start.23 = (bf16[512,512]{0,1:T(8,128)(2,1)S(1)}, bf16[512,512]{0,1:T(8,128)(2,1)S(1)}, u32[]{:S(2)}, u32[]{:S(2)}) collective-permute-start(bf16[512,512]{0,1:T(8,128)(2,1)S(1)} %maximum_select_fusion.7), channel_id=1, source_target_pairs={{0,2},{2,0},{4,6},{6,4},{1,3},{3,1},{5,7},{7,5},{8,10},{10,8},{12,... | collective-permute-start | bytes 1572872 | tf_op jit(solution)/shard_map/ppermute | solution.py:77

commit v4 on v3

--- a/solution.py
+++ b/solution.py
@@ -4,7 +4,7 @@
 from jax.sharding import PartitionSpec as P
 
 CHUNKS = 4
-AUX_BY_PERMUTE = True
+AUX_BY_PERMUTE = False
 Z_GATED = False
 
 

time: 203 us -> 285 us (1.40)
  waiting for transfers between devices: 137 us -> 208 us
  matrix products: 13.5 us -> 31.7 us
  between operations: 1.55 us -> 14.8 us
  starting transfers between devices: 22.2 us -> 10 us
  other arithmetic: 18.5 us -> 14 us
  local copies, waits for them, and re-layouts: 9.14 us -> 5.36 us
    reduce_scatter x0 -> x4, waiting for transfers between devices: none -> 90.7 us  [reduce(): lax.psum_scatter(partial, 'aux', scatter_dimension=0, tiled=True)]
    ppermute x16 -> x0, waiting for transfers between devices: 56.5 us -> none  [the longest x8 30.3 us: aux_reduce_scatter(): x = keep + lax.ppermute(send, 'aux', xor_pairs(count, step))]
    all_gather x0 -> x4, waiting for transfers between devices: none -> 18.6 us  [amplitudes_of(): return lax.all_gather(amplitudes, 'aux', axis=0, tiled=True)]
    ppermute x8, waiting for transfers between devices: 80.8 us -> 99.1 us  [shifted_2(): lax.ppermute(value, axis, [(i, (i + by) % count) for i in range(count)])]
    ppermute x16 -> x0, starting transfers between devices: 16.9 us -> none  [the longest x8 8.47 us: aux_reduce_scatter(): x = keep + lax.ppermute(send, 'aux', xor_pairs(count, step))]
    dot_general x4, matrix products: 6.81 us -> 16.5 us  [paired_plan(): term = jnp.dot(gathered[c], blocks[c], preferred_element_type=jnp.float32)]
    dot_general x4, matrix products: 6.73 us -> 15.2 us  [reduce(): jnp.einsum('aq,bq->ab', own, block, preferred_element_type=jnp.float32)]
    add x8 -> x0, other arithmetic: 7.14 us -> none  [aux_reduce_scatter(): x = keep + lax.ppermute(send, 'aux', xor_pairs(count, step))]
  transfers between devices with their start and end apart: 24 -> 16, of which waited for: 17 -> 14; matrix products, arithmetic and copies ran while one was open for 12% -> 11% of each run, Pallas kernels for 0% -> 0%
where the time goes in v4:
time: 285 us; the launch traced here: 284 us
  waiting for transfers between devices  208 us (73%)
  matrix products  31.7 us (11%)
  between operations  14.8 us (5%)
  other arithmetic  14 us (5%)
  starting transfers between devices  10 us (4%)
  local copies, waits for them, and re-layouts  5.36 us (2%)
    ppermute x8, waiting for transfers between devices, shifted_2(): lax.ppermute(value, axis, [(i, (i + by) % count) for i in range(count)])  99.1 us
    reduce_scatter x4, waiting for transfers between devices, reduce(): lax.psum_scatter(partial, 'aux', scatter_dimension=0, tiled=True)  90.7 us
    all_gather x4, waiting for transfers between devices, amplitudes_of(): return lax.all_gather(amplitudes, 'aux', axis=0, tiled=True)  18.6 us
    dot_general x4, matrix products, paired_plan(): term = jnp.dot(gathered[c], blocks[c], preferred_element_type=jnp.float32)  16.5 us
    dot_general x4, matrix products, reduce(): jnp.einsum('aq,bq->ab', own, block, preferred_element_type=jnp.float32)  15.2 us
    ppermute x8, starting transfers between devices, shifted_2(): lax.ppermute(value, axis, [(i, (i + by) % count) for i in range(count)])  9.56 us
    convert_element_type x4, other arithmetic, amplitudes_of(): (summed / (pair_level - row_level[:, None] - col_level[None, :])).astype(...  7.58 us
  transfers between devices with their start and end apart: 16, of which 14 were waited for; matrix products, arithmetic and copies ran while one was open for 11% of the time, Pallas kernels for 0%

profile of v4, /device:TPU:1, one launch (start us, length us, event | category | flops | bytes accessed | tf_op | source)
XLA Modules:
  0.0 284.4 jit_solution(10130402411361232367)
XLA Ops:
  6.5 2.7 slice_bitcast_fusion
  9.2 3.1 %collective-permute-start.3 = (bf16[256,1024]{1,0:T(8,128)(2,1)S(1)}, bf16[256,1024]{1,0:T(8,128)(2,1)S(1)}, u32[]{:S(2)}, u32[]{:S(2)}) collective-permute-start(bf16[256,1024]{1,0:T(8,128)(2,1)S(1)} %get-tuple-element.41), channel_id=1, source_target_pairs={{0,16},{8,24},{16,0},{24,8},{1,17},{9,25},{17,1},{25,9},{2,18},{10... | collective-permute-start | bytes 1572872 | tf_op jit(solution)/shard_map/ppermute | solution.py:13
  12.4 22.9 %collective-permute-done.3 = bf16[256,1024]{1,0:T(8,128)(2,1)S(1)} collective-permute-done((bf16[256,1024]{1,0:T(8,128)(2,1)S(1)}, bf16[256,1024]{1,0:T(8,128)(2,1)S(1)}, u32[]{:S(2)}, u32[]{:S(2)}) %collective-permute-start.3) | collective-permute-done | bytes 524320 | tf_op jit(solution)/shard_map/ppermute | solution.py:13
  36.2 11.2 %collective-permute-done.4 = bf16[256,1024]{1,0:T(8,128)(2,1)S(1)} collective-permute-done((bf16[256,1024]{1,0:T(8,128)(2,1)S(1)}, bf16[256,1024]{1,0:T(8,128)(2,1)S(1)}, u32[]{:S(2)}, u32[]{:S(2)}) %collective-permute-start.4) | collective-permute-done | bytes 524320 | tf_op jit(solution)/shard_map/ppermute | solution.py:13
  47.5 12.8 %collective-permute-done.2 = bf16[256,1024]{1,0:T(8,128)(2,1)S(1)} collective-permute-done((bf16[256,1024]{1,0:T(8,128)(2,1)S(1)}, bf16[256,1024]{1,0:T(8,128)(2,1)S(1)}, u32[]{:S(2)}, u32[]{:S(2)}) %collective-permute-start.2) | collective-permute-done | bytes 524320 | tf_op jit(solution)/shard_map/ppermute | solution.py:13
  60.3 2.6 fusion.8
  65.7 8.4 %collective-permute-done.5 = bf16[256,1024]{1,0:T(8,128)(2,1)} collective-permute-done((bf16[256,1024]{1,0:T(8,128)(2,1)S(1)}, bf16[256,1024]{1,0:T(8,128)(2,1)}, u32[]{:S(2)}, u32[]{:S(2)}) %collective-permute-start.5) | collective-permute-done | bytes 524320 | tf_op jit(solution)/shard_map/ppermute | solution.py:13
  75.2 14.5 %collective-permute-done.1 = bf16[256,1024]{1,0:T(8,128)(2,1)S(1)} collective-permute-done((bf16[256,1024]{1,0:T(8,128)(2,1)}, bf16[256,1024]{1,0:T(8,128)(2,1)S(1)}, u32[]{:S(2)}, u32[]{:S(2)}) %collective-permute-start.1) | collective-permute-done | bytes 524320 | tf_op jit(solution)/shard_map/ppermute | solution.py:13
  89.7 4.4 %reduce-scatter.5.cloned.1.call-done = f32[256,512]{0,1:T(8,128)} async-done(((f32[1024,512]{0,1:T(8,128)}), f32[256,512]{0,1:T(8,128)}) %reduce-scatter.5.cloned.1.call-update) | async-done | bytes 524304 | tf_op jit(solution)/shard_map/reduce_scatter | solution.py:114
  94.1 1.9 divide_convert_fusion.3
  96.1 4.2 %fusion.11 = f32[1024,512]{0,1:T(8,128)} fusion(bf16[512,1024]{1,0:T(8,128)(2,1)S(1)} %pad_maximum_fusion.1, bf16[1,1024,1024]{2,1,0:T(8,128)(2,1)} %param.3), kind=kOutput, calls=%fused_computation.11 | convolution fusion | flops 1073741824 | bytes 5242880 | tf_op jit(solution)/shard_map/aq,bq->ab/dot_general | solution.py:111
  100.4 1.3 collective-permute-start.6
  101.6 2.1 collective-permute-start
  103.8 9.5 %collective-permute-done.6 = bf16[256,1024]{1,0:T(8,128)(2,1)S(1)} collective-permute-done((bf16[256,1024]{1,0:T(8,128)(2,1)S(1)}, bf16[256,1024]{1,0:T(8,128)(2,1)S(1)}, u32[]{:S(2)}, u32[]{:S(2)}) %collective-permute-start.6) | collective-permute-done | bytes 524320 | tf_op jit(solution)/shard_map/ppermute | solution.py:13
  114.4 12.6 %collective-permute-done = bf16[256,1024]{1,0:T(8,128)(2,1)} collective-permute-done((bf16[256,1024]{1,0:T(8,128)(2,1)}, bf16[256,1024]{1,0:T(8,128)(2,1)}, u32[]{:S(2)}, u32[]{:S(2)}) %collective-permute-start) | collective-permute-done | bytes 524320 | tf_op jit(solution)/shard_map/ppermute | solution.py:13
  127.0 20.2 %reduce-scatter.7.cloned.1.call-done = f32[256,512]{0,1:T(8,128)} async-done(((f32[1024,512]{0,1:T(8,128)}), f32[256,512]{0,1:T(8,128)}) %reduce-scatter.7.cloned.1.call-update) | async-done | bytes 524304 | tf_op jit(solution)/shard_map/reduce_scatter | solution.py:114
  147.2 1.9 divide_convert_fusion.2
  149.2 4.2 %fusion.14 = f32[1024,512]{0,1:T(8,128)} fusion(bf16[512,1024]{1,0:T(8,128)(2,1)S(1)} %pad_maximum_fusion.2, bf16[1,1024,1024]{2,1,0:T(8,128)(2,1)} %param.3), kind=kOutput, calls=%fused_computation.12 | convolution fusion | flops 1073741824 | bytes 5242880 | tf_op jit(solution)/shard_map/aq,bq->ab/dot_general | solution.py:111
  153.4 1.3 collective-permute-start.7
  154.7 4.5 %fusion.23 = f32[1024,1024]{1,0:T(8,128)} fusion(bf16[1024,512]{0,1:T(8,128)(2,1)} %all-gather.5.cloned.1.call-done, bf16[512,1024]{1,0:T(8,128)(2,1)S(1)} %pad_maximum_fusion), kind=kOutput, calls=%fused_computation.34 | convolution fusion | flops 1073741824 | bytes 6291456 | tf_op jit(solution)/shard_map/dot_general | solution.py:174
  159.2 7.3 %collective-permute-done.7 = bf16[256,1024]{1,0:T(8,128)(2,1)S(1)} collective-permute-done((bf16[256,1024]{1,0:T(8,128)(2,1)}, bf16[256,1024]{1,0:T(8,128)(2,1)S(1)}, u32[]{:S(2)}, u32[]{:S(2)}) %collective-permute-start.7) | collective-permute-done | bytes 524320 | tf_op jit(solution)/shard_map/ppermute | solution.py:13
  167.6 32.3 %reduce-scatter.9.cloned.1.call-done = f32[256,512]{0,1:T(8,128)} async-done(((f32[1024,512]{0,1:T(8,128)}), f32[256,512]{0,1:T(8,128)}) %reduce-scatter.9.cloned.1.call-update) | async-done | bytes 524304 | tf_op jit(solution)/shard_map/reduce_scatter | solution.py:114
  200.0 1.9 divide_convert_fusion.1
  202.0 4.2 %fusion.17 = f32[1024,512]{0,1:T(8,128)} fusion(bf16[512,1024]{1,0:T(8,128)(2,1)S(1)} %pad_maximum_fusion.3, bf16[1,1024,1024]{2,1,0:T(8,128)(2,1)} %param.3), kind=kOutput, calls=%fused_computation.13 | convolution fusion | flops 1073741824 | bytes 5242880 | tf_op jit(solution)/shard_map/aq,bq->ab/dot_general | solution.py:111
  207.4 1.3 fusion.24
  209.7 2.9 %add.120 = f32[1024,1024]{1,0:T(8,128)} add(f32[1024,1024]{1,0:T(8,128)S(1)} %copy-done, f32[1024,1024]{1,0:T(8,128)S(1)} %fusion.24) | non-fusion elementwise | flops 1048576 | bytes 12582912 | tf_op jit(solution)/shard_map/add | solution.py:175
  212.6 6.7 %all-gather.9.cloned.1.call-done = bf16[1024,512]{0,1:T(8,128)(2,1)} async-done(((bf16[256,512]{0,1:T(8,128)(2,1)}), bf16[1024,512]{0,1:T(8,128)(2,1)}) %all-gather.9.cloned.1.call-update) | async-done | bytes 1048592 | tf_op jit(solution)/shard_map/all_gather | solution.py:123
  219.3 33.7 %reduce-scatter.11.cloned.1.call-done = f32[256,512]{0,1:T(8,128)} async-done(((f32[1024,512]{0,1:T(8,128)}), f32[256,512]{0,1:T(8,128)}) %reduce-scatter.11.cloned.1.call-update) | async-done | bytes 524304 | tf_op jit(solution)/shard_map/reduce_scatter | solution.py:114
  253.1 1.9 divide_convert_fusion
  255.0 5.5 %convolution_add_fusion = f32[1024,1024]{1,0:T(8,128)} fusion(f32[1024,1024]{1,0:T(8,128)} %add.120, bf16[1024,512]{0,1:T(8,128)(2,1)S(1)} %copy-done.1, bf16[512,1024]{1,0:T(8,128)(2,1)S(1)} %pad_maximum_fusion.2), kind=kOutput, calls=%fused_computation.1 | convolution fusion | flops 1074790400 | bytes 10485760 | tf_op jit(solution)/shard_map/dot_general | solution.py:174
  260.5 11.9 %all-gather.11.cloned.1.call-done = bf16[1024,512]{0,1:T(8,128)(2,1)} async-done(((bf16[256,512]{0,1:T(8,128)(2,1)}), bf16[1024,512]{0,1:T(8,128)(2,1)}) %all-gather.11.cloned.1.call-update) | async-done | bytes 1048592 | tf_op jit(solution)/shard_map/all_gather | solution.py:123
  272.4 5.1 %fusion.20 = bf16[1,1024,1024]{2,1,0:T(8,128)(2,1)} fusion(f32[1024,1024]{1,0:T(8,128)} %convolution_add_fusion, bf16[1024,512]{0,1:T(8,128)(2,1)} %all-gather.11.cloned.1.call-done, bf16[512,1024]{1,0:T(8,128)(2,1)S(1)} %copy-done.5), kind=kOutput, calls=%fused_computation.14 | convolution fusion | flops 1076887552 | bytes 8388608 | tf_op jit(solution)/shard_map/dot_general | solution.py:174
  (50 shorter events, 8.6 us)
Async XLA Ops:
  6.5 87.6 %reduce-scatter.5.cloned.1.call-start = ((), (), s32[]{:S(2)}) async-start(), calls=%async_computation.4 | async-start | bytes 2621440 | tf_op jit(solution)/shard_map/reduce_scatter | solution.py:114
  9.2 51.1 %copy-start.2 = (bf16[1,1024,1024]{2,1,0:T(8,128)(2,1)S(1)}, bf16[1,1024,1024]{2,1,0:T(8,128)(2,1)}, u32[]{:S(2)}) copy-start(bf16[1,1024,1024]{2,1,0:T(8,128)(2,1)} %param.3) | copy-start | bytes 6291460
  9.2 26.0 %collective-permute-start.3 = (bf16[256,1024]{1,0:T(8,128)(2,1)S(1)}, bf16[256,1024]{1,0:T(8,128)(2,1)S(1)}, u32[]{:S(2)}, u32[]{:S(2)}) collective-permute-start(bf16[256,1024]{1,0:T(8,128)(2,1)S(1)} %get-tuple-element.41), channel_id=1, source_target_pairs={{0,16},{8,24},{16,0},{24,8},{1,17},{9,25},{17,1},{25,9},{2,18},{10... | collective-permute-start | bytes 1572872 | tf_op jit(solution)/shard_map/ppermute | solution.py:13
  35.2 12.2 %collective-permute-start.4 = (bf16[256,1024]{1,0:T(8,128)(2,1)S(1)}, bf16[256,1024]{1,0:T(8,128)(2,1)S(1)}, u32[]{:S(2)}, u32[]{:S(2)}) collective-permute-start(bf16[256,1024]{1,0:T(8,128)(2,1)S(1)} %collective-permute-done.3), channel_id=1, source_target_pairs={{0,1},{1,0},{2,3},{3,2},{4,5},{5,4},{6,7},{7,6},{8,9},{9,8},{10,11... | collective-permute-start | bytes 1572872 | tf_op jit(solution)/shard_map/ppermute | solution.py:13
  36.2 24.0 %collective-permute-start.2 = (bf16[256,1024]{1,0:T(8,128)(2,1)S(1)}, bf16[256,1024]{1,0:T(8,128)(2,1)S(1)}, u32[]{:S(2)}, u32[]{:S(2)}) collective-permute-start(bf16[256,1024]{1,0:T(8,128)(2,1)S(1)} %get-tuple-element.42), channel_id=1, source_target_pairs={{0,16},{8,24},{16,0},{24,8},{1,17},{9,25},{17,1},{25,9},{2,18},{10... | collective-permute-start | bytes 1572872 | tf_op jit(solution)/shard_map/ppermute | solution.py:13
  62.9 0.9 copy-start.8
  62.9 2.7 copy-start.7
  62.9 64.1 %all-gather.5.cloned.1.call-start = ((), (), s32[]{:S(2)}) async-start(), calls=%async_computation.5 | async-start | bytes 1310720 | tf_op jit(solution)/shard_map/all_gather | solution.py:123
  63.0 11.1 %collective-permute-start.5 = (bf16[256,1024]{1,0:T(8,128)(2,1)S(1)}, bf16[256,1024]{1,0:T(8,128)(2,1)}, u32[]{:S(2)}, u32[]{:S(2)}) collective-permute-start(bf16[256,1024]{1,0:T(8,128)(2,1)S(1)} %collective-permute-done.2), channel_id=1, source_target_pairs={{0,1},{1,0},{2,3},{3,2},{4,5},{5,4},{6,7},{7,6},{8,9},{9,8},{10,11... | collective-permute-start | bytes 1572872 | tf_op jit(solution)/shard_map/ppermute | solution.py:13
  63.8 25.9 %collective-permute-start.1 = (bf16[256,1024]{1,0:T(8,128)(2,1)}, bf16[256,1024]{1,0:T(8,128)(2,1)S(1)}, u32[]{:S(2)}, u32[]{:S(2)}) collective-permute-start(bf16[256,1024]{1,0:T(8,128)(2,1)} %get-tuple-element.43), channel_id=1, source_target_pairs={{0,16},{8,24},{16,0},{24,8},{1,17},{9,25},{17,1},{25,9},{2,18},{10... | collective-permute-start | bytes 1572872 | tf_op jit(solution)/shard_map/ppermute | solution.py:13
  89.7 10.7 %copy-start.6 = (bf16[256,1024]{1,0:T(8,128)(2,1)}, bf16[256,1024]{1,0:T(8,128)(2,1)S(1)}, u32[]{:S(2)}) copy-start(bf16[256,1024]{1,0:T(8,128)(2,1)S(1)} %collective-permute-done.1) | copy-start | bytes 1572868
  96.0 51.1 %reduce-scatter.7.cloned.1.call-start = ((), (), s32[]{:S(2)}) async-start(), calls=%async_computation.6 | async-start | bytes 2621440 | tf_op jit(solution)/shard_map/reduce_scatter | solution.py:114
  100.3 67.3 %all-gather.7.cloned.1.call-start = ((), (), s32[]{:S(2)}) async-start(), calls=%async_computation.7 | async-start | bytes 1310720 | tf_op jit(solution)/shard_map/all_gather | solution.py:123
  100.4 12.9 %collective-permute-start.6 = (bf16[256,1024]{1,0:T(8,128)(2,1)S(1)}, bf16[256,1024]{1,0:T(8,128)(2,1)S(1)}, u32[]{:S(2)}, u32[]{:S(2)}) collective-permute-start(bf16[256,1024]{1,0:T(8,128)(2,1)S(1)} %collective-permute-done.1), channel_id=1, source_target_pairs={{0,1},{1,0},{2,3},{3,2},{4,5},{5,4},{6,7},{7,6},{8,9},{9,8},{10,11... | collective-permute-start | bytes 1572872 | tf_op jit(solution)/shard_map/ppermute | solution.py:13
  101.6 25.3 %collective-permute-start = (bf16[256,1024]{1,0:T(8,128)(2,1)}, bf16[256,1024]{1,0:T(8,128)(2,1)}, u32[]{:S(2)}, u32[]{:S(2)}) collective-permute-start(bf16[256,1024]{1,0:T(8,128)(2,1)} %get-tuple-element.44), channel_id=1, source_target_pairs={{0,16},{8,24},{16,0},{24,8},{1,17},{9,25},{17,1},{25,9},{2,18},{10... | collective-permute-start | bytes 1572872 | tf_op jit(solution)/shard_map/ppermute | solution.py:13
  149.1 50.9 %reduce-scatter.9.cloned.1.call-start = ((), (), s32[]{:S(2)}) async-start(), calls=%async_computation.8 | async-start | bytes 2621440 | tf_op jit(solution)/shard_map/reduce_scatter | solution.py:114
  153.4 66.0 %all-gather.9.cloned.1.call-start = ((), (), s32[]{:S(2)}) async-start(), calls=%async_computation.9 | async-start | bytes 1310720 | tf_op jit(solution)/shard_map/all_gather | solution.py:123
  153.4 13.1 %collective-permute-start.7 = (bf16[256,1024]{1,0:T(8,128)(2,1)}, bf16[256,1024]{1,0:T(8,128)(2,1)S(1)}, u32[]{:S(2)}, u32[]{:S(2)}) collective-permute-start(bf16[256,1024]{1,0:T(8,128)(2,1)} %collective-permute-done), channel_id=1, source_target_pairs={{0,1},{1,0},{2,3},{3,2},{4,5},{5,4},{6,7},{7,6},{8,9},{9,8},{10,11... | collective-permute-start | bytes 1572872 | tf_op jit(solution)/shard_map/ppermute | solution.py:13
  167.6 34.4 %copy-start.4 = (bf16[512,1024]{1,0:T(8,128)(2,1)}, bf16[512,1024]{1,0:T(8,128)(2,1)S(1)}, u32[]{:S(2)}) copy-start(bf16[512,1024]{1,0:T(8,128)(2,1)S(1)} %pad_maximum_fusion.3) | copy-start | bytes 3145732
  201.9 51.2 %reduce-scatter.11.cloned.1.call-start = ((), (), s32[]{:S(2)}) async-start(), calls=%async_computation.10 | async-start | bytes 2621440 | tf_op jit(solution)/shard_map/reduce_scatter | solution.py:114
  206.2 1.2 copy-start.3
  206.2 66.2 %all-gather.11.cloned.1.call-start = ((), (), s32[]{:S(2)}) async-start(), calls=%async_computation.11 | async-start | bytes 1310720 | tf_op jit(solution)/shard_map/all_gather | solution.py:123
  207.4 2.3 copy-start
  219.3 35.6 %copy-start.1 = (bf16[1024,512]{0,1:T(8,128)(2,1)S(1)}, bf16[1024,512]{0,1:T(8,128)(2,1)}, u32[]{:S(2)}) copy-start(bf16[1024,512]{0,1:T(8,128)(2,1)} %all-gather.9.cloned.1.call-done) | copy-start | bytes 3145732
  255.0 17.4 %copy-start.5 = (bf16[512,1024]{1,0:T(8,128)(2,1)S(1)}, bf16[512,1024]{1,0:T(8,128)(2,1)}, u32[]{:S(2)}) copy-start(bf16[512,1024]{1,0:T(8,128)(2,1)} %copy-done.4) | copy-start | bytes 3145732
Sparse Core Ops, SparseCore 0:
  63.0 31.0 reduce-scatter.4
  96.2 17.2 all-gather.4
  116.1 31.0 reduce-scatter.6
  149.2 17.2 all-gather.6
  168.9 31.0 reduce-scatter.8
  202.0 17.2 all-gather.8
  222.0 31.0 reduce-scatter.10
  255.1 17.2 all-gather.10

commit v5 on v1

--- a/solution.py
+++ b/solution.py
@@ -5,6 +5,7 @@
 
 CHUNKS = 4
 AUX_BY_PERMUTE = True
+NARROW_FAR = False
 
 
 def shifted_2(value, axis, by):
@@ -61,7 +62,10 @@
         bit = (k // step) % 2
         keep = lax.dynamic_slice_in_dim(x, bit * half, half, 0)
         send = lax.dynamic_slice_in_dim(x, (1 - bit) * half, half, 0)
-        x = keep + lax.ppermute(send, "aux", xor_pairs(count, step))
+        if step > 1 and NARROW_FAR:
+            x = keep + lax.ppermute(send.astype(jnp.bfloat16), "aux", xor_pairs(count, step))
+        else:
+            x = keep + lax.ppermute(send, "aux", xor_pairs(count, step))
         first = first + bit * half
         step *= 2
     return x, first
@@ -96,6 +100,7 @@
 
     total = None
     previous = None
+    rows_done = None
     for c in range(CHUNKS):
         piece = own[c * width:(c + 1) * width]
         if previous is not None:
@@ -118,6 +123,8 @@
         else:
             summed = lax.psum_scatter(partial, "aux", scatter_dimension=0, tiled=True)
             first = first_row
+        if rows_done is not None:
+            summed, _ = lax.optimization_barrier((summed, rows_done))
         row_level = lax.dynamic_slice_in_dim(vir_energy, vir_pos * vir_rows + first, share)
         amplitudes = (summed / (pair_level - row_level[:, None] - col_level[None, :])).astype(
             jnp.bfloat16
@@ -126,6 +133,7 @@
             rows = aux_all_gather(amplitudes)
         else:
             rows = lax.all_gather(amplitudes, "aux", axis=0, tiled=True)
+        rows_done = rows
         term = jnp.dot(rows, block, preferred_element_type=jnp.float32)
         total = term if total is None else total + term
     gamma_own = total

time: 206 us -> 176 us (0.85)
  waiting for transfers between devices: 148 us -> 109 us
  starting transfers between devices: 25.2 us -> 37.9 us
  local copies, waits for them, and re-layouts: 11.5 us -> 8.45 us
    ppermute x8, waiting for transfers between devices: 38.2 us -> 13.9 us  [aux_reduce_scatter(): x = keep + lax.ppermute(send, 'aux', xor_pairs(count, step))]
    ppermute x8, starting transfers between devices: 9.98 us -> 22.9 us  [aux_all_gather(): other = lax.ppermute(x, 'aux', xor_pairs(count, step))]
    ppermute x8, waiting for transfers between devices: 95.8 us -> 86.7 us  [shifted_2(): lax.ppermute(value, axis, [(i, (i + by) % count) for i in range(count)])]
    ppermute x8, waiting for transfers between devices: 13.6 us -> 8.3 us  [aux_all_gather(): other = lax.ppermute(x, 'aux', xor_pairs(count, step))]
    convert_element_type x1 -> x4, other arithmetic: 2.89 us -> 0.57 us  [paired_plan(): (summed / (pair_level - row_level[:, None] - col_level[None, :])).astype(...]
    dynamic_slice x8, local copies, waits for them, and re-layouts: 3.83 us -> 1.53 us  [aux_reduce_scatter(): send = lax.dynamic_slice_in_dim(x, (1 - bit) * half, half, 0)]
  transfers between devices with their start and end apart: 24 -> 24, of which waited for: 12 -> 12; matrix products, arithmetic and copies ran while one was open for 10% -> 11% of each run, Pallas kernels for 0% -> 0%
where the time goes in v5:
time: 176 us; the launch traced here: 175 us
  waiting for transfers between devices  109 us (62%)
  starting transfers between devices  37.9 us (22%)
  matrix products  14 us (8%)
  local copies, waits for them, and re-layouts  8.45 us (5%)
  other arithmetic  4.46 us (3%)
    ppermute x8, waiting for transfers between devices, shifted_2(): lax.ppermute(value, axis, [(i, (i + by) % count) for i in range(count)])  86.7 us
    ppermute x8, starting transfers between devices, aux_all_gather(): other = lax.ppermute(x, 'aux', xor_pairs(count, step))  22.9 us
    ppermute x8, waiting for transfers between devices, aux_reduce_scatter(): x = keep + lax.ppermute(send, 'aux', xor_pairs(count, step))  13.9 us
    ppermute x8, starting transfers between devices, aux_reduce_scatter(): x = keep + lax.ppermute(send, 'aux', xor_pairs(count, step))  8.82 us
    ppermute x8, waiting for transfers between devices, aux_all_gather(): other = lax.ppermute(x, 'aux', xor_pairs(count, step))  8.3 us
    dot_general x4, matrix products, paired_plan(): term = jnp.dot(rows, block, preferred_element_type=jnp.float32)  7.22 us
    dot_general x4, matrix products, paired_plan(): jnp.einsum('aq,bq->ab', own, block, preferred_element_type=jnp.float32)  6.73 us
    ppermute x8, starting transfers between devices, shifted_2(): lax.ppermute(value, axis, [(i, (i + by) % count) for i in range(count)])  6.26 us
  transfers between devices with their start and end apart: 24, of which 12 were waited for; matrix products, arithmetic and copies ran while one was open for 11% of the time, Pallas kernels for 0%

profile of v5, /device:TPU:1, one launch (start us, length us, event | category | flops | bytes accessed | tf_op | source)
XLA Modules:
  0.0 175.2 jit_solution(4197749450663393195)
XLA Ops:
  0.0 2.7 %slice_bitcast_fusion = (bf16[256,1024]{1,0:T(8,128)(2,1)}, bf16[256,1024]{1,0:T(8,128)(2,1)S(1)}, bf16[256,1024]{1,0:T(8,128)(2,1)S(1)}, bf16[256,1024]{1,0:T(8,128)(2,1)}) fusion(bf16[1,1024,1024]{2,1,0:T(8,128)(2,1)} %param.3), kind=kLoop, calls=%fused_computation.35 | loop fusion | bytes 4194304 | tf_op jit(solution)/shard_map/slice | solution.py:105
  2.7 3.1 %collective-permute-start = (bf16[256,1024]{1,0:T(8,128)(2,1)S(1)}, bf16[256,1024]{1,0:T(8,128)(2,1)S(1)}, u32[]{:S(2)}, u32[]{:S(2)}) collective-permute-start(bf16[256,1024]{1,0:T(8,128)(2,1)S(1)} %get-tuple-element.19), channel_id=1, source_target_pairs={{0,16},{8,24},{16,0},{24,8},{1,17},{9,25},{17,1},{25,9},{2,18},{10... | collective-permute-start | bytes 1572872 | tf_op jit(solution)/shard_map/ppermute | solution.py:13
  5.9 22.9 %collective-permute-done = bf16[256,1024]{1,0:T(8,128)(2,1)S(1)} collective-permute-done((bf16[256,1024]{1,0:T(8,128)(2,1)S(1)}, bf16[256,1024]{1,0:T(8,128)(2,1)S(1)}, u32[]{:S(2)}, u32[]{:S(2)}) %collective-permute-start) | collective-permute-done | bytes 524320 | tf_op jit(solution)/shard_map/ppermute | solution.py:13
  31.7 21.5 %collective-permute-done.6 = bf16[256,1024]{1,0:T(8,128)(2,1)} collective-permute-done((bf16[256,1024]{1,0:T(8,128)(2,1)S(1)}, bf16[256,1024]{1,0:T(8,128)(2,1)}, u32[]{:S(2)}, u32[]{:S(2)}) %collective-permute-start.6) | collective-permute-done | bytes 524320 | tf_op jit(solution)/shard_map/ppermute | solution.py:13
  54.0 2.9 %fusion.7 = f32[512,1024]{1,0:T(8,128)S(1)} fusion(bf16[512,1024]{1,0:T(8,128)(2,1)S(1)} %constant_dynamic-update-slice_fusion, bf16[1,1024,1024]{2,1,0:T(8,128)(2,1)} %param.3), kind=kOutput, calls=%fused_computation.8 | convolution fusion | flops 1073741824 | bytes 5242880 | tf_op jit(solution)/shard_map/aq,bq->ab/dot_general | solution.py:120
  57.9 2.7 %collective-permute-start.2 = (f32[512,512]{0,1:T(8,128)}, f32[512,512]{0,1:T(8,128)}, u32[]{:S(2)}, u32[]{:S(2)}) collective-permute-start(f32[512,512]{0,1:T(8,128)} %dynamic-slice_bitcast_fusion.3), channel_id=1, source_target_pairs={{0,2},{2,0},{4,6},{6,4},{1,3},{3,1},{5,7},{7,5},{8,10},{10,8},{12,... | collective-permute-start | bytes 3145736 | tf_op jit(solution)/shard_map/ppermute | solution.py:68
  61.9 17.4 %collective-permute-done.12 = bf16[256,1024]{1,0:T(8,128)(2,1)} collective-permute-done((bf16[256,1024]{1,0:T(8,128)(2,1)}, bf16[256,1024]{1,0:T(8,128)(2,1)}, u32[]{:S(2)}, u32[]{:S(2)}) %collective-permute-start.12) | collective-permute-done | bytes 524320 | tf_op jit(solution)/shard_map/ppermute | solution.py:13
  80.4 1.3 fusion.5
  84.4 1.4 bitcast_add_fusion.3
  87.2 9.1 %collective-permute-done.13 = bf16[256,1024]{1,0:T(8,128)(2,1)S(1)} collective-permute-done((bf16[256,1024]{1,0:T(8,128)(2,1)}, bf16[256,1024]{1,0:T(8,128)(2,1)S(1)}, u32[]{:S(2)}, u32[]{:S(2)}) %collective-permute-start.13) | collective-permute-done | bytes 524320 | tf_op jit(solution)/shard_map/ppermute | solution.py:13
  96.3 1.3 fusion.3
  98.6 5.6 %collective-permute-done.18 = bf16[256,1024]{1,0:T(8,128)(2,1)S(1)} collective-permute-done((bf16[256,1024]{1,0:T(8,128)(2,1)}, bf16[256,1024]{1,0:T(8,128)(2,1)S(1)}, u32[]{:S(2)}, u32[]{:S(2)}) %collective-permute-start.18) | collective-permute-done | bytes 524320 | tf_op jit(solution)/shard_map/ppermute | solution.py:13
  107.0 10.2 %collective-permute-done.19 = bf16[256,1024]{1,0:T(8,128)(2,1)S(1)} collective-permute-done((bf16[256,1024]{1,0:T(8,128)(2,1)S(1)}, bf16[256,1024]{1,0:T(8,128)(2,1)S(1)}, u32[]{:S(2)}, u32[]{:S(2)}) %collective-permute-start.19) | collective-permute-done | bytes 524320 | tf_op jit(solution)/shard_map/ppermute | solution.py:13
  117.3 1.3 fusion.1
  118.7 1.4 collective-permute-start.5
  120.3 3.2 %collective-permute-done.9 = f32[256,512]{0,1:T(8,128)S(1)} collective-permute-done((f32[256,512]{0,1:T(8,128)S(1)}, f32[256,512]{0,1:T(8,128)S(1)}, u32[]{:S(2)}, u32[]{:S(2)}) %collective-permute-start.9) | collective-permute-done | bytes 524320 | tf_op jit(solution)/shard_map/ppermute | solution.py:68
  124.1 1.3 collective-permute-start.10
  125.8 2.3 %collective-permute-start.20 = (f32[512,512]{0,1:T(8,128)S(1)}, f32[512,512]{0,1:T(8,128)S(1)}, u32[]{:S(2)}, u32[]{:S(2)}) collective-permute-start(f32[512,512]{0,1:T(8,128)S(1)} %dynamic-slice_bitcast_fusion), channel_id=1, source_target_pairs={{0,2},{2,0},{4,6},{6,4},{1,3},{3,1},{5,7},{7,5},{8,10},{10,8},{12,... | collective-permute-start | bytes 3145736 | tf_op jit(solution)/shard_map/ppermute | solution.py:68
  128.1 2.2 %collective-permute-done.10 = bf16[256,512]{0,1:T(8,128)(2,1)S(1)} collective-permute-done((bf16[256,512]{0,1:T(8,128)(2,1)S(1)}, bf16[256,512]{0,1:T(8,128)(2,1)S(1)}, u32[]{:S(2)}, u32[]{:S(2)}) %collective-permute-start.10) | collective-permute-done | bytes 262176 | tf_op jit(solution)/shard_map/ppermute | solution.py:80
  130.4 4.8 %collective-permute-start.11 = (bf16[512,512]{0,1:T(8,128)(2,1)S(1)}, bf16[512,512]{0,1:T(8,128)(2,1)S(1)}, u32[]{:S(2)}, u32[]{:S(2)}) collective-permute-start(bf16[512,512]{0,1:T(8,128)(2,1)S(1)} %maximum_select_fusion.8), channel_id=1, source_target_pairs={{0,2},{2,0},{4,6},{6,4},{1,3},{3,1},{5,7},{7,5},{8,10},{10,8},{12,... | collective-permute-start | bytes 1572872 | tf_op jit(solution)/shard_map/ppermute | solution.py:80
  135.2 6.3 %collective-permute-done.15 = f32[256,512]{0,1:T(8,128)S(1)} collective-permute-done((f32[256,512]{0,1:T(8,128)S(1)}, f32[256,512]{0,1:T(8,128)S(1)}, u32[]{:S(2)}, u32[]{:S(2)}) %collective-permute-start.15) | collective-permute-done | bytes 524320 | tf_op jit(solution)/shard_map/ppermute | solution.py:68
  142.1 1.3 collective-permute-start.16
  143.9 3.4 %collective-permute-done.16 = bf16[256,512]{0,1:T(8,128)(2,1)S(1)} collective-permute-done((bf16[256,512]{0,1:T(8,128)(2,1)S(1)}, bf16[256,512]{0,1:T(8,128)(2,1)S(1)}, u32[]{:S(2)}, u32[]{:S(2)}) %collective-permute-start.16) | collective-permute-done | bytes 262176 | tf_op jit(solution)/shard_map/ppermute | solution.py:80
  147.5 6.7 %collective-permute-start.17 = (bf16[512,512]{0,1:T(8,128)(2,1)S(1)}, bf16[512,512]{0,1:T(8,128)(2,1)S(1)}, u32[]{:S(2)}, u32[]{:S(2)}) collective-permute-start(bf16[512,512]{0,1:T(8,128)(2,1)S(1)} %maximum_select_fusion.9), channel_id=1, source_target_pairs={{0,2},{2,0},{4,6},{6,4},{1,3},{3,1},{5,7},{7,5},{8,10},{10,8},{12,... | collective-permute-start | bytes 1572872 | tf_op jit(solution)/shard_map/ppermute | solution.py:80
  154.2 4.4 %collective-permute-done.21 = f32[256,512]{0,1:T(8,128)S(1)} collective-permute-done((f32[256,512]{0,1:T(8,128)S(1)}, f32[256,512]{0,1:T(8,128)S(1)}, u32[]{:S(2)}, u32[]{:S(2)}) %collective-permute-start.21) | collective-permute-done | bytes 524320 | tf_op jit(solution)/shard_map/ppermute | solution.py:68
  159.2 1.3 collective-permute-start.22
  160.5 1.3 fusion.19
  161.8 2.7 %collective-permute-done.22 = bf16[256,512]{0,1:T(8,128)(2,1)S(1)} collective-permute-done((bf16[256,512]{0,1:T(8,128)(2,1)S(1)}, bf16[256,512]{0,1:T(8,128)(2,1)S(1)}, u32[]{:S(2)}, u32[]{:S(2)}) %collective-permute-start.22) | collective-permute-done | bytes 262176 | tf_op jit(solution)/shard_map/ppermute | solution.py:80
  164.6 4.7 %collective-permute-start.23 = (bf16[512,512]{0,1:T(8,128)(2,1)S(1)}, bf16[512,512]{0,1:T(8,128)(2,1)S(1)}, u32[]{:S(2)}, u32[]{:S(2)}) collective-permute-start(bf16[512,512]{0,1:T(8,128)(2,1)S(1)} %maximum_select_fusion.10), channel_id=1, source_target_pairs={{0,2},{2,0},{4,6},{6,4},{1,3},{3,1},{5,7},{7,5},{8,10},{10,8},{12,... | collective-permute-start | bytes 1572872 | tf_op jit(solution)/shard_map/ppermute | solution.py:80
  169.3 1.5 fusion.20
  170.8 1.3 fusion.21
  172.1 3.1 %fusion = bf16[1,1024,1024]{2,1,0:T(8,128)(2,1)} fusion(f32[1024,1024]{1,0:T(8,128)S(1)} %fusion.21, f32[1024,1024]{1,0:T(8,128)S(1)} %fusion.19, f32[1024,1024]{1,0:T(8,128)S(1)} %fusion.20, bf16[512,1024]{1,0:T(8,128)(2,1)S(1)} %constant_dynamic-update-slice_fusion.6, bf16[512,512]{0,1:T(8,128)(2,1)S(1)} %collective-permute-done.23, ...), kind=kOutput, calls=%fused_computation.1 | convolution fusion | flops 1083703296 | bytes 16777216 | tf_op jit(solution)/shard_map/dot_general | solution.py:137
  (71 shorter events, 17.0 us)
Async XLA Ops:
  0.0 29.8 %copy-start.2 = (f32[4]{0:T(128)S(1)}, f32[4]{0:T(128)}, u32[]{:S(2)}) copy-start(f32[4]{0:T(128)} %param.4) | copy-start | bytes 52
  0.0 31.6 %copy-start.1 = (f32[2048]{0:T(1024)S(1)}, f32[2048]{0:T(1024)}, u32[]{:S(2)}) copy-start(f32[2048]{0:T(1024)} %param.5) | copy-start | bytes 24580
  2.7 26.0 %collective-permute-start = (bf16[256,1024]{1,0:T(8,128)(2,1)S(1)}, bf16[256,1024]{1,0:T(8,128)(2,1)S(1)}, u32[]{:S(2)}, u32[]{:S(2)}) collective-permute-start(bf16[256,1024]{1,0:T(8,128)(2,1)S(1)} %get-tuple-element.19), channel_id=1, source_target_pairs={{0,16},{8,24},{16,0},{24,8},{1,17},{9,25},{17,1},{25,9},{2,18},{10... | collective-permute-start | bytes 1572872 | tf_op jit(solution)/shard_map/ppermute | solution.py:13
  28.8 24.4 %collective-permute-start.6 = (bf16[256,1024]{1,0:T(8,128)(2,1)S(1)}, bf16[256,1024]{1,0:T(8,128)(2,1)}, u32[]{:S(2)}, u32[]{:S(2)}) collective-permute-start(bf16[256,1024]{1,0:T(8,128)(2,1)S(1)} %get-tuple-element.11), channel_id=1, source_target_pairs={{0,16},{8,24},{16,0},{24,8},{1,17},{9,25},{17,1},{25,9},{2,18},{10... | collective-permute-start | bytes 1572872 | tf_op jit(solution)/shard_map/ppermute | solution.py:13
  28.8 25.1 %collective-permute-start.1 = (bf16[256,1024]{1,0:T(8,128)(2,1)S(1)}, bf16[256,1024]{1,0:T(8,128)(2,1)S(1)}, u32[]{:S(2)}, u32[]{:S(2)}) collective-permute-start(bf16[256,1024]{1,0:T(8,128)(2,1)S(1)} %collective-permute-done), channel_id=1, source_target_pairs={{0,1},{1,0},{2,3},{3,2},{4,5},{5,4},{6,7},{7,6},{8,9},{9,8},{10,11... | collective-permute-start | bytes 1572872 | tf_op jit(solution)/shard_map/ppermute | solution.py:13
  53.2 26.1 %collective-permute-start.12 = (bf16[256,1024]{1,0:T(8,128)(2,1)}, bf16[256,1024]{1,0:T(8,128)(2,1)}, u32[]{:S(2)}, u32[]{:S(2)}) collective-permute-start(bf16[256,1024]{1,0:T(8,128)(2,1)} %get-tuple-element.13), channel_id=1, source_target_pairs={{0,16},{8,24},{16,0},{24,8},{1,17},{9,25},{17,1},{25,9},{2,18},{10... | collective-permute-start | bytes 1572872 | tf_op jit(solution)/shard_map/ppermute | solution.py:13
  53.2 26.1 %collective-permute-start.7 = (bf16[256,1024]{1,0:T(8,128)(2,1)}, bf16[256,1024]{1,0:T(8,128)(2,1)}, u32[]{:S(2)}, u32[]{:S(2)}) collective-permute-start(bf16[256,1024]{1,0:T(8,128)(2,1)} %collective-permute-done.6), channel_id=1, source_target_pairs={{0,1},{1,0},{2,3},{3,2},{4,5},{5,4},{6,7},{7,6},{8,9},{9,8},{10,11... | collective-permute-start | bytes 1572872 | tf_op jit(solution)/shard_map/ppermute | solution.py:13
  57.9 26.5 %collective-permute-start.2 = (f32[512,512]{0,1:T(8,128)}, f32[512,512]{0,1:T(8,128)}, u32[]{:S(2)}, u32[]{:S(2)}) collective-permute-start(f32[512,512]{0,1:T(8,128)} %dynamic-slice_bitcast_fusion.3), channel_id=1, source_target_pairs={{0,2},{2,0},{4,6},{6,4},{1,3},{3,1},{5,7},{7,5},{8,10},{10,8},{12,... | collective-permute-start | bytes 3145736 | tf_op jit(solution)/shard_map/ppermute | solution.py:68
  60.6 19.8 %copy-start = (bf16[1,1024,1024]{2,1,0:T(8,128)(2,1)S(1)}, bf16[1,1024,1024]{2,1,0:T(8,128)(2,1)}, u32[]{:S(2)}) copy-start(bf16[1,1024,1024]{2,1,0:T(8,128)(2,1)} %param.3) | copy-start | bytes 6291460
  79.3 24.9 %collective-permute-start.18 = (bf16[256,1024]{1,0:T(8,128)(2,1)}, bf16[256,1024]{1,0:T(8,128)(2,1)S(1)}, u32[]{:S(2)}, u32[]{:S(2)}) collective-permute-start(bf16[256,1024]{1,0:T(8,128)(2,1)} %get-tuple-element.15), channel_id=1, source_target_pairs={{0,16},{8,24},{16,0},{24,8},{1,17},{9,25},{17,1},{25,9},{2,18},{10... | collective-permute-start | bytes 1572872 | tf_op jit(solution)/shard_map/ppermute | solution.py:13
  81.8 24.6 %collective-permute-start.8 = (f32[512,512]{0,1:T(8,128)S(1)}, f32[512,512]{0,1:T(8,128)S(1)}, u32[]{:S(2)}, u32[]{:S(2)}) collective-permute-start(f32[512,512]{0,1:T(8,128)S(1)} %dynamic-slice_bitcast_fusion.2), channel_id=1, source_target_pairs={{0,2},{2,0},{4,6},{6,4},{1,3},{3,1},{5,7},{7,5},{8,10},{10,8},{12,... | collective-permute-start | bytes 3145736 | tf_op jit(solution)/shard_map/ppermute | solution.py:68
  82.6 13.7 %collective-permute-start.13 = (bf16[256,1024]{1,0:T(8,128)(2,1)}, bf16[256,1024]{1,0:T(8,128)(2,1)S(1)}, u32[]{:S(2)}, u32[]{:S(2)}) collective-permute-start(bf16[256,1024]{1,0:T(8,128)(2,1)} %collective-permute-done.12), channel_id=1, source_target_pairs={{0,1},{1,0},{2,3},{3,2},{4,5},{5,4},{6,7},{7,6},{8,9},{9,8},{10,11... | collective-permute-start | bytes 1572872 | tf_op jit(solution)/shard_map/ppermute | solution.py:13
  85.9 19.1 %collective-permute-start.3 = (f32[256,512]{0,1:T(8,128)S(1)}, f32[256,512]{0,1:T(8,128)S(1)}, u32[]{:S(2)}, u32[]{:S(2)}) collective-permute-start(f32[256,512]{0,1:T(8,128)S(1)} %constant_dynamic-slice_fusion.3), channel_id=1, source_target_pairs={{0,4},{2,6},{4,0},{6,2},{1,5},{3,7},{5,1},{7,3},{8,12},{10,14},{12... | collective-permute-start | bytes 1572872 | tf_op jit(solution)/shard_map/ppermute | solution.py:68
  97.7 22.4 %collective-permute-start.14 = (f32[512,512]{0,1:T(8,128)S(1)}, f32[512,512]{0,1:T(8,128)S(1)}, u32[]{:S(2)}, u32[]{:S(2)}) collective-permute-start(f32[512,512]{0,1:T(8,128)S(1)} %dynamic-slice_bitcast_fusion.1), channel_id=1, source_target_pairs={{0,2},{2,0},{4,6},{6,4},{1,3},{3,1},{5,7},{7,5},{8,10},{10,8},{12,... | collective-permute-start | bytes 3145736 | tf_op jit(solution)/shard_map/ppermute | solution.py:68
  104.2 13.0 %collective-permute-start.19 = (bf16[256,1024]{1,0:T(8,128)(2,1)S(1)}, bf16[256,1024]{1,0:T(8,128)(2,1)S(1)}, u32[]{:S(2)}, u32[]{:S(2)}) collective-permute-start(bf16[256,1024]{1,0:T(8,128)(2,1)S(1)} %collective-permute-done.18), channel_id=1, source_target_pairs={{0,1},{1,0},{2,3},{3,2},{4,5},{5,4},{6,7},{7,6},{8,9},{9,8},{10,11... | collective-permute-start | bytes 1572872 | tf_op jit(solution)/shard_map/ppermute | solution.py:13
  105.1 13.4 %collective-permute-start.4 = (bf16[256,512]{0,1:T(8,128)(2,1)S(1)}, bf16[256,512]{0,1:T(8,128)(2,1)S(1)}, u32[]{:S(2)}, u32[]{:S(2)}) collective-permute-start(bf16[256,512]{0,1:T(8,128)(2,1)S(1)} %divide_convert_fusion.3), channel_id=1, source_target_pairs={{0,4},{2,6},{4,0},{6,2},{1,5},{3,7},{5,1},{7,3},{8,12},{10,14},{12... | collective-permute-start | bytes 786440 | tf_op jit(solution)/shard_map/ppermute | solution.py:80
  106.7 16.8 %collective-permute-start.9 = (f32[256,512]{0,1:T(8,128)S(1)}, f32[256,512]{0,1:T(8,128)S(1)}, u32[]{:S(2)}, u32[]{:S(2)}) collective-permute-start(f32[256,512]{0,1:T(8,128)S(1)} %constant_dynamic-slice_fusion.2), channel_id=1, source_target_pairs={{0,4},{2,6},{4,0},{6,2},{1,5},{3,7},{5,1},{7,3},{8,12},{10,14},{12... | collective-permute-start | bytes 1572872 | tf_op jit(solution)/shard_map/ppermute | solution.py:68
  118.7 4.9 %collective-permute-start.5 = (bf16[512,512]{0,1:T(8,128)(2,1)S(1)}, bf16[512,512]{0,1:T(8,128)(2,1)S(1)}, u32[]{:S(2)}, u32[]{:S(2)}) collective-permute-start(bf16[512,512]{0,1:T(8,128)(2,1)S(1)} %maximum_select_fusion.7), channel_id=1, source_target_pairs={{0,2},{2,0},{4,6},{6,4},{1,3},{3,1},{5,7},{7,5},{8,10},{10,8},{12,... | collective-permute-start | bytes 1572872 | tf_op jit(solution)/shard_map/ppermute | solution.py:80
  124.1 6.2 %collective-permute-start.10 = (bf16[256,512]{0,1:T(8,128)(2,1)S(1)}, bf16[256,512]{0,1:T(8,128)(2,1)S(1)}, u32[]{:S(2)}, u32[]{:S(2)}) collective-permute-start(bf16[256,512]{0,1:T(8,128)(2,1)S(1)} %divide_convert_fusion.2), channel_id=1, source_target_pairs={{0,4},{2,6},{4,0},{6,2},{1,5},{3,7},{5,1},{7,3},{8,12},{10,14},{12... | collective-permute-start | bytes 786440 | tf_op jit(solution)/shard_map/ppermute | solution.py:80
  125.4 16.1 %collective-permute-start.15 = (f32[256,512]{0,1:T(8,128)S(1)}, f32[256,512]{0,1:T(8,128)S(1)}, u32[]{:S(2)}, u32[]{:S(2)}) collective-permute-start(f32[256,512]{0,1:T(8,128)S(1)} %constant_dynamic-slice_fusion.1), channel_id=1, source_target_pairs={{0,4},{2,6},{4,0},{6,2},{1,5},{3,7},{5,1},{7,3},{8,12},{10,14},{12... | collective-permute-start | bytes 1572872 | tf_op jit(solution)/shard_map/ppermute | solution.py:68
  125.8 17.6 %collective-permute-start.20 = (f32[512,512]{0,1:T(8,128)S(1)}, f32[512,512]{0,1:T(8,128)S(1)}, u32[]{:S(2)}, u32[]{:S(2)}) collective-permute-start(f32[512,512]{0,1:T(8,128)S(1)} %dynamic-slice_bitcast_fusion), channel_id=1, source_target_pairs={{0,2},{2,0},{4,6},{6,4},{1,3},{3,1},{5,7},{7,5},{8,10},{10,8},{12,... | collective-permute-start | bytes 3145736 | tf_op jit(solution)/shard_map/ppermute | solution.py:68
  130.4 11.2 %collective-permute-start.11 = (bf16[512,512]{0,1:T(8,128)(2,1)S(1)}, bf16[512,512]{0,1:T(8,128)(2,1)S(1)}, u32[]{:S(2)}, u32[]{:S(2)}) collective-permute-start(bf16[512,512]{0,1:T(8,128)(2,1)S(1)} %maximum_select_fusion.8), channel_id=1, source_target_pairs={{0,2},{2,0},{4,6},{6,4},{1,3},{3,1},{5,7},{7,5},{8,10},{10,8},{12,... | collective-permute-start | bytes 1572872 | tf_op jit(solution)/shard_map/ppermute | solution.py:80
  142.1 5.3 %collective-permute-start.16 = (bf16[256,512]{0,1:T(8,128)(2,1)S(1)}, bf16[256,512]{0,1:T(8,128)(2,1)S(1)}, u32[]{:S(2)}, u32[]{:S(2)}) collective-permute-start(bf16[256,512]{0,1:T(8,128)(2,1)S(1)} %divide_convert_fusion.1), channel_id=1, source_target_pairs={{0,4},{2,6},{4,0},{6,2},{1,5},{3,7},{5,1},{7,3},{8,12},{10,14},{12... | collective-permute-start | bytes 786440 | tf_op jit(solution)/shard_map/ppermute | solution.py:80
  143.7 14.9 %collective-permute-start.21 = (f32[256,512]{0,1:T(8,128)S(1)}, f32[256,512]{0,1:T(8,128)S(1)}, u32[]{:S(2)}, u32[]{:S(2)}) collective-permute-start(f32[256,512]{0,1:T(8,128)S(1)} %constant_dynamic-slice_fusion), channel_id=1, source_target_pairs={{0,4},{2,6},{4,0},{6,2},{1,5},{3,7},{5,1},{7,3},{8,12},{10,14},{12... | collective-permute-start | bytes 1572872 | tf_op jit(solution)/shard_map/ppermute | solution.py:68
  147.5 11.2 %collective-permute-start.17 = (bf16[512,512]{0,1:T(8,128)(2,1)S(1)}, bf16[512,512]{0,1:T(8,128)(2,1)S(1)}, u32[]{:S(2)}, u32[]{:S(2)}) collective-permute-start(bf16[512,512]{0,1:T(8,128)(2,1)S(1)} %maximum_select_fusion.9), channel_id=1, source_target_pairs={{0,2},{2,0},{4,6},{6,4},{1,3},{3,1},{5,7},{7,5},{8,10},{10,8},{12,... | collective-permute-start | bytes 1572872 | tf_op jit(solution)/shard_map/ppermute | solution.py:80
  159.2 5.3 %collective-permute-start.22 = (bf16[256,512]{0,1:T(8,128)(2,1)S(1)}, bf16[256,512]{0,1:T(8,128)(2,1)S(1)}, u32[]{:S(2)}, u32[]{:S(2)}) collective-permute-start(bf16[256,512]{0,1:T(8,128)(2,1)S(1)} %divide_convert_fusion), channel_id=1, source_target_pairs={{0,4},{2,6},{4,0},{6,2},{1,5},{3,7},{5,1},{7,3},{8,12},{10,14},{12... | collective-permute-start | bytes 786440 | tf_op jit(solution)/shard_map/ppermute | solution.py:80
  164.6 7.5 %collective-permute-start.23 = (bf16[512,512]{0,1:T(8,128)(2,1)S(1)}, bf16[512,512]{0,1:T(8,128)(2,1)S(1)}, u32[]{:S(2)}, u32[]{:S(2)}) collective-permute-start(bf16[512,512]{0,1:T(8,128)(2,1)S(1)} %maximum_select_fusion.10), channel_id=1, source_target_pairs={{0,2},{2,0},{4,6},{6,4},{1,3},{3,1},{5,7},{7,5},{8,10},{10,8},{12,... | collective-permute-start | bytes 1572872 | tf_op jit(solution)/shard_map/ppermute | solution.py:80

commit v6 on v5

--- a/solution.py
+++ b/solution.py
@@ -3,7 +3,7 @@
 from jax import lax
 from jax.sharding import PartitionSpec as P
 
-CHUNKS = 4
+CHUNKS = 8
 AUX_BY_PERMUTE = True
 NARROW_FAR = False
 

time: 176 us -> 189 us (1.074)
  matrix products: 14 us -> 24.3 us
  starting transfers between devices: 37.9 us -> 42.1 us
    ppermute x8 -> x16, waiting for transfers between devices: 8.3 us -> 25.2 us  [aux_all_gather(): other = lax.ppermute(x, 'aux', xor_pairs(count, step))]
    dot_general x4 -> x8, matrix products: 7.22 us -> 18.3 us  [paired_plan(): term = jnp.dot(rows, block, preferred_element_type=jnp.float32)]
    ppermute x8 -> x16, waiting for transfers between devices: 86.7 us -> 76.5 us  [shifted_2(): lax.ppermute(value, axis, [(i, (i + by) % count) for i in range(count)])]
    ppermute x8 -> x16, starting transfers between devices: 8.82 us -> 17.3 us  [aux_reduce_scatter(): x = keep + lax.ppermute(send, 'aux', xor_pairs(count, step))]
    ppermute x8 -> x16, starting transfers between devices: 22.9 us -> 15.6 us  [aux_all_gather(): other = lax.ppermute(x, 'aux', xor_pairs(count, step))]
    ppermute x8 -> x16, waiting for transfers between devices: 13.9 us -> 7.53 us  [aux_reduce_scatter(): x = keep + lax.ppermute(send, 'aux', xor_pairs(count, step))]
    ppermute x8 -> x16, starting transfers between devices: 6.26 us -> 9.21 us  [shifted_2(): lax.ppermute(value, axis, [(i, (i + by) % count) for i in range(count)])]
    dot_general x4 -> x8, matrix products: 6.73 us -> 5.98 us  [paired_plan(): jnp.einsum('aq,bq->ab', own, block, preferred_element_type=jnp.float32)]
  transfers between devices with their start and end apart: 24 -> 48, of which waited for: 12 -> 19; matrix products, arithmetic and copies ran while one was open for 11% -> 13% of each run, Pallas kernels for 0% -> 0%
where the time goes in v6:
time: 189 us
  waiting for transfers between devices  109 us (58%)
  starting transfers between devices  42.1 us (22%)
  matrix products  24.3 us (13%)
  local copies, waits for them, and re-layouts  7.2 us (4%)
  other arithmetic  4.01 us (2%)
  between operations  1.9 us (1%)
    ppermute x16, waiting for transfers between devices, shifted_2(): lax.ppermute(value, axis, [(i, (i + by) % count) for i in range(count)])  76.5 us
    ppermute x16, waiting for transfers between devices, aux_all_gather(): other = lax.ppermute(x, 'aux', xor_pairs(count, step))  25.2 us
    dot_general x8, matrix products, paired_plan(): term = jnp.dot(rows, block, preferred_element_type=jnp.float32)  18.3 us
    ppermute x16, starting transfers between devices, aux_reduce_scatter(): x = keep + lax.ppermute(send, 'aux', xor_pairs(count, step))  17.3 us
    ppermute x16, starting transfers between devices, aux_all_gather(): other = lax.ppermute(x, 'aux', xor_pairs(count, step))  15.6 us
    ppermute x16, starting transfers between devices, shifted_2(): lax.ppermute(value, axis, [(i, (i + by) % count) for i in range(count)])  9.21 us
    ppermute x16, waiting for transfers between devices, aux_reduce_scatter(): x = keep + lax.ppermute(send, 'aux', xor_pairs(count, step))  7.53 us
    dot_general x8, matrix products, paired_plan(): jnp.einsum('aq,bq->ab', own, block, preferred_element_type=jnp.float32)  5.98 us
  transfers between devices with their start and end apart: 48, of which 19 were waited for; matrix products, arithmetic and copies ran while one was open for 13% of the time, Pallas kernels for 0%

profile of v6, /device:TPU:1, one launch (start us, length us, event | category | flops | bytes accessed | tf_op | source)
XLA Modules:
  0.0 188.7 jit_solution(3022463061532644918)
XLA Ops:
  0.0 2.7 %slice_bitcast_fusion = (bf16[128,1024]{1,0:T(8,128)(2,1)S(1)}, bf16[128,1024]{1,0:T(8,128)(2,1)S(1)}, bf16[128,1024]{1,0:T(8,128)(2,1)S(1)}, bf16[128,1024]{1,0...) fusion(bf16[1,1024,1024]{2,1,0:T(8,128)(2,1)} %param.3), kind=kLoop, calls=%fused_computation.59 | loop fusion | bytes 4194304 | tf_op jit(solution)/shard_map/slice | solution.py:105
  2.7 3.1 %collective-permute-start = (bf16[128,1024]{1,0:T(8,128)(2,1)}, bf16[128,1024]{1,0:T(8,128)(2,1)}, u32[]{:S(2)}, u32[]{:S(2)}) collective-permute-start(bf16[128,1024]{1,0:T(8,128)(2,1)} %get-tuple-element.39), channel_id=1, source_target_pairs={{0,16},{8,24},{16,0},{24,8},{1,17},{9,25},{17,1},{25,9},{2,18},{10... | collective-permute-start | bytes 786440 | tf_op jit(solution)/shard_map/ppermute | solution.py:13
  6.0 11.8 %collective-permute-done = bf16[128,1024]{1,0:T(8,128)(2,1)} collective-permute-done((bf16[128,1024]{1,0:T(8,128)(2,1)}, bf16[128,1024]{1,0:T(8,128)(2,1)}, u32[]{:S(2)}, u32[]{:S(2)}) %collective-permute-start) | collective-permute-done | bytes 262176 | tf_op jit(solution)/shard_map/ppermute | solution.py:13
  21.8 9.4 %collective-permute-done.6 = bf16[128,1024]{1,0:T(8,128)(2,1)} collective-permute-done((bf16[128,1024]{1,0:T(8,128)(2,1)}, bf16[128,1024]{1,0:T(8,128)(2,1)}, u32[]{:S(2)}, u32[]{:S(2)}) %collective-permute-start.6) | collective-permute-done | bytes 262176 | tf_op jit(solution)/shard_map/ppermute | solution.py:13
  33.7 2.8 %collective-permute-start.2 = (f32[512,256]{0,1:T(8,128)S(1)}, f32[512,256]{0,1:T(8,128)S(1)}, u32[]{:S(2)}, u32[]{:S(2)}) collective-permute-start(f32[512,256]{0,1:T(8,128)S(1)} %dynamic-slice_bitcast_fusion.7), channel_id=1, source_target_pairs={{0,2},{2,0},{4,6},{6,4},{1,3},{3,1},{5,7},{7,5},{8,10},{10,8},{12,... | collective-permute-start | bytes 1572872 | tf_op jit(solution)/shard_map/ppermute | solution.py:68
  37.5 8.5 %collective-permute-done.12 = bf16[128,1024]{1,0:T(8,128)(2,1)S(1)} collective-permute-done((bf16[128,1024]{1,0:T(8,128)(2,1)}, bf16[128,1024]{1,0:T(8,128)(2,1)S(1)}, u32[]{:S(2)}, u32[]{:S(2)}) %collective-permute-start.12) | collective-permute-done | bytes 262176 | tf_op jit(solution)/shard_map/ppermute | solution.py:13
  48.3 11.2 %collective-permute-done.18 = bf16[128,1024]{1,0:T(8,128)(2,1)S(1)} collective-permute-done((bf16[128,1024]{1,0:T(8,128)(2,1)S(1)}, bf16[128,1024]{1,0:T(8,128)(2,1)S(1)}, u32[]{:S(2)}, u32[]{:S(2)}) %collective-permute-start.18) | collective-permute-done | bytes 262176 | tf_op jit(solution)/shard_map/ppermute | solution.py:13
  62.0 1.3 collective-permute-start.19
  63.3 10.7 %collective-permute-done.24 = bf16[128,1024]{1,0:T(8,128)(2,1)S(1)} collective-permute-done((bf16[128,1024]{1,0:T(8,128)(2,1)S(1)}, bf16[128,1024]{1,0:T(8,128)(2,1)S(1)}, u32[]{:S(2)}, u32[]{:S(2)}) %collective-permute-start.24) | collective-permute-done | bytes 262176 | tf_op jit(solution)/shard_map/ppermute | solution.py:13
  74.6 1.2 collective-permute-start.9
  79.2 2.6 %collective-permute-start.5 = (bf16[512,256]{0,1:T(8,128)(2,1)S(1)}, bf16[512,256]{0,1:T(8,128)(2,1)S(1)}, u32[]{:S(2)}, u32[]{:S(2)}) collective-permute-start(bf16[512,256]{0,1:T(8,128)(2,1)S(1)} %maximum_select_fusion.11), channel_id=1, source_target_pairs={{0,2},{2,0},{4,6},{6,4},{1,3},{3,1},{5,7},{7,5},{8,10},{10,8},{12,... | collective-permute-start | bytes 786440 | tf_op jit(solution)/shard_map/ppermute | solution.py:80
  82.0 5.5 %collective-permute-done.30 = bf16[128,1024]{1,0:T(8,128)(2,1)S(1)} collective-permute-done((bf16[128,1024]{1,0:T(8,128)(2,1)S(1)}, bf16[128,1024]{1,0:T(8,128)(2,1)S(1)}, u32[]{:S(2)}, u32[]{:S(2)}) %collective-permute-start.30) | collective-permute-done | bytes 262176 | tf_op jit(solution)/shard_map/ppermute | solution.py:13
  89.0 2.3 %collective-permute-start.26 = (f32[512,256]{0,1:T(8,128)S(1)}, f32[512,256]{0,1:T(8,128)S(1)}, u32[]{:S(2)}, u32[]{:S(2)}) collective-permute-start(f32[512,256]{0,1:T(8,128)S(1)} %dynamic-slice_bitcast_fusion.3), channel_id=1, source_target_pairs={{0,2},{2,0},{4,6},{6,4},{1,3},{3,1},{5,7},{7,5},{8,10},{10,8},{12,... | collective-permute-start | bytes 1572872 | tf_op jit(solution)/shard_map/ppermute | solution.py:68
  92.8 2.1 %collective-permute-done.15 = f32[256,256]{0,1:T(8,128)S(1)} collective-permute-done((f32[256,256]{0,1:T(8,128)S(1)}, f32[256,256]{0,1:T(8,128)S(1)}, u32[]{:S(2)}, u32[]{:S(2)}) %collective-permute-start.15) | collective-permute-done | bytes 262176 | tf_op jit(solution)/shard_map/ppermute | solution.py:68
  95.6 6.8 %collective-permute-done.36 = bf16[128,1024]{1,0:T(8,128)(2,1)S(1)} collective-permute-done((bf16[128,1024]{1,0:T(8,128)(2,1)S(1)}, bf16[128,1024]{1,0:T(8,128)(2,1)S(1)}, u32[]{:S(2)}, u32[]{:S(2)}) %collective-permute-start.36) | collective-permute-done | bytes 262176 | tf_op jit(solution)/shard_map/ppermute | solution.py:13
  103.2 1.2 collective-permute-start.21
  106.3 1.3 collective-permute-start.16
  107.7 5.7 %collective-permute-done.37 = bf16[128,1024]{1,0:T(8,128)(2,1)S(1)} collective-permute-done((bf16[128,1024]{1,0:T(8,128)(2,1)S(1)}, bf16[128,1024]{1,0:T(8,128)(2,1)S(1)}, u32[]{:S(2)}, u32[]{:S(2)}) %collective-permute-start.37) | collective-permute-done | bytes 262176 | tf_op jit(solution)/shard_map/ppermute | solution.py:13
  116.7 1.2 collective-permute-start.43
  118.6 6.0 %collective-permute-done.43 = bf16[128,1024]{1,0:T(8,128)(2,1)S(1)} collective-permute-done((bf16[128,1024]{1,0:T(8,128)(2,1)S(1)}, bf16[128,1024]{1,0:T(8,128)(2,1)S(1)}, u32[]{:S(2)}, u32[]{:S(2)}) %collective-permute-start.43) | collective-permute-done | bytes 262176 | tf_op jit(solution)/shard_map/ppermute | solution.py:13
  129.4 8.2 %collective-permute-done.22 = bf16[256,256]{0,1:T(8,128)(2,1)S(1)} collective-permute-done((bf16[256,256]{0,1:T(8,128)(2,1)S(1)}, bf16[256,256]{0,1:T(8,128)(2,1)S(1)}, u32[]{:S(2)}, u32[]{:S(2)}) %collective-permute-start.22) | collective-permute-done | bytes 131104 | tf_op jit(solution)/shard_map/ppermute | solution.py:80
  141.2 8.2 %collective-permute-done.28 = bf16[256,256]{0,1:T(8,128)(2,1)S(1)} collective-permute-done((bf16[256,256]{0,1:T(8,128)(2,1)S(1)}, bf16[256,256]{0,1:T(8,128)(2,1)S(1)}, u32[]{:S(2)}, u32[]{:S(2)}) %collective-permute-start.28) | collective-permute-done | bytes 131104 | tf_op jit(solution)/shard_map/ppermute | solution.py:80
  153.1 3.5 %collective-permute-done.34 = bf16[256,256]{0,1:T(8,128)(2,1)S(1)} collective-permute-done((bf16[256,256]{0,1:T(8,128)(2,1)S(1)}, bf16[256,256]{0,1:T(8,128)(2,1)S(1)}, u32[]{:S(2)}, u32[]{:S(2)}) %collective-permute-start.34) | collective-permute-done | bytes 131104 | tf_op jit(solution)/shard_map/ppermute | solution.py:80
  156.7 1.3 collective-permute-start.35
  158.0 1.2 collective-permute-start.45
  160.6 5.4 %collective-permute-done.45 = f32[256,256]{0,1:T(8,128)S(1)} collective-permute-done((f32[256,256]{0,1:T(8,128)S(1)}, f32[256,256]{0,1:T(8,128)S(1)}, u32[]{:S(2)}, u32[]{:S(2)}) %collective-permute-start.45) | collective-permute-done | bytes 262176 | tf_op jit(solution)/shard_map/ppermute | solution.py:68
  166.0 2.8 %collective-permute-done.40 = bf16[256,256]{0,1:T(8,128)(2,1)S(1)} collective-permute-done((bf16[256,256]{0,1:T(8,128)(2,1)S(1)}, bf16[256,256]{0,1:T(8,128)(2,1)S(1)}, u32[]{:S(2)}, u32[]{:S(2)}) %collective-permute-start.40) | collective-permute-done | bytes 131104 | tf_op jit(solution)/shard_map/ppermute | solution.py:80
  169.8 2.8 %fusion.31 = f32[1024,1024]{1,0:T(8,128)} fusion(bf16[1024,256]{0,1:T(8,128)(2,1)S(1)} %maximum_select_fusion.4, bf16[256,1024]{1,0:T(8,128)(2,1)S(1)} %constant_dynamic-update-slice_fusion.8), kind=kOutput, calls=%fused_computation.120 | convolution fusion | flops 536870912 | bytes 5242880 | tf_op jit(solution)/shard_map/dot_general | solution.py:137
  172.9 1.2 collective-permute-start.46
  174.1 2.8 %fusion.32 = f32[1024,1024]{1,0:T(8,128)} fusion(bf16[1024,256]{0,1:T(8,128)(2,1)S(1)} %maximum_select_fusion.5, bf16[256,1024]{1,0:T(8,128)(2,1)S(1)} %constant_dynamic-update-slice_fusion.10), kind=kOutput, calls=%fused_computation.121 | convolution fusion | flops 536870912 | bytes 5242880 | tf_op jit(solution)/shard_map/dot_general | solution.py:137
  179.0 2.7 %fusion.33 = f32[1024,1024]{1,0:T(8,128)} fusion(bf16[1024,256]{0,1:T(8,128)(2,1)S(1)} %maximum_select_fusion.6, bf16[256,1024]{1,0:T(8,128)(2,1)S(1)} %constant_dynamic-update-slice_fusion.12), kind=kOutput, calls=%fused_computation.122 | convolution fusion | flops 536870912 | bytes 5242880 | tf_op jit(solution)/shard_map/dot_general | solution.py:137
  181.8 6.9 %fusion = bf16[1,1024,1024]{2,1,0:T(8,128)(2,1)} fusion(f32[1024,1024]{1,0:T(8,128)} %fusion.33, f32[1024,1024]{1,0:T(8,128)} %fusion.32, f32[1024,1024]{1,0:T(8,128)} %fusion.31, f32[1024,1024]{1,0:T(8,128)S(1)} %fusion.30, f32[1024,1024]{1,0:T(8,128)S(1)} %fusion.29, f32[1024,1024]{1,0:T(8,128)S(1)} %fusion.27, f32[1024,1024]{1,0:T(8,128)S(1)} %fusion.28, ...), kind=kOutput, calls=%fused_computation.1 | convolution fusion | flops 548667392 | bytes 32505856 | tf_op jit(solution)/shard_map/dot_general | solution.py:137
  (167 shorter events, 42.5 us)
Async XLA Ops:
  2.7 15.1 %collective-permute-start = (bf16[128,1024]{1,0:T(8,128)(2,1)}, bf16[128,1024]{1,0:T(8,128)(2,1)}, u32[]{:S(2)}, u32[]{:S(2)}) collective-permute-start(bf16[128,1024]{1,0:T(8,128)(2,1)} %get-tuple-element.39), channel_id=1, source_target_pairs={{0,16},{8,24},{16,0},{24,8},{1,17},{9,25},{17,1},{25,9},{2,18},{10... | collective-permute-start | bytes 786440 | tf_op jit(solution)/shard_map/ppermute | solution.py:13
  17.8 13.4 %collective-permute-start.6 = (bf16[128,1024]{1,0:T(8,128)(2,1)}, bf16[128,1024]{1,0:T(8,128)(2,1)}, u32[]{:S(2)}, u32[]{:S(2)}) collective-permute-start(bf16[128,1024]{1,0:T(8,128)(2,1)} %get-tuple-element.19), channel_id=1, source_target_pairs={{0,16},{8,24},{16,0},{24,8},{1,17},{9,25},{17,1},{25,9},{2,18},{10... | collective-permute-start | bytes 786440 | tf_op jit(solution)/shard_map/ppermute | solution.py:13
  17.8 14.1 %collective-permute-start.1 = (bf16[128,1024]{1,0:T(8,128)(2,1)}, bf16[128,1024]{1,0:T(8,128)(2,1)}, u32[]{:S(2)}, u32[]{:S(2)}) collective-permute-start(bf16[128,1024]{1,0:T(8,128)(2,1)} %collective-permute-done), channel_id=1, source_target_pairs={{0,1},{1,0},{2,3},{3,2},{4,5},{5,4},{6,7},{7,6},{8,9},{9,8},{10,11... | collective-permute-start | bytes 786440 | tf_op jit(solution)/shard_map/ppermute | solution.py:13
  31.2 14.8 %collective-permute-start.12 = (bf16[128,1024]{1,0:T(8,128)(2,1)}, bf16[128,1024]{1,0:T(8,128)(2,1)S(1)}, u32[]{:S(2)}, u32[]{:S(2)}) collective-permute-start(bf16[128,1024]{1,0:T(8,128)(2,1)} %get-tuple-element.21), channel_id=1, source_target_pairs={{0,16},{8,24},{16,0},{24,8},{1,17},{9,25},{17,1},{25,9},{2,18},{10... | collective-permute-start | bytes 786440 | tf_op jit(solution)/shard_map/ppermute | solution.py:13
  31.2 14.8 %collective-permute-start.7 = (bf16[128,1024]{1,0:T(8,128)(2,1)}, bf16[128,1024]{1,0:T(8,128)(2,1)S(1)}, u32[]{:S(2)}, u32[]{:S(2)}) collective-permute-start(bf16[128,1024]{1,0:T(8,128)(2,1)} %collective-permute-done.6), channel_id=1, source_target_pairs={{0,1},{1,0},{2,3},{3,2},{4,5},{5,4},{6,7},{7,6},{8,9},{9,8},{10,11... | collective-permute-start | bytes 786440 | tf_op jit(solution)/shard_map/ppermute | solution.py:13
  33.7 25.8 %collective-permute-start.2 = (f32[512,256]{0,1:T(8,128)S(1)}, f32[512,256]{0,1:T(8,128)S(1)}, u32[]{:S(2)}, u32[]{:S(2)}) collective-permute-start(f32[512,256]{0,1:T(8,128)S(1)} %dynamic-slice_bitcast_fusion.7), channel_id=1, source_target_pairs={{0,2},{2,0},{4,6},{6,4},{1,3},{3,1},{5,7},{7,5},{8,10},{10,8},{12,... | collective-permute-start | bytes 1572872 | tf_op jit(solution)/shard_map/ppermute | solution.py:68
  46.0 13.5 %collective-permute-start.18 = (bf16[128,1024]{1,0:T(8,128)(2,1)S(1)}, bf16[128,1024]{1,0:T(8,128)(2,1)S(1)}, u32[]{:S(2)}, u32[]{:S(2)}) collective-permute-start(bf16[128,1024]{1,0:T(8,128)(2,1)S(1)} %get-tuple-element.23), channel_id=1, source_target_pairs={{0,16},{8,24},{16,0},{24,8},{1,17},{9,25},{17,1},{25,9},{2,18},{10... | collective-permute-start | bytes 786440 | tf_op jit(solution)/shard_map/ppermute | solution.py:13
  46.8 27.7 %collective-permute-start.8 = (f32[512,256]{0,1:T(8,128)S(1)}, f32[512,256]{0,1:T(8,128)S(1)}, u32[]{:S(2)}, u32[]{:S(2)}) collective-permute-start(f32[512,256]{0,1:T(8,128)S(1)} %dynamic-slice_bitcast_fusion.6), channel_id=1, source_target_pairs={{0,2},{2,0},{4,6},{6,4},{1,3},{3,1},{5,7},{7,5},{8,10},{10,8},{12,... | collective-permute-start | bytes 1572872 | tf_op jit(solution)/shard_map/ppermute | solution.py:68
  47.6 12.8 %collective-permute-start.13 = (bf16[128,1024]{1,0:T(8,128)(2,1)S(1)}, bf16[128,1024]{1,0:T(8,128)(2,1)S(1)}, u32[]{:S(2)}, u32[]{:S(2)}) collective-permute-start(bf16[128,1024]{1,0:T(8,128)(2,1)S(1)} %collective-permute-done.12), channel_id=1, source_target_pairs={{0,1},{1,0},{2,3},{3,2},{4,5},{5,4},{6,7},{7,6},{8,9},{9,8},{10,11... | collective-permute-start | bytes 786440 | tf_op jit(solution)/shard_map/ppermute | solution.py:13
  59.5 14.6 %collective-permute-start.24 = (bf16[128,1024]{1,0:T(8,128)(2,1)S(1)}, bf16[128,1024]{1,0:T(8,128)(2,1)S(1)}, u32[]{:S(2)}, u32[]{:S(2)}) collective-permute-start(bf16[128,1024]{1,0:T(8,128)(2,1)S(1)} %get-tuple-element.25), channel_id=1, source_target_pairs={{0,16},{8,24},{16,0},{24,8},{1,17},{9,25},{17,1},{25,9},{2,18},{10... | collective-permute-start | bytes 786440 | tf_op jit(solution)/shard_map/ppermute | solution.py:13
  59.6 14.4 %collective-permute-start.3 = (f32[256,256]{0,1:T(8,128)S(1)}, f32[256,256]{0,1:T(8,128)S(1)}, u32[]{:S(2)}, u32[]{:S(2)}) collective-permute-start(f32[256,256]{0,1:T(8,128)S(1)} %constant_dynamic-slice_fusion.7), channel_id=1, source_target_pairs={{0,4},{2,6},{4,0},{6,2},{1,5},{3,7},{5,1},{7,3},{8,12},{10,14},{12... | collective-permute-start | bytes 786440 | tf_op jit(solution)/shard_map/ppermute | solution.py:68
  61.2 18.1 %collective-permute-start.14 = (f32[512,256]{0,1:T(8,128)S(1)}, f32[512,256]{0,1:T(8,128)S(1)}, u32[]{:S(2)}, u32[]{:S(2)}) collective-permute-start(f32[512,256]{0,1:T(8,128)S(1)} %dynamic-slice_bitcast_fusion.5), channel_id=1, source_target_pairs={{0,2},{2,0},{4,6},{6,4},{1,3},{3,1},{5,7},{7,5},{8,10},{10,8},{12,... | collective-permute-start | bytes 1572872 | tf_op jit(solution)/shard_map/ppermute | solution.py:68
  62.0 13.9 %collective-permute-start.19 = (bf16[128,1024]{1,0:T(8,128)(2,1)S(1)}, bf16[128,1024]{1,0:T(8,128)(2,1)S(1)}, u32[]{:S(2)}, u32[]{:S(2)}) collective-permute-start(bf16[128,1024]{1,0:T(8,128)(2,1)S(1)} %collective-permute-done.18), channel_id=1, source_target_pairs={{0,1},{1,0},{2,3},{3,2},{4,5},{5,4},{6,7},{7,6},{8,9},{9,8},{10,11... | collective-permute-start | bytes 786440 | tf_op jit(solution)/shard_map/ppermute | solution.py:13
  74.0 13.5 %collective-permute-start.30 = (bf16[128,1024]{1,0:T(8,128)(2,1)S(1)}, bf16[128,1024]{1,0:T(8,128)(2,1)S(1)}, u32[]{:S(2)}, u32[]{:S(2)}) collective-permute-start(bf16[128,1024]{1,0:T(8,128)(2,1)S(1)} %get-tuple-element.27), channel_id=1, source_target_pairs={{0,16},{8,24},{16,0},{24,8},{1,17},{9,25},{17,1},{25,9},{2,18},{10... | collective-permute-start | bytes 786440 | tf_op jit(solution)/shard_map/ppermute | solution.py:13
  74.6 14.4 %collective-permute-start.9 = (f32[256,256]{0,1:T(8,128)S(1)}, f32[256,256]{0,1:T(8,128)S(1)}, u32[]{:S(2)}, u32[]{:S(2)}) collective-permute-start(f32[256,256]{0,1:T(8,128)S(1)} %constant_dynamic-slice_fusion.6), channel_id=1, source_target_pairs={{0,4},{2,6},{4,0},{6,2},{1,5},{3,7},{5,1},{7,3},{8,12},{10,14},{12... | collective-permute-start | bytes 786440 | tf_op jit(solution)/shard_map/ppermute | solution.py:68
  76.7 26.4 %collective-permute-start.20 = (f32[512,256]{0,1:T(8,128)S(1)}, f32[512,256]{0,1:T(8,128)S(1)}, u32[]{:S(2)}, u32[]{:S(2)}) collective-permute-start(f32[512,256]{0,1:T(8,128)S(1)} %dynamic-slice_bitcast_fusion.4), channel_id=1, source_target_pairs={{0,2},{2,0},{4,6},{6,4},{1,3},{3,1},{5,7},{7,5},{8,10},{10,8},{12,... | collective-permute-start | bytes 1572872 | tf_op jit(solution)/shard_map/ppermute | solution.py:68
  78.8 9.4 %collective-permute-start.25 = (bf16[128,1024]{1,0:T(8,128)(2,1)S(1)}, bf16[128,1024]{1,0:T(8,128)(2,1)S(1)}, u32[]{:S(2)}, u32[]{:S(2)}) collective-permute-start(bf16[128,1024]{1,0:T(8,128)(2,1)S(1)} %collective-permute-done.24), channel_id=1, source_target_pairs={{0,1},{1,0},{2,3},{3,2},{4,5},{5,4},{6,7},{7,6},{8,9},{9,8},{10,11... | collective-permute-start | bytes 786440 | tf_op jit(solution)/shard_map/ppermute | solution.py:13
  79.2 12.1 %collective-permute-start.5 = (bf16[512,256]{0,1:T(8,128)(2,1)S(1)}, bf16[512,256]{0,1:T(8,128)(2,1)S(1)}, u32[]{:S(2)}, u32[]{:S(2)}) collective-permute-start(bf16[512,256]{0,1:T(8,128)(2,1)S(1)} %maximum_select_fusion.11), channel_id=1, source_target_pairs={{0,2},{2,0},{4,6},{6,4},{1,3},{3,1},{5,7},{7,5},{8,10},{10,8},{12,... | collective-permute-start | bytes 786440 | tf_op jit(solution)/shard_map/ppermute | solution.py:80
  88.2 14.2 %collective-permute-start.36 = (bf16[128,1024]{1,0:T(8,128)(2,1)S(1)}, bf16[128,1024]{1,0:T(8,128)(2,1)S(1)}, u32[]{:S(2)}, u32[]{:S(2)}) collective-permute-start(bf16[128,1024]{1,0:T(8,128)(2,1)S(1)} %get-tuple-element.29), channel_id=1, source_target_pairs={{0,16},{8,24},{16,0},{24,8},{1,17},{9,25},{17,1},{25,9},{2,18},{10... | collective-permute-start | bytes 786440 | tf_op jit(solution)/shard_map/ppermute | solution.py:13
  89.0 17.2 %collective-permute-start.26 = (f32[512,256]{0,1:T(8,128)S(1)}, f32[512,256]{0,1:T(8,128)S(1)}, u32[]{:S(2)}, u32[]{:S(2)}) collective-permute-start(f32[512,256]{0,1:T(8,128)S(1)} %dynamic-slice_bitcast_fusion.3), channel_id=1, source_target_pairs={{0,2},{2,0},{4,6},{6,4},{1,3},{3,1},{5,7},{7,5},{8,10},{10,8},{12,... | collective-permute-start | bytes 1572872 | tf_op jit(solution)/shard_map/ppermute | solution.py:68
  91.4 13.0 %collective-permute-start.31 = (bf16[128,1024]{1,0:T(8,128)(2,1)S(1)}, bf16[128,1024]{1,0:T(8,128)(2,1)S(1)}, u32[]{:S(2)}, u32[]{:S(2)}) collective-permute-start(bf16[128,1024]{1,0:T(8,128)(2,1)S(1)} %collective-permute-done.30), channel_id=1, source_target_pairs={{0,1},{1,0},{2,3},{3,2},{4,5},{5,4},{6,7},{7,6},{8,9},{9,8},{10,11... | collective-permute-start | bytes 786440 | tf_op jit(solution)/shard_map/ppermute | solution.py:13
  102.4 13.8 %collective-permute-start.42 = (bf16[128,1024]{1,0:T(8,128)(2,1)S(1)}, bf16[128,1024]{1,0:T(8,128)(2,1)S(1)}, u32[]{:S(2)}, u32[]{:S(2)}) collective-permute-start(bf16[128,1024]{1,0:T(8,128)(2,1)S(1)} %get-tuple-element.31), channel_id=1, source_target_pairs={{0,16},{8,24},{16,0},{24,8},{1,17},{9,25},{17,1},{25,9},{2,18},{10... | collective-permute-start | bytes 786440 | tf_op jit(solution)/shard_map/ppermute | solution.py:13
  103.2 13.5 %collective-permute-start.21 = (f32[256,256]{0,1:T(8,128)S(1)}, f32[256,256]{0,1:T(8,128)S(1)}, u32[]{:S(2)}, u32[]{:S(2)}) collective-permute-start(f32[256,256]{0,1:T(8,128)S(1)} %constant_dynamic-slice_fusion.4), channel_id=1, source_target_pairs={{0,4},{2,6},{4,0},{6,2},{1,5},{3,7},{5,1},{7,3},{8,12},{10,14},{12... | collective-permute-start | bytes 786440 | tf_op jit(solution)/shard_map/ppermute | solution.py:68
  105.2 21.2 %collective-permute-start.32 = (f32[512,256]{0,1:T(8,128)S(1)}, f32[512,256]{0,1:T(8,128)S(1)}, u32[]{:S(2)}, u32[]{:S(2)}) collective-permute-start(f32[512,256]{0,1:T(8,128)S(1)} %dynamic-slice_bitcast_fusion.2), channel_id=1, source_target_pairs={{0,2},{2,0},{4,6},{6,4},{1,3},{3,1},{5,7},{7,5},{8,10},{10,8},{12,... | collective-permute-start | bytes 1572872 | tf_op jit(solution)/shard_map/ppermute | solution.py:68
  106.3 11.7 %collective-permute-start.16 = (bf16[256,256]{0,1:T(8,128)(2,1)S(1)}, bf16[256,256]{0,1:T(8,128)(2,1)S(1)}, u32[]{:S(2)}, u32[]{:S(2)}) collective-permute-start(bf16[256,256]{0,1:T(8,128)(2,1)S(1)} %divide_convert_fusion.5), channel_id=1, source_target_pairs={{0,4},{2,6},{4,0},{6,2},{1,5},{3,7},{5,1},{7,3},{8,12},{10,14},{12... | collective-permute-start | bytes 393224 | tf_op jit(solution)/shard_map/ppermute | solution.py:80
  113.4 13.0 %collective-permute-start.27 = (f32[256,256]{0,1:T(8,128)S(1)}, f32[256,256]{0,1:T(8,128)S(1)}, u32[]{:S(2)}, u32[]{:S(2)}) collective-permute-start(f32[256,256]{0,1:T(8,128)S(1)} %constant_dynamic-slice_fusion.3), channel_id=1, source_target_pairs={{0,4},{2,6},{4,0},{6,2},{1,5},{3,7},{5,1},{7,3},{8,12},{10,14},{12... | collective-permute-start | bytes 786440 | tf_op jit(solution)/shard_map/ppermute | solution.py:68
  116.2 22.3 %collective-permute-start.38 = (f32[512,256]{0,1:T(8,128)S(1)}, f32[512,256]{0,1:T(8,128)S(1)}, u32[]{:S(2)}, u32[]{:S(2)}) collective-permute-start(f32[512,256]{0,1:T(8,128)S(1)} %dynamic-slice_bitcast_fusion.1), channel_id=1, source_target_pairs={{0,2},{2,0},{4,6},{6,4},{1,3},{3,1},{5,7},{7,5},{8,10},{10,8},{12,... | collective-permute-start | bytes 1572872 | tf_op jit(solution)/shard_map/ppermute | solution.py:68
  118.2 9.8 %collective-permute-start.17 = (bf16[512,256]{0,1:T(8,128)(2,1)S(1)}, bf16[512,256]{0,1:T(8,128)(2,1)S(1)}, u32[]{:S(2)}, u32[]{:S(2)}) collective-permute-start(bf16[512,256]{0,1:T(8,128)(2,1)S(1)} %maximum_select_fusion.13), channel_id=1, source_target_pairs={{0,2},{2,0},{4,6},{6,4},{1,3},{3,1},{5,7},{7,5},{8,10},{10,8},{12,... | collective-permute-start | bytes 786440 | tf_op jit(solution)/shard_map/ppermute | solution.py:80
  125.5 27.6 %collective-permute-start.44 = (f32[512,256]{0,1:T(8,128)S(1)}, f32[512,256]{0,1:T(8,128)S(1)}, u32[]{:S(2)}, u32[]{:S(2)}) collective-permute-start(f32[512,256]{0,1:T(8,128)S(1)} %dynamic-slice_bitcast_fusion), channel_id=1, source_target_pairs={{0,2},{2,0},{4,6},{6,4},{1,3},{3,1},{5,7},{7,5},{8,10},{10,8},{12,... | collective-permute-start | bytes 1572872 | tf_op jit(solution)/shard_map/ppermute | solution.py:68
  126.7 14.4 %collective-permute-start.33 = (f32[256,256]{0,1:T(8,128)S(1)}, f32[256,256]{0,1:T(8,128)S(1)}, u32[]{:S(2)}, u32[]{:S(2)}) collective-permute-start(f32[256,256]{0,1:T(8,128)S(1)} %constant_dynamic-slice_fusion.2), channel_id=1, source_target_pairs={{0,4},{2,6},{4,0},{6,2},{1,5},{3,7},{5,1},{7,3},{8,12},{10,14},{12... | collective-permute-start | bytes 786440 | tf_op jit(solution)/shard_map/ppermute | solution.py:68
  138.6 20.6 %collective-permute-start.39 = (f32[256,256]{0,1:T(8,128)S(1)}, f32[256,256]{0,1:T(8,128)S(1)}, u32[]{:S(2)}, u32[]{:S(2)}) collective-permute-start(f32[256,256]{0,1:T(8,128)S(1)} %constant_dynamic-slice_fusion.1), channel_id=1, source_target_pairs={{0,4},{2,6},{4,0},{6,2},{1,5},{3,7},{5,1},{7,3},{8,12},{10,14},{12... | collective-permute-start | bytes 786440 | tf_op jit(solution)/shard_map/ppermute | solution.py:68
  140.1 9.3 %collective-permute-start.28 = (bf16[256,256]{0,1:T(8,128)(2,1)S(1)}, bf16[256,256]{0,1:T(8,128)(2,1)S(1)}, u32[]{:S(2)}, u32[]{:S(2)}) collective-permute-start(bf16[256,256]{0,1:T(8,128)(2,1)S(1)} %divide_convert_fusion.3), channel_id=1, source_target_pairs={{0,4},{2,6},{4,0},{6,2},{1,5},{3,7},{5,1},{7,3},{8,12},{10,14},{12... | collective-permute-start | bytes 393224 | tf_op jit(solution)/shard_map/ppermute | solution.py:80
  (19 other events, 146.5 us)

commit v7 on v5

--- a/solution.py
+++ b/solution.py
@@ -52,12 +52,11 @@
     return [(j, j ^ step) for j in range(count)]
 
 
-def aux_reduce_scatter(x):
+def aux_reduce_scatter(x, first=0, step=1, stop=None):
     count = lax.axis_size("aux")
     k = lax.axis_index("aux")
-    first = 0
-    step = 1
-    while step < count:
+    stop = count if stop is None else stop
+    while step < stop:
         half = x.shape[0] // 2
         bit = (k // step) % 2
         keep = lax.dynamic_slice_in_dim(x, bit * half, half, 0)
@@ -101,10 +100,12 @@
     total = None
     previous = None
     rows_done = None
+    near, far = [], []
     for c in range(CHUNKS):
         piece = own[c * width:(c + 1) * width]
         if previous is not None:
-            piece, _ = lax.optimization_barrier((piece, previous))
+            gate = [previous] + [s for s in (near[c - 2:c - 1] + far[c - 3:c - 2]) if c >= 2]
+            piece, _ = lax.optimization_barrier((piece, gate))
         arrived = shifted_2(piece, "occ", 2)
         previous = arrived
         if vir_count == 2:
@@ -119,7 +120,10 @@
         )
         partial = jnp.einsum("aq,bq->ab", own, block, preferred_element_type=jnp.float32)
         if AUX_BY_PERMUTE:
-            summed, first = aux_reduce_scatter(partial)
+            summed, first = aux_reduce_scatter(partial, stop=2)
+            near.append(summed)
+            summed, first = aux_reduce_scatter(summed, first, step=2)
+            far.append(summed)
         else:
             summed = lax.psum_scatter(partial, "aux", scatter_dimension=0, tiled=True)
             first = first_row

time: 176 us -> 197 us (1.12)
  waiting for transfers between devices: 109 us -> 130 us
  starting transfers between devices: 37.9 us -> 32.9 us
  other arithmetic: 4.46 us -> 7.01 us
    ppermute x8, waiting for transfers between devices: 13.9 us -> 29.3 us  [aux_reduce_scatter(): x = keep + lax.ppermute(send, 'aux', xor_pairs(count, step))]
    ppermute x8, starting transfers between devices: 22.9 us -> 13.5 us  [aux_all_gather(): other = lax.ppermute(x, 'aux', xor_pairs(count, step))]
    ppermute x8, waiting for transfers between devices: 8.3 us -> 15.1 us  [aux_all_gather(): other = lax.ppermute(x, 'aux', xor_pairs(count, step))]
    ppermute x8, starting transfers between devices: 8.82 us -> 13.5 us  [aux_reduce_scatter(): x = keep + lax.ppermute(send, 'aux', xor_pairs(count, step))]
  transfers between devices with their start and end apart: 24 -> 24, of which waited for: 12 -> 14; matrix products, arithmetic and copies ran while one was open for 11% -> 13% of each run, Pallas kernels for 0% -> 0%
where the time goes in v7:
time: 197 us; the launch traced here: 196 us
  waiting for transfers between devices  130 us (66%)
  starting transfers between devices  32.9 us (17%)
  matrix products  15.5 us (8%)
  local copies, waits for them, and re-layouts  9.12 us (5%)
  other arithmetic  7.01 us (4%)
    ppermute x8, waiting for transfers between devices, shifted_2(): lax.ppermute(value, axis, [(i, (i + by) % count) for i in range(count)])  86 us
    ppermute x8, waiting for transfers between devices, aux_reduce_scatter(): x = keep + lax.ppermute(send, 'aux', xor_pairs(count, step))  29.3 us
    ppermute x8, waiting for transfers between devices, aux_all_gather(): other = lax.ppermute(x, 'aux', xor_pairs(count, step))  15.1 us
    ppermute x8, starting transfers between devices, aux_reduce_scatter(): x = keep + lax.ppermute(send, 'aux', xor_pairs(count, step))  13.5 us
    ppermute x8, starting transfers between devices, aux_all_gather(): other = lax.ppermute(x, 'aux', xor_pairs(count, step))  13.5 us
    dot_general x4, matrix products, paired_plan(): jnp.einsum('aq,bq->ab', own, block, preferred_element_type=jnp.float32)  8.32 us
    dot_general x4, matrix products, paired_plan(): term = jnp.dot(rows, block, preferred_element_type=jnp.float32)  7.22 us
    ppermute x8, starting transfers between devices, shifted_2(): lax.ppermute(value, axis, [(i, (i + by) % count) for i in range(count)])  5.89 us
  transfers between devices with their start and end apart: 24, of which 14 were waited for; matrix products, arithmetic and copies ran while one was open for 13% of the time, Pallas kernels for 0%

profile of v7, /device:TPU:1, one launch (start us, length us, event | category | flops | bytes accessed | tf_op | source)
XLA Modules:
  0.0 196.5 jit_solution(15439190552065942102)
XLA Ops:
  0.0 2.8 %slice_bitcast_fusion = (bf16[256,1024]{1,0:T(8,128)(2,1)}, bf16[256,1024]{1,0:T(8,128)(2,1)S(1)}, bf16[256,1024]{1,0:T(8,128)(2,1)S(1)}, bf16[256,1024]{1,0:T(8,128)(2,1)}) fusion(bf16[1,1024,1024]{2,1,0:T(8,128)(2,1)} %param.3), kind=kLoop, calls=%fused_computation.35 | loop fusion | bytes 4194304 | tf_op jit(solution)/shard_map/slice | solution.py:105
  2.8 3.1 %collective-permute-start = (bf16[256,1024]{1,0:T(8,128)(2,1)S(1)}, bf16[256,1024]{1,0:T(8,128)(2,1)S(1)}, u32[]{:S(2)}, u32[]{:S(2)}) collective-permute-start(bf16[256,1024]{1,0:T(8,128)(2,1)S(1)} %get-tuple-element.21), channel_id=1, source_target_pairs={{0,16},{8,24},{16,0},{24,8},{1,17},{9,25},{17,1},{25,9},{2,18},{10... | collective-permute-start | bytes 1572872 | tf_op jit(solution)/shard_map/ppermute | solution.py:13
  5.9 22.9 %collective-permute-done = bf16[256,1024]{1,0:T(8,128)(2,1)S(1)} collective-permute-done((bf16[256,1024]{1,0:T(8,128)(2,1)S(1)}, bf16[256,1024]{1,0:T(8,128)(2,1)S(1)}, u32[]{:S(2)}, u32[]{:S(2)}) %collective-permute-start) | collective-permute-done | bytes 524320 | tf_op jit(solution)/shard_map/ppermute | solution.py:13
  29.8 11.2 %collective-permute-done.1 = bf16[256,1024]{1,0:T(8,128)(2,1)S(1)} collective-permute-done((bf16[256,1024]{1,0:T(8,128)(2,1)S(1)}, bf16[256,1024]{1,0:T(8,128)(2,1)S(1)}, u32[]{:S(2)}, u32[]{:S(2)}) %collective-permute-start.1) | collective-permute-done | bytes 524320 | tf_op jit(solution)/shard_map/ppermute | solution.py:13
  41.0 2.9 %fusion.7 = f32[512,1024]{1,0:T(8,128)S(1)} fusion(bf16[512,1024]{1,0:T(8,128)(2,1)S(1)} %constant_dynamic-update-slice_fusion, bf16[1,1024,1024]{2,1,0:T(8,128)(2,1)} %param.3), kind=kOutput, calls=%fused_computation.8 | convolution fusion | flops 1073741824 | bytes 5242880 | tf_op jit(solution)/shard_map/aq,bq->ab/dot_general | solution.py:121
  43.9 10.0 %collective-permute-done.6 = bf16[256,1024]{1,0:T(8,128)(2,1)} collective-permute-done((bf16[256,1024]{1,0:T(8,128)(2,1)S(1)}, bf16[256,1024]{1,0:T(8,128)(2,1)}, u32[]{:S(2)}, u32[]{:S(2)}) %collective-permute-start.6) | collective-permute-done | bytes 524320 | tf_op jit(solution)/shard_map/ppermute | solution.py:13
  54.7 2.5 %collective-permute-start.2 = (f32[512,512]{0,1:T(8,128)S(1)}, f32[512,512]{0,1:T(8,128)}, u32[]{:S(2)}, u32[]{:S(2)}) collective-permute-start(f32[512,512]{0,1:T(8,128)S(1)} %dynamic-slice_bitcast_fusion.3), channel_id=1, source_target_pairs={{0,2},{2,0},{4,6},{6,4},{1,3},{3,1},{5,7},{7,5},{8,10},{10,8},{12,... | collective-permute-start | bytes 3145736 | tf_op jit(solution)/shard_map/ppermute | solution.py:67
  58.3 6.9 %collective-permute-done.7 = bf16[256,1024]{1,0:T(8,128)(2,1)} collective-permute-done((bf16[256,1024]{1,0:T(8,128)(2,1)}, bf16[256,1024]{1,0:T(8,128)(2,1)}, u32[]{:S(2)}, u32[]{:S(2)}) %collective-permute-start.7) | collective-permute-done | bytes 524320 | tf_op jit(solution)/shard_map/ppermute | solution.py:13
  66.3 2.9 %fusion.5 = f32[512,1024]{1,0:T(8,128)S(1)} fusion(bf16[512,1024]{1,0:T(8,128)(2,1)S(1)} %constant_dynamic-update-slice_fusion.2, bf16[1,1024,1024]{2,1,0:T(8,128)(2,1)} %param.3), kind=kOutput, calls=%fused_computation.6 | convolution fusion | flops 1073741824 | bytes 5242880 | tf_op jit(solution)/shard_map/aq,bq->ab/dot_general | solution.py:121
  70.2 3.4 %collective-permute-start.8 = (f32[512,512]{0,1:T(8,128)}, f32[512,512]{0,1:T(8,128)}, u32[]{:S(2)}, u32[]{:S(2)}) collective-permute-start(f32[512,512]{0,1:T(8,128)} %dynamic-slice_bitcast_fusion.2), channel_id=1, source_target_pairs={{0,2},{2,0},{4,6},{6,4},{1,3},{3,1},{5,7},{7,5},{8,10},{10,8},{12,... | collective-permute-start | bytes 3145736 | tf_op jit(solution)/shard_map/ppermute | solution.py:67
  73.6 1.4 bitcast_add_fusion.3
  79.2 8.7 %collective-permute-done.3 = f32[256,512]{0,1:T(8,128)} collective-permute-done((f32[256,512]{0,1:T(8,128)}, f32[256,512]{0,1:T(8,128)}, u32[]{:S(2)}, u32[]{:S(2)}) %collective-permute-start.3) | collective-permute-done | bytes 524320 | tf_op jit(solution)/shard_map/ppermute | solution.py:67
  90.5 14.0 %collective-permute-done.12 = bf16[256,1024]{1,0:T(8,128)(2,1)} collective-permute-done((bf16[256,1024]{1,0:T(8,128)(2,1)}, bf16[256,1024]{1,0:T(8,128)(2,1)}, u32[]{:S(2)}, u32[]{:S(2)}) %collective-permute-start.12) | collective-permute-done | bytes 524320 | tf_op jit(solution)/shard_map/ppermute | solution.py:13
  104.7 1.7 bitcast_add_fusion.2
  108.8 1.8 collective-permute-start.5
  110.5 6.2 %collective-permute-done.13 = bf16[256,1024]{1,0:T(8,128)(2,1)S(1)} collective-permute-done((bf16[256,1024]{1,0:T(8,128)(2,1)}, bf16[256,1024]{1,0:T(8,128)(2,1)S(1)}, u32[]{:S(2)}, u32[]{:S(2)}) %collective-permute-start.13) | collective-permute-done | bytes 524320 | tf_op jit(solution)/shard_map/ppermute | solution.py:13
  118.2 2.4 %collective-permute-start.14 = (f32[512,512]{0,1:T(8,128)S(1)}, f32[512,512]{0,1:T(8,128)S(1)}, u32[]{:S(2)}, u32[]{:S(2)}) collective-permute-start(f32[512,512]{0,1:T(8,128)S(1)} %dynamic-slice_bitcast_fusion.1), channel_id=1, source_target_pairs={{0,2},{2,0},{4,6},{6,4},{1,3},{3,1},{5,7},{7,5},{8,10},{10,8},{12,... | collective-permute-start | bytes 3145736 | tf_op jit(solution)/shard_map/ppermute | solution.py:67
  120.5 12.2 %collective-permute-done.18 = bf16[256,1024]{1,0:T(8,128)(2,1)S(1)} collective-permute-done((bf16[256,1024]{1,0:T(8,128)(2,1)S(1)}, bf16[256,1024]{1,0:T(8,128)(2,1)S(1)}, u32[]{:S(2)}, u32[]{:S(2)}) %collective-permute-start.18) | collective-permute-done | bytes 524320 | tf_op jit(solution)/shard_map/ppermute | solution.py:13
  134.0 1.3 collective-permute-start.10
  135.4 5.8 %collective-permute-done.10 = bf16[256,512]{0,1:T(8,128)(2,1)S(1)} collective-permute-done((bf16[256,512]{0,1:T(8,128)(2,1)S(1)}, bf16[256,512]{0,1:T(8,128)(2,1)S(1)}, u32[]{:S(2)}, u32[]{:S(2)}) %collective-permute-start.10) | collective-permute-done | bytes 262176 | tf_op jit(solution)/shard_map/ppermute | solution.py:79
  141.3 1.7 collective-permute-start.11
  143.0 2.7 %collective-permute-done.19 = bf16[256,1024]{1,0:T(8,128)(2,1)S(1)} collective-permute-done((bf16[256,1024]{1,0:T(8,128)(2,1)S(1)}, bf16[256,1024]{1,0:T(8,128)(2,1)S(1)}, u32[]{:S(2)}, u32[]{:S(2)}) %collective-permute-start.19) | collective-permute-done | bytes 524320 | tf_op jit(solution)/shard_map/ppermute | solution.py:13
  147.2 1.4 collective-permute-start.20
  149.9 12.5 %collective-permute-done.15 = f32[256,512]{0,1:T(8,128)S(1)} collective-permute-done((f32[256,512]{0,1:T(8,128)S(1)}, f32[256,512]{0,1:T(8,128)S(1)}, u32[]{:S(2)}, u32[]{:S(2)}) %collective-permute-start.15) | collective-permute-done | bytes 524320 | tf_op jit(solution)/shard_map/ppermute | solution.py:67
  164.5 5.2 %collective-permute-done.16 = bf16[256,512]{0,1:T(8,128)(2,1)S(1)} collective-permute-done((bf16[256,512]{0,1:T(8,128)(2,1)S(1)}, bf16[256,512]{0,1:T(8,128)(2,1)S(1)}, u32[]{:S(2)}, u32[]{:S(2)}) %collective-permute-start.16) | collective-permute-done | bytes 262176 | tf_op jit(solution)/shard_map/ppermute | solution.py:79
  169.9 3.1 %collective-permute-start.17 = (bf16[512,512]{0,1:T(8,128)(2,1)S(1)}, bf16[512,512]{0,1:T(8,128)(2,1)S(1)}, u32[]{:S(2)}, u32[]{:S(2)}) collective-permute-start(bf16[512,512]{0,1:T(8,128)(2,1)S(1)} %maximum_select_fusion.9), channel_id=1, source_target_pairs={{0,2},{2,0},{4,6},{6,4},{1,3},{3,1},{5,7},{7,5},{8,10},{10,8},{12,... | collective-permute-start | bytes 1572872 | tf_op jit(solution)/shard_map/ppermute | solution.py:79
  173.0 8.0 %collective-permute-done.21 = f32[256,512]{0,1:T(8,128)S(1)} collective-permute-done((f32[256,512]{0,1:T(8,128)S(1)}, f32[256,512]{0,1:T(8,128)S(1)}, u32[]{:S(2)}, u32[]{:S(2)}) %collective-permute-start.21) | collective-permute-done | bytes 524320 | tf_op jit(solution)/shard_map/ppermute | solution.py:67
  182.4 1.3 fusion.19
  183.7 4.0 %collective-permute-done.22 = bf16[256,512]{0,1:T(8,128)(2,1)S(1)} collective-permute-done((bf16[256,512]{0,1:T(8,128)(2,1)S(1)}, bf16[256,512]{0,1:T(8,128)(2,1)S(1)}, u32[]{:S(2)}, u32[]{:S(2)}) %collective-permute-start.22) | collective-permute-done | bytes 262176 | tf_op jit(solution)/shard_map/ppermute | solution.py:79
  187.9 2.7 %collective-permute-start.23 = (bf16[512,512]{0,1:T(8,128)(2,1)S(1)}, bf16[512,512]{0,1:T(8,128)(2,1)S(1)}, u32[]{:S(2)}, u32[]{:S(2)}) collective-permute-start(bf16[512,512]{0,1:T(8,128)(2,1)S(1)} %maximum_select_fusion.10), channel_id=1, source_target_pairs={{0,2},{2,0},{4,6},{6,4},{1,3},{3,1},{5,7},{7,5},{8,10},{10,8},{12,... | collective-permute-start | bytes 1572872 | tf_op jit(solution)/shard_map/ppermute | solution.py:79
  190.5 1.5 fusion.20
  193.4 3.1 %fusion = bf16[1,1024,1024]{2,1,0:T(8,128)(2,1)} fusion(f32[1024,1024]{1,0:T(8,128)S(1)} %fusion.21, f32[1024,1024]{1,0:T(8,128)S(1)} %fusion.19, f32[1024,1024]{1,0:T(8,128)S(1)} %fusion.20, bf16[512,1024]{1,0:T(8,128)(2,1)S(1)} %constant_dynamic-update-slice_fusion.6, bf16[512,512]{0,1:T(8,128)(2,1)S(1)} %collective-permute-done.23, ...), kind=kOutput, calls=%fused_computation.1 | convolution fusion | flops 1083703296 | bytes 16777216 | tf_op jit(solution)/shard_map/dot_general | solution.py:141
  (79 shorter events, 23.6 us)
Async XLA Ops:
  2.8 26.0 %collective-permute-start = (bf16[256,1024]{1,0:T(8,128)(2,1)S(1)}, bf16[256,1024]{1,0:T(8,128)(2,1)S(1)}, u32[]{:S(2)}, u32[]{:S(2)}) collective-permute-start(bf16[256,1024]{1,0:T(8,128)(2,1)S(1)} %get-tuple-element.21), channel_id=1, source_target_pairs={{0,16},{8,24},{16,0},{24,8},{1,17},{9,25},{17,1},{25,9},{2,18},{10... | collective-permute-start | bytes 1572872 | tf_op jit(solution)/shard_map/ppermute | solution.py:13
  28.8 12.2 %collective-permute-start.1 = (bf16[256,1024]{1,0:T(8,128)(2,1)S(1)}, bf16[256,1024]{1,0:T(8,128)(2,1)S(1)}, u32[]{:S(2)}, u32[]{:S(2)}) collective-permute-start(bf16[256,1024]{1,0:T(8,128)(2,1)S(1)} %collective-permute-done), channel_id=1, source_target_pairs={{0,1},{1,0},{2,3},{3,2},{4,5},{5,4},{6,7},{7,6},{8,9},{9,8},{10,11... | collective-permute-start | bytes 1572872 | tf_op jit(solution)/shard_map/ppermute | solution.py:13
  29.8 24.1 %collective-permute-start.6 = (bf16[256,1024]{1,0:T(8,128)(2,1)S(1)}, bf16[256,1024]{1,0:T(8,128)(2,1)}, u32[]{:S(2)}, u32[]{:S(2)}) collective-permute-start(bf16[256,1024]{1,0:T(8,128)(2,1)S(1)} %get-tuple-element.11), channel_id=1, source_target_pairs={{0,16},{8,24},{16,0},{24,8},{1,17},{9,25},{17,1},{25,9},{2,18},{10... | collective-permute-start | bytes 1572872 | tf_op jit(solution)/shard_map/ppermute | solution.py:13
  43.9 10.7 %copy-start.1 = (f32[512,1024]{1,0:T(8,128)}, f32[512,1024]{1,0:T(8,128)S(1)}, u32[]{:S(2)}) copy-start(f32[512,1024]{1,0:T(8,128)S(1)} %fusion.7) | copy-start | bytes 6291460
  53.9 11.3 %collective-permute-start.7 = (bf16[256,1024]{1,0:T(8,128)(2,1)}, bf16[256,1024]{1,0:T(8,128)(2,1)}, u32[]{:S(2)}, u32[]{:S(2)}) collective-permute-start(bf16[256,1024]{1,0:T(8,128)(2,1)} %collective-permute-done.6), channel_id=1, source_target_pairs={{0,1},{1,0},{2,3},{3,2},{4,5},{5,4},{6,7},{7,6},{8,9},{9,8},{10,11... | collective-permute-start | bytes 1572872 | tf_op jit(solution)/shard_map/ppermute | solution.py:13
  54.7 18.9 %collective-permute-start.2 = (f32[512,512]{0,1:T(8,128)S(1)}, f32[512,512]{0,1:T(8,128)}, u32[]{:S(2)}, u32[]{:S(2)}) collective-permute-start(f32[512,512]{0,1:T(8,128)S(1)} %dynamic-slice_bitcast_fusion.3), channel_id=1, source_target_pairs={{0,2},{2,0},{4,6},{6,4},{1,3},{3,1},{5,7},{7,5},{8,10},{10,8},{12,... | collective-permute-start | bytes 3145736 | tf_op jit(solution)/shard_map/ppermute | solution.py:67
  69.2 5.9 %copy-start = (f32[512,1024]{1,0:T(8,128)}, f32[512,1024]{1,0:T(8,128)S(1)}, u32[]{:S(2)}) copy-start(f32[512,1024]{1,0:T(8,128)S(1)} %fusion.5) | copy-start | bytes 6291460
  69.2 4.4 %copy-start.2 = (f32[512,1024]{1,0:T(8,128)S(1)}, f32[512,1024]{1,0:T(8,128)}, u32[]{:S(2)}) copy-start(f32[512,1024]{1,0:T(8,128)} %copy-done.1) | copy-start | bytes 6291460
  70.2 6.9 %copy-start.6 = (f32[4]{0:T(128)S(1)}, f32[4]{0:T(128)}, u32[]{:S(2)}) copy-start(f32[4]{0:T(128)} %param.4) | copy-start | bytes 52
  70.2 8.8 %copy-start.5 = (f32[2048]{0:T(1024)S(1)}, f32[2048]{0:T(1024)}, u32[]{:S(2)}) copy-start(f32[2048]{0:T(1024)} %param.5) | copy-start | bytes 24580
  70.2 34.5 %collective-permute-start.8 = (f32[512,512]{0,1:T(8,128)}, f32[512,512]{0,1:T(8,128)}, u32[]{:S(2)}, u32[]{:S(2)}) collective-permute-start(f32[512,512]{0,1:T(8,128)} %dynamic-slice_bitcast_fusion.2), channel_id=1, source_target_pairs={{0,2},{2,0},{4,6},{6,4},{1,3},{3,1},{5,7},{7,5},{8,10},{10,8},{12,... | collective-permute-start | bytes 3145736 | tf_op jit(solution)/shard_map/ppermute | solution.py:67
  75.9 12.1 %collective-permute-start.3 = (f32[256,512]{0,1:T(8,128)}, f32[256,512]{0,1:T(8,128)}, u32[]{:S(2)}, u32[]{:S(2)}) collective-permute-start(f32[256,512]{0,1:T(8,128)} %constant_dynamic-slice_fusion.3), channel_id=1, source_target_pairs={{0,4},{2,6},{4,0},{6,2},{1,5},{3,7},{5,1},{7,3},{8,12},{10,14},{12... | collective-permute-start | bytes 1572872 | tf_op jit(solution)/shard_map/ppermute | solution.py:67
  79.0 25.5 %collective-permute-start.12 = (bf16[256,1024]{1,0:T(8,128)(2,1)}, bf16[256,1024]{1,0:T(8,128)(2,1)}, u32[]{:S(2)}, u32[]{:S(2)}) collective-permute-start(bf16[256,1024]{1,0:T(8,128)(2,1)} %get-tuple-element.13), channel_id=1, source_target_pairs={{0,16},{8,24},{16,0},{24,8},{1,17},{9,25},{17,1},{25,9},{2,18},{10... | collective-permute-start | bytes 1572872 | tf_op jit(solution)/shard_map/ppermute | solution.py:13
  89.1 18.4 %copy-start.4 = (bf16[256,1024]{1,0:T(8,128)(2,1)S(1)}, bf16[256,1024]{1,0:T(8,128)(2,1)}, u32[]{:S(2)}) copy-start(bf16[256,1024]{1,0:T(8,128)(2,1)} %get-tuple-element.15) | copy-start | bytes 1572868
  89.2 19.5 %collective-permute-start.4 = (bf16[256,512]{0,1:T(8,128)(2,1)S(1)}, bf16[256,512]{0,1:T(8,128)(2,1)S(1)}, u32[]{:S(2)}, u32[]{:S(2)}) collective-permute-start(bf16[256,512]{0,1:T(8,128)(2,1)S(1)} %divide_convert_fusion.3), channel_id=1, source_target_pairs={{0,4},{2,6},{4,0},{6,2},{1,5},{3,7},{5,1},{7,3},{8,12},{10,14},{12... | collective-permute-start | bytes 786440 | tf_op jit(solution)/shard_map/ppermute | solution.py:79
  104.5 12.3 %collective-permute-start.13 = (bf16[256,1024]{1,0:T(8,128)(2,1)}, bf16[256,1024]{1,0:T(8,128)(2,1)S(1)}, u32[]{:S(2)}, u32[]{:S(2)}) collective-permute-start(bf16[256,1024]{1,0:T(8,128)(2,1)} %collective-permute-done.12), channel_id=1, source_target_pairs={{0,1},{1,0},{2,3},{3,2},{4,5},{5,4},{6,7},{7,6},{8,9},{9,8},{10,11... | collective-permute-start | bytes 1572872 | tf_op jit(solution)/shard_map/ppermute | solution.py:13
  106.4 10.3 %copy-start.3 = (bf16[1,1024,1024]{2,1,0:T(8,128)(2,1)S(1)}, bf16[1,1024,1024]{2,1,0:T(8,128)(2,1)}, u32[]{:S(2)}) copy-start(bf16[1,1024,1024]{2,1,0:T(8,128)(2,1)} %param.3) | copy-start | bytes 6291460
  106.5 27.0 %collective-permute-start.9 = (f32[256,512]{0,1:T(8,128)S(1)}, f32[256,512]{0,1:T(8,128)S(1)}, u32[]{:S(2)}, u32[]{:S(2)}) collective-permute-start(f32[256,512]{0,1:T(8,128)S(1)} %constant_dynamic-slice_fusion.2), channel_id=1, source_target_pairs={{0,4},{2,6},{4,0},{6,2},{1,5},{3,7},{5,1},{7,3},{8,12},{10,14},{12... | collective-permute-start | bytes 1572872 | tf_op jit(solution)/shard_map/ppermute | solution.py:67
  107.6 25.2 %collective-permute-start.18 = (bf16[256,1024]{1,0:T(8,128)(2,1)S(1)}, bf16[256,1024]{1,0:T(8,128)(2,1)S(1)}, u32[]{:S(2)}, u32[]{:S(2)}) collective-permute-start(bf16[256,1024]{1,0:T(8,128)(2,1)S(1)} %copy-done.4), channel_id=1, source_target_pairs={{0,16},{8,24},{16,0},{24,8},{1,17},{9,25},{17,1},{25,9},{2,18},{10... | collective-permute-start | bytes 1572872 | tf_op jit(solution)/shard_map/ppermute | solution.py:13
  108.8 24.8 %collective-permute-start.5 = (bf16[512,512]{0,1:T(8,128)(2,1)S(1)}, bf16[512,512]{0,1:T(8,128)(2,1)S(1)}, u32[]{:S(2)}, u32[]{:S(2)}) collective-permute-start(bf16[512,512]{0,1:T(8,128)(2,1)S(1)} %maximum_select_fusion.7), channel_id=1, source_target_pairs={{0,2},{2,0},{4,6},{6,4},{1,3},{3,1},{5,7},{7,5},{8,10},{10,8},{12,... | collective-permute-start | bytes 1572872 | tf_op jit(solution)/shard_map/ppermute | solution.py:79
  118.2 30.4 %collective-permute-start.14 = (f32[512,512]{0,1:T(8,128)S(1)}, f32[512,512]{0,1:T(8,128)S(1)}, u32[]{:S(2)}, u32[]{:S(2)}) collective-permute-start(f32[512,512]{0,1:T(8,128)S(1)} %dynamic-slice_bitcast_fusion.1), channel_id=1, source_target_pairs={{0,2},{2,0},{4,6},{6,4},{1,3},{3,1},{5,7},{7,5},{8,10},{10,8},{12,... | collective-permute-start | bytes 3145736 | tf_op jit(solution)/shard_map/ppermute | solution.py:67
  132.7 13.0 %collective-permute-start.19 = (bf16[256,1024]{1,0:T(8,128)(2,1)S(1)}, bf16[256,1024]{1,0:T(8,128)(2,1)S(1)}, u32[]{:S(2)}, u32[]{:S(2)}) collective-permute-start(bf16[256,1024]{1,0:T(8,128)(2,1)S(1)} %collective-permute-done.18), channel_id=1, source_target_pairs={{0,1},{1,0},{2,3},{3,2},{4,5},{5,4},{6,7},{7,6},{8,9},{9,8},{10,11... | collective-permute-start | bytes 1572872 | tf_op jit(solution)/shard_map/ppermute | solution.py:13
  134.0 7.1 %collective-permute-start.10 = (bf16[256,512]{0,1:T(8,128)(2,1)S(1)}, bf16[256,512]{0,1:T(8,128)(2,1)S(1)}, u32[]{:S(2)}, u32[]{:S(2)}) collective-permute-start(bf16[256,512]{0,1:T(8,128)(2,1)S(1)} %divide_convert_fusion.2), channel_id=1, source_target_pairs={{0,4},{2,6},{4,0},{6,2},{1,5},{3,7},{5,1},{7,3},{8,12},{10,14},{12... | collective-permute-start | bytes 786440 | tf_op jit(solution)/shard_map/ppermute | solution.py:79
  141.3 8.3 %collective-permute-start.11 = (bf16[512,512]{0,1:T(8,128)(2,1)S(1)}, bf16[512,512]{0,1:T(8,128)(2,1)S(1)}, u32[]{:S(2)}, u32[]{:S(2)}) collective-permute-start(bf16[512,512]{0,1:T(8,128)(2,1)S(1)} %maximum_select_fusion.8), channel_id=1, source_target_pairs={{0,2},{2,0},{4,6},{6,4},{1,3},{3,1},{5,7},{7,5},{8,10},{10,8},{12,... | collective-permute-start | bytes 1572872 | tf_op jit(solution)/shard_map/ppermute | solution.py:79
  147.2 16.3 %collective-permute-start.20 = (f32[512,512]{0,1:T(8,128)S(1)}, f32[512,512]{0,1:T(8,128)S(1)}, u32[]{:S(2)}, u32[]{:S(2)}) collective-permute-start(f32[512,512]{0,1:T(8,128)S(1)} %dynamic-slice_bitcast_fusion), channel_id=1, source_target_pairs={{0,2},{2,0},{4,6},{6,4},{1,3},{3,1},{5,7},{7,5},{8,10},{10,8},{12,... | collective-permute-start | bytes 3145736 | tf_op jit(solution)/shard_map/ppermute | solution.py:67
  148.8 13.6 %collective-permute-start.15 = (f32[256,512]{0,1:T(8,128)S(1)}, f32[256,512]{0,1:T(8,128)S(1)}, u32[]{:S(2)}, u32[]{:S(2)}) collective-permute-start(f32[256,512]{0,1:T(8,128)S(1)} %constant_dynamic-slice_fusion.1), channel_id=1, source_target_pairs={{0,4},{2,6},{4,0},{6,2},{1,5},{3,7},{5,1},{7,3},{8,12},{10,14},{12... | collective-permute-start | bytes 1572872 | tf_op jit(solution)/shard_map/ppermute | solution.py:67
  162.7 7.1 %collective-permute-start.16 = (bf16[256,512]{0,1:T(8,128)(2,1)S(1)}, bf16[256,512]{0,1:T(8,128)(2,1)S(1)}, u32[]{:S(2)}, u32[]{:S(2)}) collective-permute-start(bf16[256,512]{0,1:T(8,128)(2,1)S(1)} %divide_convert_fusion.1), channel_id=1, source_target_pairs={{0,4},{2,6},{4,0},{6,2},{1,5},{3,7},{5,1},{7,3},{8,12},{10,14},{12... | collective-permute-start | bytes 786440 | tf_op jit(solution)/shard_map/ppermute | solution.py:79
  163.8 17.2 %collective-permute-start.21 = (f32[256,512]{0,1:T(8,128)S(1)}, f32[256,512]{0,1:T(8,128)S(1)}, u32[]{:S(2)}, u32[]{:S(2)}) collective-permute-start(f32[256,512]{0,1:T(8,128)S(1)} %constant_dynamic-slice_fusion), channel_id=1, source_target_pairs={{0,4},{2,6},{4,0},{6,2},{1,5},{3,7},{5,1},{7,3},{8,12},{10,14},{12... | collective-permute-start | bytes 1572872 | tf_op jit(solution)/shard_map/ppermute | solution.py:67
  169.9 11.2 %collective-permute-start.17 = (bf16[512,512]{0,1:T(8,128)(2,1)S(1)}, bf16[512,512]{0,1:T(8,128)(2,1)S(1)}, u32[]{:S(2)}, u32[]{:S(2)}) collective-permute-start(bf16[512,512]{0,1:T(8,128)(2,1)S(1)} %maximum_select_fusion.9), channel_id=1, source_target_pairs={{0,2},{2,0},{4,6},{6,4},{1,3},{3,1},{5,7},{7,5},{8,10},{10,8},{12,... | collective-permute-start | bytes 1572872 | tf_op jit(solution)/shard_map/ppermute | solution.py:79
  181.6 6.2 %collective-permute-start.22 = (bf16[256,512]{0,1:T(8,128)(2,1)S(1)}, bf16[256,512]{0,1:T(8,128)(2,1)S(1)}, u32[]{:S(2)}, u32[]{:S(2)}) collective-permute-start(bf16[256,512]{0,1:T(8,128)(2,1)S(1)} %divide_convert_fusion), channel_id=1, source_target_pairs={{0,4},{2,6},{4,0},{6,2},{1,5},{3,7},{5,1},{7,3},{8,12},{10,14},{12... | collective-permute-start | bytes 786440 | tf_op jit(solution)/shard_map/ppermute | solution.py:79
  187.9 5.5 %collective-permute-start.23 = (bf16[512,512]{0,1:T(8,128)(2,1)S(1)}, bf16[512,512]{0,1:T(8,128)(2,1)S(1)}, u32[]{:S(2)}, u32[]{:S(2)}) collective-permute-start(bf16[512,512]{0,1:T(8,128)(2,1)S(1)} %maximum_select_fusion.10), channel_id=1, source_target_pairs={{0,2},{2,0},{4,6},{6,4},{1,3},{3,1},{5,7},{7,5},{8,10},{10,8},{12,... | collective-permute-start | bytes 1572872 | tf_op jit(solution)/shard_map/ppermute | solution.py:79

commit v8 on v5

--- a/solution.py
+++ b/solution.py
@@ -124,7 +124,7 @@
             summed = lax.psum_scatter(partial, "aux", scatter_dimension=0, tiled=True)
             first = first_row
         if rows_done is not None:
-            summed, _ = lax.optimization_barrier((summed, rows_done))
+            summed, _ = lax.optimization_barrier((summed, (rows_done, total)))
         row_level = lax.dynamic_slice_in_dim(vir_energy, vir_pos * vir_rows + first, share)
         amplitudes = (summed / (pair_level - row_level[:, None] - col_level[None, :])).astype(
             jnp.bfloat16

time: 176 us -> 181 us (1.028)
  local copies, waits for them, and re-layouts: 8.45 us -> 14.2 us
  other arithmetic: 4.46 us -> 6.72 us
    ppermute x8, waiting for transfers between devices: 86.7 us -> 76.3 us  [shifted_2(): lax.ppermute(value, axis, [(i, (i + by) % count) for i in range(count)])]
    ppermute x8, waiting for transfers between devices: 8.3 us -> 15.9 us  [aux_all_gather(): other = lax.ppermute(x, 'aux', xor_pairs(count, step))]
    ppermute x8, starting transfers between devices: 8.82 us -> 5.2 us  [aux_reduce_scatter(): x = keep + lax.ppermute(send, 'aux', xor_pairs(count, step))]
    unnamed x10 -> x20, local copies, waits for them, and re-layouts: 2.41 us -> 5.24 us
    concatenate x4, local copies, waits for them, and re-layouts: 1.18 us -> 3.27 us  [paired_plan(): block = jnp.concatenate([arrived, mate])]
    ppermute x8, waiting for transfers between devices: 13.9 us -> 15.8 us  [aux_reduce_scatter(): x = keep + lax.ppermute(send, 'aux', xor_pairs(count, step))]
  transfers between devices with their start and end apart: 24 -> 24, of which waited for: 12 -> 12; matrix products, arithmetic and copies ran while one was open for 11% -> 15% of each run, Pallas kernels for 0% -> 0%
where the time goes in v8:
time: 181 us; the launch traced here: 180 us
  waiting for transfers between devices  108 us (60%)
  starting transfers between devices  36.1 us (20%)
  local copies, waits for them, and re-layouts  14.2 us (8%)
  matrix products  13.3 us (7%)
  other arithmetic  6.72 us (4%)
    ppermute x8, waiting for transfers between devices, shifted_2(): lax.ppermute(value, axis, [(i, (i + by) % count) for i in range(count)])  76.3 us
    ppermute x8, starting transfers between devices, aux_all_gather(): other = lax.ppermute(x, 'aux', xor_pairs(count, step))  24.6 us
    ppermute x8, waiting for transfers between devices, aux_all_gather(): other = lax.ppermute(x, 'aux', xor_pairs(count, step))  15.9 us
    ppermute x8, waiting for transfers between devices, aux_reduce_scatter(): x = keep + lax.ppermute(send, 'aux', xor_pairs(count, step))  15.8 us
    dot_general x4, matrix products, paired_plan(): jnp.einsum('aq,bq->ab', own, block, preferred_element_type=jnp.float32)  6.73 us
    dot_general x4, matrix products, paired_plan(): term = jnp.dot(rows, block, preferred_element_type=jnp.float32)  6.6 us
    ppermute x8, starting transfers between devices, shifted_2(): lax.ppermute(value, axis, [(i, (i + by) % count) for i in range(count)])  6.31 us
    unnamed x20, local copies, waits for them, and re-layouts  5.24 us
  transfers between devices with their start and end apart: 24, of which 12 were waited for; matrix products, arithmetic and copies ran while one was open for 15% of the time, Pallas kernels for 0%

profile of v8, /device:TPU:1, one launch (start us, length us, event | category | flops | bytes accessed | tf_op | source)
XLA Modules:
  0.0 179.9 jit_solution(15626561315971025199)
XLA Ops:
  0.0 2.7 %slice_bitcast_fusion = (bf16[256,1024]{1,0:T(8,128)(2,1)}, bf16[256,1024]{1,0:T(8,128)(2,1)}, bf16[256,1024]{1,0:T(8,128)(2,1)S(1)}, bf16[256,1024]{1,0:T(8,128)(2,1)}) fusion(bf16[1,1024,1024]{2,1,0:T(8,128)(2,1)} %param.3), kind=kLoop, calls=%fused_computation.36 | loop fusion | bytes 4194304 | tf_op jit(solution)/shard_map/slice | solution.py:105
  2.7 3.1 %collective-permute-start = (bf16[256,1024]{1,0:T(8,128)(2,1)S(1)}, bf16[256,1024]{1,0:T(8,128)(2,1)}, u32[]{:S(2)}, u32[]{:S(2)}) collective-permute-start(bf16[256,1024]{1,0:T(8,128)(2,1)S(1)} %get-tuple-element.19), channel_id=1, source_target_pairs={{0,16},{8,24},{16,0},{24,8},{1,17},{9,25},{17,1},{25,9},{2,18},{10... | collective-permute-start | bytes 1572872 | tf_op jit(solution)/shard_map/ppermute | solution.py:13
  5.8 23.0 %collective-permute-done = bf16[256,1024]{1,0:T(8,128)(2,1)} collective-permute-done((bf16[256,1024]{1,0:T(8,128)(2,1)S(1)}, bf16[256,1024]{1,0:T(8,128)(2,1)}, u32[]{:S(2)}, u32[]{:S(2)}) %collective-permute-start) | collective-permute-done | bytes 524320 | tf_op jit(solution)/shard_map/ppermute | solution.py:13
  30.9 22.5 %collective-permute-done.6 = bf16[256,1024]{1,0:T(8,128)(2,1)} collective-permute-done((bf16[256,1024]{1,0:T(8,128)(2,1)}, bf16[256,1024]{1,0:T(8,128)(2,1)}, u32[]{:S(2)}, u32[]{:S(2)}) %collective-permute-start.6) | collective-permute-done | bytes 524320 | tf_op jit(solution)/shard_map/ppermute | solution.py:13
  54.6 1.3 fusion.6
  57.3 2.3 %collective-permute-start.2 = (f32[512,512]{0,1:T(8,128)S(1)}, f32[512,512]{0,1:T(8,128)}, u32[]{:S(2)}, u32[]{:S(2)}) collective-permute-start(f32[512,512]{0,1:T(8,128)S(1)} %dynamic-slice_bitcast_fusion.3), channel_id=1, source_target_pairs={{0,2},{2,0},{4,6},{6,4},{1,3},{3,1},{5,7},{7,5},{8,10},{10,8},{12,... | collective-permute-start | bytes 3145736 | tf_op jit(solution)/shard_map/ppermute | solution.py:68
  62.5 17.0 %collective-permute-done.12 = bf16[256,1024]{1,0:T(8,128)(2,1)} collective-permute-done((bf16[256,1024]{1,0:T(8,128)(2,1)}, bf16[256,1024]{1,0:T(8,128)(2,1)}, u32[]{:S(2)}, u32[]{:S(2)}) %collective-permute-start.12) | collective-permute-done | bytes 524320 | tf_op jit(solution)/shard_map/ppermute | solution.py:13
  80.7 2.9 %fusion.4 = f32[512,1024]{1,0:T(8,128)S(1)} fusion(bf16[512,1024]{1,0:T(8,128)(2,1)S(1)} %constant_dynamic-update-slice_fusion.2, bf16[1,1024,1024]{2,1,0:T(8,128)(2,1)} %param.3), kind=kOutput, calls=%fused_computation.7 | convolution fusion | flops 1073741824 | bytes 5242880 | tf_op jit(solution)/shard_map/aq,bq->ab/dot_general | solution.py:120
  86.3 1.4 bitcast_add_fusion.3
  90.8 13.8 %collective-permute-done.18 = bf16[256,1024]{1,0:T(8,128)(2,1)} collective-permute-done((bf16[256,1024]{1,0:T(8,128)(2,1)}, bf16[256,1024]{1,0:T(8,128)(2,1)}, u32[]{:S(2)}, u32[]{:S(2)}) %collective-permute-start.18) | collective-permute-done | bytes 524320 | tf_op jit(solution)/shard_map/ppermute | solution.py:13
  107.6 1.3 collective-permute-start.4
  108.9 1.4 bitcast_add_fusion.2
  110.9 1.3 fusion.2
  112.2 2.6 %collective-permute-done.4 = bf16[256,512]{0,1:T(8,128)(2,1)S(1)} collective-permute-done((bf16[256,512]{0,1:T(8,128)(2,1)S(1)}, bf16[256,512]{0,1:T(8,128)(2,1)S(1)}, u32[]{:S(2)}, u32[]{:S(2)}) %collective-permute-start.4) | collective-permute-done | bytes 262176 | tf_op jit(solution)/shard_map/ppermute | solution.py:80
  114.9 3.0 %collective-permute-start.5 = (bf16[512,512]{0,1:T(8,128)(2,1)S(1)}, bf16[512,512]{0,1:T(8,128)(2,1)S(1)}, u32[]{:S(2)}, u32[]{:S(2)}) collective-permute-start(bf16[512,512]{0,1:T(8,128)(2,1)S(1)} %maximum_select_fusion.5), channel_id=1, source_target_pairs={{0,2},{2,0},{4,6},{6,4},{1,3},{3,1},{5,7},{7,5},{8,10},{10,8},{12,... | collective-permute-start | bytes 1572872 | tf_op jit(solution)/shard_map/ppermute | solution.py:80
  119.2 6.8 %collective-permute-done.9 = f32[256,512]{0,1:T(8,128)S(1)} collective-permute-done((f32[256,512]{0,1:T(8,128)S(1)}, f32[256,512]{0,1:T(8,128)S(1)}, u32[]{:S(2)}, u32[]{:S(2)}) %collective-permute-start.9) | collective-permute-done | bytes 524320 | tf_op jit(solution)/shard_map/ppermute | solution.py:68
  126.4 1.3 fusion.18
  127.8 1.3 collective-permute-start.10
  129.7 4.3 %collective-permute-done.10 = bf16[256,512]{0,1:T(8,128)(2,1)S(1)} collective-permute-done((bf16[256,512]{0,1:T(8,128)(2,1)S(1)}, bf16[256,512]{0,1:T(8,128)(2,1)S(1)}, u32[]{:S(2)}, u32[]{:S(2)}) %collective-permute-start.10) | collective-permute-done | bytes 262176 | tf_op jit(solution)/shard_map/ppermute | solution.py:80
  134.2 4.8 %collective-permute-start.11 = (bf16[512,512]{0,1:T(8,128)(2,1)S(1)}, bf16[512,512]{0,1:T(8,128)(2,1)S(1)}, u32[]{:S(2)}, u32[]{:S(2)}) collective-permute-start(bf16[512,512]{0,1:T(8,128)(2,1)S(1)} %maximum_select_fusion.6), channel_id=1, source_target_pairs={{0,2},{2,0},{4,6},{6,4},{1,3},{3,1},{5,7},{7,5},{8,10},{10,8},{12,... | collective-permute-start | bytes 1572872 | tf_op jit(solution)/shard_map/ppermute | solution.py:80
  140.5 4.8 %collective-permute-done.15 = f32[256,512]{0,1:T(8,128)S(1)} collective-permute-done((f32[256,512]{0,1:T(8,128)S(1)}, f32[256,512]{0,1:T(8,128)S(1)}, u32[]{:S(2)}, u32[]{:S(2)}) %collective-permute-start.15) | collective-permute-done | bytes 524320 | tf_op jit(solution)/shard_map/ppermute | solution.py:68
  145.7 1.3 convolution_add_fusion.1
  147.2 1.3 collective-permute-start.16
  149.0 3.4 %collective-permute-done.16 = bf16[256,512]{0,1:T(8,128)(2,1)S(1)} collective-permute-done((bf16[256,512]{0,1:T(8,128)(2,1)S(1)}, bf16[256,512]{0,1:T(8,128)(2,1)S(1)}, u32[]{:S(2)}, u32[]{:S(2)}) %collective-permute-start.16) | collective-permute-done | bytes 262176 | tf_op jit(solution)/shard_map/ppermute | solution.py:80
  152.6 6.8 %collective-permute-start.17 = (bf16[512,512]{0,1:T(8,128)(2,1)S(1)}, bf16[512,512]{0,1:T(8,128)(2,1)S(1)}, u32[]{:S(2)}, u32[]{:S(2)}) collective-permute-start(bf16[512,512]{0,1:T(8,128)(2,1)S(1)} %maximum_select_fusion.7), channel_id=1, source_target_pairs={{0,2},{2,0},{4,6},{6,4},{1,3},{3,1},{5,7},{7,5},{8,10},{10,8},{12,... | collective-permute-start | bytes 1572872 | tf_op jit(solution)/shard_map/ppermute | solution.py:80
  159.5 4.2 %collective-permute-done.21 = f32[256,512]{0,1:T(8,128)S(1)} collective-permute-done((f32[256,512]{0,1:T(8,128)S(1)}, f32[256,512]{0,1:T(8,128)S(1)}, u32[]{:S(2)}, u32[]{:S(2)}) %collective-permute-start.21) | collective-permute-done | bytes 524320 | tf_op jit(solution)/shard_map/ppermute | solution.py:68
  164.1 1.4 convolution_add_fusion
  165.6 1.3 collective-permute-start.22
  166.9 4.0 %collective-permute-done.22 = bf16[256,512]{0,1:T(8,128)(2,1)S(1)} collective-permute-done((bf16[256,512]{0,1:T(8,128)(2,1)S(1)}, bf16[256,512]{0,1:T(8,128)(2,1)S(1)}, u32[]{:S(2)}, u32[]{:S(2)}) %collective-permute-start.22) | collective-permute-done | bytes 262176 | tf_op jit(solution)/shard_map/ppermute | solution.py:80
  171.0 4.7 %collective-permute-start.23 = (bf16[512,512]{0,1:T(8,128)(2,1)S(1)}, bf16[512,512]{0,1:T(8,128)(2,1)S(1)}, u32[]{:S(2)}, u32[]{:S(2)}) collective-permute-start(bf16[512,512]{0,1:T(8,128)(2,1)S(1)} %maximum_select_fusion.8), channel_id=1, source_target_pairs={{0,2},{2,0},{4,6},{6,4},{1,3},{3,1},{5,7},{7,5},{8,10},{10,8},{12,... | collective-permute-start | bytes 1572872 | tf_op jit(solution)/shard_map/ppermute | solution.py:80
  175.8 1.5 collective-permute-done.23
  177.3 2.6 %fusion.8 = bf16[1,1024,1024]{2,1,0:T(8,128)(2,1)} fusion(f32[1024,1024]{1,0:T(8,128)S(1)} %convolution_add_fusion, bf16[512,1024]{1,0:T(8,128)(2,1)S(1)} %constant_dynamic-update-slice_fusion.6, bf16[512,512]{0,1:T(8,128)(2,1)S(1)} %collective-permute-done.23, bf16[512,512]{0,1:T(8,128)(2,1)S(1)} %maximum_select_fusion.8, pred[]{:T(512)S(6)} %eq.30), kind=kOutput, calls=%fused_computation.11 | convolution fusion | flops 1081606144 | bytes 8388609 | tf_op jit(solution)/shard_map/dot_general | solution.py:137
  (81 shorter events, 22.8 us)
Async XLA Ops:
  2.7 51.9 %copy-start.4 = (bf16[1,1024,1024]{2,1,0:T(8,128)(2,1)S(1)}, bf16[1,1024,1024]{2,1,0:T(8,128)(2,1)}, u32[]{:S(2)}) copy-start(bf16[1,1024,1024]{2,1,0:T(8,128)(2,1)} %param.3) | copy-start | bytes 6291460
  2.7 26.1 %collective-permute-start = (bf16[256,1024]{1,0:T(8,128)(2,1)S(1)}, bf16[256,1024]{1,0:T(8,128)(2,1)}, u32[]{:S(2)}, u32[]{:S(2)}) collective-permute-start(bf16[256,1024]{1,0:T(8,128)(2,1)S(1)} %get-tuple-element.19), channel_id=1, source_target_pairs={{0,16},{8,24},{16,0},{24,8},{1,17},{9,25},{17,1},{25,9},{2,18},{10... | collective-permute-start | bytes 1572872 | tf_op jit(solution)/shard_map/ppermute | solution.py:13
  28.8 24.6 %collective-permute-start.6 = (bf16[256,1024]{1,0:T(8,128)(2,1)}, bf16[256,1024]{1,0:T(8,128)(2,1)}, u32[]{:S(2)}, u32[]{:S(2)}) collective-permute-start(bf16[256,1024]{1,0:T(8,128)(2,1)} %get-tuple-element.11), channel_id=1, source_target_pairs={{0,16},{8,24},{16,0},{24,8},{1,17},{9,25},{17,1},{25,9},{2,18},{10... | collective-permute-start | bytes 1572872 | tf_op jit(solution)/shard_map/ppermute | solution.py:13
  28.8 24.7 %collective-permute-start.1 = (bf16[256,1024]{1,0:T(8,128)(2,1)}, bf16[256,1024]{1,0:T(8,128)(2,1)}, u32[]{:S(2)}, u32[]{:S(2)}) collective-permute-start(bf16[256,1024]{1,0:T(8,128)(2,1)} %collective-permute-done), channel_id=1, source_target_pairs={{0,1},{1,0},{2,3},{3,2},{4,5},{5,4},{6,7},{7,6},{8,9},{9,8},{10,11... | collective-permute-start | bytes 1572872 | tf_op jit(solution)/shard_map/ppermute | solution.py:13
  53.5 26.1 %collective-permute-start.12 = (bf16[256,1024]{1,0:T(8,128)(2,1)}, bf16[256,1024]{1,0:T(8,128)(2,1)}, u32[]{:S(2)}, u32[]{:S(2)}) collective-permute-start(bf16[256,1024]{1,0:T(8,128)(2,1)} %get-tuple-element.13), channel_id=1, source_target_pairs={{0,16},{8,24},{16,0},{24,8},{1,17},{9,25},{17,1},{25,9},{2,18},{10... | collective-permute-start | bytes 1572872 | tf_op jit(solution)/shard_map/ppermute | solution.py:13
  55.9 1.3 copy-start
  55.9 3.6 %copy-start.7 = (f32[4]{0:T(128)S(1)}, f32[4]{0:T(128)}, u32[]{:S(2)}) copy-start(f32[4]{0:T(128)} %param.4) | copy-start | bytes 52
  55.9 5.4 %copy-start.6 = (f32[2048]{0:T(1024)S(1)}, f32[2048]{0:T(1024)}, u32[]{:S(2)}) copy-start(f32[2048]{0:T(1024)} %param.5) | copy-start | bytes 24580
  55.9 23.7 %collective-permute-start.7 = (bf16[256,1024]{1,0:T(8,128)(2,1)}, bf16[256,1024]{1,0:T(8,128)(2,1)}, u32[]{:S(2)}, u32[]{:S(2)}) collective-permute-start(bf16[256,1024]{1,0:T(8,128)(2,1)} %collective-permute-done.6), channel_id=1, source_target_pairs={{0,1},{1,0},{2,3},{3,2},{4,5},{5,4},{6,7},{7,6},{8,9},{9,8},{10,11... | collective-permute-start | bytes 1572872 | tf_op jit(solution)/shard_map/ppermute | solution.py:13
  57.3 28.8 %collective-permute-start.2 = (f32[512,512]{0,1:T(8,128)S(1)}, f32[512,512]{0,1:T(8,128)}, u32[]{:S(2)}, u32[]{:S(2)}) collective-permute-start(f32[512,512]{0,1:T(8,128)S(1)} %dynamic-slice_bitcast_fusion.3), channel_id=1, source_target_pairs={{0,2},{2,0},{4,6},{6,4},{1,3},{3,1},{5,7},{7,5},{8,10},{10,8},{12,... | collective-permute-start | bytes 3145736 | tf_op jit(solution)/shard_map/ppermute | solution.py:68
  79.6 25.0 %collective-permute-start.18 = (bf16[256,1024]{1,0:T(8,128)(2,1)}, bf16[256,1024]{1,0:T(8,128)(2,1)}, u32[]{:S(2)}, u32[]{:S(2)}) collective-permute-start(bf16[256,1024]{1,0:T(8,128)(2,1)} %get-tuple-element.15), channel_id=1, source_target_pairs={{0,16},{8,24},{16,0},{24,8},{1,17},{9,25},{17,1},{25,9},{2,18},{10... | collective-permute-start | bytes 1572872 | tf_op jit(solution)/shard_map/ppermute | solution.py:13
  83.5 4.2 %copy-start.2 = (f32[512,1024]{1,0:T(8,128)}, f32[512,1024]{1,0:T(8,128)S(1)}, u32[]{:S(2)}) copy-start(f32[512,1024]{1,0:T(8,128)S(1)} %fusion.4) | copy-start | bytes 6291460
  83.5 2.7 %copy-start.1 = (f32[512,1024]{1,0:T(8,128)S(1)}, f32[512,1024]{1,0:T(8,128)}, u32[]{:S(2)}) copy-start(f32[512,1024]{1,0:T(8,128)} %copy-done) | copy-start | bytes 6291460
  84.7 24.2 %collective-permute-start.8 = (f32[512,512]{0,1:T(8,128)}, f32[512,512]{0,1:T(8,128)}, u32[]{:S(2)}, u32[]{:S(2)}) collective-permute-start(f32[512,512]{0,1:T(8,128)} %dynamic-slice_bitcast_fusion.2), channel_id=1, source_target_pairs={{0,2},{2,0},{4,6},{6,4},{1,3},{3,1},{5,7},{7,5},{8,10},{10,8},{12,... | collective-permute-start | bytes 3145736 | tf_op jit(solution)/shard_map/ppermute | solution.py:68
  85.4 19.9 %collective-permute-start.13 = (bf16[256,1024]{1,0:T(8,128)(2,1)}, bf16[256,1024]{1,0:T(8,128)(2,1)}, u32[]{:S(2)}, u32[]{:S(2)}) collective-permute-start(bf16[256,1024]{1,0:T(8,128)(2,1)} %collective-permute-done.12), channel_id=1, source_target_pairs={{0,1},{1,0},{2,3},{3,2},{4,5},{5,4},{6,7},{7,6},{8,9},{9,8},{10,11... | collective-permute-start | bytes 1572872 | tf_op jit(solution)/shard_map/ppermute | solution.py:13
  88.6 17.8 %collective-permute-start.3 = (f32[256,512]{0,1:T(8,128)}, f32[256,512]{0,1:T(8,128)}, u32[]{:S(2)}, u32[]{:S(2)}) collective-permute-start(f32[256,512]{0,1:T(8,128)} %constant_dynamic-slice_fusion.3), channel_id=1, source_target_pairs={{0,4},{2,6},{4,0},{6,2},{1,5},{3,7},{5,1},{7,3},{8,12},{10,14},{12... | collective-permute-start | bytes 1572872 | tf_op jit(solution)/shard_map/ppermute | solution.py:68
  89.6 19.3 %copy-start.3 = (f32[512,1024]{1,0:T(8,128)S(1)}, f32[512,1024]{1,0:T(8,128)}, u32[]{:S(2)}) copy-start(f32[512,1024]{1,0:T(8,128)} %copy-done.2) | copy-start | bytes 6291460
  104.6 14.5 %collective-permute-start.19 = (bf16[256,1024]{1,0:T(8,128)(2,1)}, bf16[256,1024]{1,0:T(8,128)(2,1)S(1)}, u32[]{:S(2)}, u32[]{:S(2)}) collective-permute-start(bf16[256,1024]{1,0:T(8,128)(2,1)} %collective-permute-done.18), channel_id=1, source_target_pairs={{0,1},{1,0},{2,3},{3,2},{4,5},{5,4},{6,7},{7,6},{8,9},{9,8},{10,11... | collective-permute-start | bytes 1572872 | tf_op jit(solution)/shard_map/ppermute | solution.py:13
  107.6 3.3 %copy-start.5 = (bf16[1,1024,1024]{2,1,0:T(8,128)(2,1)S(1)}, bf16[1,1024,1024]{2,1,0:T(8,128)(2,1)}, u32[]{:S(2)}) copy-start(bf16[1,1024,1024]{2,1,0:T(8,128)(2,1)} %param.3) | copy-start | bytes 6291460
  107.6 7.1 %collective-permute-start.4 = (bf16[256,512]{0,1:T(8,128)(2,1)S(1)}, bf16[256,512]{0,1:T(8,128)(2,1)S(1)}, u32[]{:S(2)}, u32[]{:S(2)}) collective-permute-start(bf16[256,512]{0,1:T(8,128)(2,1)S(1)} %divide_convert_fusion.3), channel_id=1, source_target_pairs={{0,4},{2,6},{4,0},{6,2},{1,5},{3,7},{5,1},{7,3},{8,12},{10,14},{12... | collective-permute-start | bytes 786440 | tf_op jit(solution)/shard_map/ppermute | solution.py:80
  110.4 15.6 %collective-permute-start.9 = (f32[256,512]{0,1:T(8,128)S(1)}, f32[256,512]{0,1:T(8,128)S(1)}, u32[]{:S(2)}, u32[]{:S(2)}) collective-permute-start(f32[256,512]{0,1:T(8,128)S(1)} %constant_dynamic-slice_fusion.2), channel_id=1, source_target_pairs={{0,4},{2,6},{4,0},{6,2},{1,5},{3,7},{5,1},{7,3},{8,12},{10,14},{12... | collective-permute-start | bytes 1572872 | tf_op jit(solution)/shard_map/ppermute | solution.py:68
  114.9 11.2 %collective-permute-start.5 = (bf16[512,512]{0,1:T(8,128)(2,1)S(1)}, bf16[512,512]{0,1:T(8,128)(2,1)S(1)}, u32[]{:S(2)}, u32[]{:S(2)}) collective-permute-start(bf16[512,512]{0,1:T(8,128)(2,1)S(1)} %maximum_select_fusion.5), channel_id=1, source_target_pairs={{0,2},{2,0},{4,6},{6,4},{1,3},{3,1},{5,7},{7,5},{8,10},{10,8},{12,... | collective-permute-start | bytes 1572872 | tf_op jit(solution)/shard_map/ppermute | solution.py:80
  117.9 11.2 %collective-permute-start.14 = (f32[512,512]{0,1:T(8,128)S(1)}, f32[512,512]{0,1:T(8,128)S(1)}, u32[]{:S(2)}, u32[]{:S(2)}) collective-permute-start(f32[512,512]{0,1:T(8,128)S(1)} %dynamic-slice_bitcast_fusion.1), channel_id=1, source_target_pairs={{0,2},{2,0},{4,6},{6,4},{1,3},{3,1},{5,7},{7,5},{8,10},{10,8},{12,... | collective-permute-start | bytes 3145736 | tf_op jit(solution)/shard_map/ppermute | solution.py:68
  127.8 6.2 %collective-permute-start.10 = (bf16[256,512]{0,1:T(8,128)(2,1)S(1)}, bf16[256,512]{0,1:T(8,128)(2,1)S(1)}, u32[]{:S(2)}, u32[]{:S(2)}) collective-permute-start(bf16[256,512]{0,1:T(8,128)(2,1)S(1)} %divide_convert_fusion.2), channel_id=1, source_target_pairs={{0,4},{2,6},{4,0},{6,2},{1,5},{3,7},{5,1},{7,3},{8,12},{10,14},{12... | collective-permute-start | bytes 786440 | tf_op jit(solution)/shard_map/ppermute | solution.py:80
  129.4 15.9 %collective-permute-start.15 = (f32[256,512]{0,1:T(8,128)S(1)}, f32[256,512]{0,1:T(8,128)S(1)}, u32[]{:S(2)}, u32[]{:S(2)}) collective-permute-start(f32[256,512]{0,1:T(8,128)S(1)} %constant_dynamic-slice_fusion.1), channel_id=1, source_target_pairs={{0,4},{2,6},{4,0},{6,2},{1,5},{3,7},{5,1},{7,3},{8,12},{10,14},{12... | collective-permute-start | bytes 1572872 | tf_op jit(solution)/shard_map/ppermute | solution.py:68
  134.2 11.2 %collective-permute-start.11 = (bf16[512,512]{0,1:T(8,128)(2,1)S(1)}, bf16[512,512]{0,1:T(8,128)(2,1)S(1)}, u32[]{:S(2)}, u32[]{:S(2)}) collective-permute-start(bf16[512,512]{0,1:T(8,128)(2,1)S(1)} %maximum_select_fusion.6), channel_id=1, source_target_pairs={{0,2},{2,0},{4,6},{6,4},{1,3},{3,1},{5,7},{7,5},{8,10},{10,8},{12,... | collective-permute-start | bytes 1572872 | tf_op jit(solution)/shard_map/ppermute | solution.py:80
  140.4 8.1 %collective-permute-start.20 = (f32[512,512]{0,1:T(8,128)S(1)}, f32[512,512]{0,1:T(8,128)S(1)}, u32[]{:S(2)}, u32[]{:S(2)}) collective-permute-start(f32[512,512]{0,1:T(8,128)S(1)} %dynamic-slice_bitcast_fusion), channel_id=1, source_target_pairs={{0,2},{2,0},{4,6},{6,4},{1,3},{3,1},{5,7},{7,5},{8,10},{10,8},{12,... | collective-permute-start | bytes 3145736 | tf_op jit(solution)/shard_map/ppermute | solution.py:68
  147.2 5.3 %collective-permute-start.16 = (bf16[256,512]{0,1:T(8,128)(2,1)S(1)}, bf16[256,512]{0,1:T(8,128)(2,1)S(1)}, u32[]{:S(2)}, u32[]{:S(2)}) collective-permute-start(bf16[256,512]{0,1:T(8,128)(2,1)S(1)} %divide_convert_fusion.1), channel_id=1, source_target_pairs={{0,4},{2,6},{4,0},{6,2},{1,5},{3,7},{5,1},{7,3},{8,12},{10,14},{12... | collective-permute-start | bytes 786440 | tf_op jit(solution)/shard_map/ppermute | solution.py:80
  148.7 15.0 %collective-permute-start.21 = (f32[256,512]{0,1:T(8,128)S(1)}, f32[256,512]{0,1:T(8,128)S(1)}, u32[]{:S(2)}, u32[]{:S(2)}) collective-permute-start(f32[256,512]{0,1:T(8,128)S(1)} %constant_dynamic-slice_fusion), channel_id=1, source_target_pairs={{0,4},{2,6},{4,0},{6,2},{1,5},{3,7},{5,1},{7,3},{8,12},{10,14},{12... | collective-permute-start | bytes 1572872 | tf_op jit(solution)/shard_map/ppermute | solution.py:68
  152.6 11.2 %collective-permute-start.17 = (bf16[512,512]{0,1:T(8,128)(2,1)S(1)}, bf16[512,512]{0,1:T(8,128)(2,1)S(1)}, u32[]{:S(2)}, u32[]{:S(2)}) collective-permute-start(bf16[512,512]{0,1:T(8,128)(2,1)S(1)} %maximum_select_fusion.7), channel_id=1, source_target_pairs={{0,2},{2,0},{4,6},{6,4},{1,3},{3,1},{5,7},{7,5},{8,10},{10,8},{12,... | collective-permute-start | bytes 1572872 | tf_op jit(solution)/shard_map/ppermute | solution.py:80
  165.6 5.3 %collective-permute-start.22 = (bf16[256,512]{0,1:T(8,128)(2,1)S(1)}, bf16[256,512]{0,1:T(8,128)(2,1)S(1)}, u32[]{:S(2)}, u32[]{:S(2)}) collective-permute-start(bf16[256,512]{0,1:T(8,128)(2,1)S(1)} %divide_convert_fusion), channel_id=1, source_target_pairs={{0,4},{2,6},{4,0},{6,2},{1,5},{3,7},{5,1},{7,3},{8,12},{10,14},{12... | collective-permute-start | bytes 786440 | tf_op jit(solution)/shard_map/ppermute | solution.py:80
  171.0 6.3 %collective-permute-start.23 = (bf16[512,512]{0,1:T(8,128)(2,1)S(1)}, bf16[512,512]{0,1:T(8,128)(2,1)S(1)}, u32[]{:S(2)}, u32[]{:S(2)}) collective-permute-start(bf16[512,512]{0,1:T(8,128)(2,1)S(1)} %maximum_select_fusion.8), channel_id=1, source_target_pairs={{0,2},{2,0},{4,6},{6,4},{1,3},{3,1},{5,7},{7,5},{8,10},{10,8},{12,... | collective-permute-start | bytes 1572872 | tf_op jit(solution)/shard_map/ppermute | solution.py:80

commit v9 on v5

--- a/solution.py
+++ b/solution.py
@@ -6,6 +6,7 @@
 CHUNKS = 4
 AUX_BY_PERMUTE = True
 NARROW_FAR = False
+Z_DEPTH = 2
 
 
 def shifted_2(value, axis, by):
@@ -99,14 +100,14 @@
         first_row = lax.axis_index("aux") * share
 
     total = None
-    previous = None
+    landed = []
     rows_done = None
     for c in range(CHUNKS):
         piece = own[c * width:(c + 1) * width]
-        if previous is not None:
-            piece, _ = lax.optimization_barrier((piece, previous))
+        if c >= Z_DEPTH:
+            piece, _ = lax.optimization_barrier((piece, landed[c - Z_DEPTH]))
         arrived = shifted_2(piece, "occ", 2)
-        previous = arrived
+        landed.append(arrived)
         if vir_count == 2:
             mate = shifted_2(arrived, "vir", 1)
             block = jnp.concatenate([arrived, mate])

time: 176 us -> 204 us (1.16)
  waiting for transfers between devices: 109 us -> 144 us
  local copies, waits for them, and re-layouts: 8.45 us -> 5.38 us
    ppermute x8, waiting for transfers between devices: 8.3 us -> 28.6 us  [aux_all_gather(): other = lax.ppermute(x, 'aux', xor_pairs(count, step))]
    ppermute x8, waiting for transfers between devices: 13.9 us -> 25.3 us  [aux_reduce_scatter(): x = keep + lax.ppermute(send, 'aux', xor_pairs(count, step))]
    ppermute x8, starting transfers between devices: 22.9 us -> 14.2 us  [aux_all_gather(): other = lax.ppermute(x, 'aux', xor_pairs(count, step))]
    ppermute x8, starting transfers between devices: 8.82 us -> 14.6 us  [aux_reduce_scatter(): x = keep + lax.ppermute(send, 'aux', xor_pairs(count, step))]
    ppermute x8, waiting for transfers between devices: 86.7 us -> 89.7 us  [shifted_2(): lax.ppermute(value, axis, [(i, (i + by) % count) for i in range(count)])]
    ppermute x8, starting transfers between devices: 6.26 us -> 8.75 us  [shifted_2(): lax.ppermute(value, axis, [(i, (i + by) % count) for i in range(count)])]
    unnamed x10, local copies, waits for them, and re-layouts: 2.41 us -> 0.15 us
  transfers between devices with their start and end apart: 24 -> 24, of which waited for: 12 -> 13; matrix products, arithmetic and copies ran while one was open for 11% -> 7% of each run, Pallas kernels for 0% -> 0%
where the time goes in v9:
time: 204 us
  waiting for transfers between devices  144 us (71%)
  starting transfers between devices  37.5 us (18%)
  matrix products  12.3 us (6%)
  local copies, waits for them, and re-layouts  5.38 us (3%)
  other arithmetic  3.2 us (2%)
    ppermute x8, waiting for transfers between devices, shifted_2(): lax.ppermute(value, axis, [(i, (i + by) % count) for i in range(count)])  89.7 us
    ppermute x8, waiting for transfers between devices, aux_all_gather(): other = lax.ppermute(x, 'aux', xor_pairs(count, step))  28.6 us
    ppermute x8, waiting for transfers between devices, aux_reduce_scatter(): x = keep + lax.ppermute(send, 'aux', xor_pairs(count, step))  25.3 us
    ppermute x8, starting transfers between devices, aux_reduce_scatter(): x = keep + lax.ppermute(send, 'aux', xor_pairs(count, step))  14.6 us
    ppermute x8, starting transfers between devices, aux_all_gather(): other = lax.ppermute(x, 'aux', xor_pairs(count, step))  14.2 us
    ppermute x8, starting transfers between devices, shifted_2(): lax.ppermute(value, axis, [(i, (i + by) % count) for i in range(count)])  8.75 us
    dot_general x4, matrix products, paired_plan(): term = jnp.dot(rows, block, preferred_element_type=jnp.float32)  7.2 us
    dot_general x4, matrix products, paired_plan(): jnp.einsum('aq,bq->ab', own, block, preferred_element_type=jnp.float32)  5.15 us
  transfers between devices with their start and end apart: 24, of which 13 were waited for; matrix products, arithmetic and copies ran while one was open for 7% of the time, Pallas kernels for 0%

profile of v9, /device:TPU:1, one launch (start us, length us, event | category | flops | bytes accessed | tf_op | source)
XLA Modules:
  0.0 203.6 jit_solution(1072710138344047516)
XLA Ops:
  0.0 2.9 %slice_bitcast_fusion = (bf16[256,1024]{1,0:T(8,128)(2,1)}, bf16[256,1024]{1,0:T(8,128)(2,1)}, bf16[256,1024]{1,0:T(8,128)(2,1)}, bf16[256,1024]{1,0:T(8,128)(2,1)}) fusion(bf16[1,1024,1024]{2,1,0:T(8,128)(2,1)} %param.3), kind=kLoop, calls=%fused_computation.35 | loop fusion | bytes 4194304 | tf_op jit(solution)/shard_map/slice | solution.py:106
  2.9 3.1 %collective-permute-start = (bf16[256,1024]{1,0:T(8,128)(2,1)}, bf16[256,1024]{1,0:T(8,128)(2,1)S(1)}, u32[]{:S(2)}, u32[]{:S(2)}) collective-permute-start(bf16[256,1024]{1,0:T(8,128)(2,1)} %get-tuple-element.17), channel_id=1, source_target_pairs={{0,16},{8,24},{16,0},{24,8},{1,17},{9,25},{17,1},{25,9},{2,18},{10... | collective-permute-start | bytes 1572872 | tf_op jit(solution)/shard_map/ppermute | solution.py:14
  7.9 32.5 %collective-permute-done = bf16[256,1024]{1,0:T(8,128)(2,1)S(1)} collective-permute-done((bf16[256,1024]{1,0:T(8,128)(2,1)}, bf16[256,1024]{1,0:T(8,128)(2,1)S(1)}, u32[]{:S(2)}, u32[]{:S(2)}) %collective-permute-start) | collective-permute-done | bytes 524320 | tf_op jit(solution)/shard_map/ppermute | solution.py:14
  41.5 10.1 %collective-permute-done.6 = bf16[256,1024]{1,0:T(8,128)(2,1)S(1)} collective-permute-done((bf16[256,1024]{1,0:T(8,128)(2,1)}, bf16[256,1024]{1,0:T(8,128)(2,1)S(1)}, u32[]{:S(2)}, u32[]{:S(2)}) %collective-permute-start.6) | collective-permute-done | bytes 524320 | tf_op jit(solution)/shard_map/ppermute | solution.py:14
  51.6 2.4 %collective-permute-start.12 = (bf16[256,1024]{1,0:T(8,128)(2,1)}, bf16[256,1024]{1,0:T(8,128)(2,1)S(1)}, u32[]{:S(2)}, u32[]{:S(2)}) collective-permute-start(bf16[256,1024]{1,0:T(8,128)(2,1)} %get-tuple-element.11), channel_id=1, source_target_pairs={{0,16},{8,24},{16,0},{24,8},{1,17},{9,25},{17,1},{25,9},{2,18},{10... | collective-permute-start | bytes 1572872 | tf_op jit(solution)/shard_map/ppermute | solution.py:14
  55.1 1.1 constant_dynamic-update-slice_fusion
  56.2 1.3 fusion.7
  57.6 2.4 %collective-permute-start.2 = (f32[512,512]{0,1:T(8,128)S(1)}, f32[512,512]{0,1:T(8,128)S(1)}, u32[]{:S(2)}, u32[]{:S(2)}) collective-permute-start(f32[512,512]{0,1:T(8,128)S(1)} %dynamic-slice_bitcast_fusion.3), channel_id=1, source_target_pairs={{0,2},{2,0},{4,6},{6,4},{1,3},{3,1},{5,7},{7,5},{8,10},{10,8},{12,... | collective-permute-start | bytes 3145736 | tf_op jit(solution)/shard_map/ppermute | solution.py:69
  60.0 38.6 %collective-permute-done.12 = bf16[256,1024]{1,0:T(8,128)(2,1)S(1)} collective-permute-done((bf16[256,1024]{1,0:T(8,128)(2,1)}, bf16[256,1024]{1,0:T(8,128)(2,1)S(1)}, u32[]{:S(2)}, u32[]{:S(2)}) %collective-permute-start.12) | collective-permute-done | bytes 524320 | tf_op jit(solution)/shard_map/ppermute | solution.py:14
  99.4 1.3 fusion.5
  100.8 2.8 %collective-permute-start.8 = (f32[512,512]{0,1:T(8,128)S(1)}, f32[512,512]{0,1:T(8,128)S(1)}, u32[]{:S(2)}, u32[]{:S(2)}) collective-permute-start(f32[512,512]{0,1:T(8,128)S(1)} %dynamic-slice_bitcast_fusion.2), channel_id=1, source_target_pairs={{0,2},{2,0},{4,6},{6,4},{1,3},{3,1},{5,7},{7,5},{8,10},{10,8},{12,... | collective-permute-start | bytes 3145736 | tf_op jit(solution)/shard_map/ppermute | solution.py:69
  104.1 5.8 %collective-permute-done.13 = bf16[256,1024]{1,0:T(8,128)(2,1)S(1)} collective-permute-done((bf16[256,1024]{1,0:T(8,128)(2,1)S(1)}, bf16[256,1024]{1,0:T(8,128)(2,1)S(1)}, u32[]{:S(2)}, u32[]{:S(2)}) %collective-permute-start.13) | collective-permute-done | bytes 524320 | tf_op jit(solution)/shard_map/ppermute | solution.py:14
  109.9 1.3 fusion.3
  111.3 5.8 %collective-permute-start.14 = (f32[512,512]{0,1:T(8,128)S(1)}, f32[512,512]{0,1:T(8,128)S(1)}, u32[]{:S(2)}, u32[]{:S(2)}) collective-permute-start(f32[512,512]{0,1:T(8,128)S(1)} %dynamic-slice_bitcast_fusion.1), channel_id=1, source_target_pairs={{0,2},{2,0},{4,6},{6,4},{1,3},{3,1},{5,7},{7,5},{8,10},{10,8},{12,... | collective-permute-start | bytes 3145736 | tf_op jit(solution)/shard_map/ppermute | solution.py:69
  118.4 2.7 %collective-permute-done.19 = bf16[256,1024]{1,0:T(8,128)(2,1)S(1)} collective-permute-done((bf16[256,1024]{1,0:T(8,128)(2,1)S(1)}, bf16[256,1024]{1,0:T(8,128)(2,1)S(1)}, u32[]{:S(2)}, u32[]{:S(2)}) %collective-permute-start.19) | collective-permute-done | bytes 524320 | tf_op jit(solution)/shard_map/ppermute | solution.py:14
  121.9 9.1 %collective-permute-done.3 = f32[256,512]{0,1:T(8,128)S(1)} collective-permute-done((f32[256,512]{0,1:T(8,128)S(1)}, f32[256,512]{0,1:T(8,128)S(1)}, u32[]{:S(2)}, u32[]{:S(2)}) %collective-permute-start.3) | collective-permute-done | bytes 524320 | tf_op jit(solution)/shard_map/ppermute | solution.py:69
  132.2 1.3 fusion.1
  133.5 14.4 %collective-permute-done.4 = bf16[256,512]{0,1:T(8,128)(2,1)S(1)} collective-permute-done((bf16[256,512]{0,1:T(8,128)(2,1)S(1)}, bf16[256,512]{0,1:T(8,128)(2,1)S(1)}, u32[]{:S(2)}, u32[]{:S(2)}) %collective-permute-start.4) | collective-permute-done | bytes 262176 | tf_op jit(solution)/shard_map/ppermute | solution.py:81
  149.2 1.2 collective-permute-done.5
  153.6 4.9 %collective-permute-done.10 = bf16[256,512]{0,1:T(8,128)(2,1)S(1)} collective-permute-done((bf16[256,512]{0,1:T(8,128)(2,1)S(1)}, bf16[256,512]{0,1:T(8,128)(2,1)S(1)}, u32[]{:S(2)}, u32[]{:S(2)}) %collective-permute-start.10) | collective-permute-done | bytes 262176 | tf_op jit(solution)/shard_map/ppermute | solution.py:81
  158.6 2.1 %collective-permute-start.11 = (bf16[512,512]{0,1:T(8,128)(2,1)S(1)}, bf16[512,512]{0,1:T(8,128)(2,1)S(1)}, u32[]{:S(2)}, u32[]{:S(2)}) collective-permute-start(bf16[512,512]{0,1:T(8,128)(2,1)S(1)} %maximum_select_fusion.8), channel_id=1, source_target_pairs={{0,2},{2,0},{4,6},{6,4},{1,3},{3,1},{5,7},{7,5},{8,10},{10,8},{12,... | collective-permute-start | bytes 1572872 | tf_op jit(solution)/shard_map/ppermute | solution.py:81
  160.6 9.0 %collective-permute-done.15 = f32[256,512]{0,1:T(8,128)S(1)} collective-permute-done((f32[256,512]{0,1:T(8,128)S(1)}, f32[256,512]{0,1:T(8,128)S(1)}, u32[]{:S(2)}, u32[]{:S(2)}) %collective-permute-start.15) | collective-permute-done | bytes 524320 | tf_op jit(solution)/shard_map/ppermute | solution.py:69
  172.1 4.8 %collective-permute-done.16 = bf16[256,512]{0,1:T(8,128)(2,1)S(1)} collective-permute-done((bf16[256,512]{0,1:T(8,128)(2,1)S(1)}, bf16[256,512]{0,1:T(8,128)(2,1)S(1)}, u32[]{:S(2)}, u32[]{:S(2)}) %collective-permute-start.16) | collective-permute-done | bytes 262176 | tf_op jit(solution)/shard_map/ppermute | solution.py:81
  177.0 3.9 %collective-permute-start.17 = (bf16[512,512]{0,1:T(8,128)(2,1)S(1)}, bf16[512,512]{0,1:T(8,128)(2,1)S(1)}, u32[]{:S(2)}, u32[]{:S(2)}) collective-permute-start(bf16[512,512]{0,1:T(8,128)(2,1)S(1)} %maximum_select_fusion.9), channel_id=1, source_target_pairs={{0,2},{2,0},{4,6},{6,4},{1,3},{3,1},{5,7},{7,5},{8,10},{10,8},{12,... | collective-permute-start | bytes 1572872 | tf_op jit(solution)/shard_map/ppermute | solution.py:81
  180.9 7.2 %collective-permute-done.21 = f32[256,512]{0,1:T(8,128)S(1)} collective-permute-done((f32[256,512]{0,1:T(8,128)S(1)}, f32[256,512]{0,1:T(8,128)S(1)}, u32[]{:S(2)}, u32[]{:S(2)}) %collective-permute-start.21) | collective-permute-done | bytes 524320 | tf_op jit(solution)/shard_map/ppermute | solution.py:69
  188.7 1.1 collective-permute-start.22
  189.8 1.3 fusion.19
  191.1 3.4 %collective-permute-done.22 = bf16[256,512]{0,1:T(8,128)(2,1)S(1)} collective-permute-done((bf16[256,512]{0,1:T(8,128)(2,1)S(1)}, bf16[256,512]{0,1:T(8,128)(2,1)S(1)}, u32[]{:S(2)}, u32[]{:S(2)}) %collective-permute-start.22) | collective-permute-done | bytes 262176 | tf_op jit(solution)/shard_map/ppermute | solution.py:81
  194.6 3.1 %collective-permute-start.23 = (bf16[512,512]{0,1:T(8,128)(2,1)S(1)}, bf16[512,512]{0,1:T(8,128)(2,1)S(1)}, u32[]{:S(2)}, u32[]{:S(2)}) collective-permute-start(bf16[512,512]{0,1:T(8,128)(2,1)S(1)} %maximum_select_fusion.10), channel_id=1, source_target_pairs={{0,2},{2,0},{4,6},{6,4},{1,3},{3,1},{5,7},{7,5},{8,10},{10,8},{12,... | collective-permute-start | bytes 1572872 | tf_op jit(solution)/shard_map/ppermute | solution.py:81
  197.7 1.5 fusion.20
  199.2 1.3 fusion.21
  200.5 3.1 %fusion = bf16[1,1024,1024]{2,1,0:T(8,128)(2,1)} fusion(f32[1024,1024]{1,0:T(8,128)S(1)} %fusion.21, f32[1024,1024]{1,0:T(8,128)S(1)} %fusion.19, f32[1024,1024]{1,0:T(8,128)S(1)} %fusion.20, bf16[512,1024]{1,0:T(8,128)(2,1)S(1)} %constant_dynamic-update-slice_fusion.6, bf16[512,512]{0,1:T(8,128)(2,1)S(1)} %collective-permute-done.23, ...), kind=kOutput, calls=%fused_computation.1 | convolution fusion | flops 1083703296 | bytes 16777216 | tf_op jit(solution)/shard_map/dot_general | solution.py:138
  (71 shorter events, 15.5 us)
Async XLA Ops:
  0.0 6.1 %copy-start.2 = (f32[4]{0:T(128)S(1)}, f32[4]{0:T(128)}, u32[]{:S(2)}) copy-start(f32[4]{0:T(128)} %param.4) | copy-start | bytes 52
  0.0 41.4 %copy-start.1 = (f32[2048]{0:T(1024)S(1)}, f32[2048]{0:T(1024)}, u32[]{:S(2)}) copy-start(f32[2048]{0:T(1024)} %param.5) | copy-start | bytes 24580
  2.9 53.2 %copy-start = (bf16[1,1024,1024]{2,1,0:T(8,128)(2,1)S(1)}, bf16[1,1024,1024]{2,1,0:T(8,128)(2,1)}, u32[]{:S(2)}) copy-start(bf16[1,1024,1024]{2,1,0:T(8,128)(2,1)} %param.3) | copy-start | bytes 6291460
  2.9 37.5 %collective-permute-start = (bf16[256,1024]{1,0:T(8,128)(2,1)}, bf16[256,1024]{1,0:T(8,128)(2,1)S(1)}, u32[]{:S(2)}, u32[]{:S(2)}) collective-permute-start(bf16[256,1024]{1,0:T(8,128)(2,1)} %get-tuple-element.17), channel_id=1, source_target_pairs={{0,16},{8,24},{16,0},{24,8},{1,17},{9,25},{17,1},{25,9},{2,18},{10... | collective-permute-start | bytes 1572872 | tf_op jit(solution)/shard_map/ppermute | solution.py:14
  6.0 45.6 %collective-permute-start.6 = (bf16[256,1024]{1,0:T(8,128)(2,1)}, bf16[256,1024]{1,0:T(8,128)(2,1)S(1)}, u32[]{:S(2)}, u32[]{:S(2)}) collective-permute-start(bf16[256,1024]{1,0:T(8,128)(2,1)} %get-tuple-element.16), channel_id=1, source_target_pairs={{0,16},{8,24},{16,0},{24,8},{1,17},{9,25},{17,1},{25,9},{2,18},{10... | collective-permute-start | bytes 1572872 | tf_op jit(solution)/shard_map/ppermute | solution.py:14
  40.4 14.7 %collective-permute-start.1 = (bf16[256,1024]{1,0:T(8,128)(2,1)S(1)}, bf16[256,1024]{1,0:T(8,128)(2,1)}, u32[]{:S(2)}, u32[]{:S(2)}) collective-permute-start(bf16[256,1024]{1,0:T(8,128)(2,1)S(1)} %collective-permute-done), channel_id=1, source_target_pairs={{0,1},{1,0},{2,3},{3,2},{4,5},{5,4},{6,7},{7,6},{8,9},{9,8},{10,11... | collective-permute-start | bytes 1572872 | tf_op jit(solution)/shard_map/ppermute | solution.py:14
  51.6 51.9 %collective-permute-start.18 = (bf16[256,1024]{1,0:T(8,128)(2,1)}, bf16[256,1024]{1,0:T(8,128)(2,1)S(1)}, u32[]{:S(2)}, u32[]{:S(2)}) collective-permute-start(bf16[256,1024]{1,0:T(8,128)(2,1)} %get-tuple-element.13), channel_id=1, source_target_pairs={{0,16},{8,24},{16,0},{24,8},{1,17},{9,25},{17,1},{25,9},{2,18},{10... | collective-permute-start | bytes 1572872 | tf_op jit(solution)/shard_map/ppermute | solution.py:14
  51.6 47.0 %collective-permute-start.12 = (bf16[256,1024]{1,0:T(8,128)(2,1)}, bf16[256,1024]{1,0:T(8,128)(2,1)S(1)}, u32[]{:S(2)}, u32[]{:S(2)}) collective-permute-start(bf16[256,1024]{1,0:T(8,128)(2,1)} %get-tuple-element.11), channel_id=1, source_target_pairs={{0,16},{8,24},{16,0},{24,8},{1,17},{9,25},{17,1},{25,9},{2,18},{10... | collective-permute-start | bytes 1572872 | tf_op jit(solution)/shard_map/ppermute | solution.py:14
  54.0 45.4 %collective-permute-start.7 = (bf16[256,1024]{1,0:T(8,128)(2,1)S(1)}, bf16[256,1024]{1,0:T(8,128)(2,1)S(1)}, u32[]{:S(2)}, u32[]{:S(2)}) collective-permute-start(bf16[256,1024]{1,0:T(8,128)(2,1)S(1)} %collective-permute-done.6), channel_id=1, source_target_pairs={{0,1},{1,0},{2,3},{3,2},{4,5},{5,4},{6,7},{7,6},{8,9},{9,8},{10,11... | collective-permute-start | bytes 1572872 | tf_op jit(solution)/shard_map/ppermute | solution.py:14
  57.6 59.6 %collective-permute-start.2 = (f32[512,512]{0,1:T(8,128)S(1)}, f32[512,512]{0,1:T(8,128)S(1)}, u32[]{:S(2)}, u32[]{:S(2)}) collective-permute-start(f32[512,512]{0,1:T(8,128)S(1)} %dynamic-slice_bitcast_fusion.3), channel_id=1, source_target_pairs={{0,2},{2,0},{4,6},{6,4},{1,3},{3,1},{5,7},{7,5},{8,10},{10,8},{12,... | collective-permute-start | bytes 3145736 | tf_op jit(solution)/shard_map/ppermute | solution.py:69
  98.6 11.3 %collective-permute-start.13 = (bf16[256,1024]{1,0:T(8,128)(2,1)S(1)}, bf16[256,1024]{1,0:T(8,128)(2,1)S(1)}, u32[]{:S(2)}, u32[]{:S(2)}) collective-permute-start(bf16[256,1024]{1,0:T(8,128)(2,1)S(1)} %collective-permute-done.12), channel_id=1, source_target_pairs={{0,1},{1,0},{2,3},{3,2},{4,5},{5,4},{6,7},{7,6},{8,9},{9,8},{10,11... | collective-permute-start | bytes 1572872 | tf_op jit(solution)/shard_map/ppermute | solution.py:14
  100.8 20.4 %collective-permute-start.8 = (f32[512,512]{0,1:T(8,128)S(1)}, f32[512,512]{0,1:T(8,128)S(1)}, u32[]{:S(2)}, u32[]{:S(2)}) collective-permute-start(f32[512,512]{0,1:T(8,128)S(1)} %dynamic-slice_bitcast_fusion.2), channel_id=1, source_target_pairs={{0,2},{2,0},{4,6},{6,4},{1,3},{3,1},{5,7},{7,5},{8,10},{10,8},{12,... | collective-permute-start | bytes 3145736 | tf_op jit(solution)/shard_map/ppermute | solution.py:69
  103.5 17.6 %collective-permute-start.19 = (bf16[256,1024]{1,0:T(8,128)(2,1)S(1)}, bf16[256,1024]{1,0:T(8,128)(2,1)S(1)}, u32[]{:S(2)}, u32[]{:S(2)}) collective-permute-start(bf16[256,1024]{1,0:T(8,128)(2,1)S(1)} %collective-permute-done.18), channel_id=1, source_target_pairs={{0,1},{1,0},{2,3},{3,2},{4,5},{5,4},{6,7},{7,6},{8,9},{9,8},{10,11... | collective-permute-start | bytes 1572872 | tf_op jit(solution)/shard_map/ppermute | solution.py:14
  111.3 37.6 %collective-permute-start.14 = (f32[512,512]{0,1:T(8,128)S(1)}, f32[512,512]{0,1:T(8,128)S(1)}, u32[]{:S(2)}, u32[]{:S(2)}) collective-permute-start(f32[512,512]{0,1:T(8,128)S(1)} %dynamic-slice_bitcast_fusion.1), channel_id=1, source_target_pairs={{0,2},{2,0},{4,6},{6,4},{1,3},{3,1},{5,7},{7,5},{8,10},{10,8},{12,... | collective-permute-start | bytes 3145736 | tf_op jit(solution)/shard_map/ppermute | solution.py:69
  117.4 13.6 %collective-permute-start.3 = (f32[256,512]{0,1:T(8,128)S(1)}, f32[256,512]{0,1:T(8,128)S(1)}, u32[]{:S(2)}, u32[]{:S(2)}) collective-permute-start(f32[256,512]{0,1:T(8,128)S(1)} %constant_dynamic-slice_fusion.3), channel_id=1, source_target_pairs={{0,4},{2,6},{4,0},{6,2},{1,5},{3,7},{5,1},{7,3},{8,12},{10,14},{12... | collective-permute-start | bytes 1572872 | tf_op jit(solution)/shard_map/ppermute | solution.py:69
  121.5 27.4 %collective-permute-start.9 = (f32[256,512]{0,1:T(8,128)S(1)}, f32[256,512]{0,1:T(8,128)S(1)}, u32[]{:S(2)}, u32[]{:S(2)}) collective-permute-start(f32[256,512]{0,1:T(8,128)S(1)} %constant_dynamic-slice_fusion.2), channel_id=1, source_target_pairs={{0,4},{2,6},{4,0},{6,2},{1,5},{3,7},{5,1},{7,3},{8,12},{10,14},{12... | collective-permute-start | bytes 1572872 | tf_op jit(solution)/shard_map/ppermute | solution.py:69
  131.1 16.7 %collective-permute-start.4 = (bf16[256,512]{0,1:T(8,128)(2,1)S(1)}, bf16[256,512]{0,1:T(8,128)(2,1)S(1)}, u32[]{:S(2)}, u32[]{:S(2)}) collective-permute-start(bf16[256,512]{0,1:T(8,128)(2,1)S(1)} %divide_convert_fusion.3), channel_id=1, source_target_pairs={{0,4},{2,6},{4,0},{6,2},{1,5},{3,7},{5,1},{7,3},{8,12},{10,14},{12... | collective-permute-start | bytes 786440 | tf_op jit(solution)/shard_map/ppermute | solution.py:81
  148.0 2.4 %collective-permute-start.5 = (bf16[512,512]{0,1:T(8,128)(2,1)S(1)}, bf16[512,512]{0,1:T(8,128)(2,1)S(1)}, u32[]{:S(2)}, u32[]{:S(2)}) collective-permute-start(bf16[512,512]{0,1:T(8,128)(2,1)S(1)} %maximum_select_fusion.7), channel_id=1, source_target_pairs={{0,2},{2,0},{4,6},{6,4},{1,3},{3,1},{5,7},{7,5},{8,10},{10,8},{12,... | collective-permute-start | bytes 1572872 | tf_op jit(solution)/shard_map/ppermute | solution.py:81
  150.8 7.6 %collective-permute-start.10 = (bf16[256,512]{0,1:T(8,128)(2,1)S(1)}, bf16[256,512]{0,1:T(8,128)(2,1)S(1)}, u32[]{:S(2)}, u32[]{:S(2)}) collective-permute-start(bf16[256,512]{0,1:T(8,128)(2,1)S(1)} %divide_convert_fusion.2), channel_id=1, source_target_pairs={{0,4},{2,6},{4,0},{6,2},{1,5},{3,7},{5,1},{7,3},{8,12},{10,14},{12... | collective-permute-start | bytes 786440 | tf_op jit(solution)/shard_map/ppermute | solution.py:81
  151.9 17.7 %collective-permute-start.15 = (f32[256,512]{0,1:T(8,128)S(1)}, f32[256,512]{0,1:T(8,128)S(1)}, u32[]{:S(2)}, u32[]{:S(2)}) collective-permute-start(f32[256,512]{0,1:T(8,128)S(1)} %constant_dynamic-slice_fusion.1), channel_id=1, source_target_pairs={{0,4},{2,6},{4,0},{6,2},{1,5},{3,7},{5,1},{7,3},{8,12},{10,14},{12... | collective-permute-start | bytes 1572872 | tf_op jit(solution)/shard_map/ppermute | solution.py:69
  152.6 18.7 %collective-permute-start.20 = (f32[512,512]{0,1:T(8,128)S(1)}, f32[512,512]{0,1:T(8,128)S(1)}, u32[]{:S(2)}, u32[]{:S(2)}) collective-permute-start(f32[512,512]{0,1:T(8,128)S(1)} %dynamic-slice_bitcast_fusion), channel_id=1, source_target_pairs={{0,2},{2,0},{4,6},{6,4},{1,3},{3,1},{5,7},{7,5},{8,10},{10,8},{12,... | collective-permute-start | bytes 3145736 | tf_op jit(solution)/shard_map/ppermute | solution.py:69
  158.6 11.2 %collective-permute-start.11 = (bf16[512,512]{0,1:T(8,128)(2,1)S(1)}, bf16[512,512]{0,1:T(8,128)(2,1)S(1)}, u32[]{:S(2)}, u32[]{:S(2)}) collective-permute-start(bf16[512,512]{0,1:T(8,128)(2,1)S(1)} %maximum_select_fusion.8), channel_id=1, source_target_pairs={{0,2},{2,0},{4,6},{6,4},{1,3},{3,1},{5,7},{7,5},{8,10},{10,8},{12,... | collective-permute-start | bytes 1572872 | tf_op jit(solution)/shard_map/ppermute | solution.py:81
  170.2 6.7 %collective-permute-start.16 = (bf16[256,512]{0,1:T(8,128)(2,1)S(1)}, bf16[256,512]{0,1:T(8,128)(2,1)S(1)}, u32[]{:S(2)}, u32[]{:S(2)}) collective-permute-start(bf16[256,512]{0,1:T(8,128)(2,1)S(1)} %divide_convert_fusion.1), channel_id=1, source_target_pairs={{0,4},{2,6},{4,0},{6,2},{1,5},{3,7},{5,1},{7,3},{8,12},{10,14},{12... | collective-permute-start | bytes 786440 | tf_op jit(solution)/shard_map/ppermute | solution.py:81
  171.5 16.6 %collective-permute-start.21 = (f32[256,512]{0,1:T(8,128)S(1)}, f32[256,512]{0,1:T(8,128)S(1)}, u32[]{:S(2)}, u32[]{:S(2)}) collective-permute-start(f32[256,512]{0,1:T(8,128)S(1)} %constant_dynamic-slice_fusion), channel_id=1, source_target_pairs={{0,4},{2,6},{4,0},{6,2},{1,5},{3,7},{5,1},{7,3},{8,12},{10,14},{12... | collective-permute-start | bytes 1572872 | tf_op jit(solution)/shard_map/ppermute | solution.py:69
  177.0 11.2 %collective-permute-start.17 = (bf16[512,512]{0,1:T(8,128)(2,1)S(1)}, bf16[512,512]{0,1:T(8,128)(2,1)S(1)}, u32[]{:S(2)}, u32[]{:S(2)}) collective-permute-start(bf16[512,512]{0,1:T(8,128)(2,1)S(1)} %maximum_select_fusion.9), channel_id=1, source_target_pairs={{0,2},{2,0},{4,6},{6,4},{1,3},{3,1},{5,7},{7,5},{8,10},{10,8},{12,... | collective-permute-start | bytes 1572872 | tf_op jit(solution)/shard_map/ppermute | solution.py:81
  188.7 5.7 %collective-permute-start.22 = (bf16[256,512]{0,1:T(8,128)(2,1)S(1)}, bf16[256,512]{0,1:T(8,128)(2,1)S(1)}, u32[]{:S(2)}, u32[]{:S(2)}) collective-permute-start(bf16[256,512]{0,1:T(8,128)(2,1)S(1)} %divide_convert_fusion), channel_id=1, source_target_pairs={{0,4},{2,6},{4,0},{6,2},{1,5},{3,7},{5,1},{7,3},{8,12},{10,14},{12... | collective-permute-start | bytes 786440 | tf_op jit(solution)/shard_map/ppermute | solution.py:81
  194.6 5.9 %collective-permute-start.23 = (bf16[512,512]{0,1:T(8,128)(2,1)S(1)}, bf16[512,512]{0,1:T(8,128)(2,1)S(1)}, u32[]{:S(2)}, u32[]{:S(2)}) collective-permute-start(bf16[512,512]{0,1:T(8,128)(2,1)S(1)} %maximum_select_fusion.10), channel_id=1, source_target_pairs={{0,2},{2,0},{4,6},{6,4},{1,3},{3,1},{5,7},{7,5},{8,10},{10,8},{12,... | collective-permute-start | bytes 1572872 | tf_op jit(solution)/shard_map/ppermute | solution.py:81

commit v10 on v5

--- a/solution.py
+++ b/solution.py
@@ -1,11 +1,12 @@
 import jax
 import jax.numpy as jnp
 from jax import lax
-from jax.sharding import PartitionSpec as P
+from jax.sharding import Mesh, PartitionSpec as P
 
 CHUNKS = 4
 AUX_BY_PERMUTE = True
 NARROW_FAR = False
+Z_BY_GATHER = True
 
 
 def shifted_2(value, axis, by):
@@ -83,11 +84,11 @@
     return x
 
 
-def paired_plan(integrals, occ_energy, vir_energy):
+def paired_plan(integrals, occ_energy, vir_energy, occ="occ", gather_z=False):
     own = integrals[0]
     vir_rows, _ = own.shape
-    cycle_size = lax.axis_size("occ")
-    position = lax.axis_index("occ")
+    cycle_size = lax.axis_size(occ)
+    position = lax.axis_index(occ)
     pair_level = occ_energy[position] + occ_energy[(position - 2) % cycle_size]
     vir_pos = lax.axis_index("vir")
     vir_count = lax.axis_size("vir")
@@ -103,10 +104,14 @@
     rows_done = None
     for c in range(CHUNKS):
         piece = own[c * width:(c + 1) * width]
-        if previous is not None:
-            piece, _ = lax.optimization_barrier((piece, previous))
-        arrived = shifted_2(piece, "occ", 2)
-        previous = arrived
+        if gather_z:
+            pair = lax.all_gather(piece, "occ_hi", axis=0)
+            arrived = lax.dynamic_index_in_dim(pair, 1 - lax.axis_index("occ_hi"), 0, False)
+        else:
+            if previous is not None:
+                piece, _ = lax.optimization_barrier((piece, previous))
+            arrived = shifted_2(piece, "occ", 2)
+            previous = arrived
         if vir_count == 2:
             mate = shifted_2(arrived, "vir", 1)
             block = jnp.concatenate([arrived, mate])
@@ -149,7 +154,24 @@
 
 
 def solution(mesh):
+    if Z_BY_GATHER and mesh.shape["occ"] == 4:
+        names = list(mesh.axis_names)
+        at = names.index("occ")
+        devices = mesh.devices.reshape(
+            mesh.devices.shape[:at] + (2, 2) + mesh.devices.shape[at + 1:]
+        )
+        split = Mesh(devices, tuple(names[:at] + ["occ_hi", "occ_lo"] + names[at + 1:]))
+        occ = ("occ_hi", "occ_lo")
+        spec = P(occ, "vir", "aux")
+        return jax.shard_map(
+            paired_on_split, mesh=split, in_specs=(spec, P(), P()), out_specs=spec,
+            check_vma=False,
+        )
     placed = (P("occ", "vir", "aux"), P(), P())
     return jax.shard_map(
         on_device, mesh=mesh, in_specs=placed, out_specs=P("occ", "vir", "aux"), check_vma=False
     )
+
+
+def paired_on_split(integrals, occ_energy, vir_energy):
+    return paired_plan(integrals, occ_energy, vir_energy, ("occ_hi", "occ_lo"), True)

time: 176 us -> 250 us (1.42)
  waiting for transfers between devices: 109 us -> 170 us
  between operations: 1.54 us -> 14.8 us
  starting transfers between devices: 37.9 us -> 27.6 us
  matrix products: 14 us -> 19.7 us
  local copies, waits for them, and re-layouts: 8.45 us -> 11.9 us
    all_gather x0 -> x4, waiting for transfers between devices: none -> 117 us  [paired_plan(): pair = lax.all_gather(piece, 'occ_hi', axis=0)]
    ppermute x8 -> x4, waiting for transfers between devices: 86.7 us -> 0.01 us  [shifted_2(): lax.ppermute(value, axis, [(i, (i + by) % count) for i in range(count)])]
    ppermute x8, waiting for transfers between devices: 8.3 us -> 27.1 us  [aux_all_gather(): other = lax.ppermute(x, 'aux', xor_pairs(count, step))]
    ppermute x8, waiting for transfers between devices: 13.9 us -> 24.3 us  [aux_reduce_scatter(): x = keep + lax.ppermute(send, 'aux', xor_pairs(count, step))]
    ppermute x8, starting transfers between devices: 22.9 us -> 16.1 us  [aux_all_gather(): other = lax.ppermute(x, 'aux', xor_pairs(count, step))]
    squeeze x0 -> x4, local copies, waits for them, and re-layouts: none -> 5.09 us  [paired_plan(): lax.dynamic_index_in_dim(pair, 1 - lax.axis_index('occ_hi'), 0, False)]
    dot_general x4, matrix products: 7.22 us -> 10.5 us  [paired_plan(): term = jnp.dot(rows, block, preferred_element_type=jnp.float32)]
    ppermute x8 -> x4, starting transfers between devices: 6.26 us -> 4.97 us  [shifted_2(): lax.ppermute(value, axis, [(i, (i + by) % count) for i in range(count)])]
  transfers between devices with their start and end apart: 24 -> 24, of which waited for: 12 -> 12; matrix products, arithmetic and copies ran while one was open for 11% -> 12% of each run, Pallas kernels for 0% -> 0%
where the time goes in v10:
time: 250 us; the launch traced here: 249 us
  waiting for transfers between devices  170 us (68%)
  starting transfers between devices  27.6 us (11%)
  matrix products  19.7 us (8%)
  between operations  14.8 us (6%)
  local copies, waits for them, and re-layouts  11.9 us (5%)
  other arithmetic  5.66 us (2%)
    all_gather x4, waiting for transfers between devices, paired_plan(): pair = lax.all_gather(piece, 'occ_hi', axis=0)  117 us
    ppermute x8, waiting for transfers between devices, aux_all_gather(): other = lax.ppermute(x, 'aux', xor_pairs(count, step))  27.1 us
    ppermute x8, waiting for transfers between devices, aux_reduce_scatter(): x = keep + lax.ppermute(send, 'aux', xor_pairs(count, step))  24.3 us
    ppermute x8, starting transfers between devices, aux_all_gather(): other = lax.ppermute(x, 'aux', xor_pairs(count, step))  16.1 us
    dot_general x4, matrix products, paired_plan(): term = jnp.dot(rows, block, preferred_element_type=jnp.float32)  10.5 us
    dot_general x4, matrix products, paired_plan(): jnp.einsum('aq,bq->ab', own, block, preferred_element_type=jnp.float32)  9.19 us
    ppermute x8, starting transfers between devices, aux_reduce_scatter(): x = keep + lax.ppermute(send, 'aux', xor_pairs(count, step))  6.38 us
    squeeze x4, local copies, waits for them, and re-layouts, paired_plan(): lax.dynamic_index_in_dim(pair, 1 - lax.axis_index('occ_hi'), 0, False)  5.09 us
  transfers between devices with their start and end apart: 24, of which 12 were waited for; matrix products, arithmetic and copies ran while one was open for 12% of the time, Pallas kernels for 0%

profile of v10, /device:TPU:1, one launch (start us, length us, event | category | flops | bytes accessed | tf_op | source)
XLA Modules:
  0.0 249.2 jit_solution(18065844483226767568)
XLA Ops:
  6.5 2.9 %fusion.27 = (bf16[1,256,1024]{2,1,0:T(8,128)(2,1)}, bf16[1,256,1024]{2,1,0:T(8,128)(2,1)}, bf16[1,256,1024]{2,1,0:T(8,128)(2,1)}, bf16[1,256,1024]{2,1,0:T(8,128)(2,1)}) fusion(bf16[1,1024,1024]{2,1,0:T(8,128)(2,1)} %param.3), kind=kLoop, calls=%fused_computation.68 | loop fusion | bytes 4194304 | tf_op jit(solution)/shard_map/slice | solution.py:106
  11.0 34.2 %all-gather.5.cloned.1.call-done = bf16[2,256,1024]{2,1,0:T(8,128)(2,1)} async-done(((bf16[1,256,1024]{2,1,0:T(8,128)(2,1)}), bf16[2,256,1024]{2,1,0:T(8,128)(2,1)}) %all-gather.5.cloned.1.call-update) | async-done | bytes 1048592 | tf_op jit(solution)/shard_map/all_gather | solution.py:108
  49.6 29.6 %all-gather.7.cloned.1.call-done = bf16[2,256,1024]{2,1,0:T(8,128)(2,1)} async-done(((bf16[1,256,1024]{2,1,0:T(8,128)(2,1)}), bf16[2,256,1024]{2,1,0:T(8,128)(2,1)}) %all-gather.7.cloned.1.call-update) | async-done | bytes 1048592 | tf_op jit(solution)/shard_map/all_gather | solution.py:108
  80.3 1.3 collective-permute-start.5
  81.5 31.7 %all-gather.9.cloned.1.call-done = bf16[2,256,1024]{2,1,0:T(8,128)(2,1)} async-done(((bf16[1,256,1024]{2,1,0:T(8,128)(2,1)}), bf16[2,256,1024]{2,1,0:T(8,128)(2,1)}) %all-gather.9.cloned.1.call-update) | async-done | bytes 1048592 | tf_op jit(solution)/shard_map/all_gather | solution.py:108
  113.2 1.9 dynamic-slice_bitcast_fusion.5
  116.3 2.3 fusion.7
  121.5 2.4 fusion.5
  125.9 21.3 %all-gather.11.cloned.1.call-done = bf16[2,256,1024]{2,1,0:T(8,128)(2,1)} async-done(((bf16[1,256,1024]{2,1,0:T(8,128)(2,1)}), bf16[2,256,1024]{2,1,0:T(8,128)(2,1)}) %all-gather.11.cloned.1.call-update) | async-done | bytes 1048592 | tf_op jit(solution)/shard_map/all_gather | solution.py:108
  149.5 3.2 %fusion.3 = f32[512,1024]{1,0:T(8,128)S(1)} fusion(bf16[1,1024,1024]{2,1,0:T(8,128)(2,1)} %param.3, bf16[256,1024]{1,0:T(8,128)(2,1)} %collective-permute-done.10, bf16[256,1024]{1,0:T(8,128)(2,1)} %dynamic-slice_bitcast_fusion.5), kind=kOutput, calls=%fused_computation.4 | convolution fusion | flops 1075838976 | bytes 5242880 | tf_op jit(solution)/shard_map/aq,bq->ab/dot_general | solution.py:125
  152.7 1.4 bitcast_add_fusion.3
  155.6 1.3 collective-permute-start.11
  156.9 1.4 bitcast_add_fusion.2
  158.7 8.0 %collective-permute-done.2 = f32[256,512]{0,1:T(8,128)S(1)} collective-permute-done((f32[256,512]{0,1:T(8,128)S(1)}, f32[256,512]{0,1:T(8,128)S(1)}, u32[]{:S(2)}, u32[]{:S(2)}) %collective-permute-start.2) | collective-permute-done | bytes 524320 | tf_op jit(solution)/shard_map/ppermute | solution.py:69
  166.9 1.3 collective-permute-start.3
  168.2 1.3 fusion.1
  169.5 14.1 %collective-permute-done.3 = bf16[256,512]{0,1:T(8,128)(2,1)S(1)} collective-permute-done((bf16[256,512]{0,1:T(8,128)(2,1)S(1)}, bf16[256,512]{0,1:T(8,128)(2,1)S(1)}, u32[]{:S(2)}, u32[]{:S(2)}) %collective-permute-start.3) | collective-permute-done | bytes 262176 | tf_op jit(solution)/shard_map/ppermute | solution.py:81
  183.8 1.9 collective-permute-start.4
  190.4 4.9 %collective-permute-done.8 = bf16[256,512]{0,1:T(8,128)(2,1)S(1)} collective-permute-done((bf16[256,512]{0,1:T(8,128)(2,1)S(1)}, bf16[256,512]{0,1:T(8,128)(2,1)S(1)}, u32[]{:S(2)}, u32[]{:S(2)}) %collective-permute-start.8) | collective-permute-done | bytes 262176 | tf_op jit(solution)/shard_map/ppermute | solution.py:81
  195.4 2.1 collective-permute-start.9
  197.5 9.0 %collective-permute-done.12 = f32[256,512]{0,1:T(8,128)S(1)} collective-permute-done((f32[256,512]{0,1:T(8,128)S(1)}, f32[256,512]{0,1:T(8,128)S(1)}, u32[]{:S(2)}, u32[]{:S(2)}) %collective-permute-start.12) | collective-permute-done | bytes 524320 | tf_op jit(solution)/shard_map/ppermute | solution.py:69
  207.1 1.3 collective-permute-start.13
  208.9 4.8 %collective-permute-done.13 = bf16[256,512]{0,1:T(8,128)(2,1)S(1)} collective-permute-done((bf16[256,512]{0,1:T(8,128)(2,1)S(1)}, bf16[256,512]{0,1:T(8,128)(2,1)S(1)}, u32[]{:S(2)}, u32[]{:S(2)}) %collective-permute-start.13) | collective-permute-done | bytes 262176 | tf_op jit(solution)/shard_map/ppermute | solution.py:81
  213.9 3.9 %collective-permute-start.14 = (bf16[512,512]{0,1:T(8,128)(2,1)S(1)}, bf16[512,512]{0,1:T(8,128)(2,1)S(1)}, u32[]{:S(2)}, u32[]{:S(2)}) collective-permute-start(bf16[512,512]{0,1:T(8,128)(2,1)S(1)} %maximum_select_fusion.9), channel_id=1, source_target_pairs={{0,2},{2,0},{4,6},{6,4},{1,3},{3,1},{5,7},{7,5},{8,10},{10,8},{12,... | collective-permute-start | bytes 1572872 | tf_op jit(solution)/shard_map/ppermute | solution.py:81
  217.8 7.2 %collective-permute-done.17 = f32[256,512]{0,1:T(8,128)S(1)} collective-permute-done((f32[256,512]{0,1:T(8,128)S(1)}, f32[256,512]{0,1:T(8,128)S(1)}, u32[]{:S(2)}, u32[]{:S(2)}) %collective-permute-start.17) | collective-permute-done | bytes 524320 | tf_op jit(solution)/shard_map/ppermute | solution.py:69
  225.5 1.3 collective-permute-start.18
  226.8 2.3 fusion.18
  229.2 2.1 collective-permute-done.18
  231.4 3.1 %collective-permute-start.19 = (bf16[512,512]{0,1:T(8,128)(2,1)S(1)}, bf16[512,512]{0,1:T(8,128)(2,1)S(1)}, u32[]{:S(2)}, u32[]{:S(2)}) collective-permute-start(bf16[512,512]{0,1:T(8,128)(2,1)S(1)} %maximum_select_fusion.10), channel_id=1, source_target_pairs={{0,2},{2,0},{4,6},{6,4},{1,3},{3,1},{5,7},{7,5},{8,10},{10,8},{12,... | collective-permute-start | bytes 1572872 | tf_op jit(solution)/shard_map/ppermute | solution.py:81
  234.5 2.5 fusion.17
  237.0 2.5 %fusion.16 = f32[1024,1024]{1,0:T(8,128)S(1)} fusion(bf16[1024,512]{0,1:T(8,128)(2,1)S(1)} %maximum_select_fusion.2, bf16[256,1024]{1,0:T(8,128)(2,1)} %collective-permute-done.10, bf16[256,1024]{1,0:T(8,128)(2,1)} %dynamic-slice_bitcast_fusion.5), kind=kOutput, calls=%fused_computation.33 | convolution fusion | flops 1075838976 | bytes 6291456 | tf_op jit(solution)/shard_map/dot_general | solution.py:142
  239.5 3.1 %fusion = bf16[1,1024,1024]{2,1,0:T(8,128)(2,1)} fusion(f32[1024,1024]{1,0:T(8,128)S(1)} %fusion.16, f32[1024,1024]{1,0:T(8,128)S(1)} %fusion.18, f32[1024,1024]{1,0:T(8,128)S(1)} %fusion.17, bf16[512,512]{0,1:T(8,128)(2,1)S(1)} %collective-permute-done.19, bf16[512,512]{0,1:T(8,128)(2,1)S(1)} %maximum_select_fusion.10, pred[]{:T(512)S(6)} %eq.30, ...), kind=kOutput, calls=%fused_computation.1 | convolution fusion | flops 1085800448 | bytes 16777216 | tf_op jit(solution)/shard_map/dot_general | solution.py:142
  (79 shorter events, 22.8 us)
Async XLA Ops:
  6.5 38.6 %all-gather.5.cloned.1.call-start = ((), (), s32[]{:S(2)}) async-start(), calls=%async_computation | async-start | bytes 1572864 | tf_op jit(solution)/shard_map/all_gather | solution.py:108
  9.4 38.2 %copy-start.6 = (f32[4]{0:T(128)S(1)}, f32[4]{0:T(128)}, u32[]{:S(2)}) copy-start(f32[4]{0:T(128)} %param.4) | copy-start | bytes 52
  9.4 40.1 %copy-start.5 = (f32[2048]{0:T(1024)S(1)}, f32[2048]{0:T(1024)}, u32[]{:S(2)}) copy-start(f32[2048]{0:T(1024)} %param.5) | copy-start | bytes 24580
  9.4 69.8 %all-gather.7.cloned.1.call-start = ((), (), s32[]{:S(2)}) async-start(), calls=%async_computation.1 | async-start | bytes 1572864 | tf_op jit(solution)/shard_map/all_gather | solution.py:108
  10.2 103.1 %all-gather.9.cloned.1.call-start = ((), (), s32[]{:S(2)}) async-start(), calls=%async_computation.2 | async-start | bytes 1572864 | tf_op jit(solution)/shard_map/all_gather | solution.py:108
  10.9 105.4 %copy-start.2 = (bf16[1,1024,1024]{2,1,0:T(8,128)(2,1)S(1)}, bf16[1,1024,1024]{2,1,0:T(8,128)(2,1)}, u32[]{:S(2)}) copy-start(bf16[1,1024,1024]{2,1,0:T(8,128)(2,1)} %param.3) | copy-start | bytes 6291460
  10.9 136.2 %all-gather.11.cloned.1.call-start = ((), (), s32[]{:S(2)}) async-start(), calls=%async_computation.3 | async-start | bytes 1572864 | tf_op jit(solution)/shard_map/all_gather | solution.py:108
  46.2 70.1 %collective-permute-start = (bf16[256,1024]{1,0:T(8,128)(2,1)S(1)}, bf16[256,1024]{1,0:T(8,128)(2,1)}, u32[]{:S(2)}, u32[]{:S(2)}) collective-permute-start(bf16[256,1024]{1,0:T(8,128)(2,1)S(1)} %dynamic-slice_bitcast_fusion.7), channel_id=1, source_target_pairs={{0,1},{1,0},{2,3},{3,2},{4,5},{5,4},{6,7},{7,6},{8,9},{9,8},{10,11... | collective-permute-start | bytes 1572872 | tf_op jit(solution)/shard_map/ppermute | solution.py:14
  80.3 40.4 %collective-permute-start.5 = (bf16[256,1024]{1,0:T(8,128)(2,1)S(1)}, bf16[256,1024]{1,0:T(8,128)(2,1)}, u32[]{:S(2)}, u32[]{:S(2)}) collective-permute-start(bf16[256,1024]{1,0:T(8,128)(2,1)S(1)} %dynamic-slice_bitcast_fusion.6), channel_id=1, source_target_pairs={{0,1},{1,0},{2,3},{3,2},{4,5},{5,4},{6,7},{7,6},{8,9},{9,8},{10,11... | collective-permute-start | bytes 1572872 | tf_op jit(solution)/shard_map/ppermute | solution.py:14
  115.1 34.4 %collective-permute-start.10 = (bf16[256,1024]{1,0:T(8,128)(2,1)}, bf16[256,1024]{1,0:T(8,128)(2,1)}, u32[]{:S(2)}, u32[]{:S(2)}) collective-permute-start(bf16[256,1024]{1,0:T(8,128)(2,1)} %dynamic-slice_bitcast_fusion.5), channel_id=1, source_target_pairs={{0,1},{1,0},{2,3},{3,2},{4,5},{5,4},{6,7},{7,6},{8,9},{9,8},{10,11... | collective-permute-start | bytes 1572872 | tf_op jit(solution)/shard_map/ppermute | solution.py:14
  118.6 5.2 %copy-start = (f32[512,1024]{1,0:T(8,128)}, f32[512,1024]{1,0:T(8,128)S(1)}, u32[]{:S(2)}) copy-start(f32[512,1024]{1,0:T(8,128)S(1)} %fusion.7) | copy-start | bytes 6291460
  118.7 2.8 %copy-start.3 = (bf16[1,1024,1024]{2,1,0:T(8,128)(2,1)S(1)}, bf16[1,1024,1024]{2,1,0:T(8,128)(2,1)}, u32[]{:S(2)}) copy-start(bf16[1,1024,1024]{2,1,0:T(8,128)(2,1)} %param.3) | copy-start | bytes 6291460
  119.7 33.0 %collective-permute-start.1 = (f32[512,512]{0,1:T(8,128)}, f32[512,512]{0,1:T(8,128)}, u32[]{:S(2)}, u32[]{:S(2)}) collective-permute-start(f32[512,512]{0,1:T(8,128)} %dynamic-slice_bitcast_fusion.3), channel_id=1, source_target_pairs={{0,2},{2,0},{4,6},{6,4},{1,3},{3,1},{5,7},{7,5},{8,10},{10,8},{12,... | collective-permute-start | bytes 3145736 | tf_op jit(solution)/shard_map/ppermute | solution.py:69
  125.0 31.9 %collective-permute-start.6 = (f32[512,512]{0,1:T(8,128)}, f32[512,512]{0,1:T(8,128)}, u32[]{:S(2)}, u32[]{:S(2)}) collective-permute-start(f32[512,512]{0,1:T(8,128)} %dynamic-slice_bitcast_fusion.2), channel_id=1, source_target_pairs={{0,2},{2,0},{4,6},{6,4},{1,3},{3,1},{5,7},{7,5},{8,10},{10,8},{12,... | collective-permute-start | bytes 3145736 | tf_op jit(solution)/shard_map/ppermute | solution.py:69
  148.2 4.5 %copy-start.1 = (f32[512,1024]{1,0:T(8,128)S(1)}, f32[512,1024]{1,0:T(8,128)}, u32[]{:S(2)}) copy-start(f32[512,1024]{1,0:T(8,128)} %copy-done) | copy-start | bytes 6291460
  148.2 19.9 %collective-permute-start.15 = (bf16[256,1024]{1,0:T(8,128)(2,1)S(1)}, bf16[256,1024]{1,0:T(8,128)(2,1)S(1)}, u32[]{:S(2)}, u32[]{:S(2)}) collective-permute-start(bf16[256,1024]{1,0:T(8,128)(2,1)S(1)} %dynamic-slice_bitcast_fusion.4), channel_id=1, source_target_pairs={{0,1},{1,0},{2,3},{3,2},{4,5},{5,4},{6,7},{7,6},{8,9},{9,8},{10,11... | collective-permute-start | bytes 1572872 | tf_op jit(solution)/shard_map/ppermute | solution.py:14
  154.2 12.5 %collective-permute-start.2 = (f32[256,512]{0,1:T(8,128)S(1)}, f32[256,512]{0,1:T(8,128)S(1)}, u32[]{:S(2)}, u32[]{:S(2)}) collective-permute-start(f32[256,512]{0,1:T(8,128)S(1)} %constant_dynamic-slice_fusion.3), channel_id=1, source_target_pairs={{0,4},{2,6},{4,0},{6,2},{1,5},{3,7},{5,1},{7,3},{8,12},{10,14},{12... | collective-permute-start | bytes 1572872 | tf_op jit(solution)/shard_map/ppermute | solution.py:69
  155.6 12.6 %copy-start.4 = (bf16[1,1024,1024]{2,1,0:T(8,128)(2,1)S(1)}, bf16[1,1024,1024]{2,1,0:T(8,128)(2,1)}, u32[]{:S(2)}) copy-start(bf16[1,1024,1024]{2,1,0:T(8,128)(2,1)} %param.3) | copy-start | bytes 6291460
  155.6 30.1 %collective-permute-start.11 = (f32[512,512]{0,1:T(8,128)S(1)}, f32[512,512]{0,1:T(8,128)S(1)}, u32[]{:S(2)}, u32[]{:S(2)}) collective-permute-start(f32[512,512]{0,1:T(8,128)S(1)} %dynamic-slice_bitcast_fusion.1), channel_id=1, source_target_pairs={{0,2},{2,0},{4,6},{6,4},{1,3},{3,1},{5,7},{7,5},{8,10},{10,8},{12,... | collective-permute-start | bytes 3145736 | tf_op jit(solution)/shard_map/ppermute | solution.py:69
  158.4 27.5 %collective-permute-start.7 = (f32[256,512]{0,1:T(8,128)S(1)}, f32[256,512]{0,1:T(8,128)S(1)}, u32[]{:S(2)}, u32[]{:S(2)}) collective-permute-start(f32[256,512]{0,1:T(8,128)S(1)} %constant_dynamic-slice_fusion.2), channel_id=1, source_target_pairs={{0,4},{2,6},{4,0},{6,2},{1,5},{3,7},{5,1},{7,3},{8,12},{10,14},{12... | collective-permute-start | bytes 1572872 | tf_op jit(solution)/shard_map/ppermute | solution.py:69
  166.9 16.7 %collective-permute-start.3 = (bf16[256,512]{0,1:T(8,128)(2,1)S(1)}, bf16[256,512]{0,1:T(8,128)(2,1)S(1)}, u32[]{:S(2)}, u32[]{:S(2)}) collective-permute-start(bf16[256,512]{0,1:T(8,128)(2,1)S(1)} %divide_convert_fusion.3), channel_id=1, source_target_pairs={{0,4},{2,6},{4,0},{6,2},{1,5},{3,7},{5,1},{7,3},{8,12},{10,14},{12... | collective-permute-start | bytes 786440 | tf_op jit(solution)/shard_map/ppermute | solution.py:81
  183.8 3.5 %collective-permute-start.4 = (bf16[512,512]{0,1:T(8,128)(2,1)S(1)}, bf16[512,512]{0,1:T(8,128)(2,1)S(1)}, u32[]{:S(2)}, u32[]{:S(2)}) collective-permute-start(bf16[512,512]{0,1:T(8,128)(2,1)S(1)} %maximum_select_fusion.7), channel_id=1, source_target_pairs={{0,2},{2,0},{4,6},{6,4},{1,3},{3,1},{5,7},{7,5},{8,10},{10,8},{12,... | collective-permute-start | bytes 1572872 | tf_op jit(solution)/shard_map/ppermute | solution.py:81
  187.7 7.6 %collective-permute-start.8 = (bf16[256,512]{0,1:T(8,128)(2,1)S(1)}, bf16[256,512]{0,1:T(8,128)(2,1)S(1)}, u32[]{:S(2)}, u32[]{:S(2)}) collective-permute-start(bf16[256,512]{0,1:T(8,128)(2,1)S(1)} %divide_convert_fusion.2), channel_id=1, source_target_pairs={{0,4},{2,6},{4,0},{6,2},{1,5},{3,7},{5,1},{7,3},{8,12},{10,14},{12... | collective-permute-start | bytes 786440 | tf_op jit(solution)/shard_map/ppermute | solution.py:81
  189.0 17.5 %collective-permute-start.12 = (f32[256,512]{0,1:T(8,128)S(1)}, f32[256,512]{0,1:T(8,128)S(1)}, u32[]{:S(2)}, u32[]{:S(2)}) collective-permute-start(f32[256,512]{0,1:T(8,128)S(1)} %constant_dynamic-slice_fusion.1), channel_id=1, source_target_pairs={{0,4},{2,6},{4,0},{6,2},{1,5},{3,7},{5,1},{7,3},{8,12},{10,14},{12... | collective-permute-start | bytes 1572872 | tf_op jit(solution)/shard_map/ppermute | solution.py:69
  189.4 18.9 %collective-permute-start.16 = (f32[512,512]{0,1:T(8,128)S(1)}, f32[512,512]{0,1:T(8,128)S(1)}, u32[]{:S(2)}, u32[]{:S(2)}) collective-permute-start(f32[512,512]{0,1:T(8,128)S(1)} %dynamic-slice_bitcast_fusion), channel_id=1, source_target_pairs={{0,2},{2,0},{4,6},{6,4},{1,3},{3,1},{5,7},{7,5},{8,10},{10,8},{12,... | collective-permute-start | bytes 3145736 | tf_op jit(solution)/shard_map/ppermute | solution.py:69
  195.4 11.2 %collective-permute-start.9 = (bf16[512,512]{0,1:T(8,128)(2,1)S(1)}, bf16[512,512]{0,1:T(8,128)(2,1)S(1)}, u32[]{:S(2)}, u32[]{:S(2)}) collective-permute-start(bf16[512,512]{0,1:T(8,128)(2,1)S(1)} %maximum_select_fusion.8), channel_id=1, source_target_pairs={{0,2},{2,0},{4,6},{6,4},{1,3},{3,1},{5,7},{7,5},{8,10},{10,8},{12,... | collective-permute-start | bytes 1572872 | tf_op jit(solution)/shard_map/ppermute | solution.py:81
  207.1 6.7 %collective-permute-start.13 = (bf16[256,512]{0,1:T(8,128)(2,1)S(1)}, bf16[256,512]{0,1:T(8,128)(2,1)S(1)}, u32[]{:S(2)}, u32[]{:S(2)}) collective-permute-start(bf16[256,512]{0,1:T(8,128)(2,1)S(1)} %divide_convert_fusion.1), channel_id=1, source_target_pairs={{0,4},{2,6},{4,0},{6,2},{1,5},{3,7},{5,1},{7,3},{8,12},{10,14},{12... | collective-permute-start | bytes 786440 | tf_op jit(solution)/shard_map/ppermute | solution.py:81
  208.6 16.3 %collective-permute-start.17 = (f32[256,512]{0,1:T(8,128)S(1)}, f32[256,512]{0,1:T(8,128)S(1)}, u32[]{:S(2)}, u32[]{:S(2)}) collective-permute-start(f32[256,512]{0,1:T(8,128)S(1)} %constant_dynamic-slice_fusion), channel_id=1, source_target_pairs={{0,4},{2,6},{4,0},{6,2},{1,5},{3,7},{5,1},{7,3},{8,12},{10,14},{12... | collective-permute-start | bytes 1572872 | tf_op jit(solution)/shard_map/ppermute | solution.py:69
  213.9 11.2 %collective-permute-start.14 = (bf16[512,512]{0,1:T(8,128)(2,1)S(1)}, bf16[512,512]{0,1:T(8,128)(2,1)S(1)}, u32[]{:S(2)}, u32[]{:S(2)}) collective-permute-start(bf16[512,512]{0,1:T(8,128)(2,1)S(1)} %maximum_select_fusion.9), channel_id=1, source_target_pairs={{0,2},{2,0},{4,6},{6,4},{1,3},{3,1},{5,7},{7,5},{8,10},{10,8},{12,... | collective-permute-start | bytes 1572872 | tf_op jit(solution)/shard_map/ppermute | solution.py:81
  225.5 5.7 %collective-permute-start.18 = (bf16[256,512]{0,1:T(8,128)(2,1)S(1)}, bf16[256,512]{0,1:T(8,128)(2,1)S(1)}, u32[]{:S(2)}, u32[]{:S(2)}) collective-permute-start(bf16[256,512]{0,1:T(8,128)(2,1)S(1)} %divide_convert_fusion), channel_id=1, source_target_pairs={{0,4},{2,6},{4,0},{6,2},{1,5},{3,7},{5,1},{7,3},{8,12},{10,14},{12... | collective-permute-start | bytes 786440 | tf_op jit(solution)/shard_map/ppermute | solution.py:81
  231.4 8.1 %collective-permute-start.19 = (bf16[512,512]{0,1:T(8,128)(2,1)S(1)}, bf16[512,512]{0,1:T(8,128)(2,1)S(1)}, u32[]{:S(2)}, u32[]{:S(2)}) collective-permute-start(bf16[512,512]{0,1:T(8,128)(2,1)S(1)} %maximum_select_fusion.10), channel_id=1, source_target_pairs={{0,2},{2,0},{4,6},{6,4},{1,3},{3,1},{5,7},{7,5},{8,10},{10,8},{12,... | collective-permute-start | bytes 1572872 | tf_op jit(solution)/shard_map/ppermute | solution.py:81
Sparse Core Ops, SparseCore 0:
  9.5 35.5 all-gather.4
  46.7 32.4 all-gather.6
  80.7 32.4 all-gather.8
  114.6 32.4 all-gather.10

commit v11 on v6

--- a/solution.py
+++ b/solution.py
@@ -3,7 +3,7 @@
 from jax import lax
 from jax.sharding import PartitionSpec as P
 
-CHUNKS = 8
+WIDTHS = (128, 384, 384, 128)
 AUX_BY_PERMUTE = True
 NARROW_FAR = False
 
@@ -93,7 +93,8 @@
     vir_count = lax.axis_size("vir")
     aux_count = lax.axis_size("aux")
     share = vir_rows // aux_count
-    width = vir_rows // CHUNKS
+    widths = [w * (vir_rows // sum(WIDTHS)) for w in WIDTHS]
+    starts = [sum(widths[:c]) for c in range(len(widths))]
 
     if not AUX_BY_PERMUTE:
         first_row = lax.axis_index("aux") * share
@@ -101,8 +102,8 @@
     total = None
     previous = None
     rows_done = None
-    for c in range(CHUNKS):
-        piece = own[c * width:(c + 1) * width]
+    for c, width in enumerate(widths):
+        piece = own[starts[c]:starts[c] + width]
         if previous is not None:
             piece, _ = lax.optimization_barrier((piece, previous))
         arrived = shifted_2(piece, "occ", 2)
@@ -115,7 +116,7 @@
             block = lax.all_gather(arrived, "vir", axis=0, tiled=True)
             cols = list(range(vir_count))
         col_level = jnp.concatenate(
-            [lax.dynamic_slice_in_dim(vir_energy, w * vir_rows + c * width, width) for w in cols]
+            [lax.dynamic_slice_in_dim(vir_energy, w * vir_rows + starts[c], width) for w in cols]
         )
         partial = jnp.einsum("aq,bq->ab", own, block, preferred_element_type=jnp.float32)
         if AUX_BY_PERMUTE:
@@ -143,7 +144,7 @@
 
 def on_device(integrals, occ_energy, vir_energy):
     cycle_size = lax.axis_size("occ")
-    if integrals.shape[0] == 1 and 4 % cycle_size == 0 and integrals.shape[1] % (CHUNKS * 8) == 0:
+    if integrals.shape[0] == 1 and 4 % cycle_size == 0 and integrals.shape[1] % sum(WIDTHS) == 0:
         return paired_plan(integrals, occ_energy, vir_energy)
     return general_plan(integrals, occ_energy, vir_energy)
 

time: 189 us -> 222 us (1.17)
  waiting for transfers between devices: 109 us -> 151 us
  matrix products: 24.3 us -> 12.2 us
  starting transfers between devices: 42.1 us -> 31.4 us
  local copies, waits for them, and re-layouts: 7.2 us -> 16.3 us
  other arithmetic: 4.01 us -> 9.55 us
    ppermute x16 -> x8, waiting for transfers between devices: 76.5 us -> 97.2 us  [shifted_2(): lax.ppermute(value, axis, [(i, (i + by) % count) for i in range(count)])]
    ppermute x16 -> x8, waiting for transfers between devices: 7.53 us -> 19.2 us  [aux_reduce_scatter(): x = keep + lax.ppermute(send, 'aux', xor_pairs(count, step))]
    dot_general x8 -> x4, matrix products: 18.3 us -> 7.05 us  [paired_plan(): term = jnp.dot(rows, block, preferred_element_type=jnp.float32)]
    ppermute x16 -> x8, waiting for transfers between devices: 25.2 us -> 34.2 us  [aux_all_gather(): other = lax.ppermute(x, 'aux', xor_pairs(count, step))]
    add x15 -> x7, other arithmetic: 1.15 us -> 6.13 us  [aux_reduce_scatter(): x = keep + lax.ppermute(send, 'aux', xor_pairs(count, step))]
    ppermute x16 -> x8, starting transfers between devices: 17.3 us -> 12.8 us  [aux_reduce_scatter(): x = keep + lax.ppermute(send, 'aux', xor_pairs(count, step))]
    dynamic_slice x16 -> x8, local copies, waits for them, and re-layouts: 0.57 us -> 4.69 us  [aux_reduce_scatter(): send = lax.dynamic_slice_in_dim(x, (1 - bit) * half, half, 0)]
    ppermute x16 -> x8, starting transfers between devices: 9.21 us -> 5.84 us  [shifted_2(): lax.ppermute(value, axis, [(i, (i + by) % count) for i in range(count)])]
  transfers between devices with their start and end apart: 48 -> 24, of which waited for: 19 -> 13; matrix products, arithmetic and copies ran while one was open for 13% -> 13% of each run, Pallas kernels for 0% -> 0%
where the time goes in v11:
time: 222 us
  waiting for transfers between devices  151 us (68%)
  starting transfers between devices  31.4 us (14%)
  local copies, waits for them, and re-layouts  16.3 us (7%)
  matrix products  12.2 us (5%)
  other arithmetic  9.55 us (4%)
    ppermute x8, waiting for transfers between devices, shifted_2(): lax.ppermute(value, axis, [(i, (i + by) % count) for i in range(count)])  97.2 us
    ppermute x8, waiting for transfers between devices, aux_all_gather(): other = lax.ppermute(x, 'aux', xor_pairs(count, step))  34.2 us
    ppermute x8, waiting for transfers between devices, aux_reduce_scatter(): x = keep + lax.ppermute(send, 'aux', xor_pairs(count, step))  19.2 us
    ppermute x8, starting transfers between devices, aux_reduce_scatter(): x = keep + lax.ppermute(send, 'aux', xor_pairs(count, step))  12.8 us
    ppermute x8, starting transfers between devices, aux_all_gather(): other = lax.ppermute(x, 'aux', xor_pairs(count, step))  12.7 us
    dot_general x4, matrix products, paired_plan(): term = jnp.dot(rows, block, preferred_element_type=jnp.float32)  7.05 us
    add x7, other arithmetic, aux_reduce_scatter(): x = keep + lax.ppermute(send, 'aux', xor_pairs(count, step))  6.13 us
    ppermute x8, starting transfers between devices, shifted_2(): lax.ppermute(value, axis, [(i, (i + by) % count) for i in range(count)])  5.84 us
  transfers between devices with their start and end apart: 24, of which 13 were waited for; matrix products, arithmetic and copies ran while one was open for 13% of the time, Pallas kernels for 0%

profile of v11, /device:TPU:1, one launch (start us, length us, event | category | flops | bytes accessed | tf_op | source)
XLA Modules:
  0.0 221.7 jit_solution(8346715112091557114)
XLA Ops:
  0.0 1.8 slice_bitcast_fusion.2
  1.8 3.1 %collective-permute-start = (bf16[128,1024]{1,0:T(8,128)(2,1)S(1)}, bf16[128,1024]{1,0:T(8,128)(2,1)S(1)}, u32[]{:S(2)}, u32[]{:S(2)}) collective-permute-start(bf16[128,1024]{1,0:T(8,128)(2,1)S(1)} %get-tuple-element.18), channel_id=1, source_target_pairs={{0,16},{8,24},{16,0},{24,8},{1,17},{9,25},{17,1},{25,9},{2,18},{10... | collective-permute-start | bytes 786440 | tf_op jit(solution)/shard_map/ppermute | solution.py:13
  4.9 2.4 %slice_bitcast_fusion.1 = (bf16[384,1024]{1,0:T(8,128)(2,1)S(1)}, bf16[384,1024]{1,0:T(8,128)(2,1)}) fusion(bf16[1,1024,1024]{2,1,0:T(8,128)(2,1)} %param.3), kind=kLoop, calls=%fused_computation.23 | loop fusion | bytes 3145728 | tf_op jit(solution)/shard_map/slice | solution.py:106
  7.3 9.3 %collective-permute-done = bf16[128,1024]{1,0:T(8,128)(2,1)S(1)} collective-permute-done((bf16[128,1024]{1,0:T(8,128)(2,1)S(1)}, bf16[128,1024]{1,0:T(8,128)(2,1)S(1)}, u32[]{:S(2)}, u32[]{:S(2)}) %collective-permute-start) | collective-permute-done | bytes 262176 | tf_op jit(solution)/shard_map/ppermute | solution.py:13
  17.6 34.7 %collective-permute-done.6 = bf16[384,1024]{1,0:T(8,128)(2,1)} collective-permute-done((bf16[384,1024]{1,0:T(8,128)(2,1)S(1)}, bf16[384,1024]{1,0:T(8,128)(2,1)}, u32[]{:S(2)}, u32[]{:S(2)}) %collective-permute-start.6) | collective-permute-done | bytes 786464 | tf_op jit(solution)/shard_map/ppermute | solution.py:13
  54.6 2.7 %collective-permute-start.2 = (f32[512,256]{0,1:T(8,128)}, f32[512,256]{0,1:T(8,128)}, u32[]{:S(2)}, u32[]{:S(2)}) collective-permute-start(f32[512,256]{0,1:T(8,128)} %dynamic-slice_bitcast_fusion.3), channel_id=1, source_target_pairs={{0,2},{2,0},{4,6},{6,4},{1,3},{3,1},{5,7},{7,5},{8,10},{10,8},{12,... | collective-permute-start | bytes 1572872 | tf_op jit(solution)/shard_map/ppermute | solution.py:68
  58.5 10.9 %collective-permute-done.7 = bf16[384,1024]{1,0:T(8,128)(2,1)S(1)} collective-permute-done((bf16[384,1024]{1,0:T(8,128)(2,1)}, bf16[384,1024]{1,0:T(8,128)(2,1)S(1)}, u32[]{:S(2)}, u32[]{:S(2)}) %collective-permute-start.7) | collective-permute-done | bytes 786464 | tf_op jit(solution)/shard_map/ppermute | solution.py:13
  69.5 1.8 fusion.5
  71.4 1.4 dynamic-slice_bitcast_fusion.1
  73.5 3.0 %collective-permute-start.8 = (f32[512,768]{0,1:T(8,128)}, f32[512,768]{0,1:T(8,128)}, u32[]{:S(2)}, u32[]{:S(2)}) collective-permute-start(f32[512,768]{0,1:T(8,128)} %dynamic-slice_bitcast_fusion.1), channel_id=1, source_target_pairs={{0,2},{2,0},{4,6},{6,4},{1,3},{3,1},{5,7},{7,5},{8,10},{10,8},{12,... | collective-permute-start | bytes 4718600 | tf_op jit(solution)/shard_map/ppermute | solution.py:68
  76.5 16.8 %collective-permute-done.12 = bf16[384,1024]{1,0:T(8,128)(2,1)} collective-permute-done((bf16[384,1024]{1,0:T(8,128)(2,1)S(1)}, bf16[384,1024]{1,0:T(8,128)(2,1)}, u32[]{:S(2)}, u32[]{:S(2)}) %collective-permute-start.12) | collective-permute-done | bytes 786464 | tf_op jit(solution)/shard_map/ppermute | solution.py:13
  99.2 13.1 %collective-permute-done.13 = bf16[384,1024]{1,0:T(8,128)(2,1)} collective-permute-done((bf16[384,1024]{1,0:T(8,128)(2,1)}, bf16[384,1024]{1,0:T(8,128)(2,1)}, u32[]{:S(2)}, u32[]{:S(2)}) %collective-permute-start.13) | collective-permute-done | bytes 786464 | tf_op jit(solution)/shard_map/ppermute | solution.py:13
  113.5 1.8 fusion.3
  115.3 1.3 dynamic-slice_bitcast_fusion
  117.7 1.3 collective-permute-start.14
  119.0 1.8 bitcast_add_fusion.1
  124.5 19.2 %collective-permute-done.4 = bf16[256,256]{0,1:T(8,128)(2,1)S(1)} collective-permute-done((bf16[256,256]{0,1:T(8,128)(2,1)S(1)}, bf16[256,256]{0,1:T(8,128)(2,1)S(1)}, u32[]{:S(2)}, u32[]{:S(2)}) %collective-permute-start.4) | collective-permute-done | bytes 131104 | tf_op jit(solution)/shard_map/ppermute | solution.py:80
  143.8 2.2 collective-permute-start.5
  148.5 12.5 %collective-permute-done.18 = bf16[128,1024]{1,0:T(8,128)(2,1)S(1)} collective-permute-done((bf16[128,1024]{1,0:T(8,128)(2,1)}, bf16[128,1024]{1,0:T(8,128)(2,1)S(1)}, u32[]{:S(2)}, u32[]{:S(2)}) %collective-permute-start.18) | collective-permute-done | bytes 262176 | tf_op jit(solution)/shard_map/ppermute | solution.py:13
  161.5 1.2 dynamic-slice_add_fusion.1
  163.9 1.8 bitcast_add_fusion
  166.4 6.5 %collective-permute-done.10 = bf16[256,768]{0,1:T(8,128)(2,1)S(1)} collective-permute-done((bf16[256,768]{0,1:T(8,128)(2,1)S(1)}, bf16[256,768]{0,1:T(8,128)(2,1)S(1)}, u32[]{:S(2)}, u32[]{:S(2)}) %collective-permute-start.10) | collective-permute-done | bytes 393248 | tf_op jit(solution)/shard_map/ppermute | solution.py:80
  173.1 2.9 %collective-permute-start.11 = (bf16[512,768]{0,1:T(8,128)(2,1)S(1)}, bf16[512,768]{0,1:T(8,128)(2,1)S(1)}, u32[]{:S(2)}, u32[]{:S(2)}) collective-permute-start(bf16[512,768]{0,1:T(8,128)(2,1)S(1)} %maximum_select_fusion.2), channel_id=1, source_target_pairs={{0,2},{2,0},{4,6},{6,4},{1,3},{3,1},{5,7},{7,5},{8,10},{10,8},{12,... | collective-permute-start | bytes 2359304 | tf_op jit(solution)/shard_map/ppermute | solution.py:80
  176.8 13.0 %collective-permute-done.15 = f32[256,768]{0,1:T(8,128)S(1)} collective-permute-done((f32[256,768]{0,1:T(8,128)S(1)}, f32[256,768]{0,1:T(8,128)S(1)}, u32[]{:S(2)}, u32[]{:S(2)}) %collective-permute-start.15) | collective-permute-done | bytes 786464 | tf_op jit(solution)/shard_map/ppermute | solution.py:68
  191.6 1.9 collective-permute-start.20
  193.6 6.1 %collective-permute-done.16 = bf16[256,768]{0,1:T(8,128)(2,1)S(1)} collective-permute-done((bf16[256,768]{0,1:T(8,128)(2,1)S(1)}, bf16[256,768]{0,1:T(8,128)(2,1)S(1)}, u32[]{:S(2)}, u32[]{:S(2)}) %collective-permute-start.16) | collective-permute-done | bytes 393248 | tf_op jit(solution)/shard_map/ppermute | solution.py:80
  199.8 2.6 %collective-permute-start.17 = (bf16[512,768]{0,1:T(8,128)(2,1)S(1)}, bf16[512,768]{0,1:T(8,128)(2,1)S(1)}, u32[]{:S(2)}, u32[]{:S(2)}) collective-permute-start(bf16[512,768]{0,1:T(8,128)(2,1)S(1)} %maximum_select_fusion.3), channel_id=1, source_target_pairs={{0,2},{2,0},{4,6},{6,4},{1,3},{3,1},{5,7},{7,5},{8,10},{10,8},{12,... | collective-permute-start | bytes 2359304 | tf_op jit(solution)/shard_map/ppermute | solution.py:80
  204.3 6.2 %collective-permute-done.21 = f32[256,256]{0,1:T(8,128)S(1)} collective-permute-done((f32[256,256]{0,1:T(8,128)S(1)}, f32[256,256]{0,1:T(8,128)S(1)}, u32[]{:S(2)}, u32[]{:S(2)}) %collective-permute-start.21) | collective-permute-done | bytes 262176 | tf_op jit(solution)/shard_map/ppermute | solution.py:68
  212.3 2.1 fusion.21
  215.6 1.8 collective-permute-start.23
  217.4 1.9 fusion.22
  219.3 2.4 %fusion = bf16[1,1024,1024]{2,1,0:T(8,128)(2,1)} fusion(f32[1024,1024]{1,0:T(8,128)S(1)} %fusion.22, f32[1024,1024]{1,0:T(8,128)S(1)} %fusion.20, f32[1024,1024]{1,0:T(8,128)S(1)} %fusion.21, bf16[256,1024]{1,0:T(8,128)(2,1)S(1)} %constant_dynamic-update-slice_fusion.6, bf16[512,256]{0,1:T(8,128)(2,1)S(1)} %collective-permute-done.23, ...), kind=kOutput, calls=%fused_computation.1 | convolution fusion | flops 544473088 | bytes 15728641 | tf_op jit(solution)/shard_map/dot_general | solution.py:138
  (97 shorter events, 28.8 us)
Async XLA Ops:
  1.8 51.2 %copy-start = (bf16[1,1024,1024]{2,1,0:T(8,128)(2,1)S(1)}, bf16[1,1024,1024]{2,1,0:T(8,128)(2,1)}, u32[]{:S(2)}) copy-start(bf16[1,1024,1024]{2,1,0:T(8,128)(2,1)} %param.3) | copy-start | bytes 6291460
  1.8 14.8 %collective-permute-start = (bf16[128,1024]{1,0:T(8,128)(2,1)S(1)}, bf16[128,1024]{1,0:T(8,128)(2,1)S(1)}, u32[]{:S(2)}, u32[]{:S(2)}) collective-permute-start(bf16[128,1024]{1,0:T(8,128)(2,1)S(1)} %get-tuple-element.18), channel_id=1, source_target_pairs={{0,16},{8,24},{16,0},{24,8},{1,17},{9,25},{17,1},{25,9},{2,18},{10... | collective-permute-start | bytes 786440 | tf_op jit(solution)/shard_map/ppermute | solution.py:13
  16.6 35.7 %collective-permute-start.6 = (bf16[384,1024]{1,0:T(8,128)(2,1)S(1)}, bf16[384,1024]{1,0:T(8,128)(2,1)}, u32[]{:S(2)}, u32[]{:S(2)}) collective-permute-start(bf16[384,1024]{1,0:T(8,128)(2,1)S(1)} %get-tuple-element.11), channel_id=1, source_target_pairs={{0,16},{8,24},{16,0},{24,8},{1,17},{9,25},{17,1},{25,9},{2,18},{10... | collective-permute-start | bytes 2359304 | tf_op jit(solution)/shard_map/ppermute | solution.py:13
  16.6 36.4 %collective-permute-start.1 = (bf16[128,1024]{1,0:T(8,128)(2,1)S(1)}, bf16[128,1024]{1,0:T(8,128)(2,1)S(1)}, u32[]{:S(2)}, u32[]{:S(2)}) collective-permute-start(bf16[128,1024]{1,0:T(8,128)(2,1)S(1)} %collective-permute-done), channel_id=1, source_target_pairs={{0,1},{1,0},{2,3},{3,2},{4,5},{5,4},{6,7},{7,6},{8,9},{9,8},{10,11... | collective-permute-start | bytes 786440 | tf_op jit(solution)/shard_map/ppermute | solution.py:13
  52.2 17.2 %collective-permute-start.7 = (bf16[384,1024]{1,0:T(8,128)(2,1)}, bf16[384,1024]{1,0:T(8,128)(2,1)S(1)}, u32[]{:S(2)}, u32[]{:S(2)}) collective-permute-start(bf16[384,1024]{1,0:T(8,128)(2,1)} %collective-permute-done.6), channel_id=1, source_target_pairs={{0,1},{1,0},{2,3},{3,2},{4,5},{5,4},{6,7},{7,6},{8,9},{9,8},{10,11... | collective-permute-start | bytes 2359304 | tf_op jit(solution)/shard_map/ppermute | solution.py:13
  53.0 4.3 %copy-start.8 = (bf16[384,1024]{1,0:T(8,128)(2,1)S(1)}, bf16[384,1024]{1,0:T(8,128)(2,1)}, u32[]{:S(2)}) copy-start(bf16[384,1024]{1,0:T(8,128)(2,1)} %get-tuple-element.13) | copy-start | bytes 2359300
  54.6 41.2 %collective-permute-start.2 = (f32[512,256]{0,1:T(8,128)}, f32[512,256]{0,1:T(8,128)}, u32[]{:S(2)}, u32[]{:S(2)}) collective-permute-start(f32[512,256]{0,1:T(8,128)} %dynamic-slice_bitcast_fusion.3), channel_id=1, source_target_pairs={{0,2},{2,0},{4,6},{6,4},{1,3},{3,1},{5,7},{7,5},{8,10},{10,8},{12,... | collective-permute-start | bytes 1572872 | tf_op jit(solution)/shard_map/ppermute | solution.py:68
  57.4 35.9 %collective-permute-start.12 = (bf16[384,1024]{1,0:T(8,128)(2,1)S(1)}, bf16[384,1024]{1,0:T(8,128)(2,1)}, u32[]{:S(2)}, u32[]{:S(2)}) collective-permute-start(bf16[384,1024]{1,0:T(8,128)(2,1)S(1)} %copy-done.8), channel_id=1, source_target_pairs={{0,16},{8,24},{16,0},{24,8},{1,17},{9,25},{17,1},{25,9},{2,18},{10... | collective-permute-start | bytes 2359304 | tf_op jit(solution)/shard_map/ppermute | solution.py:13
  71.4 22.4 %copy-start.14 = (f32[4]{0:T(128)S(1)}, f32[4]{0:T(128)}, u32[]{:S(2)}) copy-start(f32[4]{0:T(128)} %param.4) | copy-start | bytes 52
  71.4 24.3 %copy-start.13 = (f32[2048]{0:T(1024)S(1)}, f32[2048]{0:T(1024)}, u32[]{:S(2)}) copy-start(f32[2048]{0:T(1024)} %param.5) | copy-start | bytes 24580
  73.5 45.5 %collective-permute-start.8 = (f32[512,768]{0,1:T(8,128)}, f32[512,768]{0,1:T(8,128)}, u32[]{:S(2)}, u32[]{:S(2)}) collective-permute-start(f32[512,768]{0,1:T(8,128)} %dynamic-slice_bitcast_fusion.1), channel_id=1, source_target_pairs={{0,2},{2,0},{4,6},{6,4},{1,3},{3,1},{5,7},{7,5},{8,10},{10,8},{12,... | collective-permute-start | bytes 4718600 | tf_op jit(solution)/shard_map/ppermute | solution.py:68
  93.3 19.0 %collective-permute-start.13 = (bf16[384,1024]{1,0:T(8,128)(2,1)}, bf16[384,1024]{1,0:T(8,128)(2,1)}, u32[]{:S(2)}, u32[]{:S(2)}) collective-permute-start(bf16[384,1024]{1,0:T(8,128)(2,1)} %collective-permute-done.12), channel_id=1, source_target_pairs={{0,1},{1,0},{2,3},{3,2},{4,5},{5,4},{6,7},{7,6},{8,9},{9,8},{10,11... | collective-permute-start | bytes 2359304 | tf_op jit(solution)/shard_map/ppermute | solution.py:13
  97.0 27.1 %collective-permute-start.3 = (f32[256,256]{0,1:T(8,128)S(1)}, f32[256,256]{0,1:T(8,128)S(1)}, u32[]{:S(2)}, u32[]{:S(2)}) collective-permute-start(f32[256,256]{0,1:T(8,128)S(1)} %constant_dynamic-slice_fusion.3), channel_id=1, source_target_pairs={{0,4},{2,6},{4,0},{6,2},{1,5},{3,7},{5,1},{7,3},{8,12},{10,14},{12... | collective-permute-start | bytes 786440 | tf_op jit(solution)/shard_map/ppermute | solution.py:68
  115.3 3.7 %copy-start.5 = (f32[768,1024]{1,0:T(8,128)S(1)}, f32[768,1024]{1,0:T(8,128)}, u32[]{:S(2)}) copy-start(f32[768,1024]{1,0:T(8,128)} %copy-done.4) | copy-start | bytes 9437188
  117.7 46.2 %collective-permute-start.14 = (f32[512,768]{0,1:T(8,128)}, f32[512,768]{0,1:T(8,128)}, u32[]{:S(2)}, u32[]{:S(2)}) collective-permute-start(f32[512,768]{0,1:T(8,128)} %dynamic-slice_bitcast_fusion), channel_id=1, source_target_pairs={{0,2},{2,0},{4,6},{6,4},{1,3},{3,1},{5,7},{7,5},{8,10},{10,8},{12,... | collective-permute-start | bytes 4718600 | tf_op jit(solution)/shard_map/ppermute | solution.py:68
  122.9 38.6 %collective-permute-start.9 = (f32[256,768]{0,1:T(8,128)}, f32[256,768]{0,1:T(8,128)S(1)}, u32[]{:S(2)}, u32[]{:S(2)}) collective-permute-start(f32[256,768]{0,1:T(8,128)} %constant_dynamic-slice_fusion.2), channel_id=1, source_target_pairs={{0,4},{2,6},{4,0},{6,2},{1,5},{3,7},{5,1},{7,3},{8,12},{10,14},{12... | collective-permute-start | bytes 2359304 | tf_op jit(solution)/shard_map/ppermute | solution.py:68
  124.2 19.5 %collective-permute-start.4 = (bf16[256,256]{0,1:T(8,128)(2,1)S(1)}, bf16[256,256]{0,1:T(8,128)(2,1)S(1)}, u32[]{:S(2)}, u32[]{:S(2)}) collective-permute-start(bf16[256,256]{0,1:T(8,128)(2,1)S(1)} %divide_convert_fusion.3), channel_id=1, source_target_pairs={{0,4},{2,6},{4,0},{6,2},{1,5},{3,7},{5,1},{7,3},{8,12},{10,14},{12... | collective-permute-start | bytes 393224 | tf_op jit(solution)/shard_map/ppermute | solution.py:80
  143.8 3.5 %collective-permute-start.5 = (bf16[512,256]{0,1:T(8,128)(2,1)S(1)}, bf16[512,256]{0,1:T(8,128)(2,1)}, u32[]{:S(2)}, u32[]{:S(2)}) collective-permute-start(bf16[512,256]{0,1:T(8,128)(2,1)S(1)} %maximum_select_fusion.9), channel_id=1, source_target_pairs={{0,2},{2,0},{4,6},{6,4},{1,3},{3,1},{5,7},{7,5},{8,10},{10,8},{12,... | collective-permute-start | bytes 786440 | tf_op jit(solution)/shard_map/ppermute | solution.py:80
  146.0 14.9 %collective-permute-start.18 = (bf16[128,1024]{1,0:T(8,128)(2,1)}, bf16[128,1024]{1,0:T(8,128)(2,1)S(1)}, u32[]{:S(2)}, u32[]{:S(2)}) collective-permute-start(bf16[128,1024]{1,0:T(8,128)(2,1)} %get-tuple-element.15), channel_id=1, source_target_pairs={{0,16},{8,24},{16,0},{24,8},{1,17},{9,25},{17,1},{25,9},{2,18},{10... | collective-permute-start | bytes 786440 | tf_op jit(solution)/shard_map/ppermute | solution.py:13
  148.5 15.4 %copy-start.7 = (f32[768,1024]{1,0:T(8,128)S(1)}, f32[768,1024]{1,0:T(8,128)}, u32[]{:S(2)}) copy-start(f32[768,1024]{1,0:T(8,128)} %copy-done.6) | copy-start | bytes 9437188
  161.0 15.0 %collective-permute-start.19 = (bf16[128,1024]{1,0:T(8,128)(2,1)S(1)}, bf16[128,1024]{1,0:T(8,128)(2,1)S(1)}, u32[]{:S(2)}, u32[]{:S(2)}) collective-permute-start(bf16[128,1024]{1,0:T(8,128)(2,1)S(1)} %collective-permute-done.18), channel_id=1, source_target_pairs={{0,1},{1,0},{2,3},{3,2},{4,5},{5,4},{6,7},{7,6},{8,9},{9,8},{10,11... | collective-permute-start | bytes 786440 | tf_op jit(solution)/shard_map/ppermute | solution.py:13
  162.9 10.0 %collective-permute-start.10 = (bf16[256,768]{0,1:T(8,128)(2,1)S(1)}, bf16[256,768]{0,1:T(8,128)(2,1)S(1)}, u32[]{:S(2)}, u32[]{:S(2)}) collective-permute-start(bf16[256,768]{0,1:T(8,128)(2,1)S(1)} %divide_convert_fusion.1), channel_id=1, source_target_pairs={{0,4},{2,6},{4,0},{6,2},{1,5},{3,7},{5,1},{7,3},{8,12},{10,14},{12... | collective-permute-start | bytes 1179656 | tf_op jit(solution)/shard_map/ppermute | solution.py:80
  165.8 24.0 %collective-permute-start.15 = (f32[256,768]{0,1:T(8,128)S(1)}, f32[256,768]{0,1:T(8,128)S(1)}, u32[]{:S(2)}, u32[]{:S(2)}) collective-permute-start(f32[256,768]{0,1:T(8,128)S(1)} %constant_dynamic-slice_fusion.1), channel_id=1, source_target_pairs={{0,4},{2,6},{4,0},{6,2},{1,5},{3,7},{5,1},{7,3},{8,12},{10,14},{12... | collective-permute-start | bytes 2359304 | tf_op jit(solution)/shard_map/ppermute | solution.py:68
  173.1 16.8 %collective-permute-start.11 = (bf16[512,768]{0,1:T(8,128)(2,1)S(1)}, bf16[512,768]{0,1:T(8,128)(2,1)S(1)}, u32[]{:S(2)}, u32[]{:S(2)}) collective-permute-start(bf16[512,768]{0,1:T(8,128)(2,1)S(1)} %maximum_select_fusion.2), channel_id=1, source_target_pairs={{0,2},{2,0},{4,6},{6,4},{1,3},{3,1},{5,7},{7,5},{8,10},{10,8},{12,... | collective-permute-start | bytes 2359304 | tf_op jit(solution)/shard_map/ppermute | solution.py:80
  190.6 9.1 %collective-permute-start.16 = (bf16[256,768]{0,1:T(8,128)(2,1)S(1)}, bf16[256,768]{0,1:T(8,128)(2,1)S(1)}, u32[]{:S(2)}, u32[]{:S(2)}) collective-permute-start(bf16[256,768]{0,1:T(8,128)(2,1)S(1)} %divide_convert_fusion), channel_id=1, source_target_pairs={{0,4},{2,6},{4,0},{6,2},{1,5},{3,7},{5,1},{7,3},{8,12},{10,14},{12... | collective-permute-start | bytes 1179656 | tf_op jit(solution)/shard_map/ppermute | solution.py:80
  191.6 10.8 %collective-permute-start.20 = (f32[512,256]{0,1:T(8,128)S(1)}, f32[512,256]{0,1:T(8,128)S(1)}, u32[]{:S(2)}, u32[]{:S(2)}) collective-permute-start(f32[512,256]{0,1:T(8,128)S(1)} %dynamic-slice_bitcast_fusion.2), channel_id=1, source_target_pairs={{0,2},{2,0},{4,6},{6,4},{1,3},{3,1},{5,7},{7,5},{8,10},{10,8},{12,... | collective-permute-start | bytes 1572872 | tf_op jit(solution)/shard_map/ppermute | solution.py:68
  193.6 10.0 %copy-start.3 = (bf16[256,1024]{1,0:T(8,128)(2,1)S(1)}, bf16[256,1024]{1,0:T(8,128)(2,1)}, u32[]{:S(2)}) copy-start(bf16[256,1024]{1,0:T(8,128)(2,1)} %copy-done.2) | copy-start | bytes 1572868
  199.8 10.8 %collective-permute-start.17 = (bf16[512,768]{0,1:T(8,128)(2,1)S(1)}, bf16[512,768]{0,1:T(8,128)(2,1)S(1)}, u32[]{:S(2)}, u32[]{:S(2)}) collective-permute-start(bf16[512,768]{0,1:T(8,128)(2,1)S(1)} %maximum_select_fusion.3), channel_id=1, source_target_pairs={{0,2},{2,0},{4,6},{6,4},{1,3},{3,1},{5,7},{7,5},{8,10},{10,8},{12,... | collective-permute-start | bytes 2359304 | tf_op jit(solution)/shard_map/ppermute | solution.py:80
  202.6 8.0 %collective-permute-start.21 = (f32[256,256]{0,1:T(8,128)S(1)}, f32[256,256]{0,1:T(8,128)S(1)}, u32[]{:S(2)}, u32[]{:S(2)}) collective-permute-start(f32[256,256]{0,1:T(8,128)S(1)} %constant_dynamic-slice_fusion), channel_id=1, source_target_pairs={{0,4},{2,6},{4,0},{6,2},{1,5},{3,7},{5,1},{7,3},{8,12},{10,14},{12... | collective-permute-start | bytes 786440 | tf_op jit(solution)/shard_map/ppermute | solution.py:68
  211.2 6.2 %copy-start.12 = (bf16[768,1024]{1,0:T(8,128)(2,1)S(1)}, bf16[768,1024]{1,0:T(8,128)(2,1)}, u32[]{:S(2)}) copy-start(bf16[768,1024]{1,0:T(8,128)(2,1)} %copy-done.11) | copy-start | bytes 4718596
  211.2 4.3 %collective-permute-start.22 = (bf16[256,256]{0,1:T(8,128)(2,1)S(1)}, bf16[256,256]{0,1:T(8,128)(2,1)S(1)}, u32[]{:S(2)}, u32[]{:S(2)}) collective-permute-start(bf16[256,256]{0,1:T(8,128)(2,1)S(1)} %divide_convert_fusion.2), channel_id=1, source_target_pairs={{0,4},{2,6},{4,0},{6,2},{1,5},{3,7},{5,1},{7,3},{8,12},{10,14},{12... | collective-permute-start | bytes 393224 | tf_op jit(solution)/shard_map/ppermute | solution.py:80
  215.6 3.6 %collective-permute-start.23 = (bf16[512,256]{0,1:T(8,128)(2,1)S(1)}, bf16[512,256]{0,1:T(8,128)(2,1)S(1)}, u32[]{:S(2)}, u32[]{:S(2)}) collective-permute-start(bf16[512,256]{0,1:T(8,128)(2,1)S(1)} %maximum_select_fusion.10), channel_id=1, source_target_pairs={{0,2},{2,0},{4,6},{6,4},{1,3},{3,1},{5,7},{7,5},{8,10},{10,8},{12,... | collective-permute-start | bytes 786440 | tf_op jit(solution)/shard_map/ppermute | solution.py:80
  (7 other events, 11.9 us)

commit v12 on v5

--- a/solution.py
+++ b/solution.py
@@ -101,12 +101,16 @@
     total = None
     previous = None
     rows_done = None
+    partials = []
     for c in range(CHUNKS):
         piece = own[c * width:(c + 1) * width]
         if previous is not None:
-            piece, _ = lax.optimization_barrier((piece, previous))
+            gate = previous
+            piece, _ = lax.optimization_barrier((piece, gate))
         arrived = shifted_2(piece, "occ", 2)
         previous = arrived
+        if c >= 1:
+            arrived, _ = lax.optimization_barrier((arrived, partials[c - 1]))
         if vir_count == 2:
             mate = shifted_2(arrived, "vir", 1)
             block = jnp.concatenate([arrived, mate])
@@ -118,6 +122,7 @@
             [lax.dynamic_slice_in_dim(vir_energy, w * vir_rows + c * width, width) for w in cols]
         )
         partial = jnp.einsum("aq,bq->ab", own, block, preferred_element_type=jnp.float32)
+        partials.append(partial)
         if AUX_BY_PERMUTE:
             summed, first = aux_reduce_scatter(partial)
         else:

time: 176 us -> 188 us (1.068)
  waiting for transfers between devices: 109 us -> 117 us
  matrix products: 14 us -> 20 us
  starting transfers between devices: 37.9 us -> 32.5 us
  other arithmetic: 4.46 us -> 6.74 us
    ppermute x8, waiting for transfers between devices: 13.9 us -> 21.3 us  [aux_reduce_scatter(): x = keep + lax.ppermute(send, 'aux', xor_pairs(count, step))]
    ppermute x8, starting transfers between devices: 22.9 us -> 17.4 us  [aux_all_gather(): other = lax.ppermute(x, 'aux', xor_pairs(count, step))]
    ppermute x8, waiting for transfers between devices: 8.3 us -> 12.1 us  [aux_all_gather(): other = lax.ppermute(x, 'aux', xor_pairs(count, step))]
    ppermute x8, waiting for transfers between devices: 86.7 us -> 83.2 us  [shifted_2(): lax.ppermute(value, axis, [(i, (i + by) % count) for i in range(count)])]
    dot_general x4, matrix products: 7.22 us -> 10.7 us  [paired_plan(): term = jnp.dot(rows, block, preferred_element_type=jnp.float32)]
    dot_general x4, matrix products: 6.73 us -> 9.3 us  [paired_plan(): jnp.einsum('aq,bq->ab', own, block, preferred_element_type=jnp.float32)]
  transfers between devices with their start and end apart: 24 -> 24, of which waited for: 12 -> 12; matrix products, arithmetic and copies ran while one was open for 11% -> 13% of each run, Pallas kernels for 0% -> 0%
where the time goes in v12:
time: 188 us
  waiting for transfers between devices  117 us (62%)
  starting transfers between devices  32.5 us (17%)
  matrix products  20 us (11%)
  local copies, waits for them, and re-layouts  10.3 us (5%)
  other arithmetic  6.74 us (4%)
    ppermute x8, waiting for transfers between devices, shifted_2(): lax.ppermute(value, axis, [(i, (i + by) % count) for i in range(count)])  83.2 us
    ppermute x8, waiting for transfers between devices, aux_reduce_scatter(): x = keep + lax.ppermute(send, 'aux', xor_pairs(count, step))  21.3 us
    ppermute x8, starting transfers between devices, aux_all_gather(): other = lax.ppermute(x, 'aux', xor_pairs(count, step))  17.4 us
    ppermute x8, waiting for transfers between devices, aux_all_gather(): other = lax.ppermute(x, 'aux', xor_pairs(count, step))  12.1 us
    dot_general x4, matrix products, paired_plan(): term = jnp.dot(rows, block, preferred_element_type=jnp.float32)  10.7 us
    dot_general x4, matrix products, paired_plan(): jnp.einsum('aq,bq->ab', own, block, preferred_element_type=jnp.float32)  9.3 us
    ppermute x8, starting transfers between devices, aux_reduce_scatter(): x = keep + lax.ppermute(send, 'aux', xor_pairs(count, step))  8.46 us
    ppermute x8, starting transfers between devices, shifted_2(): lax.ppermute(value, axis, [(i, (i + by) % count) for i in range(count)])  6.61 us
  transfers between devices with their start and end apart: 24, of which 12 were waited for; matrix products, arithmetic and copies ran while one was open for 13% of the time, Pallas kernels for 0%

profile of v12, /device:TPU:1, one launch (start us, length us, event | category | flops | bytes accessed | tf_op | source)
XLA Modules:
  0.0 187.7 jit_solution(12016597514875067348)
XLA Ops:
  0.0 2.7 %slice_bitcast_fusion.3 = (bf16[256,1024]{1,0:T(8,128)(2,1)S(1)}, bf16[256,1024]{1,0:T(8,128)(2,1)}, bf16[256,1024]{1,0:T(8,128)(2,1)}, bf16[256,1024]{1,0:T(8,128)(2,1)}) fusion(bf16[1,1024,1024]{2,1,0:T(8,128)(2,1)} %param.3), kind=kLoop, calls=%fused_computation.48 | loop fusion | bytes 4194304 | tf_op jit(solution)/shard_map/slice | solution.py:106
  2.7 3.1 %collective-permute-start = (bf16[256,1024]{1,0:T(8,128)(2,1)S(1)}, bf16[256,1024]{1,0:T(8,128)(2,1)}, u32[]{:S(2)}, u32[]{:S(2)}) collective-permute-start(bf16[256,1024]{1,0:T(8,128)(2,1)S(1)} %get-tuple-element.17), channel_id=1, source_target_pairs={{0,16},{8,24},{16,0},{24,8},{1,17},{9,25},{17,1},{25,9},{2,18},{10... | collective-permute-start | bytes 1572872 | tf_op jit(solution)/shard_map/ppermute | solution.py:13
  5.9 23.0 %collective-permute-done = bf16[256,1024]{1,0:T(8,128)(2,1)} collective-permute-done((bf16[256,1024]{1,0:T(8,128)(2,1)S(1)}, bf16[256,1024]{1,0:T(8,128)(2,1)}, u32[]{:S(2)}, u32[]{:S(2)}) %collective-permute-start) | collective-permute-done | bytes 524320 | tf_op jit(solution)/shard_map/ppermute | solution.py:13
  31.0 10.4 %collective-permute-done.1 = bf16[256,1024]{1,0:T(8,128)(2,1)} collective-permute-done((bf16[256,1024]{1,0:T(8,128)(2,1)}, bf16[256,1024]{1,0:T(8,128)(2,1)}, u32[]{:S(2)}, u32[]{:S(2)}) %collective-permute-start.1) | collective-permute-done | bytes 524320 | tf_op jit(solution)/shard_map/ppermute | solution.py:13
  42.4 1.3 fusion.6
  43.7 1.3 copy-done
  46.1 2.1 %collective-permute-start.2 = (f32[512,512]{0,1:T(8,128)}, f32[512,512]{0,1:T(8,128)}, u32[]{:S(2)}, u32[]{:S(2)}) collective-permute-start(f32[512,512]{0,1:T(8,128)} %dynamic-slice_bitcast_fusion.3), channel_id=1, source_target_pairs={{0,2},{2,0},{4,6},{6,4},{1,3},{3,1},{5,7},{7,5},{8,10},{10,8},{12,... | collective-permute-start | bytes 3145736 | tf_op jit(solution)/shard_map/ppermute | solution.py:68
  48.3 5.9 %collective-permute-done.6 = bf16[256,1024]{1,0:T(8,128)(2,1)} collective-permute-done((bf16[256,1024]{1,0:T(8,128)(2,1)}, bf16[256,1024]{1,0:T(8,128)(2,1)}, u32[]{:S(2)}, u32[]{:S(2)}) %collective-permute-start.6) | collective-permute-done | bytes 524320 | tf_op jit(solution)/shard_map/ppermute | solution.py:13
  56.9 23.1 %collective-permute-done.12 = bf16[256,1024]{1,0:T(8,128)(2,1)} collective-permute-done((bf16[256,1024]{1,0:T(8,128)(2,1)}, bf16[256,1024]{1,0:T(8,128)(2,1)}, u32[]{:S(2)}, u32[]{:S(2)}) %collective-permute-start.12) | collective-permute-done | bytes 524320 | tf_op jit(solution)/shard_map/ppermute | solution.py:13
  81.0 2.5 %fusion.4 = f32[512,1024]{1,0:T(8,128)S(1)} fusion(bf16[1,1024,1024]{2,1,0:T(8,128)(2,1)S(1)} %copy-done.4, bf16[256,1024]{1,0:T(8,128)(2,1)} %collective-permute-done.7, bf16[256,1024]{1,0:T(8,128)(2,1)} %collective-permute-done.6), kind=kOutput, calls=%fused_computation.5 | convolution fusion | flops 1075838976 | bytes 5242880 | tf_op jit(solution)/shard_map/aq,bq->ab/dot_general | solution.py:124
  85.8 1.4 bitcast_add_fusion.3
  88.5 16.8 %collective-permute-done.18 = bf16[256,1024]{1,0:T(8,128)(2,1)} collective-permute-done((bf16[256,1024]{1,0:T(8,128)(2,1)}, bf16[256,1024]{1,0:T(8,128)(2,1)}, u32[]{:S(2)}, u32[]{:S(2)}) %collective-permute-start.18) | collective-permute-done | bytes 524320 | tf_op jit(solution)/shard_map/ppermute | solution.py:13
  106.0 3.2 %fusion.2 = f32[512,1024]{1,0:T(8,128)S(1)} fusion(bf16[1,1024,1024]{2,1,0:T(8,128)(2,1)} %param.3, bf16[256,1024]{1,0:T(8,128)(2,1)} %collective-permute-done.13, bf16[256,1024]{1,0:T(8,128)(2,1)} %collective-permute-done.12), kind=kOutput, calls=%fused_computation.3 | convolution fusion | flops 1075838976 | bytes 5242880 | tf_op jit(solution)/shard_map/aq,bq->ab/dot_general | solution.py:124
  110.2 1.2 divide_convert_fusion.3
  112.2 1.4 bitcast_add_fusion.2
  114.5 4.0 %collective-permute-done.19 = bf16[256,1024]{1,0:T(8,128)(2,1)S(1)} collective-permute-done((bf16[256,1024]{1,0:T(8,128)(2,1)}, bf16[256,1024]{1,0:T(8,128)(2,1)S(1)}, u32[]{:S(2)}, u32[]{:S(2)}) %collective-permute-start.19) | collective-permute-done | bytes 524320 | tf_op jit(solution)/shard_map/ppermute | solution.py:13
  118.5 2.3 %fusion = f32[512,1024]{1,0:T(8,128)S(1)} fusion(bf16[1,1024,1024]{2,1,0:T(8,128)(2,1)S(1)} %copy-done.5, bf16[256,1024]{1,0:T(8,128)(2,1)S(1)} %collective-permute-done.19, bf16[256,1024]{1,0:T(8,128)(2,1)} %collective-permute-done.18), kind=kOutput, calls=%fused_computation.1 | convolution fusion | flops 1075838976 | bytes 5242880 | tf_op jit(solution)/shard_map/aq,bq->ab/dot_general | solution.py:124
  121.0 1.4 collective-permute-start.5
  122.7 7.8 %collective-permute-done.9 = f32[256,512]{0,1:T(8,128)S(1)} collective-permute-done((f32[256,512]{0,1:T(8,128)S(1)}, f32[256,512]{0,1:T(8,128)S(1)}, u32[]{:S(2)}, u32[]{:S(2)}) %collective-permute-start.9) | collective-permute-done | bytes 524320 | tf_op jit(solution)/shard_map/ppermute | solution.py:68
  132.8 1.6 collective-permute-start.20
  134.4 3.6 %collective-permute-done.10 = bf16[256,512]{0,1:T(8,128)(2,1)S(1)} collective-permute-done((bf16[256,512]{0,1:T(8,128)(2,1)S(1)}, bf16[256,512]{0,1:T(8,128)(2,1)S(1)}, u32[]{:S(2)}, u32[]{:S(2)}) %collective-permute-start.10) | collective-permute-done | bytes 262176 | tf_op jit(solution)/shard_map/ppermute | solution.py:80
  138.1 3.4 %collective-permute-start.11 = (bf16[512,512]{0,1:T(8,128)(2,1)S(1)}, bf16[512,512]{0,1:T(8,128)(2,1)S(1)}, u32[]{:S(2)}, u32[]{:S(2)}) collective-permute-start(bf16[512,512]{0,1:T(8,128)(2,1)S(1)} %maximum_select_fusion.6), channel_id=1, source_target_pairs={{0,2},{2,0},{4,6},{6,4},{1,3},{3,1},{5,7},{7,5},{8,10},{10,8},{12,... | collective-permute-start | bytes 1572872 | tf_op jit(solution)/shard_map/ppermute | solution.py:80
  141.5 7.7 %collective-permute-done.15 = f32[256,512]{0,1:T(8,128)S(1)} collective-permute-done((f32[256,512]{0,1:T(8,128)S(1)}, f32[256,512]{0,1:T(8,128)S(1)}, u32[]{:S(2)}, u32[]{:S(2)}) %collective-permute-start.15) | collective-permute-done | bytes 524320 | tf_op jit(solution)/shard_map/ppermute | solution.py:68
  151.6 4.1 %collective-permute-done.16 = bf16[256,512]{0,1:T(8,128)(2,1)S(1)} collective-permute-done((bf16[256,512]{0,1:T(8,128)(2,1)S(1)}, bf16[256,512]{0,1:T(8,128)(2,1)S(1)}, u32[]{:S(2)}, u32[]{:S(2)}) %collective-permute-start.16) | collective-permute-done | bytes 262176 | tf_op jit(solution)/shard_map/ppermute | solution.py:80
  155.9 5.3 %collective-permute-start.17 = (bf16[512,512]{0,1:T(8,128)(2,1)S(1)}, bf16[512,512]{0,1:T(8,128)(2,1)S(1)}, u32[]{:S(2)}, u32[]{:S(2)}) collective-permute-start(bf16[512,512]{0,1:T(8,128)(2,1)S(1)} %maximum_select_fusion.7), channel_id=1, source_target_pairs={{0,2},{2,0},{4,6},{6,4},{1,3},{3,1},{5,7},{7,5},{8,10},{10,8},{12,... | collective-permute-start | bytes 1572872 | tf_op jit(solution)/shard_map/ppermute | solution.py:80
  161.2 5.8 %collective-permute-done.21 = f32[256,512]{0,1:T(8,128)S(1)} collective-permute-done((f32[256,512]{0,1:T(8,128)S(1)}, f32[256,512]{0,1:T(8,128)S(1)}, u32[]{:S(2)}, u32[]{:S(2)}) %collective-permute-start.21) | collective-permute-done | bytes 524320 | tf_op jit(solution)/shard_map/ppermute | solution.py:68
  168.4 4.4 %collective-permute-done.22 = bf16[256,512]{0,1:T(8,128)(2,1)S(1)} collective-permute-done((bf16[256,512]{0,1:T(8,128)(2,1)S(1)}, bf16[256,512]{0,1:T(8,128)(2,1)S(1)}, u32[]{:S(2)}, u32[]{:S(2)}) %collective-permute-start.22) | collective-permute-done | bytes 262176 | tf_op jit(solution)/shard_map/ppermute | solution.py:80
  173.0 4.0 %collective-permute-start.23 = (bf16[512,512]{0,1:T(8,128)(2,1)S(1)}, bf16[512,512]{0,1:T(8,128)(2,1)S(1)}, u32[]{:S(2)}, u32[]{:S(2)}) collective-permute-start(bf16[512,512]{0,1:T(8,128)(2,1)S(1)} %maximum_select_fusion.8), channel_id=1, source_target_pairs={{0,2},{2,0},{4,6},{6,4},{1,3},{3,1},{5,7},{7,5},{8,10},{10,8},{12,... | collective-permute-start | bytes 1572872 | tf_op jit(solution)/shard_map/ppermute | solution.py:80
  177.0 2.5 %fusion.17 = f32[1024,1024]{1,0:T(8,128)S(1)} fusion(bf16[1024,512]{0,1:T(8,128)(2,1)S(1)} %maximum_select_fusion.1, bf16[256,1024]{1,0:T(8,128)(2,1)} %collective-permute-done.7, bf16[256,1024]{1,0:T(8,128)(2,1)} %collective-permute-done.6), kind=kOutput, calls=%fused_computation.33 | convolution fusion | flops 1075838976 | bytes 6291456 | tf_op jit(solution)/shard_map/dot_general | solution.py:142
  179.5 2.7 %fusion.16 = f32[1024,1024]{1,0:T(8,128)S(1)} fusion(bf16[1024,512]{0,1:T(8,128)(2,1)S(1)} %maximum_select_fusion.2, bf16[256,1024]{1,0:T(8,128)(2,1)} %collective-permute-done.13, bf16[256,1024]{1,0:T(8,128)(2,1)} %collective-permute-done.12), kind=kOutput, calls=%fused_computation.32 | convolution fusion | flops 1075838976 | bytes 6291456 | tf_op jit(solution)/shard_map/dot_general | solution.py:142
  182.2 2.3 %fusion.9 = f32[1024,1024]{1,0:T(8,128)S(1)} fusion(bf16[512,512]{0,1:T(8,128)(2,1)S(1)} %collective-permute-done.23, bf16[512,512]{0,1:T(8,128)(2,1)S(1)} %maximum_select_fusion.8, pred[]{:T(512)S(6)} %eq.30, bf16[256,1024]{1,0:T(8,128)(2,1)S(1)} %collective-permute-done.19, bf16[256,1024]{1,0:T(8,128)(2,1)} %collective-permute-done.18), kind=kOutput, calls=%fused_computation.17 | convolution fusion | flops 1080557568 | bytes 6291457 | tf_op jit(solution)/shard_map/dot_general | solution.py:142
  184.5 3.1 %fusion.8 = bf16[1,1024,1024]{2,1,0:T(8,128)(2,1)} fusion(f32[1024,1024]{1,0:T(8,128)S(1)} %fusion.9, f32[1024,1024]{1,0:T(8,128)S(1)} %fusion.16, f32[1024,1024]{1,0:T(8,128)S(1)} %fusion.17, bf16[1024,512]{0,1:T(8,128)(2,1)S(1)} %maximum_select_fusion, bf16[512,1024]{1,0:T(8,128)(2,1)S(1)} %constant_dynamic-update-slice_fusion), kind=kOutput, calls=%fused_computation.9 | convolution fusion | flops 1078984704 | bytes 16777216 | tf_op jit(solution)/shard_map/dot_general | solution.py:142
  (75 shorter events, 20.4 us)
Async XLA Ops:
  2.7 39.7 %copy-start.4 = (bf16[1,1024,1024]{2,1,0:T(8,128)(2,1)S(1)}, bf16[1,1024,1024]{2,1,0:T(8,128)(2,1)}, u32[]{:S(2)}) copy-start(bf16[1,1024,1024]{2,1,0:T(8,128)(2,1)} %param.3) | copy-start | bytes 6291460
  2.7 26.1 %collective-permute-start = (bf16[256,1024]{1,0:T(8,128)(2,1)S(1)}, bf16[256,1024]{1,0:T(8,128)(2,1)}, u32[]{:S(2)}, u32[]{:S(2)}) collective-permute-start(bf16[256,1024]{1,0:T(8,128)(2,1)S(1)} %get-tuple-element.17), channel_id=1, source_target_pairs={{0,16},{8,24},{16,0},{24,8},{1,17},{9,25},{17,1},{25,9},{2,18},{10... | collective-permute-start | bytes 1572872 | tf_op jit(solution)/shard_map/ppermute | solution.py:13
  28.8 12.5 %collective-permute-start.1 = (bf16[256,1024]{1,0:T(8,128)(2,1)}, bf16[256,1024]{1,0:T(8,128)(2,1)}, u32[]{:S(2)}, u32[]{:S(2)}) collective-permute-start(bf16[256,1024]{1,0:T(8,128)(2,1)} %collective-permute-done), channel_id=1, source_target_pairs={{0,1},{1,0},{2,3},{3,2},{4,5},{5,4},{6,7},{7,6},{8,9},{9,8},{10,11... | collective-permute-start | bytes 1572872 | tf_op jit(solution)/shard_map/ppermute | solution.py:13
  29.8 24.3 %collective-permute-start.6 = (bf16[256,1024]{1,0:T(8,128)(2,1)}, bf16[256,1024]{1,0:T(8,128)(2,1)}, u32[]{:S(2)}, u32[]{:S(2)}) collective-permute-start(bf16[256,1024]{1,0:T(8,128)(2,1)} %get-tuple-element.11), channel_id=1, source_target_pairs={{0,16},{8,24},{16,0},{24,8},{1,17},{9,25},{17,1},{25,9},{2,18},{10... | collective-permute-start | bytes 1572872 | tf_op jit(solution)/shard_map/ppermute | solution.py:13
  43.7 1.4 copy-start
  45.1 9.8 %copy-start.7 = (f32[4]{0:T(128)S(1)}, f32[4]{0:T(128)}, u32[]{:S(2)}) copy-start(f32[4]{0:T(128)} %param.4) | copy-start | bytes 52
  45.1 11.6 %copy-start.6 = (f32[2048]{0:T(1024)S(1)}, f32[2048]{0:T(1024)}, u32[]{:S(2)}) copy-start(f32[2048]{0:T(1024)} %param.5) | copy-start | bytes 24580
  46.1 38.5 %collective-permute-start.2 = (f32[512,512]{0,1:T(8,128)}, f32[512,512]{0,1:T(8,128)}, u32[]{:S(2)}, u32[]{:S(2)}) collective-permute-start(f32[512,512]{0,1:T(8,128)} %dynamic-slice_bitcast_fusion.3), channel_id=1, source_target_pairs={{0,2},{2,0},{4,6},{6,4},{1,3},{3,1},{5,7},{7,5},{8,10},{10,8},{12,... | collective-permute-start | bytes 3145736 | tf_op jit(solution)/shard_map/ppermute | solution.py:68
  54.2 25.7 %collective-permute-start.12 = (bf16[256,1024]{1,0:T(8,128)(2,1)}, bf16[256,1024]{1,0:T(8,128)(2,1)}, u32[]{:S(2)}, u32[]{:S(2)}) collective-permute-start(bf16[256,1024]{1,0:T(8,128)(2,1)} %get-tuple-element.13), channel_id=1, source_target_pairs={{0,16},{8,24},{16,0},{24,8},{1,17},{9,25},{17,1},{25,9},{2,18},{10... | collective-permute-start | bytes 1572872 | tf_op jit(solution)/shard_map/ppermute | solution.py:13
  54.2 26.8 %collective-permute-start.7 = (bf16[256,1024]{1,0:T(8,128)(2,1)}, bf16[256,1024]{1,0:T(8,128)(2,1)}, u32[]{:S(2)}, u32[]{:S(2)}) collective-permute-start(bf16[256,1024]{1,0:T(8,128)(2,1)} %collective-permute-done.6), channel_id=1, source_target_pairs={{0,1},{1,0},{2,3},{3,2},{4,5},{5,4},{6,7},{7,6},{8,9},{9,8},{10,11... | collective-permute-start | bytes 1572872 | tf_op jit(solution)/shard_map/ppermute | solution.py:13
  79.9 25.4 %collective-permute-start.18 = (bf16[256,1024]{1,0:T(8,128)(2,1)}, bf16[256,1024]{1,0:T(8,128)(2,1)}, u32[]{:S(2)}, u32[]{:S(2)}) collective-permute-start(bf16[256,1024]{1,0:T(8,128)(2,1)} %get-tuple-element.15), channel_id=1, source_target_pairs={{0,16},{8,24},{16,0},{24,8},{1,17},{9,25},{17,1},{25,9},{2,18},{10... | collective-permute-start | bytes 1572872 | tf_op jit(solution)/shard_map/ppermute | solution.py:13
  79.9 26.1 %collective-permute-start.13 = (bf16[256,1024]{1,0:T(8,128)(2,1)}, bf16[256,1024]{1,0:T(8,128)(2,1)}, u32[]{:S(2)}, u32[]{:S(2)}) collective-permute-start(bf16[256,1024]{1,0:T(8,128)(2,1)} %collective-permute-done.12), channel_id=1, source_target_pairs={{0,1},{1,0},{2,3},{3,2},{4,5},{5,4},{6,7},{7,6},{8,9},{9,8},{10,11... | collective-permute-start | bytes 1572872 | tf_op jit(solution)/shard_map/ppermute | solution.py:13
  83.5 3.8 %copy-start.2 = (f32[512,1024]{1,0:T(8,128)}, f32[512,1024]{1,0:T(8,128)S(1)}, u32[]{:S(2)}) copy-start(f32[512,1024]{1,0:T(8,128)S(1)} %fusion.4) | copy-start | bytes 6291460
  83.5 2.3 %copy-start.1 = (f32[512,1024]{1,0:T(8,128)S(1)}, f32[512,1024]{1,0:T(8,128)}, u32[]{:S(2)}) copy-start(f32[512,1024]{1,0:T(8,128)} %copy-done) | copy-start | bytes 6291460
  83.6 28.7 %collective-permute-start.8 = (f32[512,512]{0,1:T(8,128)S(1)}, f32[512,512]{0,1:T(8,128)}, u32[]{:S(2)}, u32[]{:S(2)}) collective-permute-start(f32[512,512]{0,1:T(8,128)S(1)} %dynamic-slice_bitcast_fusion.2), channel_id=1, source_target_pairs={{0,2},{2,0},{4,6},{6,4},{1,3},{3,1},{5,7},{7,5},{8,10},{10,8},{12,... | collective-permute-start | bytes 3145736 | tf_op jit(solution)/shard_map/ppermute | solution.py:68
  88.1 22.1 %collective-permute-start.3 = (f32[256,512]{0,1:T(8,128)}, f32[256,512]{0,1:T(8,128)}, u32[]{:S(2)}, u32[]{:S(2)}) collective-permute-start(f32[256,512]{0,1:T(8,128)} %constant_dynamic-slice_fusion.3), channel_id=1, source_target_pairs={{0,4},{2,6},{4,0},{6,2},{1,5},{3,7},{5,1},{7,3},{8,12},{10,14},{12... | collective-permute-start | bytes 1572872 | tf_op jit(solution)/shard_map/ppermute | solution.py:68
  105.3 13.2 %collective-permute-start.19 = (bf16[256,1024]{1,0:T(8,128)(2,1)}, bf16[256,1024]{1,0:T(8,128)(2,1)S(1)}, u32[]{:S(2)}, u32[]{:S(2)}) collective-permute-start(bf16[256,1024]{1,0:T(8,128)(2,1)} %collective-permute-done.18), channel_id=1, source_target_pairs={{0,1},{1,0},{2,3},{3,2},{4,5},{5,4},{6,7},{7,6},{8,9},{9,8},{10,11... | collective-permute-start | bytes 1572872 | tf_op jit(solution)/shard_map/ppermute | solution.py:13
  109.3 3.0 %copy-start.3 = (f32[512,1024]{1,0:T(8,128)S(1)}, f32[512,1024]{1,0:T(8,128)}, u32[]{:S(2)}) copy-start(f32[512,1024]{1,0:T(8,128)} %copy-done.2) | copy-start | bytes 6291460
  109.4 13.1 %collective-permute-start.14 = (f32[512,512]{0,1:T(8,128)S(1)}, f32[512,512]{0,1:T(8,128)S(1)}, u32[]{:S(2)}, u32[]{:S(2)}) collective-permute-start(f32[512,512]{0,1:T(8,128)S(1)} %dynamic-slice_bitcast_fusion.1), channel_id=1, source_target_pairs={{0,2},{2,0},{4,6},{6,4},{1,3},{3,1},{5,7},{7,5},{8,10},{10,8},{12,... | collective-permute-start | bytes 3145736 | tf_op jit(solution)/shard_map/ppermute | solution.py:68
  111.4 7.1 %copy-start.5 = (bf16[1,1024,1024]{2,1,0:T(8,128)(2,1)S(1)}, bf16[1,1024,1024]{2,1,0:T(8,128)(2,1)}, u32[]{:S(2)}) copy-start(bf16[1,1024,1024]{2,1,0:T(8,128)(2,1)} %param.3) | copy-start | bytes 6291460
  111.4 9.5 %collective-permute-start.4 = (bf16[256,512]{0,1:T(8,128)(2,1)S(1)}, bf16[256,512]{0,1:T(8,128)(2,1)S(1)}, u32[]{:S(2)}, u32[]{:S(2)}) collective-permute-start(bf16[256,512]{0,1:T(8,128)(2,1)S(1)} %divide_convert_fusion.3), channel_id=1, source_target_pairs={{0,4},{2,6},{4,0},{6,2},{1,5},{3,7},{5,1},{7,3},{8,12},{10,14},{12... | collective-permute-start | bytes 786440 | tf_op jit(solution)/shard_map/ppermute | solution.py:80
  113.7 16.8 %collective-permute-start.9 = (f32[256,512]{0,1:T(8,128)S(1)}, f32[256,512]{0,1:T(8,128)S(1)}, u32[]{:S(2)}, u32[]{:S(2)}) collective-permute-start(f32[256,512]{0,1:T(8,128)S(1)} %constant_dynamic-slice_fusion.2), channel_id=1, source_target_pairs={{0,4},{2,6},{4,0},{6,2},{1,5},{3,7},{5,1},{7,3},{8,12},{10,14},{12... | collective-permute-start | bytes 1572872 | tf_op jit(solution)/shard_map/ppermute | solution.py:68
  121.0 9.6 %collective-permute-start.5 = (bf16[512,512]{0,1:T(8,128)(2,1)S(1)}, bf16[512,512]{0,1:T(8,128)(2,1)S(1)}, u32[]{:S(2)}, u32[]{:S(2)}) collective-permute-start(bf16[512,512]{0,1:T(8,128)(2,1)S(1)} %maximum_select_fusion.5), channel_id=1, source_target_pairs={{0,2},{2,0},{4,6},{6,4},{1,3},{3,1},{5,7},{7,5},{8,10},{10,8},{12,... | collective-permute-start | bytes 1572872 | tf_op jit(solution)/shard_map/ppermute | solution.py:80
  131.1 6.9 %collective-permute-start.10 = (bf16[256,512]{0,1:T(8,128)(2,1)S(1)}, bf16[256,512]{0,1:T(8,128)(2,1)S(1)}, u32[]{:S(2)}, u32[]{:S(2)}) collective-permute-start(bf16[256,512]{0,1:T(8,128)(2,1)S(1)} %divide_convert_fusion.2), channel_id=1, source_target_pairs={{0,4},{2,6},{4,0},{6,2},{1,5},{3,7},{5,1},{7,3},{8,12},{10,14},{12... | collective-permute-start | bytes 786440 | tf_op jit(solution)/shard_map/ppermute | solution.py:80
  131.9 17.3 %collective-permute-start.15 = (f32[256,512]{0,1:T(8,128)S(1)}, f32[256,512]{0,1:T(8,128)S(1)}, u32[]{:S(2)}, u32[]{:S(2)}) collective-permute-start(f32[256,512]{0,1:T(8,128)S(1)} %constant_dynamic-slice_fusion.1), channel_id=1, source_target_pairs={{0,4},{2,6},{4,0},{6,2},{1,5},{3,7},{5,1},{7,3},{8,12},{10,14},{12... | collective-permute-start | bytes 1572872 | tf_op jit(solution)/shard_map/ppermute | solution.py:68
  132.8 17.8 %collective-permute-start.20 = (f32[512,512]{0,1:T(8,128)S(1)}, f32[512,512]{0,1:T(8,128)S(1)}, u32[]{:S(2)}, u32[]{:S(2)}) collective-permute-start(f32[512,512]{0,1:T(8,128)S(1)} %dynamic-slice_bitcast_fusion), channel_id=1, source_target_pairs={{0,2},{2,0},{4,6},{6,4},{1,3},{3,1},{5,7},{7,5},{8,10},{10,8},{12,... | collective-permute-start | bytes 3145736 | tf_op jit(solution)/shard_map/ppermute | solution.py:68
  138.1 11.2 %collective-permute-start.11 = (bf16[512,512]{0,1:T(8,128)(2,1)S(1)}, bf16[512,512]{0,1:T(8,128)(2,1)S(1)}, u32[]{:S(2)}, u32[]{:S(2)}) collective-permute-start(bf16[512,512]{0,1:T(8,128)(2,1)S(1)} %maximum_select_fusion.6), channel_id=1, source_target_pairs={{0,2},{2,0},{4,6},{6,4},{1,3},{3,1},{5,7},{7,5},{8,10},{10,8},{12,... | collective-permute-start | bytes 1572872 | tf_op jit(solution)/shard_map/ppermute | solution.py:80
  149.8 6.0 %collective-permute-start.16 = (bf16[256,512]{0,1:T(8,128)(2,1)S(1)}, bf16[256,512]{0,1:T(8,128)(2,1)S(1)}, u32[]{:S(2)}, u32[]{:S(2)}) collective-permute-start(bf16[256,512]{0,1:T(8,128)(2,1)S(1)} %divide_convert_fusion.1), channel_id=1, source_target_pairs={{0,4},{2,6},{4,0},{6,2},{1,5},{3,7},{5,1},{7,3},{8,12},{10,14},{12... | collective-permute-start | bytes 786440 | tf_op jit(solution)/shard_map/ppermute | solution.py:80
  150.9 16.1 %collective-permute-start.21 = (f32[256,512]{0,1:T(8,128)S(1)}, f32[256,512]{0,1:T(8,128)S(1)}, u32[]{:S(2)}, u32[]{:S(2)}) collective-permute-start(f32[256,512]{0,1:T(8,128)S(1)} %constant_dynamic-slice_fusion), channel_id=1, source_target_pairs={{0,4},{2,6},{4,0},{6,2},{1,5},{3,7},{5,1},{7,3},{8,12},{10,14},{12... | collective-permute-start | bytes 1572872 | tf_op jit(solution)/shard_map/ppermute | solution.py:68
  155.9 11.2 %collective-permute-start.17 = (bf16[512,512]{0,1:T(8,128)(2,1)S(1)}, bf16[512,512]{0,1:T(8,128)(2,1)S(1)}, u32[]{:S(2)}, u32[]{:S(2)}) collective-permute-start(bf16[512,512]{0,1:T(8,128)(2,1)S(1)} %maximum_select_fusion.7), channel_id=1, source_target_pairs={{0,2},{2,0},{4,6},{6,4},{1,3},{3,1},{5,7},{7,5},{8,10},{10,8},{12,... | collective-permute-start | bytes 1572872 | tf_op jit(solution)/shard_map/ppermute | solution.py:80
  167.5 5.3 %collective-permute-start.22 = (bf16[256,512]{0,1:T(8,128)(2,1)S(1)}, bf16[256,512]{0,1:T(8,128)(2,1)S(1)}, u32[]{:S(2)}, u32[]{:S(2)}) collective-permute-start(bf16[256,512]{0,1:T(8,128)(2,1)S(1)} %divide_convert_fusion), channel_id=1, source_target_pairs={{0,4},{2,6},{4,0},{6,2},{1,5},{3,7},{5,1},{7,3},{8,12},{10,14},{12... | collective-permute-start | bytes 786440 | tf_op jit(solution)/shard_map/ppermute | solution.py:80
  173.0 9.2 %collective-permute-start.23 = (bf16[512,512]{0,1:T(8,128)(2,1)S(1)}, bf16[512,512]{0,1:T(8,128)(2,1)S(1)}, u32[]{:S(2)}, u32[]{:S(2)}) collective-permute-start(bf16[512,512]{0,1:T(8,128)(2,1)S(1)} %maximum_select_fusion.8), channel_id=1, source_target_pairs={{0,2},{2,0},{4,6},{6,4},{1,3},{3,1},{5,7},{7,5},{8,10},{10,8},{12,... | collective-permute-start | bytes 1572872 | tf_op jit(solution)/shard_map/ppermute | solution.py:80

commit v13 on v5

--- a/solution.py
+++ b/solution.py
@@ -102,9 +102,10 @@
     previous = None
     rows_done = None
     for c in range(CHUNKS):
-        piece = own[c * width:(c + 1) * width]
+        source = own
         if previous is not None:
-            piece, _ = lax.optimization_barrier((piece, previous))
+            source, _ = lax.optimization_barrier((own, previous))
+        piece = source[c * width:(c + 1) * width]
         arrived = shifted_2(piece, "occ", 2)
         previous = arrived
         if vir_count == 2:

time: 176 us -> 178 us (1.011)
  local copies, waits for them, and re-layouts: 8.45 us -> 10.9 us
    slice x1 -> x4, local copies, waits for them, and re-layouts: 2.74 us -> 5.14 us  [paired_plan(): piece = source[c * width:(c + 1) * width]]
  transfers between devices with their start and end apart: 24 -> 24, of which waited for: 12 -> 12; matrix products, arithmetic and copies ran while one was open for 11% -> 13% of each run, Pallas kernels for 0% -> 0%
where the time goes in v13:
time: 178 us
  waiting for transfers between devices  108 us (61%)
  starting transfers between devices  38.2 us (21%)
  matrix products  13.9 us (8%)
  local copies, waits for them, and re-layouts  10.9 us (6%)
  other arithmetic  4.46 us (3%)
    ppermute x8, waiting for transfers between devices, shifted_2(): lax.ppermute(value, axis, [(i, (i + by) % count) for i in range(count)])  86.2 us
    ppermute x8, starting transfers between devices, aux_all_gather(): other = lax.ppermute(x, 'aux', xor_pairs(count, step))  22.9 us
    ppermute x8, waiting for transfers between devices, aux_reduce_scatter(): x = keep + lax.ppermute(send, 'aux', xor_pairs(count, step))  13.9 us
    ppermute x8, starting transfers between devices, aux_reduce_scatter(): x = keep + lax.ppermute(send, 'aux', xor_pairs(count, step))  8.82 us
    ppermute x8, waiting for transfers between devices, aux_all_gather(): other = lax.ppermute(x, 'aux', xor_pairs(count, step))  8.3 us
    dot_general x4, matrix products, paired_plan(): term = jnp.dot(rows, block, preferred_element_type=jnp.float32)  7.21 us
    dot_general x4, matrix products, paired_plan(): jnp.einsum('aq,bq->ab', own, block, preferred_element_type=jnp.float32)  6.73 us
    ppermute x8, starting transfers between devices, shifted_2(): lax.ppermute(value, axis, [(i, (i + by) % count) for i in range(count)])  6.51 us
  transfers between devices with their start and end apart: 24, of which 12 were waited for; matrix products, arithmetic and copies ran while one was open for 13% of the time, Pallas kernels for 0%

profile of v13, /device:TPU:1, one launch (start us, length us, event | category | flops | bytes accessed | tf_op | source)
XLA Modules:
  0.0 177.6 jit_solution(684046622702913130)
XLA Ops:
  1.1 3.2 %collective-permute-start = (bf16[256,1024]{1,0:T(8,128)(2,1)S(1)}, bf16[256,1024]{1,0:T(8,128)(2,1)S(1)}, u32[]{:S(2)}, u32[]{:S(2)}) collective-permute-start(bf16[256,1024]{1,0:T(8,128)(2,1)S(1)} %slice_bitcast_fusion), channel_id=1, source_target_pairs={{0,16},{8,24},{16,0},{24,8},{1,17},{9,25},{17,1},{25,9},{2,18},{10... | collective-permute-start | bytes 1572872 | tf_op jit(solution)/shard_map/ppermute | solution.py:13
  4.3 22.9 %collective-permute-done = bf16[256,1024]{1,0:T(8,128)(2,1)S(1)} collective-permute-done((bf16[256,1024]{1,0:T(8,128)(2,1)S(1)}, bf16[256,1024]{1,0:T(8,128)(2,1)S(1)}, u32[]{:S(2)}, u32[]{:S(2)}) %collective-permute-start) | collective-permute-done | bytes 524320 | tf_op jit(solution)/shard_map/ppermute | solution.py:13
  31.6 21.2 %collective-permute-done.6 = bf16[256,1024]{1,0:T(8,128)(2,1)} collective-permute-done((bf16[256,1024]{1,0:T(8,128)(2,1)S(1)}, bf16[256,1024]{1,0:T(8,128)(2,1)}, u32[]{:S(2)}, u32[]{:S(2)}) %collective-permute-start.6) | collective-permute-done | bytes 524320 | tf_op jit(solution)/shard_map/ppermute | solution.py:13
  52.8 1.9 %slice.18 = bf16[256,1024]{1,0:T(8,128)(2,1)} slice(bf16[1024,1024]{1,0:T(8,128)(2,1)} %bitcast.42), slice={[512:768], [0:1024]} | slice | bytes 1048576 | tf_op jit(solution)/shard_map/slice | solution.py:108
  55.4 2.9 %fusion.15 = f32[512,1024]{1,0:T(8,128)S(1)} fusion(bf16[512,1024]{1,0:T(8,128)(2,1)S(1)} %constant_dynamic-update-slice_fusion, bf16[1,1024,1024]{2,1,0:T(8,128)(2,1)} %param.3), kind=kOutput, calls=%fused_computation.57 | convolution fusion | flops 1073741824 | bytes 5242880 | tf_op jit(solution)/shard_map/aq,bq->ab/dot_general | solution.py:121
  59.4 2.7 %collective-permute-start.2 = (f32[512,512]{0,1:T(8,128)}, f32[512,512]{0,1:T(8,128)}, u32[]{:S(2)}, u32[]{:S(2)}) collective-permute-start(f32[512,512]{0,1:T(8,128)} %dynamic-slice_bitcast_fusion.3), channel_id=1, source_target_pairs={{0,2},{2,0},{4,6},{6,4},{1,3},{3,1},{5,7},{7,5},{8,10},{10,8},{12,... | collective-permute-start | bytes 3145736 | tf_op jit(solution)/shard_map/ppermute | solution.py:68
  63.3 17.4 %collective-permute-done.12 = bf16[256,1024]{1,0:T(8,128)(2,1)} collective-permute-done((bf16[256,1024]{1,0:T(8,128)(2,1)}, bf16[256,1024]{1,0:T(8,128)(2,1)}, u32[]{:S(2)}, u32[]{:S(2)}) %collective-permute-start.12) | collective-permute-done | bytes 524320 | tf_op jit(solution)/shard_map/ppermute | solution.py:13
  83.0 1.3 fusion.13
  87.0 1.4 bitcast_add_fusion.3
  89.8 9.1 %collective-permute-done.13 = bf16[256,1024]{1,0:T(8,128)(2,1)S(1)} collective-permute-done((bf16[256,1024]{1,0:T(8,128)(2,1)}, bf16[256,1024]{1,0:T(8,128)(2,1)S(1)}, u32[]{:S(2)}, u32[]{:S(2)}) %collective-permute-start.13) | collective-permute-done | bytes 524320 | tf_op jit(solution)/shard_map/ppermute | solution.py:13
  98.9 1.3 fusion.11
  101.3 5.4 %collective-permute-done.18 = bf16[256,1024]{1,0:T(8,128)(2,1)S(1)} collective-permute-done((bf16[256,1024]{1,0:T(8,128)(2,1)S(1)}, bf16[256,1024]{1,0:T(8,128)(2,1)S(1)}, u32[]{:S(2)}, u32[]{:S(2)}) %collective-permute-start.18) | collective-permute-done | bytes 524320 | tf_op jit(solution)/shard_map/ppermute | solution.py:13
  107.5 1.3 collective-permute-start.4
  109.4 10.2 %collective-permute-done.19 = bf16[256,1024]{1,0:T(8,128)(2,1)S(1)} collective-permute-done((bf16[256,1024]{1,0:T(8,128)(2,1)S(1)}, bf16[256,1024]{1,0:T(8,128)(2,1)S(1)}, u32[]{:S(2)}, u32[]{:S(2)}) %collective-permute-start.19) | collective-permute-done | bytes 524320 | tf_op jit(solution)/shard_map/ppermute | solution.py:13
  121.1 1.4 collective-permute-start.5
  122.7 3.2 %collective-permute-done.9 = f32[256,512]{0,1:T(8,128)S(1)} collective-permute-done((f32[256,512]{0,1:T(8,128)S(1)}, f32[256,512]{0,1:T(8,128)S(1)}, u32[]{:S(2)}, u32[]{:S(2)}) %collective-permute-start.9) | collective-permute-done | bytes 524320 | tf_op jit(solution)/shard_map/ppermute | solution.py:68
  126.5 1.3 collective-permute-start.10
  128.2 2.3 %collective-permute-start.20 = (f32[512,512]{0,1:T(8,128)S(1)}, f32[512,512]{0,1:T(8,128)S(1)}, u32[]{:S(2)}, u32[]{:S(2)}) collective-permute-start(f32[512,512]{0,1:T(8,128)S(1)} %dynamic-slice_bitcast_fusion), channel_id=1, source_target_pairs={{0,2},{2,0},{4,6},{6,4},{1,3},{3,1},{5,7},{7,5},{8,10},{10,8},{12,... | collective-permute-start | bytes 3145736 | tf_op jit(solution)/shard_map/ppermute | solution.py:68
  130.5 2.2 %collective-permute-done.10 = bf16[256,512]{0,1:T(8,128)(2,1)S(1)} collective-permute-done((bf16[256,512]{0,1:T(8,128)(2,1)S(1)}, bf16[256,512]{0,1:T(8,128)(2,1)S(1)}, u32[]{:S(2)}, u32[]{:S(2)}) %collective-permute-start.10) | collective-permute-done | bytes 262176 | tf_op jit(solution)/shard_map/ppermute | solution.py:80
  132.8 4.8 %collective-permute-start.11 = (bf16[512,512]{0,1:T(8,128)(2,1)S(1)}, bf16[512,512]{0,1:T(8,128)(2,1)S(1)}, u32[]{:S(2)}, u32[]{:S(2)}) collective-permute-start(bf16[512,512]{0,1:T(8,128)(2,1)S(1)} %maximum_select_fusion.8), channel_id=1, source_target_pairs={{0,2},{2,0},{4,6},{6,4},{1,3},{3,1},{5,7},{7,5},{8,10},{10,8},{12,... | collective-permute-start | bytes 1572872 | tf_op jit(solution)/shard_map/ppermute | solution.py:80
  137.6 6.3 %collective-permute-done.15 = f32[256,512]{0,1:T(8,128)S(1)} collective-permute-done((f32[256,512]{0,1:T(8,128)S(1)}, f32[256,512]{0,1:T(8,128)S(1)}, u32[]{:S(2)}, u32[]{:S(2)}) %collective-permute-start.15) | collective-permute-done | bytes 524320 | tf_op jit(solution)/shard_map/ppermute | solution.py:68
  144.5 1.3 collective-permute-start.16
  146.3 3.4 %collective-permute-done.16 = bf16[256,512]{0,1:T(8,128)(2,1)S(1)} collective-permute-done((bf16[256,512]{0,1:T(8,128)(2,1)S(1)}, bf16[256,512]{0,1:T(8,128)(2,1)S(1)}, u32[]{:S(2)}, u32[]{:S(2)}) %collective-permute-start.16) | collective-permute-done | bytes 262176 | tf_op jit(solution)/shard_map/ppermute | solution.py:80
  149.9 6.7 %collective-permute-start.17 = (bf16[512,512]{0,1:T(8,128)(2,1)S(1)}, bf16[512,512]{0,1:T(8,128)(2,1)S(1)}, u32[]{:S(2)}, u32[]{:S(2)}) collective-permute-start(bf16[512,512]{0,1:T(8,128)(2,1)S(1)} %maximum_select_fusion.9), channel_id=1, source_target_pairs={{0,2},{2,0},{4,6},{6,4},{1,3},{3,1},{5,7},{7,5},{8,10},{10,8},{12,... | collective-permute-start | bytes 1572872 | tf_op jit(solution)/shard_map/ppermute | solution.py:80
  156.5 4.4 %collective-permute-done.21 = f32[256,512]{0,1:T(8,128)S(1)} collective-permute-done((f32[256,512]{0,1:T(8,128)S(1)}, f32[256,512]{0,1:T(8,128)S(1)}, u32[]{:S(2)}, u32[]{:S(2)}) %collective-permute-start.21) | collective-permute-done | bytes 524320 | tf_op jit(solution)/shard_map/ppermute | solution.py:68
  161.6 1.3 collective-permute-start.22
  162.9 1.3 fusion.19
  164.2 2.7 %collective-permute-done.22 = bf16[256,512]{0,1:T(8,128)(2,1)S(1)} collective-permute-done((bf16[256,512]{0,1:T(8,128)(2,1)S(1)}, bf16[256,512]{0,1:T(8,128)(2,1)S(1)}, u32[]{:S(2)}, u32[]{:S(2)}) %collective-permute-start.22) | collective-permute-done | bytes 262176 | tf_op jit(solution)/shard_map/ppermute | solution.py:80
  167.0 4.7 %collective-permute-start.23 = (bf16[512,512]{0,1:T(8,128)(2,1)S(1)}, bf16[512,512]{0,1:T(8,128)(2,1)S(1)}, u32[]{:S(2)}, u32[]{:S(2)}) collective-permute-start(bf16[512,512]{0,1:T(8,128)(2,1)S(1)} %maximum_select_fusion.10), channel_id=1, source_target_pairs={{0,2},{2,0},{4,6},{6,4},{1,3},{3,1},{5,7},{7,5},{8,10},{10,8},{12,... | collective-permute-start | bytes 1572872 | tf_op jit(solution)/shard_map/ppermute | solution.py:80
  171.7 1.5 fusion.20
  173.2 1.3 fusion.21
  174.5 3.1 %fusion = bf16[1,1024,1024]{2,1,0:T(8,128)(2,1)} fusion(f32[1024,1024]{1,0:T(8,128)S(1)} %fusion.21, f32[1024,1024]{1,0:T(8,128)S(1)} %fusion.19, f32[1024,1024]{1,0:T(8,128)S(1)} %fusion.20, bf16[512,1024]{1,0:T(8,128)(2,1)S(1)} %constant_dynamic-update-slice_fusion.6, bf16[512,512]{0,1:T(8,128)(2,1)S(1)} %collective-permute-done.23, ...), kind=kOutput, calls=%fused_computation.1 | convolution fusion | flops 1083703296 | bytes 16777216 | tf_op jit(solution)/shard_map/dot_general | solution.py:138
  (74 shorter events, 20.5 us)
Async XLA Ops:
  0.0 29.4 %copy-start.2 = (f32[4]{0:T(128)S(1)}, f32[4]{0:T(128)}, u32[]{:S(2)}) copy-start(f32[4]{0:T(128)} %param.4) | copy-start | bytes 52
  0.0 31.4 %copy-start.1 = (f32[2048]{0:T(1024)S(1)}, f32[2048]{0:T(1024)}, u32[]{:S(2)}) copy-start(f32[2048]{0:T(1024)} %param.5) | copy-start | bytes 24580
  1.1 26.1 %collective-permute-start = (bf16[256,1024]{1,0:T(8,128)(2,1)S(1)}, bf16[256,1024]{1,0:T(8,128)(2,1)S(1)}, u32[]{:S(2)}, u32[]{:S(2)}) collective-permute-start(bf16[256,1024]{1,0:T(8,128)(2,1)S(1)} %slice_bitcast_fusion), channel_id=1, source_target_pairs={{0,16},{8,24},{16,0},{24,8},{1,17},{9,25},{17,1},{25,9},{2,18},{10... | collective-permute-start | bytes 1572872 | tf_op jit(solution)/shard_map/ppermute | solution.py:13
  28.3 24.5 %collective-permute-start.6 = (bf16[256,1024]{1,0:T(8,128)(2,1)S(1)}, bf16[256,1024]{1,0:T(8,128)(2,1)}, u32[]{:S(2)}, u32[]{:S(2)}) collective-permute-start(bf16[256,1024]{1,0:T(8,128)(2,1)S(1)} %slice.17), channel_id=1, source_target_pairs={{0,16},{8,24},{16,0},{24,8},{1,17},{9,25},{17,1},{25,9},{2,18},{10... | collective-permute-start | bytes 1572872 | tf_op jit(solution)/shard_map/ppermute | solution.py:13
  28.4 27.0 %collective-permute-start.1 = (bf16[256,1024]{1,0:T(8,128)(2,1)S(1)}, bf16[256,1024]{1,0:T(8,128)(2,1)S(1)}, u32[]{:S(2)}, u32[]{:S(2)}) collective-permute-start(bf16[256,1024]{1,0:T(8,128)(2,1)S(1)} %collective-permute-done), channel_id=1, source_target_pairs={{0,1},{1,0},{2,3},{3,2},{4,5},{5,4},{6,7},{7,6},{8,9},{9,8},{10,11... | collective-permute-start | bytes 1572872 | tf_op jit(solution)/shard_map/ppermute | solution.py:13
  54.7 26.1 %collective-permute-start.12 = (bf16[256,1024]{1,0:T(8,128)(2,1)}, bf16[256,1024]{1,0:T(8,128)(2,1)}, u32[]{:S(2)}, u32[]{:S(2)}) collective-permute-start(bf16[256,1024]{1,0:T(8,128)(2,1)} %slice.18), channel_id=1, source_target_pairs={{0,16},{8,24},{16,0},{24,8},{1,17},{9,25},{17,1},{25,9},{2,18},{10... | collective-permute-start | bytes 1572872 | tf_op jit(solution)/shard_map/ppermute | solution.py:13
  54.7 27.3 %collective-permute-start.7 = (bf16[256,1024]{1,0:T(8,128)(2,1)}, bf16[256,1024]{1,0:T(8,128)(2,1)}, u32[]{:S(2)}, u32[]{:S(2)}) collective-permute-start(bf16[256,1024]{1,0:T(8,128)(2,1)} %collective-permute-done.6), channel_id=1, source_target_pairs={{0,1},{1,0},{2,3},{3,2},{4,5},{5,4},{6,7},{7,6},{8,9},{9,8},{10,11... | collective-permute-start | bytes 1572872 | tf_op jit(solution)/shard_map/ppermute | solution.py:13
  59.4 27.6 %collective-permute-start.2 = (f32[512,512]{0,1:T(8,128)}, f32[512,512]{0,1:T(8,128)}, u32[]{:S(2)}, u32[]{:S(2)}) collective-permute-start(f32[512,512]{0,1:T(8,128)} %dynamic-slice_bitcast_fusion.3), channel_id=1, source_target_pairs={{0,2},{2,0},{4,6},{6,4},{1,3},{3,1},{5,7},{7,5},{8,10},{10,8},{12,... | collective-permute-start | bytes 3145736 | tf_op jit(solution)/shard_map/ppermute | solution.py:68
  62.1 20.9 %copy-start = (bf16[1,1024,1024]{2,1,0:T(8,128)(2,1)S(1)}, bf16[1,1024,1024]{2,1,0:T(8,128)(2,1)}, u32[]{:S(2)}) copy-start(bf16[1,1024,1024]{2,1,0:T(8,128)(2,1)} %param.3) | copy-start | bytes 6291460
  81.8 24.8 %collective-permute-start.18 = (bf16[256,1024]{1,0:T(8,128)(2,1)S(1)}, bf16[256,1024]{1,0:T(8,128)(2,1)S(1)}, u32[]{:S(2)}, u32[]{:S(2)}) collective-permute-start(bf16[256,1024]{1,0:T(8,128)(2,1)S(1)} %slice.19), channel_id=1, source_target_pairs={{0,16},{8,24},{16,0},{24,8},{1,17},{9,25},{17,1},{25,9},{2,18},{10... | collective-permute-start | bytes 1572872 | tf_op jit(solution)/shard_map/ppermute | solution.py:13
  84.4 24.4 %collective-permute-start.8 = (f32[512,512]{0,1:T(8,128)S(1)}, f32[512,512]{0,1:T(8,128)S(1)}, u32[]{:S(2)}, u32[]{:S(2)}) collective-permute-start(f32[512,512]{0,1:T(8,128)S(1)} %dynamic-slice_bitcast_fusion.2), channel_id=1, source_target_pairs={{0,2},{2,0},{4,6},{6,4},{1,3},{3,1},{5,7},{7,5},{8,10},{10,8},{12,... | collective-permute-start | bytes 3145736 | tf_op jit(solution)/shard_map/ppermute | solution.py:68
  85.2 13.7 %collective-permute-start.13 = (bf16[256,1024]{1,0:T(8,128)(2,1)}, bf16[256,1024]{1,0:T(8,128)(2,1)S(1)}, u32[]{:S(2)}, u32[]{:S(2)}) collective-permute-start(bf16[256,1024]{1,0:T(8,128)(2,1)} %collective-permute-done.12), channel_id=1, source_target_pairs={{0,1},{1,0},{2,3},{3,2},{4,5},{5,4},{6,7},{7,6},{8,9},{9,8},{10,11... | collective-permute-start | bytes 1572872 | tf_op jit(solution)/shard_map/ppermute | solution.py:13
  88.5 18.9 %collective-permute-start.3 = (f32[256,512]{0,1:T(8,128)S(1)}, f32[256,512]{0,1:T(8,128)S(1)}, u32[]{:S(2)}, u32[]{:S(2)}) collective-permute-start(f32[256,512]{0,1:T(8,128)S(1)} %constant_dynamic-slice_fusion.3), channel_id=1, source_target_pairs={{0,4},{2,6},{4,0},{6,2},{1,5},{3,7},{5,1},{7,3},{8,12},{10,14},{12... | collective-permute-start | bytes 1572872 | tf_op jit(solution)/shard_map/ppermute | solution.py:68
  100.3 22.2 %collective-permute-start.14 = (f32[512,512]{0,1:T(8,128)S(1)}, f32[512,512]{0,1:T(8,128)S(1)}, u32[]{:S(2)}, u32[]{:S(2)}) collective-permute-start(f32[512,512]{0,1:T(8,128)S(1)} %dynamic-slice_bitcast_fusion.1), channel_id=1, source_target_pairs={{0,2},{2,0},{4,6},{6,4},{1,3},{3,1},{5,7},{7,5},{8,10},{10,8},{12,... | collective-permute-start | bytes 3145736 | tf_op jit(solution)/shard_map/ppermute | solution.py:68
  106.6 13.0 %collective-permute-start.19 = (bf16[256,1024]{1,0:T(8,128)(2,1)S(1)}, bf16[256,1024]{1,0:T(8,128)(2,1)S(1)}, u32[]{:S(2)}, u32[]{:S(2)}) collective-permute-start(bf16[256,1024]{1,0:T(8,128)(2,1)S(1)} %collective-permute-done.18), channel_id=1, source_target_pairs={{0,1},{1,0},{2,3},{3,2},{4,5},{5,4},{6,7},{7,6},{8,9},{9,8},{10,11... | collective-permute-start | bytes 1572872 | tf_op jit(solution)/shard_map/ppermute | solution.py:13
  107.5 13.4 %collective-permute-start.4 = (bf16[256,512]{0,1:T(8,128)(2,1)S(1)}, bf16[256,512]{0,1:T(8,128)(2,1)S(1)}, u32[]{:S(2)}, u32[]{:S(2)}) collective-permute-start(bf16[256,512]{0,1:T(8,128)(2,1)S(1)} %divide_convert_fusion.3), channel_id=1, source_target_pairs={{0,4},{2,6},{4,0},{6,2},{1,5},{3,7},{5,1},{7,3},{8,12},{10,14},{12... | collective-permute-start | bytes 786440 | tf_op jit(solution)/shard_map/ppermute | solution.py:80
  109.1 16.8 %collective-permute-start.9 = (f32[256,512]{0,1:T(8,128)S(1)}, f32[256,512]{0,1:T(8,128)S(1)}, u32[]{:S(2)}, u32[]{:S(2)}) collective-permute-start(f32[256,512]{0,1:T(8,128)S(1)} %constant_dynamic-slice_fusion.2), channel_id=1, source_target_pairs={{0,4},{2,6},{4,0},{6,2},{1,5},{3,7},{5,1},{7,3},{8,12},{10,14},{12... | collective-permute-start | bytes 1572872 | tf_op jit(solution)/shard_map/ppermute | solution.py:68
  121.1 4.9 %collective-permute-start.5 = (bf16[512,512]{0,1:T(8,128)(2,1)S(1)}, bf16[512,512]{0,1:T(8,128)(2,1)S(1)}, u32[]{:S(2)}, u32[]{:S(2)}) collective-permute-start(bf16[512,512]{0,1:T(8,128)(2,1)S(1)} %maximum_select_fusion.7), channel_id=1, source_target_pairs={{0,2},{2,0},{4,6},{6,4},{1,3},{3,1},{5,7},{7,5},{8,10},{10,8},{12,... | collective-permute-start | bytes 1572872 | tf_op jit(solution)/shard_map/ppermute | solution.py:80
  126.5 6.2 %collective-permute-start.10 = (bf16[256,512]{0,1:T(8,128)(2,1)S(1)}, bf16[256,512]{0,1:T(8,128)(2,1)S(1)}, u32[]{:S(2)}, u32[]{:S(2)}) collective-permute-start(bf16[256,512]{0,1:T(8,128)(2,1)S(1)} %divide_convert_fusion.2), channel_id=1, source_target_pairs={{0,4},{2,6},{4,0},{6,2},{1,5},{3,7},{5,1},{7,3},{8,12},{10,14},{12... | collective-permute-start | bytes 786440 | tf_op jit(solution)/shard_map/ppermute | solution.py:80
  127.8 16.1 %collective-permute-start.15 = (f32[256,512]{0,1:T(8,128)S(1)}, f32[256,512]{0,1:T(8,128)S(1)}, u32[]{:S(2)}, u32[]{:S(2)}) collective-permute-start(f32[256,512]{0,1:T(8,128)S(1)} %constant_dynamic-slice_fusion.1), channel_id=1, source_target_pairs={{0,4},{2,6},{4,0},{6,2},{1,5},{3,7},{5,1},{7,3},{8,12},{10,14},{12... | collective-permute-start | bytes 1572872 | tf_op jit(solution)/shard_map/ppermute | solution.py:68
  128.2 17.6 %collective-permute-start.20 = (f32[512,512]{0,1:T(8,128)S(1)}, f32[512,512]{0,1:T(8,128)S(1)}, u32[]{:S(2)}, u32[]{:S(2)}) collective-permute-start(f32[512,512]{0,1:T(8,128)S(1)} %dynamic-slice_bitcast_fusion), channel_id=1, source_target_pairs={{0,2},{2,0},{4,6},{6,4},{1,3},{3,1},{5,7},{7,5},{8,10},{10,8},{12,... | collective-permute-start | bytes 3145736 | tf_op jit(solution)/shard_map/ppermute | solution.py:68
  132.8 11.2 %collective-permute-start.11 = (bf16[512,512]{0,1:T(8,128)(2,1)S(1)}, bf16[512,512]{0,1:T(8,128)(2,1)S(1)}, u32[]{:S(2)}, u32[]{:S(2)}) collective-permute-start(bf16[512,512]{0,1:T(8,128)(2,1)S(1)} %maximum_select_fusion.8), channel_id=1, source_target_pairs={{0,2},{2,0},{4,6},{6,4},{1,3},{3,1},{5,7},{7,5},{8,10},{10,8},{12,... | collective-permute-start | bytes 1572872 | tf_op jit(solution)/shard_map/ppermute | solution.py:80
  144.5 5.3 %collective-permute-start.16 = (bf16[256,512]{0,1:T(8,128)(2,1)S(1)}, bf16[256,512]{0,1:T(8,128)(2,1)S(1)}, u32[]{:S(2)}, u32[]{:S(2)}) collective-permute-start(bf16[256,512]{0,1:T(8,128)(2,1)S(1)} %divide_convert_fusion.1), channel_id=1, source_target_pairs={{0,4},{2,6},{4,0},{6,2},{1,5},{3,7},{5,1},{7,3},{8,12},{10,14},{12... | collective-permute-start | bytes 786440 | tf_op jit(solution)/shard_map/ppermute | solution.py:80
  146.1 14.9 %collective-permute-start.21 = (f32[256,512]{0,1:T(8,128)S(1)}, f32[256,512]{0,1:T(8,128)S(1)}, u32[]{:S(2)}, u32[]{:S(2)}) collective-permute-start(f32[256,512]{0,1:T(8,128)S(1)} %constant_dynamic-slice_fusion), channel_id=1, source_target_pairs={{0,4},{2,6},{4,0},{6,2},{1,5},{3,7},{5,1},{7,3},{8,12},{10,14},{12... | collective-permute-start | bytes 1572872 | tf_op jit(solution)/shard_map/ppermute | solution.py:68
  149.9 11.2 %collective-permute-start.17 = (bf16[512,512]{0,1:T(8,128)(2,1)S(1)}, bf16[512,512]{0,1:T(8,128)(2,1)S(1)}, u32[]{:S(2)}, u32[]{:S(2)}) collective-permute-start(bf16[512,512]{0,1:T(8,128)(2,1)S(1)} %maximum_select_fusion.9), channel_id=1, source_target_pairs={{0,2},{2,0},{4,6},{6,4},{1,3},{3,1},{5,7},{7,5},{8,10},{10,8},{12,... | collective-permute-start | bytes 1572872 | tf_op jit(solution)/shard_map/ppermute | solution.py:80
  161.6 5.3 %collective-permute-start.22 = (bf16[256,512]{0,1:T(8,128)(2,1)S(1)}, bf16[256,512]{0,1:T(8,128)(2,1)S(1)}, u32[]{:S(2)}, u32[]{:S(2)}) collective-permute-start(bf16[256,512]{0,1:T(8,128)(2,1)S(1)} %divide_convert_fusion), channel_id=1, source_target_pairs={{0,4},{2,6},{4,0},{6,2},{1,5},{3,7},{5,1},{7,3},{8,12},{10,14},{12... | collective-permute-start | bytes 786440 | tf_op jit(solution)/shard_map/ppermute | solution.py:80
  167.0 7.5 %collective-permute-start.23 = (bf16[512,512]{0,1:T(8,128)(2,1)S(1)}, bf16[512,512]{0,1:T(8,128)(2,1)S(1)}, u32[]{:S(2)}, u32[]{:S(2)}) collective-permute-start(bf16[512,512]{0,1:T(8,128)(2,1)S(1)} %maximum_select_fusion.10), channel_id=1, source_target_pairs={{0,2},{2,0},{4,6},{6,4},{1,3},{3,1},{5,7},{7,5},{8,10},{10,8},{12,... | collective-permute-start | bytes 1572872 | tf_op jit(solution)/shard_map/ppermute | solution.py:80

commit v14 on v7

--- a/solution.py
+++ b/solution.py
@@ -100,14 +100,15 @@
     total = None
     previous = None
     rows_done = None
-    near, far = [], []
+    near = []
     for c in range(CHUNKS):
         piece = own[c * width:(c + 1) * width]
         if previous is not None:
-            gate = [previous] + [s for s in (near[c - 2:c - 1] + far[c - 3:c - 2]) if c >= 2]
-            piece, _ = lax.optimization_barrier((piece, gate))
+            piece, _ = lax.optimization_barrier((piece, previous))
         arrived = shifted_2(piece, "occ", 2)
         previous = arrived
+        if c >= 2:
+            arrived, _ = lax.optimization_barrier((arrived, near[c - 2]))
         if vir_count == 2:
             mate = shifted_2(arrived, "vir", 1)
             block = jnp.concatenate([arrived, mate])
@@ -123,7 +124,6 @@
             summed, first = aux_reduce_scatter(partial, stop=2)
             near.append(summed)
             summed, first = aux_reduce_scatter(summed, first, step=2)
-            far.append(summed)
         else:
             summed = lax.psum_scatter(partial, "aux", scatter_dimension=0, tiled=True)
             first = first_row

time: 197 us -> 181 us (0.919)
  waiting for transfers between devices: 130 us -> 116 us
    ppermute x8, waiting for transfers between devices: 86 us -> 79.1 us  [shifted_2(): lax.ppermute(value, axis, [(i, (i + by) % count) for i in range(count)])]
    ppermute x8, waiting for transfers between devices: 29.3 us -> 23.9 us  [aux_reduce_scatter(): x = keep + lax.ppermute(send, 'aux', xor_pairs(count, step))]
    ppermute x8, starting transfers between devices: 13.5 us -> 10.9 us  [aux_reduce_scatter(): x = keep + lax.ppermute(send, 'aux', xor_pairs(count, step))]
    ppermute x8, waiting for transfers between devices: 15.1 us -> 13 us  [aux_all_gather(): other = lax.ppermute(x, 'aux', xor_pairs(count, step))]
  transfers between devices with their start and end apart: 24 -> 24, of which waited for: 14 -> 15; matrix products, arithmetic and copies ran while one was open for 13% -> 13% of each run, Pallas kernels for 0% -> 0%
where the time goes in v14:
time: 181 us; the launch traced here: 180 us
  waiting for transfers between devices  116 us (64%)
  starting transfers between devices  31.1 us (17%)
  matrix products  15.6 us (9%)
  local copies, waits for them, and re-layouts  9.17 us (5%)
  other arithmetic  6.71 us (4%)
    ppermute x8, waiting for transfers between devices, shifted_2(): lax.ppermute(value, axis, [(i, (i + by) % count) for i in range(count)])  79.1 us
    ppermute x8, waiting for transfers between devices, aux_reduce_scatter(): x = keep + lax.ppermute(send, 'aux', xor_pairs(count, step))  23.9 us
    ppermute x8, starting transfers between devices, aux_all_gather(): other = lax.ppermute(x, 'aux', xor_pairs(count, step))  13.3 us
    ppermute x8, waiting for transfers between devices, aux_all_gather(): other = lax.ppermute(x, 'aux', xor_pairs(count, step))  13 us
    ppermute x8, starting transfers between devices, aux_reduce_scatter(): x = keep + lax.ppermute(send, 'aux', xor_pairs(count, step))  10.9 us
    dot_general x4, matrix products, paired_plan(): jnp.einsum('aq,bq->ab', own, block, preferred_element_type=jnp.float32)  8.35 us
    dot_general x4, matrix products, paired_plan(): term = jnp.dot(rows, block, preferred_element_type=jnp.float32)  7.25 us
    ppermute x8, starting transfers between devices, shifted_2(): lax.ppermute(value, axis, [(i, (i + by) % count) for i in range(count)])  6.85 us
  transfers between devices with their start and end apart: 24, of which 15 were waited for; matrix products, arithmetic and copies ran while one was open for 13% of the time, Pallas kernels for 0%

profile of v14, /device:TPU:1, one launch (start us, length us, event | category | flops | bytes accessed | tf_op | source)
XLA Modules:
  0.0 180.0 jit_solution(5385641502953778791)
XLA Ops:
  0.0 2.8 %slice_bitcast_fusion.3 = (bf16[256,1024]{1,0:T(8,128)(2,1)S(1)}, bf16[256,1024]{1,0:T(8,128)(2,1)S(1)}, bf16[256,1024]{1,0:T(8,128)(2,1)}, bf16[256,1024]{1,0:T(8,128)(2,1)}) fusion(bf16[1,1024,1024]{2,1,0:T(8,128)(2,1)} %param.3), kind=kLoop, calls=%fused_computation.43 | loop fusion | bytes 4194304 | tf_op jit(solution)/shard_map/slice | solution.py:105
  2.8 3.1 %collective-permute-start = (bf16[256,1024]{1,0:T(8,128)(2,1)S(1)}, bf16[256,1024]{1,0:T(8,128)(2,1)S(1)}, u32[]{:S(2)}, u32[]{:S(2)}) collective-permute-start(bf16[256,1024]{1,0:T(8,128)(2,1)S(1)} %get-tuple-element.21), channel_id=1, source_target_pairs={{0,16},{8,24},{16,0},{24,8},{1,17},{9,25},{17,1},{25,9},{2,18},{10... | collective-permute-start | bytes 1572872 | tf_op jit(solution)/shard_map/ppermute | solution.py:13
  5.9 22.9 %collective-permute-done = bf16[256,1024]{1,0:T(8,128)(2,1)S(1)} collective-permute-done((bf16[256,1024]{1,0:T(8,128)(2,1)S(1)}, bf16[256,1024]{1,0:T(8,128)(2,1)S(1)}, u32[]{:S(2)}, u32[]{:S(2)}) %collective-permute-start) | collective-permute-done | bytes 524320 | tf_op jit(solution)/shard_map/ppermute | solution.py:13
  29.8 11.2 %collective-permute-done.1 = bf16[256,1024]{1,0:T(8,128)(2,1)S(1)} collective-permute-done((bf16[256,1024]{1,0:T(8,128)(2,1)S(1)}, bf16[256,1024]{1,0:T(8,128)(2,1)S(1)}, u32[]{:S(2)}, u32[]{:S(2)}) %collective-permute-start.1) | collective-permute-done | bytes 524320 | tf_op jit(solution)/shard_map/ppermute | solution.py:13
  41.0 2.9 %fusion.6 = f32[512,1024]{1,0:T(8,128)S(1)} fusion(bf16[512,1024]{1,0:T(8,128)(2,1)S(1)} %constant_dynamic-update-slice_fusion, bf16[1,1024,1024]{2,1,0:T(8,128)(2,1)} %param.3), kind=kOutput, calls=%fused_computation.7 | convolution fusion | flops 1073741824 | bytes 5242880 | tf_op jit(solution)/shard_map/aq,bq->ab/dot_general | solution.py:122
  43.9 10.0 %collective-permute-done.6 = bf16[256,1024]{1,0:T(8,128)(2,1)} collective-permute-done((bf16[256,1024]{1,0:T(8,128)(2,1)S(1)}, bf16[256,1024]{1,0:T(8,128)(2,1)}, u32[]{:S(2)}, u32[]{:S(2)}) %collective-permute-start.6) | collective-permute-done | bytes 524320 | tf_op jit(solution)/shard_map/ppermute | solution.py:13
  54.7 2.5 %collective-permute-start.2 = (f32[512,512]{0,1:T(8,128)S(1)}, f32[512,512]{0,1:T(8,128)}, u32[]{:S(2)}, u32[]{:S(2)}) collective-permute-start(f32[512,512]{0,1:T(8,128)S(1)} %dynamic-slice_bitcast_fusion.3), channel_id=1, source_target_pairs={{0,2},{2,0},{4,6},{6,4},{1,3},{3,1},{5,7},{7,5},{8,10},{10,8},{12,... | collective-permute-start | bytes 3145736 | tf_op jit(solution)/shard_map/ppermute | solution.py:67
  58.3 6.9 %collective-permute-done.7 = bf16[256,1024]{1,0:T(8,128)(2,1)} collective-permute-done((bf16[256,1024]{1,0:T(8,128)(2,1)}, bf16[256,1024]{1,0:T(8,128)(2,1)}, u32[]{:S(2)}, u32[]{:S(2)}) %collective-permute-start.7) | collective-permute-done | bytes 524320 | tf_op jit(solution)/shard_map/ppermute | solution.py:13
  66.3 2.9 %fusion.4 = f32[512,1024]{1,0:T(8,128)S(1)} fusion(bf16[512,1024]{1,0:T(8,128)(2,1)S(1)} %constant_dynamic-update-slice_fusion.2, bf16[1,1024,1024]{2,1,0:T(8,128)(2,1)} %param.3), kind=kOutput, calls=%fused_computation.5 | convolution fusion | flops 1073741824 | bytes 5242880 | tf_op jit(solution)/shard_map/aq,bq->ab/dot_general | solution.py:122
  70.3 3.4 %collective-permute-start.8 = (f32[512,512]{0,1:T(8,128)}, f32[512,512]{0,1:T(8,128)}, u32[]{:S(2)}, u32[]{:S(2)}) collective-permute-start(f32[512,512]{0,1:T(8,128)} %dynamic-slice_bitcast_fusion.2), channel_id=1, source_target_pairs={{0,2},{2,0},{4,6},{6,4},{1,3},{3,1},{5,7},{7,5},{8,10},{10,8},{12,... | collective-permute-start | bytes 3145736 | tf_op jit(solution)/shard_map/ppermute | solution.py:67
  73.6 1.4 bitcast_add_fusion.3
  79.2 2.9 %collective-permute-done.12 = bf16[256,1024]{1,0:T(8,128)(2,1)} collective-permute-done((bf16[256,1024]{1,0:T(8,128)(2,1)}, bf16[256,1024]{1,0:T(8,128)(2,1)}, u32[]{:S(2)}, u32[]{:S(2)}) %collective-permute-start.12) | collective-permute-done | bytes 524320 | tf_op jit(solution)/shard_map/ppermute | solution.py:13
  84.2 3.8 %collective-permute-done.3 = f32[256,512]{0,1:T(8,128)} collective-permute-done((f32[256,512]{0,1:T(8,128)}, f32[256,512]{0,1:T(8,128)}, u32[]{:S(2)}, u32[]{:S(2)}) %collective-permute-start.3) | collective-permute-done | bytes 524320 | tf_op jit(solution)/shard_map/ppermute | solution.py:67
  89.2 1.3 collective-permute-start.4
  90.5 1.4 bitcast_add_fusion.2
  92.5 2.9 %collective-permute-done.13 = bf16[256,1024]{1,0:T(8,128)(2,1)S(1)} collective-permute-done((bf16[256,1024]{1,0:T(8,128)(2,1)}, bf16[256,1024]{1,0:T(8,128)(2,1)S(1)}, u32[]{:S(2)}, u32[]{:S(2)}) %collective-permute-start.13) | collective-permute-done | bytes 524320 | tf_op jit(solution)/shard_map/ppermute | solution.py:13
  96.7 11.6 %collective-permute-done.18 = bf16[256,1024]{1,0:T(8,128)(2,1)S(1)} collective-permute-done((bf16[256,1024]{1,0:T(8,128)(2,1)}, bf16[256,1024]{1,0:T(8,128)(2,1)S(1)}, u32[]{:S(2)}, u32[]{:S(2)}) %collective-permute-start.18) | collective-permute-done | bytes 524320 | tf_op jit(solution)/shard_map/ppermute | solution.py:13
  110.6 10.7 %collective-permute-done.19 = bf16[256,1024]{1,0:T(8,128)(2,1)S(1)} collective-permute-done((bf16[256,1024]{1,0:T(8,128)(2,1)S(1)}, bf16[256,1024]{1,0:T(8,128)(2,1)S(1)}, u32[]{:S(2)}, u32[]{:S(2)}) %collective-permute-start.19) | collective-permute-done | bytes 524320 | tf_op jit(solution)/shard_map/ppermute | solution.py:13
  122.8 1.3 fusion
  124.2 1.7 collective-permute-start.20
  125.9 2.4 %collective-permute-done.10 = bf16[256,512]{0,1:T(8,128)(2,1)S(1)} collective-permute-done((bf16[256,512]{0,1:T(8,128)(2,1)S(1)}, bf16[256,512]{0,1:T(8,128)(2,1)S(1)}, u32[]{:S(2)}, u32[]{:S(2)}) %collective-permute-start.10) | collective-permute-done | bytes 262176 | tf_op jit(solution)/shard_map/ppermute | solution.py:79
  128.4 2.3 %collective-permute-start.11 = (bf16[512,512]{0,1:T(8,128)(2,1)S(1)}, bf16[512,512]{0,1:T(8,128)(2,1)S(1)}, u32[]{:S(2)}, u32[]{:S(2)}) collective-permute-start(bf16[512,512]{0,1:T(8,128)(2,1)S(1)} %maximum_select_fusion.6), channel_id=1, source_target_pairs={{0,2},{2,0},{4,6},{6,4},{1,3},{3,1},{5,7},{7,5},{8,10},{10,8},{12,... | collective-permute-start | bytes 1572872 | tf_op jit(solution)/shard_map/ppermute | solution.py:79
  132.6 12.0 %collective-permute-done.15 = f32[256,512]{0,1:T(8,128)S(1)} collective-permute-done((f32[256,512]{0,1:T(8,128)S(1)}, f32[256,512]{0,1:T(8,128)S(1)}, u32[]{:S(2)}, u32[]{:S(2)}) %collective-permute-start.15) | collective-permute-done | bytes 524320 | tf_op jit(solution)/shard_map/ppermute | solution.py:67
  146.7 5.2 %collective-permute-done.16 = bf16[256,512]{0,1:T(8,128)(2,1)S(1)} collective-permute-done((bf16[256,512]{0,1:T(8,128)(2,1)S(1)}, bf16[256,512]{0,1:T(8,128)(2,1)S(1)}, u32[]{:S(2)}, u32[]{:S(2)}) %collective-permute-start.16) | collective-permute-done | bytes 262176 | tf_op jit(solution)/shard_map/ppermute | solution.py:79
  152.1 3.1 %collective-permute-start.17 = (bf16[512,512]{0,1:T(8,128)(2,1)S(1)}, bf16[512,512]{0,1:T(8,128)(2,1)S(1)}, u32[]{:S(2)}, u32[]{:S(2)}) collective-permute-start(bf16[512,512]{0,1:T(8,128)(2,1)S(1)} %maximum_select_fusion.7), channel_id=1, source_target_pairs={{0,2},{2,0},{4,6},{6,4},{1,3},{3,1},{5,7},{7,5},{8,10},{10,8},{12,... | collective-permute-start | bytes 1572872 | tf_op jit(solution)/shard_map/ppermute | solution.py:79
  155.1 8.0 %collective-permute-done.21 = f32[256,512]{0,1:T(8,128)S(1)} collective-permute-done((f32[256,512]{0,1:T(8,128)S(1)}, f32[256,512]{0,1:T(8,128)S(1)}, u32[]{:S(2)}, u32[]{:S(2)}) %collective-permute-start.21) | collective-permute-done | bytes 524320 | tf_op jit(solution)/shard_map/ppermute | solution.py:67
  164.8 5.1 %collective-permute-done.22 = bf16[256,512]{0,1:T(8,128)(2,1)S(1)} collective-permute-done((bf16[256,512]{0,1:T(8,128)(2,1)S(1)}, bf16[256,512]{0,1:T(8,128)(2,1)S(1)}, u32[]{:S(2)}, u32[]{:S(2)}) %collective-permute-start.22) | collective-permute-done | bytes 262176 | tf_op jit(solution)/shard_map/ppermute | solution.py:79
  170.1 2.7 %collective-permute-start.23 = (bf16[512,512]{0,1:T(8,128)(2,1)S(1)}, bf16[512,512]{0,1:T(8,128)(2,1)S(1)}, u32[]{:S(2)}, u32[]{:S(2)}) collective-permute-start(bf16[512,512]{0,1:T(8,128)(2,1)S(1)} %maximum_select_fusion.8), channel_id=1, source_target_pairs={{0,2},{2,0},{4,6},{6,4},{1,3},{3,1},{5,7},{7,5},{8,10},{10,8},{12,... | collective-permute-start | bytes 1572872 | tf_op jit(solution)/shard_map/ppermute | solution.py:79
  172.8 1.3 fusion.19
  174.1 1.5 fusion.20
  175.6 1.3 fusion.9
  176.9 3.1 %fusion.8 = bf16[1,1024,1024]{2,1,0:T(8,128)(2,1)} fusion(f32[1024,1024]{1,0:T(8,128)S(1)} %fusion.9, f32[1024,1024]{1,0:T(8,128)S(1)} %fusion.20, f32[1024,1024]{1,0:T(8,128)S(1)} %fusion.19, bf16[1024,512]{0,1:T(8,128)(2,1)S(1)} %maximum_select_fusion, bf16[512,1024]{1,0:T(8,128)(2,1)S(1)} %constant_dynamic-update-slice_fusion), kind=kOutput, calls=%fused_computation.9 | convolution fusion | flops 1078984704 | bytes 16777216 | tf_op jit(solution)/shard_map/dot_general | solution.py:141
  (79 shorter events, 22.8 us)
Async XLA Ops:
  2.8 26.0 %collective-permute-start = (bf16[256,1024]{1,0:T(8,128)(2,1)S(1)}, bf16[256,1024]{1,0:T(8,128)(2,1)S(1)}, u32[]{:S(2)}, u32[]{:S(2)}) collective-permute-start(bf16[256,1024]{1,0:T(8,128)(2,1)S(1)} %get-tuple-element.21), channel_id=1, source_target_pairs={{0,16},{8,24},{16,0},{24,8},{1,17},{9,25},{17,1},{25,9},{2,18},{10... | collective-permute-start | bytes 1572872 | tf_op jit(solution)/shard_map/ppermute | solution.py:13
  28.8 12.2 %collective-permute-start.1 = (bf16[256,1024]{1,0:T(8,128)(2,1)S(1)}, bf16[256,1024]{1,0:T(8,128)(2,1)S(1)}, u32[]{:S(2)}, u32[]{:S(2)}) collective-permute-start(bf16[256,1024]{1,0:T(8,128)(2,1)S(1)} %collective-permute-done), channel_id=1, source_target_pairs={{0,1},{1,0},{2,3},{3,2},{4,5},{5,4},{6,7},{7,6},{8,9},{9,8},{10,11... | collective-permute-start | bytes 1572872 | tf_op jit(solution)/shard_map/ppermute | solution.py:13
  29.8 24.1 %collective-permute-start.6 = (bf16[256,1024]{1,0:T(8,128)(2,1)S(1)}, bf16[256,1024]{1,0:T(8,128)(2,1)}, u32[]{:S(2)}, u32[]{:S(2)}) collective-permute-start(bf16[256,1024]{1,0:T(8,128)(2,1)S(1)} %get-tuple-element.13), channel_id=1, source_target_pairs={{0,16},{8,24},{16,0},{24,8},{1,17},{9,25},{17,1},{25,9},{2,18},{10... | collective-permute-start | bytes 1572872 | tf_op jit(solution)/shard_map/ppermute | solution.py:13
  43.9 10.7 %copy-start.2 = (f32[512,1024]{1,0:T(8,128)}, f32[512,1024]{1,0:T(8,128)S(1)}, u32[]{:S(2)}) copy-start(f32[512,1024]{1,0:T(8,128)S(1)} %fusion.6) | copy-start | bytes 6291460
  53.9 11.3 %collective-permute-start.7 = (bf16[256,1024]{1,0:T(8,128)(2,1)}, bf16[256,1024]{1,0:T(8,128)(2,1)}, u32[]{:S(2)}, u32[]{:S(2)}) collective-permute-start(bf16[256,1024]{1,0:T(8,128)(2,1)} %collective-permute-done.6), channel_id=1, source_target_pairs={{0,1},{1,0},{2,3},{3,2},{4,5},{5,4},{6,7},{7,6},{8,9},{9,8},{10,11... | collective-permute-start | bytes 1572872 | tf_op jit(solution)/shard_map/ppermute | solution.py:13
  54.7 18.9 %collective-permute-start.2 = (f32[512,512]{0,1:T(8,128)S(1)}, f32[512,512]{0,1:T(8,128)}, u32[]{:S(2)}, u32[]{:S(2)}) collective-permute-start(f32[512,512]{0,1:T(8,128)S(1)} %dynamic-slice_bitcast_fusion.3), channel_id=1, source_target_pairs={{0,2},{2,0},{4,6},{6,4},{1,3},{3,1},{5,7},{7,5},{8,10},{10,8},{12,... | collective-permute-start | bytes 3145736 | tf_op jit(solution)/shard_map/ppermute | solution.py:67
  57.2 24.9 %collective-permute-start.12 = (bf16[256,1024]{1,0:T(8,128)(2,1)}, bf16[256,1024]{1,0:T(8,128)(2,1)}, u32[]{:S(2)}, u32[]{:S(2)}) collective-permute-start(bf16[256,1024]{1,0:T(8,128)(2,1)} %get-tuple-element.15), channel_id=1, source_target_pairs={{0,16},{8,24},{16,0},{24,8},{1,17},{9,25},{17,1},{25,9},{2,18},{10... | collective-permute-start | bytes 1572872 | tf_op jit(solution)/shard_map/ppermute | solution.py:13
  69.2 5.9 %copy-start = (f32[512,1024]{1,0:T(8,128)}, f32[512,1024]{1,0:T(8,128)S(1)}, u32[]{:S(2)}) copy-start(f32[512,1024]{1,0:T(8,128)S(1)} %fusion.4) | copy-start | bytes 6291460
  69.2 4.4 %copy-start.3 = (f32[512,1024]{1,0:T(8,128)S(1)}, f32[512,1024]{1,0:T(8,128)}, u32[]{:S(2)}) copy-start(f32[512,1024]{1,0:T(8,128)} %copy-done.2) | copy-start | bytes 6291460
  70.2 6.9 %copy-start.6 = (f32[4]{0:T(128)S(1)}, f32[4]{0:T(128)}, u32[]{:S(2)}) copy-start(f32[4]{0:T(128)} %param.4) | copy-start | bytes 52
  70.3 8.8 %copy-start.5 = (f32[2048]{0:T(1024)S(1)}, f32[2048]{0:T(1024)}, u32[]{:S(2)}) copy-start(f32[2048]{0:T(1024)} %param.5) | copy-start | bytes 24580
  70.3 20.2 %collective-permute-start.8 = (f32[512,512]{0,1:T(8,128)}, f32[512,512]{0,1:T(8,128)}, u32[]{:S(2)}, u32[]{:S(2)}) collective-permute-start(f32[512,512]{0,1:T(8,128)} %dynamic-slice_bitcast_fusion.2), channel_id=1, source_target_pairs={{0,2},{2,0},{4,6},{6,4},{1,3},{3,1},{5,7},{7,5},{8,10},{10,8},{12,... | collective-permute-start | bytes 3145736 | tf_op jit(solution)/shard_map/ppermute | solution.py:67
  75.9 12.1 %collective-permute-start.3 = (f32[256,512]{0,1:T(8,128)}, f32[256,512]{0,1:T(8,128)}, u32[]{:S(2)}, u32[]{:S(2)}) collective-permute-start(f32[256,512]{0,1:T(8,128)} %constant_dynamic-slice_fusion.3), channel_id=1, source_target_pairs={{0,4},{2,6},{4,0},{6,2},{1,5},{3,7},{5,1},{7,3},{8,12},{10,14},{12... | collective-permute-start | bytes 1572872 | tf_op jit(solution)/shard_map/ppermute | solution.py:67
  77.1 13.4 %copy-start.1 = (f32[512,1024]{1,0:T(8,128)S(1)}, f32[512,1024]{1,0:T(8,128)}, u32[]{:S(2)}) copy-start(f32[512,1024]{1,0:T(8,128)} %copy-done) | copy-start | bytes 6291460
  82.1 26.2 %collective-permute-start.18 = (bf16[256,1024]{1,0:T(8,128)(2,1)}, bf16[256,1024]{1,0:T(8,128)(2,1)S(1)}, u32[]{:S(2)}, u32[]{:S(2)}) collective-permute-start(bf16[256,1024]{1,0:T(8,128)(2,1)} %get-tuple-element.18), channel_id=1, source_target_pairs={{0,16},{8,24},{16,0},{24,8},{1,17},{9,25},{17,1},{25,9},{2,18},{10... | collective-permute-start | bytes 1572872 | tf_op jit(solution)/shard_map/ppermute | solution.py:13
  82.1 13.3 %collective-permute-start.13 = (bf16[256,1024]{1,0:T(8,128)(2,1)}, bf16[256,1024]{1,0:T(8,128)(2,1)S(1)}, u32[]{:S(2)}, u32[]{:S(2)}) collective-permute-start(bf16[256,1024]{1,0:T(8,128)(2,1)} %collective-permute-done.12), channel_id=1, source_target_pairs={{0,1},{1,0},{2,3},{3,2},{4,5},{5,4},{6,7},{7,6},{8,9},{9,8},{10,11... | collective-permute-start | bytes 1572872 | tf_op jit(solution)/shard_map/ppermute | solution.py:13
  89.2 6.2 %copy-start.4 = (bf16[1,1024,1024]{2,1,0:T(8,128)(2,1)S(1)}, bf16[1,1024,1024]{2,1,0:T(8,128)(2,1)}, u32[]{:S(2)}) copy-start(bf16[1,1024,1024]{2,1,0:T(8,128)(2,1)} %param.3) | copy-start | bytes 6291460
  89.2 20.1 %collective-permute-start.4 = (bf16[256,512]{0,1:T(8,128)(2,1)S(1)}, bf16[256,512]{0,1:T(8,128)(2,1)S(1)}, u32[]{:S(2)}, u32[]{:S(2)}) collective-permute-start(bf16[256,512]{0,1:T(8,128)(2,1)S(1)} %divide_convert_fusion.3), channel_id=1, source_target_pairs={{0,4},{2,6},{4,0},{6,2},{1,5},{3,7},{5,1},{7,3},{8,12},{10,14},{12... | collective-permute-start | bytes 786440 | tf_op jit(solution)/shard_map/ppermute | solution.py:79
  92.0 18.5 %collective-permute-start.9 = (f32[256,512]{0,1:T(8,128)S(1)}, f32[256,512]{0,1:T(8,128)S(1)}, u32[]{:S(2)}, u32[]{:S(2)}) collective-permute-start(f32[256,512]{0,1:T(8,128)S(1)} %constant_dynamic-slice_fusion.2), channel_id=1, source_target_pairs={{0,4},{2,6},{4,0},{6,2},{1,5},{3,7},{5,1},{7,3},{8,12},{10,14},{12... | collective-permute-start | bytes 1572872 | tf_op jit(solution)/shard_map/ppermute | solution.py:67
  108.3 13.0 %collective-permute-start.19 = (bf16[256,1024]{1,0:T(8,128)(2,1)S(1)}, bf16[256,1024]{1,0:T(8,128)(2,1)S(1)}, u32[]{:S(2)}, u32[]{:S(2)}) collective-permute-start(bf16[256,1024]{1,0:T(8,128)(2,1)S(1)} %collective-permute-done.18), channel_id=1, source_target_pairs={{0,1},{1,0},{2,3},{3,2},{4,5},{5,4},{6,7},{7,6},{8,9},{9,8},{10,11... | collective-permute-start | bytes 1572872 | tf_op jit(solution)/shard_map/ppermute | solution.py:13
  109.4 11.9 %collective-permute-start.5 = (bf16[512,512]{0,1:T(8,128)(2,1)S(1)}, bf16[512,512]{0,1:T(8,128)(2,1)S(1)}, u32[]{:S(2)}, u32[]{:S(2)}) collective-permute-start(bf16[512,512]{0,1:T(8,128)(2,1)S(1)} %maximum_select_fusion.5), channel_id=1, source_target_pairs={{0,2},{2,0},{4,6},{6,4},{1,3},{3,1},{5,7},{7,5},{8,10},{10,8},{12,... | collective-permute-start | bytes 1572872 | tf_op jit(solution)/shard_map/ppermute | solution.py:79
  110.4 20.4 %collective-permute-start.14 = (f32[512,512]{0,1:T(8,128)S(1)}, f32[512,512]{0,1:T(8,128)S(1)}, u32[]{:S(2)}, u32[]{:S(2)}) collective-permute-start(f32[512,512]{0,1:T(8,128)S(1)} %dynamic-slice_bitcast_fusion.1), channel_id=1, source_target_pairs={{0,2},{2,0},{4,6},{6,4},{1,3},{3,1},{5,7},{7,5},{8,10},{10,8},{12,... | collective-permute-start | bytes 3145736 | tf_op jit(solution)/shard_map/ppermute | solution.py:67
  121.8 6.5 %collective-permute-start.10 = (bf16[256,512]{0,1:T(8,128)(2,1)S(1)}, bf16[256,512]{0,1:T(8,128)(2,1)S(1)}, u32[]{:S(2)}, u32[]{:S(2)}) collective-permute-start(bf16[256,512]{0,1:T(8,128)(2,1)S(1)} %divide_convert_fusion.2), channel_id=1, source_target_pairs={{0,4},{2,6},{4,0},{6,2},{1,5},{3,7},{5,1},{7,3},{8,12},{10,14},{12... | collective-permute-start | bytes 786440 | tf_op jit(solution)/shard_map/ppermute | solution.py:79
  124.2 21.7 %collective-permute-start.20 = (f32[512,512]{0,1:T(8,128)S(1)}, f32[512,512]{0,1:T(8,128)S(1)}, u32[]{:S(2)}, u32[]{:S(2)}) collective-permute-start(f32[512,512]{0,1:T(8,128)S(1)} %dynamic-slice_bitcast_fusion), channel_id=1, source_target_pairs={{0,2},{2,0},{4,6},{6,4},{1,3},{3,1},{5,7},{7,5},{8,10},{10,8},{12,... | collective-permute-start | bytes 3145736 | tf_op jit(solution)/shard_map/ppermute | solution.py:67
  128.4 3.9 %collective-permute-start.11 = (bf16[512,512]{0,1:T(8,128)(2,1)S(1)}, bf16[512,512]{0,1:T(8,128)(2,1)S(1)}, u32[]{:S(2)}, u32[]{:S(2)}) collective-permute-start(bf16[512,512]{0,1:T(8,128)(2,1)S(1)} %maximum_select_fusion.6), channel_id=1, source_target_pairs={{0,2},{2,0},{4,6},{6,4},{1,3},{3,1},{5,7},{7,5},{8,10},{10,8},{12,... | collective-permute-start | bytes 1572872 | tf_op jit(solution)/shard_map/ppermute | solution.py:79
  131.0 13.6 %collective-permute-start.15 = (f32[256,512]{0,1:T(8,128)S(1)}, f32[256,512]{0,1:T(8,128)S(1)}, u32[]{:S(2)}, u32[]{:S(2)}) collective-permute-start(f32[256,512]{0,1:T(8,128)S(1)} %constant_dynamic-slice_fusion.1), channel_id=1, source_target_pairs={{0,4},{2,6},{4,0},{6,2},{1,5},{3,7},{5,1},{7,3},{8,12},{10,14},{12... | collective-permute-start | bytes 1572872 | tf_op jit(solution)/shard_map/ppermute | solution.py:67
  144.9 7.1 %collective-permute-start.16 = (bf16[256,512]{0,1:T(8,128)(2,1)S(1)}, bf16[256,512]{0,1:T(8,128)(2,1)S(1)}, u32[]{:S(2)}, u32[]{:S(2)}) collective-permute-start(bf16[256,512]{0,1:T(8,128)(2,1)S(1)} %divide_convert_fusion.1), channel_id=1, source_target_pairs={{0,4},{2,6},{4,0},{6,2},{1,5},{3,7},{5,1},{7,3},{8,12},{10,14},{12... | collective-permute-start | bytes 786440 | tf_op jit(solution)/shard_map/ppermute | solution.py:79
  146.2 17.0 %collective-permute-start.21 = (f32[256,512]{0,1:T(8,128)S(1)}, f32[256,512]{0,1:T(8,128)S(1)}, u32[]{:S(2)}, u32[]{:S(2)}) collective-permute-start(f32[256,512]{0,1:T(8,128)S(1)} %constant_dynamic-slice_fusion), channel_id=1, source_target_pairs={{0,4},{2,6},{4,0},{6,2},{1,5},{3,7},{5,1},{7,3},{8,12},{10,14},{12... | collective-permute-start | bytes 1572872 | tf_op jit(solution)/shard_map/ppermute | solution.py:67
  152.1 11.2 %collective-permute-start.17 = (bf16[512,512]{0,1:T(8,128)(2,1)S(1)}, bf16[512,512]{0,1:T(8,128)(2,1)S(1)}, u32[]{:S(2)}, u32[]{:S(2)}) collective-permute-start(bf16[512,512]{0,1:T(8,128)(2,1)S(1)} %maximum_select_fusion.7), channel_id=1, source_target_pairs={{0,2},{2,0},{4,6},{6,4},{1,3},{3,1},{5,7},{7,5},{8,10},{10,8},{12,... | collective-permute-start | bytes 1572872 | tf_op jit(solution)/shard_map/ppermute | solution.py:79
  163.8 6.2 %collective-permute-start.22 = (bf16[256,512]{0,1:T(8,128)(2,1)S(1)}, bf16[256,512]{0,1:T(8,128)(2,1)S(1)}, u32[]{:S(2)}, u32[]{:S(2)}) collective-permute-start(bf16[256,512]{0,1:T(8,128)(2,1)S(1)} %divide_convert_fusion), channel_id=1, source_target_pairs={{0,4},{2,6},{4,0},{6,2},{1,5},{3,7},{5,1},{7,3},{8,12},{10,14},{12... | collective-permute-start | bytes 786440 | tf_op jit(solution)/shard_map/ppermute | solution.py:79
  170.1 5.5 %collective-permute-start.23 = (bf16[512,512]{0,1:T(8,128)(2,1)S(1)}, bf16[512,512]{0,1:T(8,128)(2,1)S(1)}, u32[]{:S(2)}, u32[]{:S(2)}) collective-permute-start(bf16[512,512]{0,1:T(8,128)(2,1)S(1)} %maximum_select_fusion.8), channel_id=1, source_target_pairs={{0,2},{2,0},{4,6},{6,4},{1,3},{3,1},{5,7},{7,5},{8,10},{10,8},{12,... | collective-permute-start | bytes 1572872 | tf_op jit(solution)/shard_map/ppermute | solution.py:79

commit v15 on v5

--- a/solution.py
+++ b/solution.py
@@ -133,7 +133,7 @@
             rows = aux_all_gather(amplitudes)
         else:
             rows = lax.all_gather(amplitudes, "aux", axis=0, tiled=True)
-        rows_done = rows
+        rows_done = amplitudes
         term = jnp.dot(rows, block, preferred_element_type=jnp.float32)
         total = term if total is None else total + term
     gamma_own = total

time: 176 us -> 180 us (1.023)
  waiting for transfers between devices: 109 us -> 124 us
  starting transfers between devices: 37.9 us -> 23.6 us
  other arithmetic: 4.46 us -> 6.64 us
    ppermute x8, waiting for transfers between devices: 8.3 us -> 26.4 us  [aux_all_gather(): other = lax.ppermute(x, 'aux', xor_pairs(count, step))]
    ppermute x8, starting transfers between devices: 22.9 us -> 7.47 us  [aux_all_gather(): other = lax.ppermute(x, 'aux', xor_pairs(count, step))]
    ppermute x8, waiting for transfers between devices: 13.9 us -> 10.9 us  [aux_reduce_scatter(): x = keep + lax.ppermute(send, 'aux', xor_pairs(count, step))]
    select_n x7 -> x4, other arithmetic: 1.4 us -> 3.58 us  [aux_all_gather(): jnp.where(bit == 0, jnp.concatenate([x, other]), jnp.concatenate([other,...]
  transfers between devices with their start and end apart: 24 -> 24, of which waited for: 12 -> 11; matrix products, arithmetic and copies ran while one was open for 11% -> 13% of each run, Pallas kernels for 0% -> 0%
where the time goes in v15:
time: 180 us; the launch traced here: 179 us
  waiting for transfers between devices  124 us (69%)
  starting transfers between devices  23.6 us (13%)
  matrix products  14.3 us (8%)
  local copies, waits for them, and re-layouts  9.35 us (5%)
  other arithmetic  6.64 us (4%)
    ppermute x8, waiting for transfers between devices, shifted_2(): lax.ppermute(value, axis, [(i, (i + by) % count) for i in range(count)])  86.6 us
    ppermute x8, waiting for transfers between devices, aux_all_gather(): other = lax.ppermute(x, 'aux', xor_pairs(count, step))  26.4 us
    ppermute x8, waiting for transfers between devices, aux_reduce_scatter(): x = keep + lax.ppermute(send, 'aux', xor_pairs(count, step))  10.9 us
    ppermute x8, starting transfers between devices, aux_reduce_scatter(): x = keep + lax.ppermute(send, 'aux', xor_pairs(count, step))  9.85 us
    ppermute x8, starting transfers between devices, aux_all_gather(): other = lax.ppermute(x, 'aux', xor_pairs(count, step))  7.47 us
    dot_general x4, matrix products, paired_plan(): term = jnp.dot(rows, block, preferred_element_type=jnp.float32)  7.16 us
    dot_general x4, matrix products, paired_plan(): jnp.einsum('aq,bq->ab', own, block, preferred_element_type=jnp.float32)  7.11 us
    ppermute x8, starting transfers between devices, shifted_2(): lax.ppermute(value, axis, [(i, (i + by) % count) for i in range(count)])  6.26 us
  transfers between devices with their start and end apart: 24, of which 11 were waited for; matrix products, arithmetic and copies ran while one was open for 13% of the time, Pallas kernels for 0%

profile of v15, /device:TPU:1, one launch (start us, length us, event | category | flops | bytes accessed | tf_op | source)
XLA Modules:
  0.0 179.3 jit_solution(15887915577557572227)
XLA Ops:
  0.0 2.8 %slice_bitcast_fusion = (bf16[256,1024]{1,0:T(8,128)(2,1)}, bf16[256,1024]{1,0:T(8,128)(2,1)S(1)}, bf16[256,1024]{1,0:T(8,128)(2,1)S(1)}, bf16[256,1024]{1,0:T(8,128)(2,1)}) fusion(bf16[1,1024,1024]{2,1,0:T(8,128)(2,1)} %param.3), kind=kLoop, calls=%fused_computation.56 | loop fusion | bytes 4194304 | tf_op jit(solution)/shard_map/slice | solution.py:105
  2.8 3.1 %collective-permute-start = (bf16[256,1024]{1,0:T(8,128)(2,1)S(1)}, bf16[256,1024]{1,0:T(8,128)(2,1)S(1)}, u32[]{:S(2)}, u32[]{:S(2)}) collective-permute-start(bf16[256,1024]{1,0:T(8,128)(2,1)S(1)} %get-tuple-element.19), channel_id=1, source_target_pairs={{0,16},{8,24},{16,0},{24,8},{1,17},{9,25},{17,1},{25,9},{2,18},{10... | collective-permute-start | bytes 1572872 | tf_op jit(solution)/shard_map/ppermute | solution.py:13
  5.9 22.9 %collective-permute-done = bf16[256,1024]{1,0:T(8,128)(2,1)S(1)} collective-permute-done((bf16[256,1024]{1,0:T(8,128)(2,1)S(1)}, bf16[256,1024]{1,0:T(8,128)(2,1)S(1)}, u32[]{:S(2)}, u32[]{:S(2)}) %collective-permute-start) | collective-permute-done | bytes 524320 | tf_op jit(solution)/shard_map/ppermute | solution.py:13
  31.8 21.4 %collective-permute-done.6 = bf16[256,1024]{1,0:T(8,128)(2,1)} collective-permute-done((bf16[256,1024]{1,0:T(8,128)(2,1)S(1)}, bf16[256,1024]{1,0:T(8,128)(2,1)}, u32[]{:S(2)}, u32[]{:S(2)}) %collective-permute-start.6) | collective-permute-done | bytes 524320 | tf_op jit(solution)/shard_map/ppermute | solution.py:13
  54.0 3.3 %fusion.7 = f32[512,1024]{1,0:T(8,128)S(1)} fusion(bf16[512,1024]{1,0:T(8,128)(2,1)S(1)} %constant_dynamic-update-slice_fusion, bf16[1,1024,1024]{2,1,0:T(8,128)(2,1)} %param.3), kind=kOutput, calls=%fused_computation.8 | convolution fusion | flops 1073741824 | bytes 5242880 | tf_op jit(solution)/shard_map/aq,bq->ab/dot_general | solution.py:120
  57.4 2.8 %collective-permute-start.2 = (f32[512,512]{0,1:T(8,128)S(1)}, f32[512,512]{0,1:T(8,128)}, u32[]{:S(2)}, u32[]{:S(2)}) collective-permute-start(f32[512,512]{0,1:T(8,128)S(1)} %dynamic-slice_bitcast_fusion.3), channel_id=1, source_target_pairs={{0,2},{2,0},{4,6},{6,4},{1,3},{3,1},{5,7},{7,5},{8,10},{10,8},{12,... | collective-permute-start | bytes 3145736 | tf_op jit(solution)/shard_map/ppermute | solution.py:68
  60.2 1.2 constant_dynamic-update-slice_fusion.3
  61.4 17.9 %collective-permute-done.12 = bf16[256,1024]{1,0:T(8,128)(2,1)} collective-permute-done((bf16[256,1024]{1,0:T(8,128)(2,1)}, bf16[256,1024]{1,0:T(8,128)(2,1)}, u32[]{:S(2)}, u32[]{:S(2)}) %collective-permute-start.12) | collective-permute-done | bytes 524320 | tf_op jit(solution)/shard_map/ppermute | solution.py:13
  80.4 1.3 fusion.5
  84.4 1.4 bitcast_add_fusion.3
  85.9 1.3 collective-permute-start.3
  87.2 9.1 %collective-permute-done.13 = bf16[256,1024]{1,0:T(8,128)(2,1)S(1)} collective-permute-done((bf16[256,1024]{1,0:T(8,128)(2,1)}, bf16[256,1024]{1,0:T(8,128)(2,1)S(1)}, u32[]{:S(2)}, u32[]{:S(2)}) %collective-permute-start.13) | collective-permute-done | bytes 524320 | tf_op jit(solution)/shard_map/ppermute | solution.py:13
  97.3 1.3 fusion.3
  99.6 4.6 %collective-permute-done.18 = bf16[256,1024]{1,0:T(8,128)(2,1)S(1)} collective-permute-done((bf16[256,1024]{1,0:T(8,128)(2,1)}, bf16[256,1024]{1,0:T(8,128)(2,1)S(1)}, u32[]{:S(2)}, u32[]{:S(2)}) %collective-permute-start.18) | collective-permute-done | bytes 524320 | tf_op jit(solution)/shard_map/ppermute | solution.py:13
  105.3 1.3 collective-permute-start.9
  106.5 10.7 %collective-permute-done.19 = bf16[256,1024]{1,0:T(8,128)(2,1)S(1)} collective-permute-done((bf16[256,1024]{1,0:T(8,128)(2,1)S(1)}, bf16[256,1024]{1,0:T(8,128)(2,1)S(1)}, u32[]{:S(2)}, u32[]{:S(2)}) %collective-permute-start.19) | collective-permute-done | bytes 524320 | tf_op jit(solution)/shard_map/ppermute | solution.py:13
  117.3 1.3 fusion.1
  118.7 1.4 collective-permute-start.20
  123.1 10.9 %collective-permute-done.15 = f32[256,512]{0,1:T(8,128)S(1)} collective-permute-done((f32[256,512]{0,1:T(8,128)S(1)}, f32[256,512]{0,1:T(8,128)S(1)}, u32[]{:S(2)}, u32[]{:S(2)}) %collective-permute-start.15) | collective-permute-done | bytes 524320 | tf_op jit(solution)/shard_map/ppermute | solution.py:68
  136.8 2.9 %collective-permute-done.4 = bf16[256,512]{0,1:T(8,128)(2,1)} collective-permute-done((bf16[256,512]{0,1:T(8,128)(2,1)S(1)}, bf16[256,512]{0,1:T(8,128)(2,1)}, u32[]{:S(2)}, u32[]{:S(2)}) %collective-permute-start.4) | collective-permute-done | bytes 262176 | tf_op jit(solution)/shard_map/ppermute | solution.py:80
  139.7 1.2 maximum_select_fusion.10
  140.8 1.3 collective-permute-start.5
  142.1 3.2 %collective-permute-done.10 = bf16[256,512]{0,1:T(8,128)(2,1)} collective-permute-done((bf16[256,512]{0,1:T(8,128)(2,1)S(1)}, bf16[256,512]{0,1:T(8,128)(2,1)}, u32[]{:S(2)}, u32[]{:S(2)}) %collective-permute-start.10) | collective-permute-done | bytes 262176 | tf_op jit(solution)/shard_map/ppermute | solution.py:80
  145.3 1.2 maximum_select_fusion.11
  146.4 1.3 collective-permute-start.11
  147.7 14.4 %collective-permute-done.16 = bf16[256,512]{0,1:T(8,128)(2,1)} collective-permute-done((bf16[256,512]{0,1:T(8,128)(2,1)S(1)}, bf16[256,512]{0,1:T(8,128)(2,1)}, u32[]{:S(2)}, u32[]{:S(2)}) %collective-permute-start.16) | collective-permute-done | bytes 262176 | tf_op jit(solution)/shard_map/ppermute | solution.py:80
  162.1 1.2 maximum_select_fusion.12
  165.2 1.3 fusion.9
  166.5 5.9 %collective-permute-done.22 = bf16[256,512]{0,1:T(8,128)(2,1)S(1)} collective-permute-done((bf16[256,512]{0,1:T(8,128)(2,1)S(1)}, bf16[256,512]{0,1:T(8,128)(2,1)S(1)}, u32[]{:S(2)}, u32[]{:S(2)}) %collective-permute-start.22) | collective-permute-done | bytes 262176 | tf_op jit(solution)/shard_map/ppermute | solution.py:80
  173.4 1.3 fusion.15
  174.7 1.5 fusion.21
  176.2 3.1 %fusion = bf16[1,1024,1024]{2,1,0:T(8,128)(2,1)} fusion(f32[1024,1024]{1,0:T(8,128)S(1)} %fusion.21, f32[1024,1024]{1,0:T(8,128)S(1)} %fusion.9, f32[1024,1024]{1,0:T(8,128)S(1)} %fusion.15, bf16[512,1024]{1,0:T(8,128)(2,1)S(1)} %constant_dynamic-update-slice_fusion.6, bf16[512,512]{0,1:T(8,128)(2,1)S(1)} %collective-permute-done.23, ...), kind=kOutput, calls=%fused_computation.1 | convolution fusion | flops 1083703296 | bytes 16777216 | tf_op jit(solution)/shard_map/dot_general | solution.py:137
  (80 shorter events, 18.3 us)
Async XLA Ops:
  0.0 29.8 %copy-start.8 = (f32[4]{0:T(128)S(1)}, f32[4]{0:T(128)}, u32[]{:S(2)}) copy-start(f32[4]{0:T(128)} %param.4) | copy-start | bytes 52
  0.0 31.7 %copy-start.7 = (f32[2048]{0:T(1024)S(1)}, f32[2048]{0:T(1024)}, u32[]{:S(2)}) copy-start(f32[2048]{0:T(1024)} %param.5) | copy-start | bytes 24580
  2.8 26.0 %collective-permute-start = (bf16[256,1024]{1,0:T(8,128)(2,1)S(1)}, bf16[256,1024]{1,0:T(8,128)(2,1)S(1)}, u32[]{:S(2)}, u32[]{:S(2)}) collective-permute-start(bf16[256,1024]{1,0:T(8,128)(2,1)S(1)} %get-tuple-element.19), channel_id=1, source_target_pairs={{0,16},{8,24},{16,0},{24,8},{1,17},{9,25},{17,1},{25,9},{2,18},{10... | collective-permute-start | bytes 1572872 | tf_op jit(solution)/shard_map/ppermute | solution.py:13
  28.8 24.4 %collective-permute-start.6 = (bf16[256,1024]{1,0:T(8,128)(2,1)S(1)}, bf16[256,1024]{1,0:T(8,128)(2,1)}, u32[]{:S(2)}, u32[]{:S(2)}) collective-permute-start(bf16[256,1024]{1,0:T(8,128)(2,1)S(1)} %get-tuple-element.11), channel_id=1, source_target_pairs={{0,16},{8,24},{16,0},{24,8},{1,17},{9,25},{17,1},{25,9},{2,18},{10... | collective-permute-start | bytes 1572872 | tf_op jit(solution)/shard_map/ppermute | solution.py:13
  28.8 25.1 %collective-permute-start.1 = (bf16[256,1024]{1,0:T(8,128)(2,1)S(1)}, bf16[256,1024]{1,0:T(8,128)(2,1)S(1)}, u32[]{:S(2)}, u32[]{:S(2)}) collective-permute-start(bf16[256,1024]{1,0:T(8,128)(2,1)S(1)} %collective-permute-done), channel_id=1, source_target_pairs={{0,1},{1,0},{2,3},{3,2},{4,5},{5,4},{6,7},{7,6},{8,9},{9,8},{10,11... | collective-permute-start | bytes 1572872 | tf_op jit(solution)/shard_map/ppermute | solution.py:13
  53.2 26.1 %collective-permute-start.12 = (bf16[256,1024]{1,0:T(8,128)(2,1)}, bf16[256,1024]{1,0:T(8,128)(2,1)}, u32[]{:S(2)}, u32[]{:S(2)}) collective-permute-start(bf16[256,1024]{1,0:T(8,128)(2,1)} %get-tuple-element.13), channel_id=1, source_target_pairs={{0,16},{8,24},{16,0},{24,8},{1,17},{9,25},{17,1},{25,9},{2,18},{10... | collective-permute-start | bytes 1572872 | tf_op jit(solution)/shard_map/ppermute | solution.py:13
  53.2 26.1 %collective-permute-start.7 = (bf16[256,1024]{1,0:T(8,128)(2,1)}, bf16[256,1024]{1,0:T(8,128)(2,1)}, u32[]{:S(2)}, u32[]{:S(2)}) collective-permute-start(bf16[256,1024]{1,0:T(8,128)(2,1)} %collective-permute-done.6), channel_id=1, source_target_pairs={{0,1},{1,0},{2,3},{3,2},{4,5},{5,4},{6,7},{7,6},{8,9},{9,8},{10,11... | collective-permute-start | bytes 1572872 | tf_op jit(solution)/shard_map/ppermute | solution.py:13
  54.0 3.3 %copy-start.1 = (bf16[512,1024]{1,0:T(8,128)(2,1)}, bf16[512,1024]{1,0:T(8,128)(2,1)S(1)}, u32[]{:S(2)}) copy-start(bf16[512,1024]{1,0:T(8,128)(2,1)S(1)} %constant_dynamic-update-slice_fusion) | copy-start | bytes 3145732
  57.4 27.1 %collective-permute-start.2 = (f32[512,512]{0,1:T(8,128)S(1)}, f32[512,512]{0,1:T(8,128)}, u32[]{:S(2)}, u32[]{:S(2)}) collective-permute-start(f32[512,512]{0,1:T(8,128)S(1)} %dynamic-slice_bitcast_fusion.3), channel_id=1, source_target_pairs={{0,2},{2,0},{4,6},{6,4},{1,3},{3,1},{5,7},{7,5},{8,10},{10,8},{12,... | collective-permute-start | bytes 3145736 | tf_op jit(solution)/shard_map/ppermute | solution.py:68
  60.1 20.3 %copy-start = (bf16[1,1024,1024]{2,1,0:T(8,128)(2,1)S(1)}, bf16[1,1024,1024]{2,1,0:T(8,128)(2,1)}, u32[]{:S(2)}) copy-start(bf16[1,1024,1024]{2,1,0:T(8,128)(2,1)} %param.3) | copy-start | bytes 6291460
  79.3 24.9 %collective-permute-start.18 = (bf16[256,1024]{1,0:T(8,128)(2,1)}, bf16[256,1024]{1,0:T(8,128)(2,1)S(1)}, u32[]{:S(2)}, u32[]{:S(2)}) collective-permute-start(bf16[256,1024]{1,0:T(8,128)(2,1)} %get-tuple-element.15), channel_id=1, source_target_pairs={{0,16},{8,24},{16,0},{24,8},{1,17},{9,25},{17,1},{25,9},{2,18},{10... | collective-permute-start | bytes 1572872 | tf_op jit(solution)/shard_map/ppermute | solution.py:13
  80.4 1.3 copy-start.5
  81.8 23.2 %collective-permute-start.8 = (f32[512,512]{0,1:T(8,128)S(1)}, f32[512,512]{0,1:T(8,128)S(1)}, u32[]{:S(2)}, u32[]{:S(2)}) collective-permute-start(f32[512,512]{0,1:T(8,128)S(1)} %dynamic-slice_bitcast_fusion.2), channel_id=1, source_target_pairs={{0,2},{2,0},{4,6},{6,4},{1,3},{3,1},{5,7},{7,5},{8,10},{10,8},{12,... | collective-permute-start | bytes 3145736 | tf_op jit(solution)/shard_map/ppermute | solution.py:68
  82.6 13.7 %collective-permute-start.13 = (bf16[256,1024]{1,0:T(8,128)(2,1)}, bf16[256,1024]{1,0:T(8,128)(2,1)S(1)}, u32[]{:S(2)}, u32[]{:S(2)}) collective-permute-start(bf16[256,1024]{1,0:T(8,128)(2,1)} %collective-permute-done.12), channel_id=1, source_target_pairs={{0,1},{1,0},{2,3},{3,2},{4,5},{5,4},{6,7},{7,6},{8,9},{9,8},{10,11... | collective-permute-start | bytes 1572872 | tf_op jit(solution)/shard_map/ppermute | solution.py:13
  85.9 35.2 %collective-permute-start.3 = (f32[256,512]{0,1:T(8,128)S(1)}, f32[256,512]{0,1:T(8,128)S(1)}, u32[]{:S(2)}, u32[]{:S(2)}) collective-permute-start(f32[256,512]{0,1:T(8,128)S(1)} %constant_dynamic-slice_fusion.3), channel_id=1, source_target_pairs={{0,4},{2,6},{4,0},{6,2},{1,5},{3,7},{5,1},{7,3},{8,12},{10,14},{12... | collective-permute-start | bytes 1572872 | tf_op jit(solution)/shard_map/ppermute | solution.py:68
  98.7 21.4 %collective-permute-start.14 = (f32[512,512]{0,1:T(8,128)S(1)}, f32[512,512]{0,1:T(8,128)S(1)}, u32[]{:S(2)}, u32[]{:S(2)}) collective-permute-start(f32[512,512]{0,1:T(8,128)S(1)} %dynamic-slice_bitcast_fusion.1), channel_id=1, source_target_pairs={{0,2},{2,0},{4,6},{6,4},{1,3},{3,1},{5,7},{7,5},{8,10},{10,8},{12,... | collective-permute-start | bytes 3145736 | tf_op jit(solution)/shard_map/ppermute | solution.py:68
  104.3 13.0 %collective-permute-start.19 = (bf16[256,1024]{1,0:T(8,128)(2,1)S(1)}, bf16[256,1024]{1,0:T(8,128)(2,1)S(1)}, u32[]{:S(2)}, u32[]{:S(2)}) collective-permute-start(bf16[256,1024]{1,0:T(8,128)(2,1)S(1)} %collective-permute-done.18), channel_id=1, source_target_pairs={{0,1},{1,0},{2,3},{3,2},{4,5},{5,4},{6,7},{7,6},{8,9},{9,8},{10,11... | collective-permute-start | bytes 1572872 | tf_op jit(solution)/shard_map/ppermute | solution.py:13
  105.3 16.8 %collective-permute-start.9 = (f32[256,512]{0,1:T(8,128)S(1)}, f32[256,512]{0,1:T(8,128)S(1)}, u32[]{:S(2)}, u32[]{:S(2)}) collective-permute-start(f32[256,512]{0,1:T(8,128)S(1)} %constant_dynamic-slice_fusion.2), channel_id=1, source_target_pairs={{0,4},{2,6},{4,0},{6,2},{1,5},{3,7},{5,1},{7,3},{8,12},{10,14},{12... | collective-permute-start | bytes 1572872 | tf_op jit(solution)/shard_map/ppermute | solution.py:68
  118.7 15.4 %collective-permute-start.20 = (f32[512,512]{0,1:T(8,128)S(1)}, f32[512,512]{0,1:T(8,128)S(1)}, u32[]{:S(2)}, u32[]{:S(2)}) collective-permute-start(f32[512,512]{0,1:T(8,128)S(1)} %dynamic-slice_bitcast_fusion), channel_id=1, source_target_pairs={{0,2},{2,0},{4,6},{6,4},{1,3},{3,1},{5,7},{7,5},{8,10},{10,8},{12,... | collective-permute-start | bytes 3145736 | tf_op jit(solution)/shard_map/ppermute | solution.py:68
  120.3 13.6 %collective-permute-start.15 = (f32[256,512]{0,1:T(8,128)S(1)}, f32[256,512]{0,1:T(8,128)S(1)}, u32[]{:S(2)}, u32[]{:S(2)}) collective-permute-start(f32[256,512]{0,1:T(8,128)S(1)} %constant_dynamic-slice_fusion.1), channel_id=1, source_target_pairs={{0,4},{2,6},{4,0},{6,2},{1,5},{3,7},{5,1},{7,3},{8,12},{10,14},{12... | collective-permute-start | bytes 1572872 | tf_op jit(solution)/shard_map/ppermute | solution.py:68
  121.2 18.4 %collective-permute-start.4 = (bf16[256,512]{0,1:T(8,128)(2,1)S(1)}, bf16[256,512]{0,1:T(8,128)(2,1)}, u32[]{:S(2)}, u32[]{:S(2)}) collective-permute-start(bf16[256,512]{0,1:T(8,128)(2,1)S(1)} %divide_convert_fusion.3), channel_id=1, source_target_pairs={{0,4},{2,6},{4,0},{6,2},{1,5},{3,7},{5,1},{7,3},{8,12},{10,14},{12... | collective-permute-start | bytes 786440 | tf_op jit(solution)/shard_map/ppermute | solution.py:80
  122.4 22.9 %collective-permute-start.10 = (bf16[256,512]{0,1:T(8,128)(2,1)S(1)}, bf16[256,512]{0,1:T(8,128)(2,1)}, u32[]{:S(2)}, u32[]{:S(2)}) collective-permute-start(bf16[256,512]{0,1:T(8,128)(2,1)S(1)} %divide_convert_fusion.2), channel_id=1, source_target_pairs={{0,4},{2,6},{4,0},{6,2},{1,5},{3,7},{5,1},{7,3},{8,12},{10,14},{12... | collective-permute-start | bytes 786440 | tf_op jit(solution)/shard_map/ppermute | solution.py:80
  135.1 29.0 %collective-permute-start.21 = (f32[256,512]{0,1:T(8,128)}, f32[256,512]{0,1:T(8,128)S(1)}, u32[]{:S(2)}, u32[]{:S(2)}) collective-permute-start(f32[256,512]{0,1:T(8,128)} %constant_dynamic-slice_fusion), channel_id=1, source_target_pairs={{0,4},{2,6},{4,0},{6,2},{1,5},{3,7},{5,1},{7,3},{8,12},{10,14},{12... | collective-permute-start | bytes 1572872 | tf_op jit(solution)/shard_map/ppermute | solution.py:68
  136.0 26.2 %collective-permute-start.16 = (bf16[256,512]{0,1:T(8,128)(2,1)S(1)}, bf16[256,512]{0,1:T(8,128)(2,1)}, u32[]{:S(2)}, u32[]{:S(2)}) collective-permute-start(bf16[256,512]{0,1:T(8,128)(2,1)S(1)} %divide_convert_fusion.1), channel_id=1, source_target_pairs={{0,4},{2,6},{4,0},{6,2},{1,5},{3,7},{5,1},{7,3},{8,12},{10,14},{12... | collective-permute-start | bytes 786440 | tf_op jit(solution)/shard_map/ppermute | solution.py:80
  140.8 24.4 %copy-start.2 = (bf16[512,1024]{1,0:T(8,128)(2,1)S(1)}, bf16[512,1024]{1,0:T(8,128)(2,1)}, u32[]{:S(2)}) copy-start(bf16[512,1024]{1,0:T(8,128)(2,1)} %copy-done.1) | copy-start | bytes 3145732
  140.8 24.4 %collective-permute-start.5 = (bf16[512,512]{0,1:T(8,128)(2,1)S(1)}, bf16[512,512]{0,1:T(8,128)(2,1)S(1)}, u32[]{:S(2)}, u32[]{:S(2)}) collective-permute-start(bf16[512,512]{0,1:T(8,128)(2,1)S(1)} %maximum_select_fusion.10), channel_id=1, source_target_pairs={{0,2},{2,0},{4,6},{6,4},{1,3},{3,1},{5,7},{7,5},{8,10},{10,8},{12,... | collective-permute-start | bytes 1572872 | tf_op jit(solution)/shard_map/ppermute | solution.py:80
  146.4 27.0 %collective-permute-start.11 = (bf16[512,512]{0,1:T(8,128)(2,1)S(1)}, bf16[512,512]{0,1:T(8,128)(2,1)S(1)}, u32[]{:S(2)}, u32[]{:S(2)}) collective-permute-start(bf16[512,512]{0,1:T(8,128)(2,1)S(1)} %maximum_select_fusion.11), channel_id=1, source_target_pairs={{0,2},{2,0},{4,6},{6,4},{1,3},{3,1},{5,7},{7,5},{8,10},{10,8},{12,... | collective-permute-start | bytes 1572872 | tf_op jit(solution)/shard_map/ppermute | solution.py:80
  163.3 11.4 %collective-permute-start.17 = (bf16[512,512]{0,1:T(8,128)(2,1)S(1)}, bf16[512,512]{0,1:T(8,128)(2,1)S(1)}, u32[]{:S(2)}, u32[]{:S(2)}) collective-permute-start(bf16[512,512]{0,1:T(8,128)(2,1)S(1)} %maximum_select_fusion.12), channel_id=1, source_target_pairs={{0,2},{2,0},{4,6},{6,4},{1,3},{3,1},{5,7},{7,5},{8,10},{10,8},{12,... | collective-permute-start | bytes 1572872 | tf_op jit(solution)/shard_map/ppermute | solution.py:80
  164.4 9.0 %copy-start.6 = (bf16[512,1024]{1,0:T(8,128)(2,1)S(1)}, bf16[512,1024]{1,0:T(8,128)(2,1)}, u32[]{:S(2)}) copy-start(bf16[512,1024]{1,0:T(8,128)(2,1)} %copy-done.5) | copy-start | bytes 3145732
  164.4 8.0 %collective-permute-start.22 = (bf16[256,512]{0,1:T(8,128)(2,1)S(1)}, bf16[256,512]{0,1:T(8,128)(2,1)S(1)}, u32[]{:S(2)}, u32[]{:S(2)}) collective-permute-start(bf16[256,512]{0,1:T(8,128)(2,1)S(1)} %divide_convert_fusion), channel_id=1, source_target_pairs={{0,4},{2,6},{4,0},{6,2},{1,5},{3,7},{5,1},{7,3},{8,12},{10,14},{12... | collective-permute-start | bytes 786440 | tf_op jit(solution)/shard_map/ppermute | solution.py:80
  172.5 2.2 %copy-start.4 = (bf16[512,1024]{1,0:T(8,128)(2,1)S(1)}, bf16[512,1024]{1,0:T(8,128)(2,1)}, u32[]{:S(2)}) copy-start(bf16[512,1024]{1,0:T(8,128)(2,1)} %copy-done.3) | copy-start | bytes 3145732
  172.5 3.7 %collective-permute-start.23 = (bf16[512,512]{0,1:T(8,128)(2,1)S(1)}, bf16[512,512]{0,1:T(8,128)(2,1)S(1)}, u32[]{:S(2)}, u32[]{:S(2)}) collective-permute-start(bf16[512,512]{0,1:T(8,128)(2,1)S(1)} %maximum_select_fusion.13), channel_id=1, source_target_pairs={{0,2},{2,0},{4,6},{6,4},{1,3},{3,1},{5,7},{7,5},{8,10},{10,8},{12,... | collective-permute-start | bytes 1572872 | tf_op jit(solution)/shard_map/ppermute | solution.py:80
  (1 other events, 1.0 us)

commit v16 on v11

--- a/solution.py
+++ b/solution.py
@@ -3,7 +3,7 @@
 from jax import lax
 from jax.sharding import PartitionSpec as P
 
-WIDTHS = (128, 384, 384, 128)
+WIDTHS = (128, 128, 256, 256, 256)
 AUX_BY_PERMUTE = True
 NARROW_FAR = False
 

time: 222 us -> 175 us (0.79)
  waiting for transfers between devices: 151 us -> 102 us
  starting transfers between devices: 31.4 us -> 44.2 us
  local copies, waits for them, and re-layouts: 16.3 us -> 8.75 us
  other arithmetic: 9.55 us -> 5.46 us
    ppermute x8 -> x10, waiting for transfers between devices: 34.2 us -> 13.4 us  [aux_all_gather(): other = lax.ppermute(x, 'aux', xor_pairs(count, step))]
    ppermute x8 -> x10, waiting for transfers between devices: 97.2 us -> 77.7 us  [shifted_2(): lax.ppermute(value, axis, [(i, (i + by) % count) for i in range(count)])]
    ppermute x8 -> x10, starting transfers between devices: 12.7 us -> 24.5 us  [aux_all_gather(): other = lax.ppermute(x, 'aux', xor_pairs(count, step))]
    ppermute x8 -> x10, waiting for transfers between devices: 19.2 us -> 11.3 us  [aux_reduce_scatter(): x = keep + lax.ppermute(send, 'aux', xor_pairs(count, step))]
    add x7 -> x9, other arithmetic: 6.13 us -> 2.18 us  [aux_reduce_scatter(): x = keep + lax.ppermute(send, 'aux', xor_pairs(count, step))]
    unnamed x34 -> x23, local copies, waits for them, and re-layouts: 5.41 us -> 2.04 us
    dynamic_slice x8 -> x10, local copies, waits for them, and re-layouts: 4.69 us -> 1.35 us  [aux_reduce_scatter(): send = lax.dynamic_slice_in_dim(x, (1 - bit) * half, half, 0)]
    ppermute x8 -> x10, starting transfers between devices: 12.8 us -> 13.4 us  [aux_reduce_scatter(): x = keep + lax.ppermute(send, 'aux', xor_pairs(count, step))]
  transfers between devices with their start and end apart: 24 -> 30, of which waited for: 13 -> 15; matrix products, arithmetic and copies ran while one was open for 13% -> 12% of each run, Pallas kernels for 0% -> 0%
where the time goes in v16:
time: 175 us
  waiting for transfers between devices  102 us (58%)
  starting transfers between devices  44.2 us (25%)
  matrix products  12.7 us (7%)
  local copies, waits for them, and re-layouts  8.75 us (5%)
  other arithmetic  5.46 us (3%)
    ppermute x10, waiting for transfers between devices, shifted_2(): lax.ppermute(value, axis, [(i, (i + by) % count) for i in range(count)])  77.7 us
    ppermute x10, starting transfers between devices, aux_all_gather(): other = lax.ppermute(x, 'aux', xor_pairs(count, step))  24.5 us
    ppermute x10, waiting for transfers between devices, aux_all_gather(): other = lax.ppermute(x, 'aux', xor_pairs(count, step))  13.4 us
    ppermute x10, starting transfers between devices, aux_reduce_scatter(): x = keep + lax.ppermute(send, 'aux', xor_pairs(count, step))  13.4 us
    ppermute x10, waiting for transfers between devices, aux_reduce_scatter(): x = keep + lax.ppermute(send, 'aux', xor_pairs(count, step))  11.3 us
    dot_general x5, matrix products, paired_plan(): term = jnp.dot(rows, block, preferred_element_type=jnp.float32)  7.34 us
    ppermute x10, starting transfers between devices, shifted_2(): lax.ppermute(value, axis, [(i, (i + by) % count) for i in range(count)])  6.39 us
    dot_general x5, matrix products, paired_plan(): jnp.einsum('aq,bq->ab', own, block, preferred_element_type=jnp.float32)  5.34 us
  transfers between devices with their start and end apart: 30, of which 15 were waited for; matrix products, arithmetic and copies ran while one was open for 12% of the time, Pallas kernels for 0%

profile of v16, /device:TPU:1, one launch (start us, length us, event | category | flops | bytes accessed | tf_op | source)
XLA Modules:
  0.0 175.1 jit_solution(9562300371208212059)
XLA Ops:
  1.1 3.2 %collective-permute-start = (bf16[128,1024]{1,0:T(8,128)(2,1)S(1)}, bf16[128,1024]{1,0:T(8,128)(2,1)S(1)}, u32[]{:S(2)}, u32[]{:S(2)}) collective-permute-start(bf16[128,1024]{1,0:T(8,128)(2,1)S(1)} %get-tuple-element.24), channel_id=1, source_target_pairs={{0,16},{8,24},{16,0},{24,8},{1,17},{9,25},{17,1},{25,9},{2,18},{10... | collective-permute-start | bytes 786440 | tf_op jit(solution)/shard_map/ppermute | solution.py:13
  5.1 2.7 %slice_bitcast_fusion = (bf16[256,1024]{1,0:T(8,128)(2,1)}, bf16[256,1024]{1,0:T(8,128)(2,1)}, bf16[256,1024]{1,0:T(8,128)(2,1)}) fusion(bf16[1,1024,1024]{2,1,0:T(8,128)(2,1)} %param.3), kind=kLoop, calls=%fused_computation.37 | loop fusion | bytes 3145728 | tf_op jit(solution)/shard_map/slice | solution.py:106
  7.8 8.1 %collective-permute-done = bf16[128,1024]{1,0:T(8,128)(2,1)S(1)} collective-permute-done((bf16[128,1024]{1,0:T(8,128)(2,1)S(1)}, bf16[128,1024]{1,0:T(8,128)(2,1)S(1)}, u32[]{:S(2)}, u32[]{:S(2)}) %collective-permute-start) | collective-permute-done | bytes 262176 | tf_op jit(solution)/shard_map/ppermute | solution.py:13
  19.0 10.1 %collective-permute-done.6 = bf16[128,1024]{1,0:T(8,128)(2,1)S(1)} collective-permute-done((bf16[128,1024]{1,0:T(8,128)(2,1)S(1)}, bf16[128,1024]{1,0:T(8,128)(2,1)S(1)}, u32[]{:S(2)}, u32[]{:S(2)}) %collective-permute-start.6) | collective-permute-done | bytes 262176 | tf_op jit(solution)/shard_map/ppermute | solution.py:13
  30.6 2.8 %collective-permute-start.2 = (f32[512,256]{0,1:T(8,128)S(1)}, f32[512,256]{0,1:T(8,128)S(1)}, u32[]{:S(2)}, u32[]{:S(2)}) collective-permute-start(f32[512,256]{0,1:T(8,128)S(1)} %dynamic-slice_bitcast_fusion.4), channel_id=1, source_target_pairs={{0,2},{2,0},{4,6},{6,4},{1,3},{3,1},{5,7},{7,5},{8,10},{10,8},{12,... | collective-permute-start | bytes 1572872 | tf_op jit(solution)/shard_map/ppermute | solution.py:68
  33.4 1.3 collective-permute-done.7
  36.4 3.1 %collective-permute-start.8 = (f32[512,256]{0,1:T(8,128)}, f32[512,256]{0,1:T(8,128)}, u32[]{:S(2)}, u32[]{:S(2)}) collective-permute-start(f32[512,256]{0,1:T(8,128)} %dynamic-slice_bitcast_fusion.3), channel_id=1, source_target_pairs={{0,2},{2,0},{4,6},{6,4},{1,3},{3,1},{5,7},{7,5},{8,10},{10,8},{12,... | collective-permute-start | bytes 1572872 | tf_op jit(solution)/shard_map/ppermute | solution.py:68
  41.2 17.1 %collective-permute-done.12 = bf16[256,1024]{1,0:T(8,128)(2,1)} collective-permute-done((bf16[256,1024]{1,0:T(8,128)(2,1)}, bf16[256,1024]{1,0:T(8,128)(2,1)}, u32[]{:S(2)}, u32[]{:S(2)}) %collective-permute-start.12) | collective-permute-done | bytes 524320 | tf_op jit(solution)/shard_map/ppermute | solution.py:13
  63.8 1.6 collective-permute-done.4
  65.5 2.3 %collective-permute-start.5 = (bf16[512,256]{0,1:T(8,128)(2,1)S(1)}, bf16[512,256]{0,1:T(8,128)(2,1)S(1)}, u32[]{:S(2)}, u32[]{:S(2)}) collective-permute-start(bf16[512,256]{0,1:T(8,128)(2,1)S(1)} %maximum_select_fusion.11), channel_id=1, source_target_pairs={{0,2},{2,0},{4,6},{6,4},{1,3},{3,1},{5,7},{7,5},{8,10},{10,8},{12,... | collective-permute-start | bytes 786440 | tf_op jit(solution)/shard_map/ppermute | solution.py:80
  67.8 16.7 %collective-permute-done.18 = bf16[256,1024]{1,0:T(8,128)(2,1)S(1)} collective-permute-done((bf16[256,1024]{1,0:T(8,128)(2,1)}, bf16[256,1024]{1,0:T(8,128)(2,1)S(1)}, u32[]{:S(2)}, u32[]{:S(2)}) %collective-permute-start.18) | collective-permute-done | bytes 524320 | tf_op jit(solution)/shard_map/ppermute | solution.py:13
  84.5 1.3 fusion.5
  89.0 2.0 %collective-permute-done.10 = bf16[256,256]{0,1:T(8,128)(2,1)S(1)} collective-permute-done((bf16[256,256]{0,1:T(8,128)(2,1)S(1)}, bf16[256,256]{0,1:T(8,128)(2,1)S(1)}, u32[]{:S(2)}, u32[]{:S(2)}) %collective-permute-start.10) | collective-permute-done | bytes 131104 | tf_op jit(solution)/shard_map/ppermute | solution.py:80
  91.1 1.7 collective-permute-start.11
  92.8 6.1 %collective-permute-done.19 = bf16[256,1024]{1,0:T(8,128)(2,1)S(1)} collective-permute-done((bf16[256,1024]{1,0:T(8,128)(2,1)S(1)}, bf16[256,1024]{1,0:T(8,128)(2,1)S(1)}, u32[]{:S(2)}, u32[]{:S(2)}) %collective-permute-start.19) | collective-permute-done | bytes 524320 | tf_op jit(solution)/shard_map/ppermute | solution.py:13
  98.9 1.3 fusion.3
  100.3 1.4 collective-permute-start.20
  101.7 7.3 %collective-permute-done.24 = bf16[256,1024]{1,0:T(8,128)(2,1)S(1)} collective-permute-done((bf16[256,1024]{1,0:T(8,128)(2,1)S(1)}, bf16[256,1024]{1,0:T(8,128)(2,1)S(1)}, u32[]{:S(2)}, u32[]{:S(2)}) %collective-permute-start.24) | collective-permute-done | bytes 524320 | tf_op jit(solution)/shard_map/ppermute | solution.py:13
  111.0 11.0 %collective-permute-done.25 = bf16[256,1024]{1,0:T(8,128)(2,1)S(1)} collective-permute-done((bf16[256,1024]{1,0:T(8,128)(2,1)S(1)}, bf16[256,1024]{1,0:T(8,128)(2,1)S(1)}, u32[]{:S(2)}, u32[]{:S(2)}) %collective-permute-start.25) | collective-permute-done | bytes 524320 | tf_op jit(solution)/shard_map/ppermute | solution.py:13
  123.8 1.3 collective-permute-start.16
  125.5 2.0 %collective-permute-start.26 = (f32[512,512]{0,1:T(8,128)S(1)}, f32[512,512]{0,1:T(8,128)S(1)}, u32[]{:S(2)}, u32[]{:S(2)}) collective-permute-start(f32[512,512]{0,1:T(8,128)S(1)} %dynamic-slice_bitcast_fusion), channel_id=1, source_target_pairs={{0,2},{2,0},{4,6},{6,4},{1,3},{3,1},{5,7},{7,5},{8,10},{10,8},{12,... | collective-permute-start | bytes 3145736 | tf_op jit(solution)/shard_map/ppermute | solution.py:68
  127.5 2.9 %collective-permute-done.16 = bf16[256,512]{0,1:T(8,128)(2,1)S(1)} collective-permute-done((bf16[256,512]{0,1:T(8,128)(2,1)S(1)}, bf16[256,512]{0,1:T(8,128)(2,1)S(1)}, u32[]{:S(2)}, u32[]{:S(2)}) %collective-permute-start.16) | collective-permute-done | bytes 262176 | tf_op jit(solution)/shard_map/ppermute | solution.py:80
  130.5 4.2 %collective-permute-start.17 = (bf16[512,512]{0,1:T(8,128)(2,1)S(1)}, bf16[512,512]{0,1:T(8,128)(2,1)S(1)}, u32[]{:S(2)}, u32[]{:S(2)}) collective-permute-start(bf16[512,512]{0,1:T(8,128)(2,1)S(1)} %maximum_select_fusion.8), channel_id=1, source_target_pairs={{0,2},{2,0},{4,6},{6,4},{1,3},{3,1},{5,7},{7,5},{8,10},{10,8},{12,... | collective-permute-start | bytes 1572872 | tf_op jit(solution)/shard_map/ppermute | solution.py:80
  134.7 6.9 %collective-permute-done.21 = f32[256,512]{0,1:T(8,128)S(1)} collective-permute-done((f32[256,512]{0,1:T(8,128)S(1)}, f32[256,512]{0,1:T(8,128)S(1)}, u32[]{:S(2)}, u32[]{:S(2)}) %collective-permute-start.21) | collective-permute-done | bytes 524320 | tf_op jit(solution)/shard_map/ppermute | solution.py:68
  144.1 3.7 %collective-permute-done.22 = bf16[256,512]{0,1:T(8,128)(2,1)S(1)} collective-permute-done((bf16[256,512]{0,1:T(8,128)(2,1)S(1)}, bf16[256,512]{0,1:T(8,128)(2,1)S(1)}, u32[]{:S(2)}, u32[]{:S(2)}) %collective-permute-start.22) | collective-permute-done | bytes 262176 | tf_op jit(solution)/shard_map/ppermute | solution.py:80
  147.9 6.0 %collective-permute-start.23 = (bf16[512,512]{0,1:T(8,128)(2,1)S(1)}, bf16[512,512]{0,1:T(8,128)(2,1)S(1)}, u32[]{:S(2)}, u32[]{:S(2)}) collective-permute-start(bf16[512,512]{0,1:T(8,128)(2,1)S(1)} %maximum_select_fusion.9), channel_id=1, source_target_pairs={{0,2},{2,0},{4,6},{6,4},{1,3},{3,1},{5,7},{7,5},{8,10},{10,8},{12,... | collective-permute-start | bytes 1572872 | tf_op jit(solution)/shard_map/ppermute | solution.py:80
  154.7 4.3 %collective-permute-done.27 = f32[256,512]{0,1:T(8,128)S(1)} collective-permute-done((f32[256,512]{0,1:T(8,128)S(1)}, f32[256,512]{0,1:T(8,128)S(1)}, u32[]{:S(2)}, u32[]{:S(2)}) %collective-permute-start.27) | collective-permute-done | bytes 524320 | tf_op jit(solution)/shard_map/ppermute | solution.py:68
  161.8 3.1 %collective-permute-done.28 = bf16[256,512]{0,1:T(8,128)(2,1)S(1)} collective-permute-done((bf16[256,512]{0,1:T(8,128)(2,1)S(1)}, bf16[256,512]{0,1:T(8,128)(2,1)S(1)}, u32[]{:S(2)}, u32[]{:S(2)}) %collective-permute-start.28) | collective-permute-done | bytes 262176 | tf_op jit(solution)/shard_map/ppermute | solution.py:80
  165.0 4.4 %collective-permute-start.29 = (bf16[512,512]{0,1:T(8,128)(2,1)S(1)}, bf16[512,512]{0,1:T(8,128)(2,1)S(1)}, u32[]{:S(2)}, u32[]{:S(2)}) collective-permute-start(bf16[512,512]{0,1:T(8,128)(2,1)S(1)} %maximum_select_fusion.10), channel_id=1, source_target_pairs={{0,2},{2,0},{4,6},{6,4},{1,3},{3,1},{5,7},{7,5},{8,10},{10,8},{12,... | collective-permute-start | bytes 1572872 | tf_op jit(solution)/shard_map/ppermute | solution.py:80
  169.4 1.3 fusion.24
  170.7 1.3 fusion.25
  172.0 3.1 %fusion = bf16[1,1024,1024]{2,1,0:T(8,128)(2,1)} fusion(f32[1024,1024]{1,0:T(8,128)S(1)} %fusion.25, f32[1024,1024]{1,0:T(8,128)S(1)} %fusion.24, f32[1024,1024]{1,0:T(8,128)S(1)} %fusion.22, f32[1024,1024]{1,0:T(8,128)S(1)} %fusion.23, bf16[512,1024]{1,0:T(8,128)(2,1)S(1)} %constant_dynamic-update-slice_fusion.8, ...), kind=kOutput, calls=%fused_computation.1 | convolution fusion | flops 1084751872 | bytes 20971520 | tf_op jit(solution)/shard_map/dot_general | solution.py:138
  (109 shorter events, 28.0 us)
Async XLA Ops:
  1.1 14.9 %collective-permute-start = (bf16[128,1024]{1,0:T(8,128)(2,1)S(1)}, bf16[128,1024]{1,0:T(8,128)(2,1)S(1)}, u32[]{:S(2)}, u32[]{:S(2)}) collective-permute-start(bf16[128,1024]{1,0:T(8,128)(2,1)S(1)} %get-tuple-element.24), channel_id=1, source_target_pairs={{0,16},{8,24},{16,0},{24,8},{1,17},{9,25},{17,1},{25,9},{2,18},{10... | collective-permute-start | bytes 786440 | tf_op jit(solution)/shard_map/ppermute | solution.py:13
  5.1 24.6 %copy-start = (bf16[1,1024,1024]{2,1,0:T(8,128)(2,1)S(1)}, bf16[1,1024,1024]{2,1,0:T(8,128)(2,1)}, u32[]{:S(2)}) copy-start(bf16[1,1024,1024]{2,1,0:T(8,128)(2,1)} %param.3) | copy-start | bytes 6291460
  16.0 13.1 %collective-permute-start.6 = (bf16[128,1024]{1,0:T(8,128)(2,1)S(1)}, bf16[128,1024]{1,0:T(8,128)(2,1)S(1)}, u32[]{:S(2)}, u32[]{:S(2)}) collective-permute-start(bf16[128,1024]{1,0:T(8,128)(2,1)S(1)} %get-tuple-element.13), channel_id=1, source_target_pairs={{0,16},{8,24},{16,0},{24,8},{1,17},{9,25},{17,1},{25,9},{2,18},{10... | collective-permute-start | bytes 786440 | tf_op jit(solution)/shard_map/ppermute | solution.py:13
  16.0 13.8 %collective-permute-start.1 = (bf16[128,1024]{1,0:T(8,128)(2,1)S(1)}, bf16[128,1024]{1,0:T(8,128)(2,1)S(1)}, u32[]{:S(2)}, u32[]{:S(2)}) collective-permute-start(bf16[128,1024]{1,0:T(8,128)(2,1)S(1)} %collective-permute-done), channel_id=1, source_target_pairs={{0,1},{1,0},{2,3},{3,2},{4,5},{5,4},{6,7},{7,6},{8,9},{9,8},{10,11... | collective-permute-start | bytes 786440 | tf_op jit(solution)/shard_map/ppermute | solution.py:13
  29.1 5.7 %collective-permute-start.7 = (bf16[128,1024]{1,0:T(8,128)(2,1)S(1)}, bf16[128,1024]{1,0:T(8,128)(2,1)S(1)}, u32[]{:S(2)}, u32[]{:S(2)}) collective-permute-start(bf16[128,1024]{1,0:T(8,128)(2,1)S(1)} %collective-permute-done.6), channel_id=1, source_target_pairs={{0,1},{1,0},{2,3},{3,2},{4,5},{5,4},{6,7},{7,6},{8,9},{9,8},{10,11... | collective-permute-start | bytes 786440 | tf_op jit(solution)/shard_map/ppermute | solution.py:13
  30.6 8.8 %collective-permute-start.2 = (f32[512,256]{0,1:T(8,128)S(1)}, f32[512,256]{0,1:T(8,128)S(1)}, u32[]{:S(2)}, u32[]{:S(2)}) collective-permute-start(f32[512,256]{0,1:T(8,128)S(1)} %dynamic-slice_bitcast_fusion.4), channel_id=1, source_target_pairs={{0,2},{2,0},{4,6},{6,4},{1,3},{3,1},{5,7},{7,5},{8,10},{10,8},{12,... | collective-permute-start | bytes 1572872 | tf_op jit(solution)/shard_map/ppermute | solution.py:68
  33.4 24.9 %collective-permute-start.12 = (bf16[256,1024]{1,0:T(8,128)(2,1)}, bf16[256,1024]{1,0:T(8,128)(2,1)}, u32[]{:S(2)}, u32[]{:S(2)}) collective-permute-start(bf16[256,1024]{1,0:T(8,128)(2,1)} %get-tuple-element.15), channel_id=1, source_target_pairs={{0,16},{8,24},{16,0},{24,8},{1,17},{9,25},{17,1},{25,9},{2,18},{10... | collective-permute-start | bytes 1572872 | tf_op jit(solution)/shard_map/ppermute | solution.py:13
  36.4 25.7 %collective-permute-start.8 = (f32[512,256]{0,1:T(8,128)}, f32[512,256]{0,1:T(8,128)}, u32[]{:S(2)}, u32[]{:S(2)}) collective-permute-start(f32[512,256]{0,1:T(8,128)} %dynamic-slice_bitcast_fusion.3), channel_id=1, source_target_pairs={{0,2},{2,0},{4,6},{6,4},{1,3},{3,1},{5,7},{7,5},{8,10},{10,8},{12,... | collective-permute-start | bytes 1572872 | tf_op jit(solution)/shard_map/ppermute | solution.py:68
  40.3 19.5 %collective-permute-start.3 = (f32[256,256]{0,1:T(8,128)S(1)}, f32[256,256]{0,1:T(8,128)}, u32[]{:S(2)}, u32[]{:S(2)}) collective-permute-start(f32[256,256]{0,1:T(8,128)S(1)} %constant_dynamic-slice_fusion.4), channel_id=1, source_target_pairs={{0,4},{2,6},{4,0},{6,2},{1,5},{3,7},{5,1},{7,3},{8,12},{10,14},{12... | collective-permute-start | bytes 786440 | tf_op jit(solution)/shard_map/ppermute | solution.py:68
  58.3 26.2 %copy-start.6 = (bf16[256,1024]{1,0:T(8,128)(2,1)S(1)}, bf16[256,1024]{1,0:T(8,128)(2,1)}, u32[]{:S(2)}) copy-start(bf16[256,1024]{1,0:T(8,128)(2,1)} %get-tuple-element.19) | copy-start | bytes 1572868
  58.3 26.2 %collective-permute-start.18 = (bf16[256,1024]{1,0:T(8,128)(2,1)}, bf16[256,1024]{1,0:T(8,128)(2,1)S(1)}, u32[]{:S(2)}, u32[]{:S(2)}) collective-permute-start(bf16[256,1024]{1,0:T(8,128)(2,1)} %get-tuple-element.17), channel_id=1, source_target_pairs={{0,16},{8,24},{16,0},{24,8},{1,17},{9,25},{17,1},{25,9},{2,18},{10... | collective-permute-start | bytes 1572872 | tf_op jit(solution)/shard_map/ppermute | solution.py:13
  58.3 26.2 %collective-permute-start.13 = (bf16[256,1024]{1,0:T(8,128)(2,1)}, bf16[256,1024]{1,0:T(8,128)(2,1)S(1)}, u32[]{:S(2)}, u32[]{:S(2)}) collective-permute-start(bf16[256,1024]{1,0:T(8,128)(2,1)} %collective-permute-done.12), channel_id=1, source_target_pairs={{0,1},{1,0},{2,3},{3,2},{4,5},{5,4},{6,7},{7,6},{8,9},{9,8},{10,11... | collective-permute-start | bytes 1572872 | tf_op jit(solution)/shard_map/ppermute | solution.py:13
  61.0 4.4 %collective-permute-start.4 = (bf16[256,256]{0,1:T(8,128)(2,1)S(1)}, bf16[256,256]{0,1:T(8,128)(2,1)S(1)}, u32[]{:S(2)}, u32[]{:S(2)}) collective-permute-start(bf16[256,256]{0,1:T(8,128)(2,1)S(1)} %divide_convert_fusion.4), channel_id=1, source_target_pairs={{0,4},{2,6},{4,0},{6,2},{1,5},{3,7},{5,1},{7,3},{8,12},{10,14},{12... | collective-permute-start | bytes 393224 | tf_op jit(solution)/shard_map/ppermute | solution.py:80
  63.2 23.1 %collective-permute-start.9 = (f32[256,256]{0,1:T(8,128)S(1)}, f32[256,256]{0,1:T(8,128)S(1)}, u32[]{:S(2)}, u32[]{:S(2)}) collective-permute-start(f32[256,256]{0,1:T(8,128)S(1)} %constant_dynamic-slice_fusion.3), channel_id=1, source_target_pairs={{0,4},{2,6},{4,0},{6,2},{1,5},{3,7},{5,1},{7,3},{8,12},{10,14},{12... | collective-permute-start | bytes 786440 | tf_op jit(solution)/shard_map/ppermute | solution.py:68
  65.5 20.9 %collective-permute-start.5 = (bf16[512,256]{0,1:T(8,128)(2,1)S(1)}, bf16[512,256]{0,1:T(8,128)(2,1)S(1)}, u32[]{:S(2)}, u32[]{:S(2)}) collective-permute-start(bf16[512,256]{0,1:T(8,128)(2,1)S(1)} %maximum_select_fusion.11), channel_id=1, source_target_pairs={{0,2},{2,0},{4,6},{6,4},{1,3},{3,1},{5,7},{7,5},{8,10},{10,8},{12,... | collective-permute-start | bytes 786440 | tf_op jit(solution)/shard_map/ppermute | solution.py:80
  84.5 24.5 %collective-permute-start.24 = (bf16[256,1024]{1,0:T(8,128)(2,1)S(1)}, bf16[256,1024]{1,0:T(8,128)(2,1)S(1)}, u32[]{:S(2)}, u32[]{:S(2)}) collective-permute-start(bf16[256,1024]{1,0:T(8,128)(2,1)S(1)} %copy-done.6), channel_id=1, source_target_pairs={{0,16},{8,24},{16,0},{24,8},{1,17},{9,25},{17,1},{25,9},{2,18},{10... | collective-permute-start | bytes 1572872 | tf_op jit(solution)/shard_map/ppermute | solution.py:13
  85.8 13.1 %collective-permute-start.19 = (bf16[256,1024]{1,0:T(8,128)(2,1)S(1)}, bf16[256,1024]{1,0:T(8,128)(2,1)S(1)}, u32[]{:S(2)}, u32[]{:S(2)}) collective-permute-start(bf16[256,1024]{1,0:T(8,128)(2,1)S(1)} %collective-permute-done.18), channel_id=1, source_target_pairs={{0,1},{1,0},{2,3},{3,2},{4,5},{5,4},{6,7},{7,6},{8,9},{9,8},{10,11... | collective-permute-start | bytes 1572872 | tf_op jit(solution)/shard_map/ppermute | solution.py:13
  86.7 4.3 %collective-permute-start.10 = (bf16[256,256]{0,1:T(8,128)(2,1)S(1)}, bf16[256,256]{0,1:T(8,128)(2,1)S(1)}, u32[]{:S(2)}, u32[]{:S(2)}) collective-permute-start(bf16[256,256]{0,1:T(8,128)(2,1)S(1)} %divide_convert_fusion.3), channel_id=1, source_target_pairs={{0,4},{2,6},{4,0},{6,2},{1,5},{3,7},{5,1},{7,3},{8,12},{10,14},{12... | collective-permute-start | bytes 393224 | tf_op jit(solution)/shard_map/ppermute | solution.py:80
  87.8 21.9 %collective-permute-start.14 = (f32[512,512]{0,1:T(8,128)S(1)}, f32[512,512]{0,1:T(8,128)S(1)}, u32[]{:S(2)}, u32[]{:S(2)}) collective-permute-start(f32[512,512]{0,1:T(8,128)S(1)} %dynamic-slice_bitcast_fusion.2), channel_id=1, source_target_pairs={{0,2},{2,0},{4,6},{6,4},{1,3},{3,1},{5,7},{7,5},{8,10},{10,8},{12,... | collective-permute-start | bytes 3145736 | tf_op jit(solution)/shard_map/ppermute | solution.py:68
  91.1 18.4 %collective-permute-start.11 = (bf16[512,256]{0,1:T(8,128)(2,1)S(1)}, bf16[512,256]{0,1:T(8,128)(2,1)S(1)}, u32[]{:S(2)}, u32[]{:S(2)}) collective-permute-start(bf16[512,256]{0,1:T(8,128)(2,1)S(1)} %maximum_select_fusion.12), channel_id=1, source_target_pairs={{0,2},{2,0},{4,6},{6,4},{1,3},{3,1},{5,7},{7,5},{8,10},{10,8},{12,... | collective-permute-start | bytes 786440 | tf_op jit(solution)/shard_map/ppermute | solution.py:80
  100.3 23.0 %collective-permute-start.20 = (f32[512,512]{0,1:T(8,128)S(1)}, f32[512,512]{0,1:T(8,128)S(1)}, u32[]{:S(2)}, u32[]{:S(2)}) collective-permute-start(f32[512,512]{0,1:T(8,128)S(1)} %dynamic-slice_bitcast_fusion.1), channel_id=1, source_target_pairs={{0,2},{2,0},{4,6},{6,4},{1,3},{3,1},{5,7},{7,5},{8,10},{10,8},{12,... | collective-permute-start | bytes 3145736 | tf_op jit(solution)/shard_map/ppermute | solution.py:68
  109.0 13.0 %collective-permute-start.25 = (bf16[256,1024]{1,0:T(8,128)(2,1)S(1)}, bf16[256,1024]{1,0:T(8,128)(2,1)S(1)}, u32[]{:S(2)}, u32[]{:S(2)}) collective-permute-start(bf16[256,1024]{1,0:T(8,128)(2,1)S(1)} %collective-permute-done.24), channel_id=1, source_target_pairs={{0,1},{1,0},{2,3},{3,2},{4,5},{5,4},{6,7},{7,6},{8,9},{9,8},{10,11... | collective-permute-start | bytes 1572872 | tf_op jit(solution)/shard_map/ppermute | solution.py:13
  110.0 13.6 %collective-permute-start.15 = (f32[256,512]{0,1:T(8,128)S(1)}, f32[256,512]{0,1:T(8,128)S(1)}, u32[]{:S(2)}, u32[]{:S(2)}) collective-permute-start(f32[256,512]{0,1:T(8,128)S(1)} %constant_dynamic-slice_fusion.2), channel_id=1, source_target_pairs={{0,4},{2,6},{4,0},{6,2},{1,5},{3,7},{5,1},{7,3},{8,12},{10,14},{12... | collective-permute-start | bytes 1572872 | tf_op jit(solution)/shard_map/ppermute | solution.py:68
  123.8 6.5 %collective-permute-start.16 = (bf16[256,512]{0,1:T(8,128)(2,1)S(1)}, bf16[256,512]{0,1:T(8,128)(2,1)S(1)}, u32[]{:S(2)}, u32[]{:S(2)}) collective-permute-start(bf16[256,512]{0,1:T(8,128)(2,1)S(1)} %divide_convert_fusion.2), channel_id=1, source_target_pairs={{0,4},{2,6},{4,0},{6,2},{1,5},{3,7},{5,1},{7,3},{8,12},{10,14},{12... | collective-permute-start | bytes 786440 | tf_op jit(solution)/shard_map/ppermute | solution.py:80
  125.2 16.4 %collective-permute-start.21 = (f32[256,512]{0,1:T(8,128)S(1)}, f32[256,512]{0,1:T(8,128)S(1)}, u32[]{:S(2)}, u32[]{:S(2)}) collective-permute-start(f32[256,512]{0,1:T(8,128)S(1)} %constant_dynamic-slice_fusion.1), channel_id=1, source_target_pairs={{0,4},{2,6},{4,0},{6,2},{1,5},{3,7},{5,1},{7,3},{8,12},{10,14},{12... | collective-permute-start | bytes 1572872 | tf_op jit(solution)/shard_map/ppermute | solution.py:68
  125.5 17.9 %collective-permute-start.26 = (f32[512,512]{0,1:T(8,128)S(1)}, f32[512,512]{0,1:T(8,128)S(1)}, u32[]{:S(2)}, u32[]{:S(2)}) collective-permute-start(f32[512,512]{0,1:T(8,128)S(1)} %dynamic-slice_bitcast_fusion), channel_id=1, source_target_pairs={{0,2},{2,0},{4,6},{6,4},{1,3},{3,1},{5,7},{7,5},{8,10},{10,8},{12,... | collective-permute-start | bytes 3145736 | tf_op jit(solution)/shard_map/ppermute | solution.py:68
  130.5 11.2 %collective-permute-start.17 = (bf16[512,512]{0,1:T(8,128)(2,1)S(1)}, bf16[512,512]{0,1:T(8,128)(2,1)S(1)}, u32[]{:S(2)}, u32[]{:S(2)}) collective-permute-start(bf16[512,512]{0,1:T(8,128)(2,1)S(1)} %maximum_select_fusion.8), channel_id=1, source_target_pairs={{0,2},{2,0},{4,6},{6,4},{1,3},{3,1},{5,7},{7,5},{8,10},{10,8},{12,... | collective-permute-start | bytes 1572872 | tf_op jit(solution)/shard_map/ppermute | solution.py:80
  142.2 5.6 %collective-permute-start.22 = (bf16[256,512]{0,1:T(8,128)(2,1)S(1)}, bf16[256,512]{0,1:T(8,128)(2,1)S(1)}, u32[]{:S(2)}, u32[]{:S(2)}) collective-permute-start(bf16[256,512]{0,1:T(8,128)(2,1)S(1)} %divide_convert_fusion.1), channel_id=1, source_target_pairs={{0,4},{2,6},{4,0},{6,2},{1,5},{3,7},{5,1},{7,3},{8,12},{10,14},{12... | collective-permute-start | bytes 786440 | tf_op jit(solution)/shard_map/ppermute | solution.py:80
  143.7 15.3 %collective-permute-start.27 = (f32[256,512]{0,1:T(8,128)S(1)}, f32[256,512]{0,1:T(8,128)S(1)}, u32[]{:S(2)}, u32[]{:S(2)}) collective-permute-start(f32[256,512]{0,1:T(8,128)S(1)} %constant_dynamic-slice_fusion), channel_id=1, source_target_pairs={{0,4},{2,6},{4,0},{6,2},{1,5},{3,7},{5,1},{7,3},{8,12},{10,14},{12... | collective-permute-start | bytes 1572872 | tf_op jit(solution)/shard_map/ppermute | solution.py:68
  147.9 11.2 %collective-permute-start.23 = (bf16[512,512]{0,1:T(8,128)(2,1)S(1)}, bf16[512,512]{0,1:T(8,128)(2,1)S(1)}, u32[]{:S(2)}, u32[]{:S(2)}) collective-permute-start(bf16[512,512]{0,1:T(8,128)(2,1)S(1)} %maximum_select_fusion.9), channel_id=1, source_target_pairs={{0,2},{2,0},{4,6},{6,4},{1,3},{3,1},{5,7},{7,5},{8,10},{10,8},{12,... | collective-permute-start | bytes 1572872 | tf_op jit(solution)/shard_map/ppermute | solution.py:80
  159.6 5.3 %collective-permute-start.28 = (bf16[256,512]{0,1:T(8,128)(2,1)S(1)}, bf16[256,512]{0,1:T(8,128)(2,1)S(1)}, u32[]{:S(2)}, u32[]{:S(2)}) collective-permute-start(bf16[256,512]{0,1:T(8,128)(2,1)S(1)} %divide_convert_fusion), channel_id=1, source_target_pairs={{0,4},{2,6},{4,0},{6,2},{1,5},{3,7},{5,1},{7,3},{8,12},{10,14},{12... | collective-permute-start | bytes 786440 | tf_op jit(solution)/shard_map/ppermute | solution.py:80
  165.0 7.0 %collective-permute-start.29 = (bf16[512,512]{0,1:T(8,128)(2,1)S(1)}, bf16[512,512]{0,1:T(8,128)(2,1)S(1)}, u32[]{:S(2)}, u32[]{:S(2)}) collective-permute-start(bf16[512,512]{0,1:T(8,128)(2,1)S(1)} %maximum_select_fusion.10), channel_id=1, source_target_pairs={{0,2},{2,0},{4,6},{6,4},{1,3},{3,1},{5,7},{7,5},{8,10},{10,8},{12,... | collective-permute-start | bytes 1572872 | tf_op jit(solution)/shard_map/ppermute | solution.py:80
  (7 other events, 57.0 us)

commit v17 on v5

--- a/solution.py
+++ b/solution.py
@@ -1,11 +1,12 @@
 import jax
 import jax.numpy as jnp
 from jax import lax
-from jax.sharding import PartitionSpec as P
+from jax.sharding import Mesh, PartitionSpec as P
 
 CHUNKS = 4
 AUX_BY_PERMUTE = True
 NARROW_FAR = False
+SPLIT_OCC = True
 
 
 def shifted_2(value, axis, by):
@@ -83,11 +84,11 @@
     return x
 
 
-def paired_plan(integrals, occ_energy, vir_energy):
+def paired_plan(integrals, occ_energy, vir_energy, occ="occ", swap=False):
     own = integrals[0]
     vir_rows, _ = own.shape
-    cycle_size = lax.axis_size("occ")
-    position = lax.axis_index("occ")
+    cycle_size = lax.axis_size(occ)
+    position = lax.axis_index(occ)
     pair_level = occ_energy[position] + occ_energy[(position - 2) % cycle_size]
     vir_pos = lax.axis_index("vir")
     vir_count = lax.axis_size("vir")
@@ -105,7 +106,11 @@
         piece = own[c * width:(c + 1) * width]
         if previous is not None:
             piece, _ = lax.optimization_barrier((piece, previous))
-        arrived = shifted_2(piece, "occ", 2)
+        if swap:
+            both = lax.all_to_all(jnp.stack([piece, piece]), "occ_hi", 0, 0)
+            arrived = lax.dynamic_index_in_dim(both, 1 - lax.axis_index("occ_hi"), 0, False)
+        else:
+            arrived = shifted_2(piece, "occ", 2)
         previous = arrived
         if vir_count == 2:
             mate = shifted_2(arrived, "vir", 1)
@@ -148,7 +153,24 @@
     return general_plan(integrals, occ_energy, vir_energy)
 
 
+def paired_on_split(integrals, occ_energy, vir_energy):
+    return paired_plan(integrals, occ_energy, vir_energy, ("occ_hi", "occ_lo"), True)
+
+
 def solution(mesh):
+    if mesh.shape["occ"] == 4 and mesh.devices.shape[1] % 4 == 0 and SPLIT_OCC:
+        names = list(mesh.axis_names)
+        at = names.index("occ")
+        shape = mesh.devices.shape
+        split = Mesh(
+            mesh.devices.reshape(shape[:at] + (2, 2) + shape[at + 1:]),
+            tuple(names[:at] + ["occ_hi", "occ_lo"] + names[at + 1:]),
+        )
+        spec = P(("occ_hi", "occ_lo"), "vir", "aux")
+        return jax.shard_map(
+            paired_on_split, mesh=split, in_specs=(spec, P(), P()), out_specs=spec,
+            check_vma=False,
+        )
     placed = (P("occ", "vir", "aux"), P(), P())
     return jax.shard_map(
         on_device, mesh=mesh, in_specs=placed, out_specs=P("occ", "vir", "aux"), check_vma=False

time: 176 us -> 185 us (1.051)
  waiting for transfers between devices: 109 us -> 91.8 us
  other arithmetic: 4.46 us -> 15.7 us
  local copies, waits for them, and re-layouts: 8.45 us -> 14.2 us
  matrix products: 14 us -> 18.9 us
  starting transfers between devices: 37.9 us -> 42 us
    ppermute x8 -> x4, waiting for transfers between devices: 86.7 us -> 15.9 us  [shifted_2(): lax.ppermute(value, axis, [(i, (i + by) % count) for i in range(count)])]
    all_to_all x0 -> x4, waiting for transfers between devices: none -> 45.2 us  [paired_plan(): both = lax.all_to_all(jnp.stack([piece, piece]), 'occ_hi', 0, 0)]
    all_to_all x0 -> x4, starting transfers between devices: none -> 15.3 us  [paired_plan(): both = lax.all_to_all(jnp.stack([piece, piece]), 'occ_hi', 0, 0)]
    ppermute x8, starting transfers between devices: 22.9 us -> 11.9 us  [aux_all_gather(): other = lax.ppermute(x, 'aux', xor_pairs(count, step))]
    another operation x0 -> x4, other arithmetic: none -> 5.42 us  [paired_plan(): both = lax.all_to_all(jnp.stack([piece, piece]), 'occ_hi', 0, 0)]
    ppermute x8, waiting for transfers between devices: 13.9 us -> 18.5 us  [aux_reduce_scatter(): x = keep + lax.ppermute(send, 'aux', xor_pairs(count, step))]
    add x7, other arithmetic: 2.34 us -> 6.59 us  [aux_reduce_scatter(): x = keep + lax.ppermute(send, 'aux', xor_pairs(count, step))]
    ppermute x8, waiting for transfers between devices: 8.3 us -> 12.2 us  [aux_all_gather(): other = lax.ppermute(x, 'aux', xor_pairs(count, step))]
  transfers between devices with their start and end apart: 24 -> 24, of which waited for: 12 -> 14; matrix products, arithmetic and copies ran while one was open for 11% -> 20% of each run, Pallas kernels for 0% -> 0%
where the time goes in v17:
time: 185 us; the launch traced here: 184 us
  waiting for transfers between devices  91.8 us (50%)
  starting transfers between devices  42 us (23%)
  matrix products  18.9 us (10%)
  other arithmetic  15.7 us (8%)
  local copies, waits for them, and re-layouts  14.2 us (8%)
    all_to_all x4, waiting for transfers between devices, paired_plan(): both = lax.all_to_all(jnp.stack([piece, piece]), 'occ_hi', 0, 0)  45.2 us
    ppermute x8, waiting for transfers between devices, aux_reduce_scatter(): x = keep + lax.ppermute(send, 'aux', xor_pairs(count, step))  18.5 us
    ppermute x4, waiting for transfers between devices, shifted_2(): lax.ppermute(value, axis, [(i, (i + by) % count) for i in range(count)])  15.9 us
    all_to_all x4, starting transfers between devices, paired_plan(): both = lax.all_to_all(jnp.stack([piece, piece]), 'occ_hi', 0, 0)  15.3 us
    ppermute x8, waiting for transfers between devices, aux_all_gather(): other = lax.ppermute(x, 'aux', xor_pairs(count, step))  12.2 us
    ppermute x8, starting transfers between devices, aux_all_gather(): other = lax.ppermute(x, 'aux', xor_pairs(count, step))  11.9 us
    ppermute x8, starting transfers between devices, aux_reduce_scatter(): x = keep + lax.ppermute(send, 'aux', xor_pairs(count, step))  11.6 us
    dot_general x4, matrix products, paired_plan(): term = jnp.dot(rows, block, preferred_element_type=jnp.float32)  10.3 us
  transfers between devices with their start and end apart: 24, of which 14 were waited for; matrix products, arithmetic and copies ran while one was open for 20% of the time, Pallas kernels for 0%

profile of v17, /device:TPU:1, one launch (start us, length us, event | category | flops | bytes accessed | tf_op | source)
XLA Modules:
  0.0 184.2 jit_solution(3353110962215595710)
XLA Ops:
  0.0 2.7 %slice_bitcast_fusion = (bf16[256,1024]{1,0:T(8,128)(2,1)}, bf16[256,1024]{1,0:T(8,128)(2,1)}, bf16[1,256,1024]{2,1,0:T(8,128)(2,1)S(1)}, bf16[256,1024]{1,0:T(8,128)(2,1)}) fusion(bf16[1,1024,1024]{2,1,0:T(8,128)(2,1)} %param.3), kind=kLoop, calls=%fused_computation.47 | loop fusion | bytes 4194304 | tf_op jit(solution)/shard_map/slice | solution.py:106
  3.8 4.4 %all-to-all-start = ((bf16[2,256,1024]{2,1,0:T(8,128)(2,1)}), bf16[2,256,1024]{2,1,0:T(8,128)(2,1)S(1)}, u32[]{:S(2)}, u32[]{:S(2)}) async-start(bf16[2,256,1024]{2,1,0:T(8,128)(2,1)} %pad_maximum_fusion), calls=%async_computation | async-start | bytes 2097152 | tf_op jit(solution)/shard_map/all_to_all | solution.py:110
  8.2 25.1 %all-to-all-done = bf16[2,256,1024]{2,1,0:T(8,128)(2,1)S(1)} async-done(((bf16[2,256,1024]{2,1,0:T(8,128)(2,1)}), bf16[2,256,1024]{2,1,0:T(8,128)(2,1)S(1)}, u32[]{:S(2)}, u32[]{:S(2)}) %all-to-all-start) | async-done | bytes 1048608 | tf_op jit(solution)/shard_map/all_to_all | solution.py:110
  35.4 2.3 %pad_maximum_fusion.2 = bf16[2,256,1024]{2,1,0:T(8,128)(2,1)} fusion(bf16[1,256,1024]{2,1,0:T(8,128)(2,1)} %bitcast.50), kind=kLoop, calls=%fused_computation.13 | loop fusion | flops 524288 | bytes 1572864 | tf_op jit(solution)/shard_map/stack | solution.py:110
  37.6 3.6 %all-to-all-start.1 = ((bf16[2,256,1024]{2,1,0:T(8,128)(2,1)}), bf16[2,256,1024]{2,1,0:T(8,128)(2,1)S(1)}, u32[]{:S(2)}, u32[]{:S(2)}) async-start(bf16[2,256,1024]{2,1,0:T(8,128)(2,1)} %pad_maximum_fusion.2), calls=%async_computation.1 | async-start | bytes 2097152 | tf_op jit(solution)/shard_map/all_to_all | solution.py:110
  41.2 5.1 %collective-permute-done = bf16[256,1024]{1,0:T(8,128)(2,1)} collective-permute-done((bf16[256,1024]{1,0:T(8,128)(2,1)}, bf16[256,1024]{1,0:T(8,128)(2,1)}, u32[]{:S(2)}, u32[]{:S(2)}) %collective-permute-start) | collective-permute-done | bytes 524320 | tf_op jit(solution)/shard_map/ppermute | solution.py:14
  46.3 2.5 %fusion.7 = f32[512,1024]{1,0:T(8,128)S(1)} fusion(bf16[1,1024,1024]{2,1,0:T(8,128)(2,1)S(1)} %copy-done.5, bf16[256,1024]{1,0:T(8,128)(2,1)} %collective-permute-done, bf16[256,1024]{1,0:T(8,128)(2,1)} %dynamic-slice_bitcast_fusion.7), kind=kOutput, calls=%fused_computation.8 | convolution fusion | flops 1075838976 | bytes 5242880 | tf_op jit(solution)/shard_map/aq,bq->ab/dot_general | solution.py:125
  51.2 2.5 %collective-permute-start.1 = (f32[512,512]{0,1:T(8,128)}, f32[512,512]{0,1:T(8,128)}, u32[]{:S(2)}, u32[]{:S(2)}) collective-permute-start(f32[512,512]{0,1:T(8,128)} %dynamic-slice_bitcast_fusion.3), channel_id=1, source_target_pairs={{0,2},{2,0},{4,6},{6,4},{1,3},{3,1},{5,7},{7,5},{8,10},{10,8},{12,... | collective-permute-start | bytes 3145736 | tf_op jit(solution)/shard_map/ppermute | solution.py:69
  53.7 13.4 %all-to-all-done.1 = bf16[2,256,1024]{2,1,0:T(8,128)(2,1)S(1)} async-done(((bf16[2,256,1024]{2,1,0:T(8,128)(2,1)}), bf16[2,256,1024]{2,1,0:T(8,128)(2,1)S(1)}, u32[]{:S(2)}, u32[]{:S(2)}) %all-to-all-start.1) | async-done | bytes 1048608 | tf_op jit(solution)/shard_map/all_to_all | solution.py:110
  68.6 3.6 %all-to-all-start.2 = ((bf16[2,256,1024]{2,1,0:T(8,128)(2,1)}), bf16[2,256,1024]{2,1,0:T(8,128)(2,1)S(1)}, u32[]{:S(2)}, u32[]{:S(2)}) async-start(bf16[2,256,1024]{2,1,0:T(8,128)(2,1)} %pad_maximum_fusion.4), calls=%async_computation.2 | async-start | bytes 2097152 | tf_op jit(solution)/shard_map/all_to_all | solution.py:110
  72.2 1.9 %bitcast_add_fusion.3 = f32[512,512]{0,1:T(8,128)S(1)} fusion(f32[512,512]{0,1:T(8,128)} %collective-permute-done.1, f32[512,1024]{1,0:T(8,128)} %copy-done.1, s32[]{:T(128)S(6)} %select_n.175), kind=kLoop, calls=%fused_computation.31 | loop fusion | flops 262144 | bytes 3145732 | tf_op jit(solution)/shard_map/add | solution.py:69
  76.1 4.1 %collective-permute-done.5 = bf16[256,1024]{1,0:T(8,128)(2,1)} collective-permute-done((bf16[256,1024]{1,0:T(8,128)(2,1)S(1)}, bf16[256,1024]{1,0:T(8,128)(2,1)}, u32[]{:S(2)}, u32[]{:S(2)}) %collective-permute-start.5) | collective-permute-done | bytes 524320 | tf_op jit(solution)/shard_map/ppermute | solution.py:14
  80.3 2.3 %fusion.5 = f32[512,1024]{1,0:T(8,128)S(1)} fusion(bf16[1,1024,1024]{2,1,0:T(8,128)(2,1)S(1)} %copy-done.6, bf16[256,1024]{1,0:T(8,128)(2,1)} %collective-permute-done.5, bf16[256,1024]{1,0:T(8,128)(2,1)S(1)} %dynamic-slice_bitcast_fusion.6), kind=kOutput, calls=%fused_computation.6 | convolution fusion | flops 1075838976 | bytes 5242880 | tf_op jit(solution)/shard_map/aq,bq->ab/dot_general | solution.py:125
  89.8 5.0 %all-to-all-done.2 = bf16[2,256,1024]{2,1,0:T(8,128)(2,1)S(1)} async-done(((bf16[2,256,1024]{2,1,0:T(8,128)(2,1)}), bf16[2,256,1024]{2,1,0:T(8,128)(2,1)S(1)}, u32[]{:S(2)}, u32[]{:S(2)}) %all-to-all-start.2) | async-done | bytes 1048608 | tf_op jit(solution)/shard_map/all_to_all | solution.py:110
  97.9 3.8 %all-to-all-start.3 = ((bf16[2,256,1024]{2,1,0:T(8,128)(2,1)}), bf16[2,256,1024]{2,1,0:T(8,128)(2,1)S(1)}, u32[]{:S(2)}, u32[]{:S(2)}) async-start(bf16[2,256,1024]{2,1,0:T(8,128)(2,1)} %pad_maximum_fusion.6), calls=%async_computation.3 | async-start | bytes 2097152 | tf_op jit(solution)/shard_map/all_to_all | solution.py:110
  106.5 2.4 %collective-permute-done.10 = bf16[256,1024]{1,0:T(8,128)(2,1)S(1)} collective-permute-done((bf16[256,1024]{1,0:T(8,128)(2,1)}, bf16[256,1024]{1,0:T(8,128)(2,1)S(1)}, u32[]{:S(2)}, u32[]{:S(2)}) %collective-permute-start.10) | collective-permute-done | bytes 524320 | tf_op jit(solution)/shard_map/ppermute | solution.py:14
  108.9 2.5 %fusion.3 = f32[512,1024]{1,0:T(8,128)S(1)} fusion(bf16[1,1024,1024]{2,1,0:T(8,128)(2,1)S(1)} %copy-done.7, bf16[256,1024]{1,0:T(8,128)(2,1)S(1)} %collective-permute-done.10, bf16[256,1024]{1,0:T(8,128)(2,1)} %dynamic-slice_bitcast_fusion.5), kind=kOutput, calls=%fused_computation.4 | convolution fusion | flops 1075838976 | bytes 5242880 | tf_op jit(solution)/shard_map/aq,bq->ab/dot_general | solution.py:125
  115.2 1.9 %maximum_select_fusion = bf16[1024,512]{0,1:T(8,128)(2,1)S(1)} fusion(bf16[512,512]{0,1:T(8,128)(2,1)} %collective-permute-done.4, bf16[512,512]{0,1:T(8,128)(2,1)} %copy-done.4, pred[]{:T(512)S(6)} %eq.30), kind=kLoop, calls=%fused_computation.12 | loop fusion | flops 4718592 | bytes 2097153 | tf_op jit(solution)/shard_map/jit(_where)/select_n | solution.py:82
  117.1 1.8 collective-permute-done.7
  123.5 3.4 %collective-permute-done.8 = bf16[256,512]{0,1:T(8,128)(2,1)S(1)} collective-permute-done((bf16[256,512]{0,1:T(8,128)(2,1)S(1)}, bf16[256,512]{0,1:T(8,128)(2,1)S(1)}, u32[]{:S(2)}, u32[]{:S(2)}) %collective-permute-start.8) | collective-permute-done | bytes 262176 | tf_op jit(solution)/shard_map/ppermute | solution.py:81
  127.0 2.1 %collective-permute-start.9 = (bf16[512,512]{0,1:T(8,128)(2,1)S(1)}, bf16[512,512]{0,1:T(8,128)(2,1)S(1)}, u32[]{:S(2)}, u32[]{:S(2)}) collective-permute-start(bf16[512,512]{0,1:T(8,128)(2,1)S(1)} %maximum_select_fusion.8), channel_id=1, source_target_pairs={{0,2},{2,0},{4,6},{6,4},{1,3},{3,1},{5,7},{7,5},{8,10},{10,8},{12,... | collective-permute-start | bytes 1572872 | tf_op jit(solution)/shard_map/ppermute | solution.py:81
  131.9 4.3 %collective-permute-done.15 = bf16[256,1024]{1,0:T(8,128)(2,1)S(1)} collective-permute-done((bf16[256,1024]{1,0:T(8,128)(2,1)S(1)}, bf16[256,1024]{1,0:T(8,128)(2,1)S(1)}, u32[]{:S(2)}, u32[]{:S(2)}) %collective-permute-start.15) | collective-permute-done | bytes 524320 | tf_op jit(solution)/shard_map/ppermute | solution.py:14
  139.3 4.7 %collective-permute-done.12 = f32[256,512]{0,1:T(8,128)S(1)} collective-permute-done((f32[256,512]{0,1:T(8,128)S(1)}, f32[256,512]{0,1:T(8,128)S(1)}, u32[]{:S(2)}, u32[]{:S(2)}) %collective-permute-start.12) | collective-permute-done | bytes 524320 | tf_op jit(solution)/shard_map/ppermute | solution.py:69
  145.6 5.6 %collective-permute-done.13 = bf16[256,512]{0,1:T(8,128)(2,1)S(1)} collective-permute-done((bf16[256,512]{0,1:T(8,128)(2,1)S(1)}, bf16[256,512]{0,1:T(8,128)(2,1)S(1)}, u32[]{:S(2)}, u32[]{:S(2)}) %collective-permute-start.13) | collective-permute-done | bytes 262176 | tf_op jit(solution)/shard_map/ppermute | solution.py:81
  151.3 1.9 %collective-permute-start.14 = (bf16[512,512]{0,1:T(8,128)(2,1)S(1)}, bf16[512,512]{0,1:T(8,128)(2,1)S(1)}, u32[]{:S(2)}, u32[]{:S(2)}) collective-permute-start(bf16[512,512]{0,1:T(8,128)(2,1)S(1)} %maximum_select_fusion.9), channel_id=1, source_target_pairs={{0,2},{2,0},{4,6},{6,4},{1,3},{3,1},{5,7},{7,5},{8,10},{10,8},{12,... | collective-permute-start | bytes 1572872 | tf_op jit(solution)/shard_map/ppermute | solution.py:81
  155.2 11.9 %collective-permute-done.17 = f32[256,512]{0,1:T(8,128)S(1)} collective-permute-done((f32[256,512]{0,1:T(8,128)S(1)}, f32[256,512]{0,1:T(8,128)S(1)}, u32[]{:S(2)}, u32[]{:S(2)}) %collective-permute-start.17) | collective-permute-done | bytes 524320 | tf_op jit(solution)/shard_map/ppermute | solution.py:69
  168.7 2.5 %fusion.18 = f32[1024,1024]{1,0:T(8,128)S(1)} fusion(bf16[1024,512]{0,1:T(8,128)(2,1)S(1)} %maximum_select_fusion, bf16[256,1024]{1,0:T(8,128)(2,1)} %collective-permute-done, bf16[256,1024]{1,0:T(8,128)(2,1)} %dynamic-slice_bitcast_fusion.7), kind=kOutput, calls=%fused_computation.39 | convolution fusion | flops 1075838976 | bytes 6291456 | tf_op jit(solution)/shard_map/dot_general | solution.py:142
  171.2 3.2 %collective-permute-done.18 = bf16[256,512]{0,1:T(8,128)(2,1)S(1)} collective-permute-done((bf16[256,512]{0,1:T(8,128)(2,1)S(1)}, bf16[256,512]{0,1:T(8,128)(2,1)S(1)}, u32[]{:S(2)}, u32[]{:S(2)}) %collective-permute-start.18) | collective-permute-done | bytes 262176 | tf_op jit(solution)/shard_map/ppermute | solution.py:81
  174.6 1.8 collective-permute-start.19
  176.4 2.3 %fusion.17 = f32[1024,1024]{1,0:T(8,128)S(1)} fusion(bf16[1024,512]{0,1:T(8,128)(2,1)S(1)} %maximum_select_fusion.1, bf16[256,1024]{1,0:T(8,128)(2,1)} %collective-permute-done.5, bf16[256,1024]{1,0:T(8,128)(2,1)S(1)} %copy-done.12), kind=kOutput, calls=%fused_computation.38 | convolution fusion | flops 1075838976 | bytes 6291456 | tf_op jit(solution)/shard_map/dot_general | solution.py:142
  178.7 2.3 %fusion.16 = f32[1024,1024]{1,0:T(8,128)S(1)} fusion(bf16[1024,512]{0,1:T(8,128)(2,1)S(1)} %maximum_select_fusion.2, bf16[256,1024]{1,0:T(8,128)(2,1)S(1)} %copy-done.14, bf16[256,1024]{1,0:T(8,128)(2,1)} %dynamic-slice_bitcast_fusion.5), kind=kOutput, calls=%fused_computation.37 | convolution fusion | flops 1075838976 | bytes 6291456 | tf_op jit(solution)/shard_map/dot_general | solution.py:142
  181.1 3.1 %fusion = bf16[1,1024,1024]{2,1,0:T(8,128)(2,1)} fusion(f32[1024,1024]{1,0:T(8,128)S(1)} %fusion.16, f32[1024,1024]{1,0:T(8,128)S(1)} %fusion.18, f32[1024,1024]{1,0:T(8,128)S(1)} %fusion.17, bf16[512,512]{0,1:T(8,128)(2,1)S(1)} %collective-permute-done.19, bf16[512,512]{0,1:T(8,128)(2,1)S(1)} %maximum_select_fusion.10, pred[]{:T(512)S(6)} %eq.30, ...), kind=kOutput, calls=%fused_computation.1 | convolution fusion | flops 1085800448 | bytes 16777216 | tf_op jit(solution)/shard_map/dot_general | solution.py:142
  (99 shorter events, 42.5 us)
Async XLA Ops:
  3.8 29.5 %all-to-all-start = ((bf16[2,256,1024]{2,1,0:T(8,128)(2,1)}), bf16[2,256,1024]{2,1,0:T(8,128)(2,1)S(1)}, u32[]{:S(2)}, u32[]{:S(2)}) async-start(bf16[2,256,1024]{2,1,0:T(8,128)(2,1)} %pad_maximum_fusion), calls=%async_computation | async-start | bytes 2097152 | tf_op jit(solution)/shard_map/all_to_all | solution.py:110
  34.1 12.2 %copy-start.5 = (bf16[1,1024,1024]{2,1,0:T(8,128)(2,1)S(1)}, bf16[1,1024,1024]{2,1,0:T(8,128)(2,1)}, u32[]{:S(2)}) copy-start(bf16[1,1024,1024]{2,1,0:T(8,128)(2,1)} %param.3) | copy-start | bytes 6291460
  34.1 12.2 %collective-permute-start = (bf16[256,1024]{1,0:T(8,128)(2,1)}, bf16[256,1024]{1,0:T(8,128)(2,1)}, u32[]{:S(2)}, u32[]{:S(2)}) collective-permute-start(bf16[256,1024]{1,0:T(8,128)(2,1)} %dynamic-slice_bitcast_fusion.7), channel_id=1, source_target_pairs={{0,1},{1,0},{2,3},{3,2},{4,5},{5,4},{6,7},{7,6},{8,9},{9,8},{10,11... | collective-permute-start | bytes 1572872 | tf_op jit(solution)/shard_map/ppermute | solution.py:14
  37.6 29.4 %all-to-all-start.1 = ((bf16[2,256,1024]{2,1,0:T(8,128)(2,1)}), bf16[2,256,1024]{2,1,0:T(8,128)(2,1)S(1)}, u32[]{:S(2)}, u32[]{:S(2)}) async-start(bf16[2,256,1024]{2,1,0:T(8,128)(2,1)} %pad_maximum_fusion.2), calls=%async_computation.1 | async-start | bytes 2097152 | tf_op jit(solution)/shard_map/all_to_all | solution.py:110
  50.1 17.4 %copy-start.10 = (bf16[256,1024]{1,0:T(8,128)(2,1)S(1)}, bf16[256,1024]{1,0:T(8,128)(2,1)}, u32[]{:S(2)}) copy-start(bf16[256,1024]{1,0:T(8,128)(2,1)} %get-tuple-element.13) | copy-start | bytes 1572868
  51.2 21.0 %collective-permute-start.1 = (f32[512,512]{0,1:T(8,128)}, f32[512,512]{0,1:T(8,128)}, u32[]{:S(2)}, u32[]{:S(2)}) collective-permute-start(f32[512,512]{0,1:T(8,128)} %dynamic-slice_bitcast_fusion.3), channel_id=1, source_target_pairs={{0,2},{2,0},{4,6},{6,4},{1,3},{3,1},{5,7},{7,5},{8,10},{10,8},{12,... | collective-permute-start | bytes 3145736 | tf_op jit(solution)/shard_map/ppermute | solution.py:69
  67.1 13.2 %copy-start.11 = (bf16[256,1024]{1,0:T(8,128)(2,1)}, bf16[256,1024]{1,0:T(8,128)(2,1)S(1)}, u32[]{:S(2)}) copy-start(bf16[256,1024]{1,0:T(8,128)(2,1)S(1)} %dynamic-slice_bitcast_fusion.6) | copy-start | bytes 1572868
  67.1 13.2 %collective-permute-start.5 = (bf16[256,1024]{1,0:T(8,128)(2,1)S(1)}, bf16[256,1024]{1,0:T(8,128)(2,1)}, u32[]{:S(2)}, u32[]{:S(2)}) collective-permute-start(bf16[256,1024]{1,0:T(8,128)(2,1)S(1)} %dynamic-slice_bitcast_fusion.6), channel_id=1, source_target_pairs={{0,1},{1,0},{2,3},{3,2},{4,5},{5,4},{6,7},{7,6},{8,9},{9,8},{10,11... | collective-permute-start | bytes 1572872 | tf_op jit(solution)/shard_map/ppermute | solution.py:14
  68.6 26.3 %all-to-all-start.2 = ((bf16[2,256,1024]{2,1,0:T(8,128)(2,1)}), bf16[2,256,1024]{2,1,0:T(8,128)(2,1)S(1)}, u32[]{:S(2)}, u32[]{:S(2)}) async-start(bf16[2,256,1024]{2,1,0:T(8,128)(2,1)} %pad_maximum_fusion.4), calls=%async_computation.2 | async-start | bytes 2097152 | tf_op jit(solution)/shard_map/all_to_all | solution.py:110
  72.1 8.1 %copy-start.6 = (bf16[1,1024,1024]{2,1,0:T(8,128)(2,1)S(1)}, bf16[1,1024,1024]{2,1,0:T(8,128)(2,1)}, u32[]{:S(2)}) copy-start(bf16[1,1024,1024]{2,1,0:T(8,128)(2,1)} %param.3) | copy-start | bytes 6291460
  74.9 13.4 %collective-permute-start.2 = (f32[256,512]{0,1:T(8,128)}, f32[256,512]{0,1:T(8,128)S(1)}, u32[]{:S(2)}, u32[]{:S(2)}) collective-permute-start(f32[256,512]{0,1:T(8,128)} %constant_dynamic-slice_fusion.3), channel_id=1, source_target_pairs={{0,4},{2,6},{4,0},{6,2},{1,5},{3,7},{5,1},{7,3},{8,12},{10,14},{12... | collective-permute-start | bytes 1572872 | tf_op jit(solution)/shard_map/ppermute | solution.py:69
  83.9 12.9 %copy-start.9 = (bf16[256,1024]{1,0:T(8,128)(2,1)S(1)}, bf16[256,1024]{1,0:T(8,128)(2,1)}, u32[]{:S(2)}) copy-start(bf16[256,1024]{1,0:T(8,128)(2,1)} %get-tuple-element.15) | copy-start | bytes 1572868
  85.0 17.6 %collective-permute-start.6 = (f32[512,512]{0,1:T(8,128)}, f32[512,512]{0,1:T(8,128)}, u32[]{:S(2)}, u32[]{:S(2)}) collective-permute-start(f32[512,512]{0,1:T(8,128)} %dynamic-slice_bitcast_fusion.2), channel_id=1, source_target_pairs={{0,2},{2,0},{4,6},{6,4},{1,3},{3,1},{5,7},{7,5},{8,10},{10,8},{12,... | collective-permute-start | bytes 3145736 | tf_op jit(solution)/shard_map/ppermute | solution.py:69
  88.5 13.1 %collective-permute-start.3 = (bf16[256,512]{0,1:T(8,128)(2,1)S(1)}, bf16[256,512]{0,1:T(8,128)(2,1)S(1)}, u32[]{:S(2)}, u32[]{:S(2)}) collective-permute-start(bf16[256,512]{0,1:T(8,128)(2,1)S(1)} %divide_convert_fusion.3), channel_id=1, source_target_pairs={{0,4},{2,6},{4,0},{6,2},{1,5},{3,7},{5,1},{7,3},{8,12},{10,14},{12... | collective-permute-start | bytes 786440 | tf_op jit(solution)/shard_map/ppermute | solution.py:81
  95.7 13.2 %collective-permute-start.10 = (bf16[256,1024]{1,0:T(8,128)(2,1)}, bf16[256,1024]{1,0:T(8,128)(2,1)S(1)}, u32[]{:S(2)}, u32[]{:S(2)}) collective-permute-start(bf16[256,1024]{1,0:T(8,128)(2,1)} %dynamic-slice_bitcast_fusion.5), channel_id=1, source_target_pairs={{0,1},{1,0},{2,3},{3,2},{4,5},{5,4},{6,7},{7,6},{8,9},{9,8},{10,11... | collective-permute-start | bytes 1572872 | tf_op jit(solution)/shard_map/ppermute | solution.py:14
  97.9 25.2 %all-to-all-start.3 = ((bf16[2,256,1024]{2,1,0:T(8,128)(2,1)}), bf16[2,256,1024]{2,1,0:T(8,128)(2,1)S(1)}, u32[]{:S(2)}, u32[]{:S(2)}) async-start(bf16[2,256,1024]{2,1,0:T(8,128)(2,1)} %pad_maximum_fusion.6), calls=%async_computation.3 | async-start | bytes 2097152 | tf_op jit(solution)/shard_map/all_to_all | solution.py:110
  101.8 7.1 %copy-start.7 = (bf16[1,1024,1024]{2,1,0:T(8,128)(2,1)S(1)}, bf16[1,1024,1024]{2,1,0:T(8,128)(2,1)}, u32[]{:S(2)}) copy-start(bf16[1,1024,1024]{2,1,0:T(8,128)(2,1)} %param.3) | copy-start | bytes 6291460
  101.8 13.4 %collective-permute-start.4 = (bf16[512,512]{0,1:T(8,128)(2,1)S(1)}, bf16[512,512]{0,1:T(8,128)(2,1)}, u32[]{:S(2)}, u32[]{:S(2)}) collective-permute-start(bf16[512,512]{0,1:T(8,128)(2,1)S(1)} %maximum_select_fusion.7), channel_id=1, source_target_pairs={{0,2},{2,0},{4,6},{6,4},{1,3},{3,1},{5,7},{7,5},{8,10},{10,8},{12,... | collective-permute-start | bytes 1572872 | tf_op jit(solution)/shard_map/ppermute | solution.py:81
  105.3 13.6 %collective-permute-start.7 = (f32[256,512]{0,1:T(8,128)}, f32[256,512]{0,1:T(8,128)}, u32[]{:S(2)}, u32[]{:S(2)}) collective-permute-start(f32[256,512]{0,1:T(8,128)} %constant_dynamic-slice_fusion.2), channel_id=1, source_target_pairs={{0,4},{2,6},{4,0},{6,2},{1,5},{3,7},{5,1},{7,3},{8,12},{10,14},{12... | collective-permute-start | bytes 1572872 | tf_op jit(solution)/shard_map/ppermute | solution.py:69
  113.8 15.3 %collective-permute-start.11 = (f32[512,512]{0,1:T(8,128)}, f32[512,512]{0,1:T(8,128)}, u32[]{:S(2)}, u32[]{:S(2)}) collective-permute-start(f32[512,512]{0,1:T(8,128)} %dynamic-slice_bitcast_fusion.1), channel_id=1, source_target_pairs={{0,2},{2,0},{4,6},{6,4},{1,3},{3,1},{5,7},{7,5},{8,10},{10,8},{12,... | collective-permute-start | bytes 3145736 | tf_op jit(solution)/shard_map/ppermute | solution.py:69
  120.1 6.8 %collective-permute-start.8 = (bf16[256,512]{0,1:T(8,128)(2,1)S(1)}, bf16[256,512]{0,1:T(8,128)(2,1)S(1)}, u32[]{:S(2)}, u32[]{:S(2)}) collective-permute-start(bf16[256,512]{0,1:T(8,128)(2,1)S(1)} %divide_convert_fusion.2), channel_id=1, source_target_pairs={{0,4},{2,6},{4,0},{6,2},{1,5},{3,7},{5,1},{7,3},{8,12},{10,14},{12... | collective-permute-start | bytes 786440 | tf_op jit(solution)/shard_map/ppermute | solution.py:81
  123.1 13.1 %collective-permute-start.15 = (bf16[256,1024]{1,0:T(8,128)(2,1)S(1)}, bf16[256,1024]{1,0:T(8,128)(2,1)S(1)}, u32[]{:S(2)}, u32[]{:S(2)}) collective-permute-start(bf16[256,1024]{1,0:T(8,128)(2,1)S(1)} %dynamic-slice_bitcast_fusion.4), channel_id=1, source_target_pairs={{0,1},{1,0},{2,3},{3,2},{4,5},{5,4},{6,7},{7,6},{8,9},{9,8},{10,11... | collective-permute-start | bytes 1572872 | tf_op jit(solution)/shard_map/ppermute | solution.py:14
  127.0 9.2 %copy-start.8 = (bf16[1,1024,1024]{2,1,0:T(8,128)(2,1)S(1)}, bf16[1,1024,1024]{2,1,0:T(8,128)(2,1)}, u32[]{:S(2)}) copy-start(bf16[1,1024,1024]{2,1,0:T(8,128)(2,1)} %param.3) | copy-start | bytes 6291460
  127.0 12.0 %collective-permute-start.9 = (bf16[512,512]{0,1:T(8,128)(2,1)S(1)}, bf16[512,512]{0,1:T(8,128)(2,1)S(1)}, u32[]{:S(2)}, u32[]{:S(2)}) collective-permute-start(bf16[512,512]{0,1:T(8,128)(2,1)S(1)} %maximum_select_fusion.8), channel_id=1, source_target_pairs={{0,2},{2,0},{4,6},{6,4},{1,3},{3,1},{5,7},{7,5},{8,10},{10,8},{12,... | collective-permute-start | bytes 1572872 | tf_op jit(solution)/shard_map/ppermute | solution.py:81
  130.6 13.4 %collective-permute-start.12 = (f32[256,512]{0,1:T(8,128)S(1)}, f32[256,512]{0,1:T(8,128)S(1)}, u32[]{:S(2)}, u32[]{:S(2)}) collective-permute-start(f32[256,512]{0,1:T(8,128)S(1)} %constant_dynamic-slice_fusion.1), channel_id=1, source_target_pairs={{0,4},{2,6},{4,0},{6,2},{1,5},{3,7},{5,1},{7,3},{8,12},{10,14},{12... | collective-permute-start | bytes 1572872 | tf_op jit(solution)/shard_map/ppermute | solution.py:69
  137.6 15.7 %collective-permute-start.16 = (f32[512,512]{0,1:T(8,128)S(1)}, f32[512,512]{0,1:T(8,128)S(1)}, u32[]{:S(2)}, u32[]{:S(2)}) collective-permute-start(f32[512,512]{0,1:T(8,128)S(1)} %dynamic-slice_bitcast_fusion), channel_id=1, source_target_pairs={{0,2},{2,0},{4,6},{6,4},{1,3},{3,1},{5,7},{7,5},{8,10},{10,8},{12,... | collective-permute-start | bytes 3145736 | tf_op jit(solution)/shard_map/ppermute | solution.py:69
  144.3 6.9 %collective-permute-start.13 = (bf16[256,512]{0,1:T(8,128)(2,1)S(1)}, bf16[256,512]{0,1:T(8,128)(2,1)S(1)}, u32[]{:S(2)}, u32[]{:S(2)}) collective-permute-start(bf16[256,512]{0,1:T(8,128)(2,1)S(1)} %divide_convert_fusion.1), channel_id=1, source_target_pairs={{0,4},{2,6},{4,0},{6,2},{1,5},{3,7},{5,1},{7,3},{8,12},{10,14},{12... | collective-permute-start | bytes 786440 | tf_op jit(solution)/shard_map/ppermute | solution.py:81
  151.3 3.5 %collective-permute-start.14 = (bf16[512,512]{0,1:T(8,128)(2,1)S(1)}, bf16[512,512]{0,1:T(8,128)(2,1)S(1)}, u32[]{:S(2)}, u32[]{:S(2)}) collective-permute-start(bf16[512,512]{0,1:T(8,128)(2,1)S(1)} %maximum_select_fusion.9), channel_id=1, source_target_pairs={{0,2},{2,0},{4,6},{6,4},{1,3},{3,1},{5,7},{7,5},{8,10},{10,8},{12,... | collective-permute-start | bytes 1572872 | tf_op jit(solution)/shard_map/ppermute | solution.py:81
  153.5 13.6 %collective-permute-start.17 = (f32[256,512]{0,1:T(8,128)S(1)}, f32[256,512]{0,1:T(8,128)S(1)}, u32[]{:S(2)}, u32[]{:S(2)}) collective-permute-start(f32[256,512]{0,1:T(8,128)S(1)} %constant_dynamic-slice_fusion), channel_id=1, source_target_pairs={{0,4},{2,6},{4,0},{6,2},{1,5},{3,7},{5,1},{7,3},{8,12},{10,14},{12... | collective-permute-start | bytes 1572872 | tf_op jit(solution)/shard_map/ppermute | solution.py:69
  167.4 9.0 %copy-start.12 = (bf16[256,1024]{1,0:T(8,128)(2,1)S(1)}, bf16[256,1024]{1,0:T(8,128)(2,1)}, u32[]{:S(2)}) copy-start(bf16[256,1024]{1,0:T(8,128)(2,1)} %copy-done.11) | copy-start | bytes 1572868
  167.4 7.1 %collective-permute-start.18 = (bf16[256,512]{0,1:T(8,128)(2,1)S(1)}, bf16[256,512]{0,1:T(8,128)(2,1)S(1)}, u32[]{:S(2)}, u32[]{:S(2)}) collective-permute-start(bf16[256,512]{0,1:T(8,128)(2,1)S(1)} %divide_convert_fusion), channel_id=1, source_target_pairs={{0,4},{2,6},{4,0},{6,2},{1,5},{3,7},{5,1},{7,3},{8,12},{10,14},{12... | collective-permute-start | bytes 786440 | tf_op jit(solution)/shard_map/ppermute | solution.py:81
  174.6 6.5 %collective-permute-start.19 = (bf16[512,512]{0,1:T(8,128)(2,1)S(1)}, bf16[512,512]{0,1:T(8,128)(2,1)S(1)}, u32[]{:S(2)}, u32[]{:S(2)}) collective-permute-start(bf16[512,512]{0,1:T(8,128)(2,1)S(1)} %maximum_select_fusion.10), channel_id=1, source_target_pairs={{0,2},{2,0},{4,6},{6,4},{1,3},{3,1},{5,7},{7,5},{8,10},{10,8},{12,... | collective-permute-start | bytes 1572872 | tf_op jit(solution)/shard_map/ppermute | solution.py:81
  (9 other events, 26.9 us)

commit v18 on v5

--- a/solution.py
+++ b/solution.py
@@ -95,44 +95,37 @@
     share = vir_rows // aux_count
     width = vir_rows // CHUNKS
 
-    if not AUX_BY_PERMUTE:
-        first_row = lax.axis_index("aux") * share
-
     total = None
     previous = None
     rows_done = None
-    for c in range(CHUNKS):
-        piece = own[c * width:(c + 1) * width]
-        if previous is not None:
-            piece, _ = lax.optimization_barrier((piece, previous))
-        arrived = shifted_2(piece, "occ", 2)
-        previous = arrived
-        if vir_count == 2:
-            mate = shifted_2(arrived, "vir", 1)
-            block = jnp.concatenate([arrived, mate])
-            cols = [vir_pos, 1 - vir_pos]
-        else:
-            block = lax.all_gather(arrived, "vir", axis=0, tiled=True)
-            cols = list(range(vir_count))
-        col_level = jnp.concatenate(
-            [lax.dynamic_slice_in_dim(vir_energy, w * vir_rows + c * width, width) for w in cols]
-        )
+    mate = None
+    for t in range(CHUNKS + 1):
+        parts, levels = [], []
+        if t < CHUNKS:
+            piece = own[t * width:(t + 1) * width]
+            if previous is not None:
+                piece, _ = lax.optimization_barrier((piece, previous))
+            arrived = shifted_2(piece, "occ", 2)
+            previous = arrived
+            parts.append(arrived)
+            levels.append(lax.dynamic_slice_in_dim(vir_energy, vir_pos * vir_rows + t * width, width))
+        if mate is not None:
+            parts.append(mate)
+            levels.append(
+                lax.dynamic_slice_in_dim(vir_energy, (1 - vir_pos) * vir_rows + (t - 1) * width, width)
+            )
+        mate = shifted_2(arrived, "vir", 1) if t < CHUNKS else None
+        block = jnp.concatenate(parts) if len(parts) > 1 else parts[0]
+        col_level = jnp.concatenate(levels) if len(levels) > 1 else levels[0]
         partial = jnp.einsum("aq,bq->ab", own, block, preferred_element_type=jnp.float32)
-        if AUX_BY_PERMUTE:
-            summed, first = aux_reduce_scatter(partial)
-        else:
-            summed = lax.psum_scatter(partial, "aux", scatter_dimension=0, tiled=True)
-            first = first_row
+        summed, first = aux_reduce_scatter(partial)
         if rows_done is not None:
             summed, _ = lax.optimization_barrier((summed, rows_done))
         row_level = lax.dynamic_slice_in_dim(vir_energy, vir_pos * vir_rows + first, share)
         amplitudes = (summed / (pair_level - row_level[:, None] - col_level[None, :])).astype(
             jnp.bfloat16
         )
-        if AUX_BY_PERMUTE:
-            rows = aux_all_gather(amplitudes)
-        else:
-            rows = lax.all_gather(amplitudes, "aux", axis=0, tiled=True)
+        rows = aux_all_gather(amplitudes)
         rows_done = rows
         term = jnp.dot(rows, block, preferred_element_type=jnp.float32)
         total = term if total is None else total + term
@@ -143,7 +136,8 @@
 
 def on_device(integrals, occ_energy, vir_energy):
     cycle_size = lax.axis_size("occ")
-    if integrals.shape[0] == 1 and 4 % cycle_size == 0 and integrals.shape[1] % (CHUNKS * 8) == 0:
+    pairs_here = integrals.shape[0] == 1 and 4 % cycle_size == 0 and lax.axis_size("vir") == 2
+    if pairs_here and integrals.shape[1] % (CHUNKS * 8) == 0:
         return paired_plan(integrals, occ_energy, vir_energy)
     return general_plan(integrals, occ_energy, vir_energy)
 

time: 176 us -> 172 us (0.977)
  waiting for transfers between devices: 109 us -> 103 us
  local copies, waits for them, and re-layouts: 8.45 us -> 11.7 us
  starting transfers between devices: 37.9 us -> 35.5 us
    ppermute x8, waiting for transfers between devices: 86.7 us -> 70.8 us  [shifted_2(): lax.ppermute(value, axis, [(i, (i + by) % count) for i in range(count)])]
    ppermute x8 -> x10, waiting for transfers between devices: 8.3 us -> 21.4 us  [aux_all_gather(): other = lax.ppermute(x, 'aux', xor_pairs(count, step))]
    ppermute x8 -> x10, starting transfers between devices: 22.9 us -> 17.5 us  [aux_all_gather(): other = lax.ppermute(x, 'aux', xor_pairs(count, step))]
    ppermute x8 -> x10, waiting for transfers between devices: 13.9 us -> 10.7 us  [aux_reduce_scatter(): x = keep + lax.ppermute(send, 'aux', xor_pairs(count, step))]
    ppermute x8 -> x10, starting transfers between devices: 8.82 us -> 10.8 us  [aux_reduce_scatter(): x = keep + lax.ppermute(send, 'aux', xor_pairs(count, step))]
    unnamed x10 -> x17, local copies, waits for them, and re-layouts: 2.41 us -> 3.7 us
    dot_general x4 -> x5, matrix products: 6.73 us -> 6.41 us  [paired_plan(): jnp.einsum('aq,bq->ab', own, block, preferred_element_type=jnp.float32)]
    dot_general x4 -> x5, matrix products: 7.22 us -> 7.44 us  [paired_plan(): term = jnp.dot(rows, block, preferred_element_type=jnp.float32)]
  transfers between devices with their start and end apart: 24 -> 28, of which waited for: 12 -> 12; matrix products, arithmetic and copies ran while one was open for 11% -> 14% of each run, Pallas kernels for 0% -> 0%
where the time goes in v18:
time: 172 us; the launch traced here: 171 us
  waiting for transfers between devices  103 us (60%)
  starting transfers between devices  35.5 us (21%)
  matrix products  13.9 us (8%)
  local copies, waits for them, and re-layouts  11.7 us (7%)
  other arithmetic  5.85 us (3%)
    ppermute x8, waiting for transfers between devices, shifted_2(): lax.ppermute(value, axis, [(i, (i + by) % count) for i in range(count)])  70.8 us
    ppermute x10, waiting for transfers between devices, aux_all_gather(): other = lax.ppermute(x, 'aux', xor_pairs(count, step))  21.4 us
    ppermute x10, starting transfers between devices, aux_all_gather(): other = lax.ppermute(x, 'aux', xor_pairs(count, step))  17.5 us
    ppermute x10, starting transfers between devices, aux_reduce_scatter(): x = keep + lax.ppermute(send, 'aux', xor_pairs(count, step))  10.8 us
    ppermute x10, waiting for transfers between devices, aux_reduce_scatter(): x = keep + lax.ppermute(send, 'aux', xor_pairs(count, step))  10.7 us
    dot_general x5, matrix products, paired_plan(): term = jnp.dot(rows, block, preferred_element_type=jnp.float32)  7.44 us
    ppermute x8, starting transfers between devices, shifted_2(): lax.ppermute(value, axis, [(i, (i + by) % count) for i in range(count)])  7.15 us
    dot_general x5, matrix products, paired_plan(): jnp.einsum('aq,bq->ab', own, block, preferred_element_type=jnp.float32)  6.41 us
  transfers between devices with their start and end apart: 28, of which 12 were waited for; matrix products, arithmetic and copies ran while one was open for 14% of the time, Pallas kernels for 0%

profile of v18, /device:TPU:1, one launch (start us, length us, event | category | flops | bytes accessed | tf_op | source)
XLA Modules:
  0.0 171.3 jit_solution(10651030653565772926)
XLA Ops:
  0.0 2.8 %slice_bitcast_fusion.3 = (bf16[256,1024]{1,0:T(8,128)(2,1)S(1)}, bf16[256,1024]{1,0:T(8,128)(2,1)}, bf16[256,1024]{1,0:T(8,128)(2,1)}, bf16[256,1024]{1,0:T(8,128)(2,1)}) fusion(bf16[1,1024,1024]{2,1,0:T(8,128)(2,1)} %param.3), kind=kLoop, calls=%fused_computation.44 | loop fusion | bytes 4194304 | tf_op jit(solution)/shard_map/slice | solution.py:105
  2.8 3.1 %collective-permute-start = (bf16[256,1024]{1,0:T(8,128)(2,1)S(1)}, bf16[256,1024]{1,0:T(8,128)(2,1)S(1)}, u32[]{:S(2)}, u32[]{:S(2)}) collective-permute-start(bf16[256,1024]{1,0:T(8,128)(2,1)S(1)} %get-tuple-element.19), channel_id=1, source_target_pairs={{0,16},{8,24},{16,0},{24,8},{1,17},{9,25},{17,1},{25,9},{2,18},{10... | collective-permute-start | bytes 1572872 | tf_op jit(solution)/shard_map/ppermute | solution.py:13
  6.0 22.9 %collective-permute-done = bf16[256,1024]{1,0:T(8,128)(2,1)S(1)} collective-permute-done((bf16[256,1024]{1,0:T(8,128)(2,1)S(1)}, bf16[256,1024]{1,0:T(8,128)(2,1)S(1)}, u32[]{:S(2)}, u32[]{:S(2)}) %collective-permute-start) | collective-permute-done | bytes 524320 | tf_op jit(solution)/shard_map/ppermute | solution.py:13
  29.7 1.8 %fusion.9 = f32[1024,256]{1,0:T(8,128)S(1)} fusion(bf16[256,1024]{1,0:T(8,128)(2,1)} %copy-done.3, bf16[1,1024,1024]{2,1,0:T(8,128)(2,1)S(1)} %copy-done), kind=kOutput, calls=%fused_computation.10 | convolution fusion | flops 536870912 | bytes 3670016 | tf_op jit(solution)/shard_map/aq,bq->ab/dot_general | solution.py:120
  35.6 1.3 collective-permute-start.6
  36.9 17.4 %collective-permute-done.5 = bf16[256,1024]{1,0:T(8,128)(2,1)} collective-permute-done((bf16[256,1024]{1,0:T(8,128)(2,1)}, bf16[256,1024]{1,0:T(8,128)(2,1)}, u32[]{:S(2)}, u32[]{:S(2)}) %collective-permute-start.5) | collective-permute-done | bytes 524320 | tf_op jit(solution)/shard_map/ppermute | solution.py:13
  63.3 3.5 %collective-permute-start.7 = (f32[512,512]{0,1:T(8,128)}, f32[512,512]{0,1:T(8,128)}, u32[]{:S(2)}, u32[]{:S(2)}) collective-permute-start(f32[512,512]{0,1:T(8,128)} %dynamic-slice_bitcast_fusion.2), channel_id=1, source_target_pairs={{0,2},{2,0},{4,6},{6,4},{1,3},{3,1},{5,7},{7,5},{8,10},{10,8},{12,... | collective-permute-start | bytes 3145736 | tf_op jit(solution)/shard_map/ppermute | solution.py:68
  66.9 2.7 %collective-permute-start.4 = (bf16[512,256]{1,0:T(8,128)(2,1)S(1)}, bf16[512,256]{1,0:T(8,128)(2,1)S(1)}, u32[]{:S(2)}, u32[]{:S(2)}) collective-permute-start(bf16[512,256]{1,0:T(8,128)(2,1)S(1)} %maximum_select_fusion.11), channel_id=1, source_target_pairs={{0,2},{2,0},{4,6},{6,4},{1,3},{3,1},{5,7},{7,5},{8,10},{10,8},{12,... | collective-permute-start | bytes 786440 | tf_op jit(solution)/shard_map/ppermute | solution.py:80
  69.6 10.8 %collective-permute-done.11 = bf16[256,1024]{1,0:T(8,128)(2,1)} collective-permute-done((bf16[256,1024]{1,0:T(8,128)(2,1)}, bf16[256,1024]{1,0:T(8,128)(2,1)}, u32[]{:S(2)}, u32[]{:S(2)}) %collective-permute-start.11) | collective-permute-done | bytes 524320 | tf_op jit(solution)/shard_map/ppermute | solution.py:13
  82.6 1.3 fusion.5
  85.7 1.4 bitcast_add_fusion.2
  88.5 16.8 %collective-permute-done.17 = bf16[256,1024]{1,0:T(8,128)(2,1)S(1)} collective-permute-done((bf16[256,1024]{1,0:T(8,128)(2,1)}, bf16[256,1024]{1,0:T(8,128)(2,1)S(1)}, u32[]{:S(2)}, u32[]{:S(2)}) %collective-permute-start.17) | collective-permute-done | bytes 524320 | tf_op jit(solution)/shard_map/ppermute | solution.py:13
  105.4 1.3 fusion.3
  108.4 1.3 collective-permute-start.9
  110.2 5.7 %collective-permute-done.9 = bf16[256,512]{0,1:T(8,128)(2,1)S(1)} collective-permute-done((bf16[256,512]{0,1:T(8,128)(2,1)S(1)}, bf16[256,512]{0,1:T(8,128)(2,1)S(1)}, u32[]{:S(2)}, u32[]{:S(2)}) %collective-permute-start.9) | collective-permute-done | bytes 262176 | tf_op jit(solution)/shard_map/ppermute | solution.py:80
  116.1 2.0 %collective-permute-start.10 = (bf16[512,512]{0,1:T(8,128)(2,1)S(1)}, bf16[512,512]{0,1:T(8,128)(2,1)S(1)}, u32[]{:S(2)}, u32[]{:S(2)}) collective-permute-start(bf16[512,512]{0,1:T(8,128)(2,1)S(1)} %maximum_select_fusion.4), channel_id=1, source_target_pairs={{0,2},{2,0},{4,6},{6,4},{1,3},{3,1},{5,7},{7,5},{8,10},{10,8},{12,... | collective-permute-start | bytes 1572872 | tf_op jit(solution)/shard_map/ppermute | solution.py:80
  118.1 2.8 %collective-permute-done.23 = bf16[256,1024]{1,0:T(8,128)(2,1)S(1)} collective-permute-done((bf16[256,1024]{1,0:T(8,128)(2,1)S(1)}, bf16[256,1024]{1,0:T(8,128)(2,1)S(1)}, u32[]{:S(2)}, u32[]{:S(2)}) %collective-permute-start.23) | collective-permute-done | bytes 524320 | tf_op jit(solution)/shard_map/ppermute | solution.py:13
  122.6 4.6 %collective-permute-done.14 = f32[256,512]{0,1:T(8,128)S(1)} collective-permute-done((f32[256,512]{0,1:T(8,128)S(1)}, f32[256,512]{0,1:T(8,128)S(1)}, u32[]{:S(2)}, u32[]{:S(2)}) %collective-permute-start.14) | collective-permute-done | bytes 524320 | tf_op jit(solution)/shard_map/ppermute | solution.py:68
  127.8 1.3 collective-permute-start.15
  129.7 4.8 %collective-permute-done.15 = bf16[256,512]{0,1:T(8,128)(2,1)S(1)} collective-permute-done((bf16[256,512]{0,1:T(8,128)(2,1)S(1)}, bf16[256,512]{0,1:T(8,128)(2,1)S(1)}, u32[]{:S(2)}, u32[]{:S(2)}) %collective-permute-start.15) | collective-permute-done | bytes 262176 | tf_op jit(solution)/shard_map/ppermute | solution.py:80
  134.6 3.9 %collective-permute-start.16 = (bf16[512,512]{0,1:T(8,128)(2,1)S(1)}, bf16[512,512]{0,1:T(8,128)(2,1)S(1)}, u32[]{:S(2)}, u32[]{:S(2)}) collective-permute-start(bf16[512,512]{0,1:T(8,128)(2,1)S(1)} %maximum_select_fusion.5), channel_id=1, source_target_pairs={{0,2},{2,0},{4,6},{6,4},{1,3},{3,1},{5,7},{7,5},{8,10},{10,8},{12,... | collective-permute-start | bytes 1572872 | tf_op jit(solution)/shard_map/ppermute | solution.py:80
  138.6 1.3 collective-permute-start.25
  139.9 5.8 %collective-permute-done.20 = f32[256,512]{0,1:T(8,128)S(1)} collective-permute-done((f32[256,512]{0,1:T(8,128)S(1)}, f32[256,512]{0,1:T(8,128)S(1)}, u32[]{:S(2)}, u32[]{:S(2)}) %collective-permute-start.20) | collective-permute-done | bytes 524320 | tf_op jit(solution)/shard_map/ppermute | solution.py:68
  146.3 1.3 collective-permute-start.21
  148.3 8.6 %collective-permute-done.21 = bf16[256,512]{0,1:T(8,128)(2,1)S(1)} collective-permute-done((bf16[256,512]{0,1:T(8,128)(2,1)S(1)}, bf16[256,512]{0,1:T(8,128)(2,1)S(1)}, u32[]{:S(2)}, u32[]{:S(2)}) %collective-permute-start.21) | collective-permute-done | bytes 262176 | tf_op jit(solution)/shard_map/ppermute | solution.py:80
  157.1 2.2 %collective-permute-start.22 = (bf16[512,512]{0,1:T(8,128)(2,1)S(1)}, bf16[512,512]{0,1:T(8,128)(2,1)S(1)}, u32[]{:S(2)}, u32[]{:S(2)}) collective-permute-start(bf16[512,512]{0,1:T(8,128)(2,1)S(1)} %maximum_select_fusion.6), channel_id=1, source_target_pairs={{0,2},{2,0},{4,6},{6,4},{1,3},{3,1},{5,7},{7,5},{8,10},{10,8},{12,... | collective-permute-start | bytes 1572872 | tf_op jit(solution)/shard_map/ppermute | solution.py:80
  159.3 1.5 fusion.22
  161.2 1.3 collective-permute-start.26
  162.5 1.3 fusion.23
  163.8 2.2 %collective-permute-done.26 = bf16[256,256]{1,0:T(8,128)(2,1)S(1)} collective-permute-done((bf16[256,256]{1,0:T(8,128)(2,1)S(1)}, bf16[256,256]{1,0:T(8,128)(2,1)S(1)}, u32[]{:S(2)}, u32[]{:S(2)}) %collective-permute-start.26) | collective-permute-done | bytes 131104 | tf_op jit(solution)/shard_map/ppermute | solution.py:80
  167.4 1.3 fusion.24
  168.7 2.6 %fusion = bf16[1,1024,1024]{2,1,0:T(8,128)(2,1)} fusion(f32[1024,1024]{1,0:T(8,128)S(1)} %fusion.24, f32[1024,1024]{1,0:T(8,128)S(1)} %fusion.23, f32[1024,1024]{1,0:T(8,128)S(1)} %fusion.21, f32[1024,1024]{1,0:T(8,128)S(1)} %fusion.22, bf16[256,1024]{1,0:T(8,128)(2,1)S(1)} %collective-permute-done.23, bf16[512,256]{1,0:T(8,128)(2,1)S(1)} %collective-permute-done.27, ...), kind=kOutput, calls=%fused_computation.1 | convolution fusion | flops 545521664 | bytes 19922944 | tf_op jit(solution)/shard_map/dot_general | solution.py:130
  (93 shorter events, 26.5 us)
Async XLA Ops:
  0.0 29.7 %copy-start = (bf16[1,1024,1024]{2,1,0:T(8,128)(2,1)S(1)}, bf16[1,1024,1024]{2,1,0:T(8,128)(2,1)}, u32[]{:S(2)}) copy-start(bf16[1,1024,1024]{2,1,0:T(8,128)(2,1)} %param.3) | copy-start | bytes 6291460
  2.8 26.0 %collective-permute-start = (bf16[256,1024]{1,0:T(8,128)(2,1)S(1)}, bf16[256,1024]{1,0:T(8,128)(2,1)S(1)}, u32[]{:S(2)}, u32[]{:S(2)}) collective-permute-start(bf16[256,1024]{1,0:T(8,128)(2,1)S(1)} %get-tuple-element.19), channel_id=1, source_target_pairs={{0,16},{8,24},{16,0},{24,8},{1,17},{9,25},{17,1},{25,9},{2,18},{10... | collective-permute-start | bytes 1572872 | tf_op jit(solution)/shard_map/ppermute | solution.py:13
  29.7 3.9 %copy-start.6 = (f32[4]{0:T(128)S(1)}, f32[4]{0:T(128)}, u32[]{:S(2)}) copy-start(f32[4]{0:T(128)} %param.4) | copy-start | bytes 52
  29.7 5.8 %copy-start.5 = (f32[2048]{0:T(1024)S(1)}, f32[2048]{0:T(1024)}, u32[]{:S(2)}) copy-start(f32[2048]{0:T(1024)} %param.5) | copy-start | bytes 24580
  29.7 24.6 %collective-permute-start.5 = (bf16[256,1024]{1,0:T(8,128)(2,1)}, bf16[256,1024]{1,0:T(8,128)(2,1)}, u32[]{:S(2)}, u32[]{:S(2)}) collective-permute-start(bf16[256,1024]{1,0:T(8,128)(2,1)} %get-tuple-element.12), channel_id=1, source_target_pairs={{0,16},{8,24},{16,0},{24,8},{1,17},{9,25},{17,1},{25,9},{2,18},{10... | collective-permute-start | bytes 1572872 | tf_op jit(solution)/shard_map/ppermute | solution.py:13
  32.3 22.0 %collective-permute-start.1 = (f32[512,256]{1,0:T(8,128)}, f32[512,256]{1,0:T(8,128)}, u32[]{:S(2)}, u32[]{:S(2)}) collective-permute-start(f32[512,256]{1,0:T(8,128)} %constant_dynamic-slice_fusion.5), channel_id=1, source_target_pairs={{0,2},{2,0},{4,6},{6,4},{1,3},{3,1},{5,7},{7,5},{8,10},{10,8},{12,... | collective-permute-start | bytes 1572872 | tf_op jit(solution)/shard_map/ppermute | solution.py:68
  35.6 23.0 %collective-permute-start.6 = (bf16[256,1024]{1,0:T(8,128)(2,1)}, bf16[256,1024]{1,0:T(8,128)(2,1)}, u32[]{:S(2)}, u32[]{:S(2)}) collective-permute-start(bf16[256,1024]{1,0:T(8,128)(2,1)} %copy-done.3), channel_id=1, source_target_pairs={{0,1},{1,0},{2,3},{3,2},{4,5},{5,4},{6,7},{7,6},{8,9},{9,8},{10,11... | collective-permute-start | bytes 1572872 | tf_op jit(solution)/shard_map/ppermute | solution.py:13
  54.3 26.1 %collective-permute-start.11 = (bf16[256,1024]{1,0:T(8,128)(2,1)}, bf16[256,1024]{1,0:T(8,128)(2,1)}, u32[]{:S(2)}, u32[]{:S(2)}) collective-permute-start(bf16[256,1024]{1,0:T(8,128)(2,1)} %get-tuple-element.14), channel_id=1, source_target_pairs={{0,16},{8,24},{16,0},{24,8},{1,17},{9,25},{17,1},{25,9},{2,18},{10... | collective-permute-start | bytes 1572872 | tf_op jit(solution)/shard_map/ppermute | solution.py:13
  55.5 5.7 %collective-permute-start.2 = (f32[256,256]{1,0:T(8,128)S(1)}, f32[256,256]{1,0:T(8,128)S(1)}, u32[]{:S(2)}, u32[]{:S(2)}) collective-permute-start(f32[256,256]{1,0:T(8,128)S(1)} %constant_dynamic-slice_fusion.4), channel_id=1, source_target_pairs={{0,4},{2,6},{4,0},{6,2},{1,5},{3,7},{5,1},{7,3},{8,12},{10,14},{12... | collective-permute-start | bytes 786440 | tf_op jit(solution)/shard_map/ppermute | solution.py:68
  56.2 25.3 %collective-permute-start.12 = (bf16[256,1024]{1,0:T(8,128)(2,1)}, bf16[256,1024]{1,0:T(8,128)(2,1)}, u32[]{:S(2)}, u32[]{:S(2)}) collective-permute-start(bf16[256,1024]{1,0:T(8,128)(2,1)} %collective-permute-done.5), channel_id=1, source_target_pairs={{0,1},{1,0},{2,3},{3,2},{4,5},{5,4},{6,7},{7,6},{8,9},{9,8},{10,11... | collective-permute-start | bytes 1572872 | tf_op jit(solution)/shard_map/ppermute | solution.py:13
  61.3 5.5 %collective-permute-start.3 = (bf16[256,256]{1,0:T(8,128)(2,1)S(1)}, bf16[256,256]{1,0:T(8,128)(2,1)S(1)}, u32[]{:S(2)}, u32[]{:S(2)}) collective-permute-start(bf16[256,256]{1,0:T(8,128)(2,1)S(1)} %divide_convert_fusion.4), channel_id=1, source_target_pairs={{0,4},{2,6},{4,0},{6,2},{1,5},{3,7},{5,1},{7,3},{8,12},{10,14},{12... | collective-permute-start | bytes 393224 | tf_op jit(solution)/shard_map/ppermute | solution.py:80
  63.3 22.4 %collective-permute-start.7 = (f32[512,512]{0,1:T(8,128)}, f32[512,512]{0,1:T(8,128)}, u32[]{:S(2)}, u32[]{:S(2)}) collective-permute-start(f32[512,512]{0,1:T(8,128)} %dynamic-slice_bitcast_fusion.2), channel_id=1, source_target_pairs={{0,2},{2,0},{4,6},{6,4},{1,3},{3,1},{5,7},{7,5},{8,10},{10,8},{12,... | collective-permute-start | bytes 3145736 | tf_op jit(solution)/shard_map/ppermute | solution.py:68
  66.9 18.6 %collective-permute-start.4 = (bf16[512,256]{1,0:T(8,128)(2,1)S(1)}, bf16[512,256]{1,0:T(8,128)(2,1)S(1)}, u32[]{:S(2)}, u32[]{:S(2)}) collective-permute-start(bf16[512,256]{1,0:T(8,128)(2,1)S(1)} %maximum_select_fusion.11), channel_id=1, source_target_pairs={{0,2},{2,0},{4,6},{6,4},{1,3},{3,1},{5,7},{7,5},{8,10},{10,8},{12,... | collective-permute-start | bytes 786440 | tf_op jit(solution)/shard_map/ppermute | solution.py:80
  80.4 24.9 %collective-permute-start.17 = (bf16[256,1024]{1,0:T(8,128)(2,1)}, bf16[256,1024]{1,0:T(8,128)(2,1)S(1)}, u32[]{:S(2)}, u32[]{:S(2)}) collective-permute-start(bf16[256,1024]{1,0:T(8,128)(2,1)} %get-tuple-element.16), channel_id=1, source_target_pairs={{0,16},{8,24},{16,0},{24,8},{1,17},{9,25},{17,1},{25,9},{2,18},{10... | collective-permute-start | bytes 1572872 | tf_op jit(solution)/shard_map/ppermute | solution.py:13
  84.0 25.7 %collective-permute-start.13 = (f32[512,512]{0,1:T(8,128)S(1)}, f32[512,512]{0,1:T(8,128)S(1)}, u32[]{:S(2)}, u32[]{:S(2)}) collective-permute-start(f32[512,512]{0,1:T(8,128)S(1)} %dynamic-slice_bitcast_fusion.1), channel_id=1, source_target_pairs={{0,2},{2,0},{4,6},{6,4},{1,3},{3,1},{5,7},{7,5},{8,10},{10,8},{12,... | collective-permute-start | bytes 3145736 | tf_op jit(solution)/shard_map/ppermute | solution.py:68
  84.8 20.6 %collective-permute-start.18 = (bf16[256,1024]{1,0:T(8,128)(2,1)}, bf16[256,1024]{1,0:T(8,128)(2,1)S(1)}, u32[]{:S(2)}, u32[]{:S(2)}) collective-permute-start(bf16[256,1024]{1,0:T(8,128)(2,1)} %collective-permute-done.11), channel_id=1, source_target_pairs={{0,1},{1,0},{2,3},{3,2},{4,5},{5,4},{6,7},{7,6},{8,9},{9,8},{10,11... | collective-permute-start | bytes 1572872 | tf_op jit(solution)/shard_map/ppermute | solution.py:13
  87.2 20.9 %collective-permute-start.8 = (f32[256,512]{0,1:T(8,128)S(1)}, f32[256,512]{0,1:T(8,128)S(1)}, u32[]{:S(2)}, u32[]{:S(2)}) collective-permute-start(f32[256,512]{0,1:T(8,128)S(1)} %constant_dynamic-slice_fusion.3), channel_id=1, source_target_pairs={{0,4},{2,6},{4,0},{6,2},{1,5},{3,7},{5,1},{7,3},{8,12},{10,14},{12... | collective-permute-start | bytes 1572872 | tf_op jit(solution)/shard_map/ppermute | solution.py:68
  106.8 22.3 %collective-permute-start.19 = (f32[512,512]{0,1:T(8,128)S(1)}, f32[512,512]{0,1:T(8,128)S(1)}, u32[]{:S(2)}, u32[]{:S(2)}) collective-permute-start(f32[512,512]{0,1:T(8,128)S(1)} %dynamic-slice_bitcast_fusion), channel_id=1, source_target_pairs={{0,2},{2,0},{4,6},{6,4},{1,3},{3,1},{5,7},{7,5},{8,10},{10,8},{12,... | collective-permute-start | bytes 3145736 | tf_op jit(solution)/shard_map/ppermute | solution.py:68
  107.4 13.5 %collective-permute-start.23 = (bf16[256,1024]{1,0:T(8,128)(2,1)S(1)}, bf16[256,1024]{1,0:T(8,128)(2,1)S(1)}, u32[]{:S(2)}, u32[]{:S(2)}) collective-permute-start(bf16[256,1024]{1,0:T(8,128)(2,1)S(1)} %collective-permute-done.17), channel_id=1, source_target_pairs={{0,1},{1,0},{2,3},{3,2},{4,5},{5,4},{6,7},{7,6},{8,9},{9,8},{10,11... | collective-permute-start | bytes 1572872 | tf_op jit(solution)/shard_map/ppermute | solution.py:13
  108.4 7.6 %collective-permute-start.9 = (bf16[256,512]{0,1:T(8,128)(2,1)S(1)}, bf16[256,512]{0,1:T(8,128)(2,1)S(1)}, u32[]{:S(2)}, u32[]{:S(2)}) collective-permute-start(bf16[256,512]{0,1:T(8,128)(2,1)S(1)} %divide_convert_fusion.2), channel_id=1, source_target_pairs={{0,4},{2,6},{4,0},{6,2},{1,5},{3,7},{5,1},{7,3},{8,12},{10,14},{12... | collective-permute-start | bytes 786440 | tf_op jit(solution)/shard_map/ppermute | solution.py:80
  109.9 17.3 %collective-permute-start.14 = (f32[256,512]{0,1:T(8,128)S(1)}, f32[256,512]{0,1:T(8,128)S(1)}, u32[]{:S(2)}, u32[]{:S(2)}) collective-permute-start(f32[256,512]{0,1:T(8,128)S(1)} %constant_dynamic-slice_fusion.2), channel_id=1, source_target_pairs={{0,4},{2,6},{4,0},{6,2},{1,5},{3,7},{5,1},{7,3},{8,12},{10,14},{12... | collective-permute-start | bytes 1572872 | tf_op jit(solution)/shard_map/ppermute | solution.py:68
  116.1 11.2 %collective-permute-start.10 = (bf16[512,512]{0,1:T(8,128)(2,1)S(1)}, bf16[512,512]{0,1:T(8,128)(2,1)S(1)}, u32[]{:S(2)}, u32[]{:S(2)}) collective-permute-start(bf16[512,512]{0,1:T(8,128)(2,1)S(1)} %maximum_select_fusion.4), channel_id=1, source_target_pairs={{0,2},{2,0},{4,6},{6,4},{1,3},{3,1},{5,7},{7,5},{8,10},{10,8},{12,... | collective-permute-start | bytes 1572872 | tf_op jit(solution)/shard_map/ppermute | solution.py:80
  121.7 16.7 %collective-permute-start.24 = (f32[512,256]{1,0:T(8,128)S(1)}, f32[512,256]{1,0:T(8,128)S(1)}, u32[]{:S(2)}, u32[]{:S(2)}) collective-permute-start(f32[512,256]{1,0:T(8,128)S(1)} %dynamic-slice_bitcast_fusion.3), channel_id=1, source_target_pairs={{0,2},{2,0},{4,6},{6,4},{1,3},{3,1},{5,7},{7,5},{8,10},{10,8},{12,... | collective-permute-start | bytes 1572872 | tf_op jit(solution)/shard_map/ppermute | solution.py:68
  127.8 6.7 %collective-permute-start.15 = (bf16[256,512]{0,1:T(8,128)(2,1)S(1)}, bf16[256,512]{0,1:T(8,128)(2,1)S(1)}, u32[]{:S(2)}, u32[]{:S(2)}) collective-permute-start(bf16[256,512]{0,1:T(8,128)(2,1)S(1)} %divide_convert_fusion.1), channel_id=1, source_target_pairs={{0,4},{2,6},{4,0},{6,2},{1,5},{3,7},{5,1},{7,3},{8,12},{10,14},{12... | collective-permute-start | bytes 786440 | tf_op jit(solution)/shard_map/ppermute | solution.py:80
  129.4 16.3 %collective-permute-start.20 = (f32[256,512]{0,1:T(8,128)S(1)}, f32[256,512]{0,1:T(8,128)S(1)}, u32[]{:S(2)}, u32[]{:S(2)}) collective-permute-start(f32[256,512]{0,1:T(8,128)S(1)} %constant_dynamic-slice_fusion.1), channel_id=1, source_target_pairs={{0,4},{2,6},{4,0},{6,2},{1,5},{3,7},{5,1},{7,3},{8,12},{10,14},{12... | collective-permute-start | bytes 1572872 | tf_op jit(solution)/shard_map/ppermute | solution.py:68
  134.6 11.2 %collective-permute-start.16 = (bf16[512,512]{0,1:T(8,128)(2,1)S(1)}, bf16[512,512]{0,1:T(8,128)(2,1)S(1)}, u32[]{:S(2)}, u32[]{:S(2)}) collective-permute-start(bf16[512,512]{0,1:T(8,128)(2,1)S(1)} %maximum_select_fusion.5), channel_id=1, source_target_pairs={{0,2},{2,0},{4,6},{6,4},{1,3},{3,1},{5,7},{7,5},{8,10},{10,8},{12,... | collective-permute-start | bytes 1572872 | tf_op jit(solution)/shard_map/ppermute | solution.py:80
  138.6 9.0 %copy-start.4 = (bf16[256,1024]{1,0:T(8,128)(2,1)S(1)}, bf16[256,1024]{1,0:T(8,128)(2,1)}, u32[]{:S(2)}) copy-start(bf16[256,1024]{1,0:T(8,128)(2,1)} %copy-done.3) | copy-start | bytes 1572868
  138.6 20.7 %collective-permute-start.25 = (f32[256,256]{1,0:T(8,128)S(1)}, f32[256,256]{1,0:T(8,128)S(1)}, u32[]{:S(2)}, u32[]{:S(2)}) collective-permute-start(f32[256,256]{1,0:T(8,128)S(1)} %constant_dynamic-slice_fusion), channel_id=1, source_target_pairs={{0,4},{2,6},{4,0},{6,2},{1,5},{3,7},{5,1},{7,3},{8,12},{10,14},{12... | collective-permute-start | bytes 786440 | tf_op jit(solution)/shard_map/ppermute | solution.py:68
  146.3 10.7 %collective-permute-start.21 = (bf16[256,512]{0,1:T(8,128)(2,1)S(1)}, bf16[256,512]{0,1:T(8,128)(2,1)S(1)}, u32[]{:S(2)}, u32[]{:S(2)}) collective-permute-start(bf16[256,512]{0,1:T(8,128)(2,1)S(1)} %divide_convert_fusion), channel_id=1, source_target_pairs={{0,4},{2,6},{4,0},{6,2},{1,5},{3,7},{5,1},{7,3},{8,12},{10,14},{12... | collective-permute-start | bytes 786440 | tf_op jit(solution)/shard_map/ppermute | solution.py:80
  157.1 3.7 %collective-permute-start.22 = (bf16[512,512]{0,1:T(8,128)(2,1)S(1)}, bf16[512,512]{0,1:T(8,128)(2,1)S(1)}, u32[]{:S(2)}, u32[]{:S(2)}) collective-permute-start(bf16[512,512]{0,1:T(8,128)(2,1)S(1)} %maximum_select_fusion.6), channel_id=1, source_target_pairs={{0,2},{2,0},{4,6},{6,4},{1,3},{3,1},{5,7},{7,5},{8,10},{10,8},{12,... | collective-permute-start | bytes 1572872 | tf_op jit(solution)/shard_map/ppermute | solution.py:80
  161.2 4.8 %collective-permute-start.26 = (bf16[256,256]{1,0:T(8,128)(2,1)S(1)}, bf16[256,256]{1,0:T(8,128)(2,1)S(1)}, u32[]{:S(2)}, u32[]{:S(2)}) collective-permute-start(bf16[256,256]{1,0:T(8,128)(2,1)S(1)} %divide_convert_fusion.3), channel_id=1, source_target_pairs={{0,4},{2,6},{4,0},{6,2},{1,5},{3,7},{5,1},{7,3},{8,12},{10,14},{12... | collective-permute-start | bytes 393224 | tf_op jit(solution)/shard_map/ppermute | solution.py:80
  166.1 2.5 %collective-permute-start.27 = (bf16[512,256]{1,0:T(8,128)(2,1)S(1)}, bf16[512,256]{1,0:T(8,128)(2,1)S(1)}, u32[]{:S(2)}, u32[]{:S(2)}) collective-permute-start(bf16[512,256]{1,0:T(8,128)(2,1)S(1)} %maximum_select_fusion.12), channel_id=1, source_target_pairs={{0,2},{2,0},{4,6},{6,4},{1,3},{3,1},{5,7},{7,5},{8,10},{10,8},{12,... | collective-permute-start | bytes 786440 | tf_op jit(solution)/shard_map/ppermute | solution.py:80
  (3 other events, 4.0 us)

commit v19 on v18

--- a/solution.py
+++ b/solution.py
@@ -102,9 +102,10 @@
     for t in range(CHUNKS + 1):
         parts, levels = [], []
         if t < CHUNKS:
-            piece = own[t * width:(t + 1) * width]
+            source = own
             if previous is not None:
-                piece, _ = lax.optimization_barrier((piece, previous))
+                source, _ = lax.optimization_barrier((own, previous))
+            piece = source[t * width:(t + 1) * width]
             arrived = shifted_2(piece, "occ", 2)
             previous = arrived
             parts.append(arrived)

time: 172 us -> 172 us (level)
    slice x1 -> x4, local copies, waits for them, and re-layouts: 2.84 us -> 4.17 us  [paired_plan(): piece = source[t * width:(t + 1) * width]]
where the time goes in v19:
time: 172 us
  waiting for transfers between devices  102 us (59%)
  starting transfers between devices  35.6 us (21%)
  matrix products  13.8 us (8%)
  local copies, waits for them, and re-layouts  12.2 us (7%)
  other arithmetic  5.9 us (3%)
  between operations  1.74 us (1%)
    ppermute x8, waiting for transfers between devices, shifted_2(): lax.ppermute(value, axis, [(i, (i + by) % count) for i in range(count)])  70.5 us
    ppermute x10, waiting for transfers between devices, aux_all_gather(): other = lax.ppermute(x, 'aux', xor_pairs(count, step))  21.4 us
    ppermute x10, starting transfers between devices, aux_all_gather(): other = lax.ppermute(x, 'aux', xor_pairs(count, step))  17.5 us
    ppermute x10, starting transfers between devices, aux_reduce_scatter(): x = keep + lax.ppermute(send, 'aux', xor_pairs(count, step))  10.8 us
    ppermute x10, waiting for transfers between devices, aux_reduce_scatter(): x = keep + lax.ppermute(send, 'aux', xor_pairs(count, step))  10.6 us
    dot_general x5, matrix products, paired_plan(): term = jnp.dot(rows, block, preferred_element_type=jnp.float32)  7.42 us
    ppermute x8, starting transfers between devices, shifted_2(): lax.ppermute(value, axis, [(i, (i + by) % count) for i in range(count)])  7.27 us
    dot_general x5, matrix products, paired_plan(): jnp.einsum('aq,bq->ab', own, block, preferred_element_type=jnp.float32)  6.4 us
  transfers between devices with their start and end apart: 28, of which 12 were waited for; matrix products, arithmetic and copies ran while one was open for 14% of the time, Pallas kernels for 0%

profile of v19, /device:TPU:1, one launch (start us, length us, event | category | flops | bytes accessed | tf_op | source)
XLA Modules:
  0.0 171.8 jit_solution(2196963776293464697)
XLA Ops:
  1.2 3.2 %collective-permute-start = (bf16[256,1024]{1,0:T(8,128)(2,1)S(1)}, bf16[256,1024]{1,0:T(8,128)(2,1)S(1)}, u32[]{:S(2)}, u32[]{:S(2)}) collective-permute-start(bf16[256,1024]{1,0:T(8,128)(2,1)S(1)} %slice_bitcast_fusion), channel_id=1, source_target_pairs={{0,16},{8,24},{16,0},{24,8},{1,17},{9,25},{17,1},{25,9},{2,18},{10... | collective-permute-start | bytes 1572872 | tf_op jit(solution)/shard_map/ppermute | solution.py:13
  4.4 22.9 %collective-permute-done = bf16[256,1024]{1,0:T(8,128)(2,1)S(1)} collective-permute-done((bf16[256,1024]{1,0:T(8,128)(2,1)S(1)}, bf16[256,1024]{1,0:T(8,128)(2,1)S(1)}, u32[]{:S(2)}, u32[]{:S(2)}) %collective-permute-start) | collective-permute-done | bytes 524320 | tf_op jit(solution)/shard_map/ppermute | solution.py:13
  27.3 2.1 %slice.17 = bf16[256,1024]{1,0:T(8,128)(2,1)} slice(bf16[1024,1024]{1,0:T(8,128)(2,1)} %bitcast.46), slice={[256:512], [0:1024]} | slice | bytes 1048576 | tf_op jit(solution)/shard_map/slice | solution.py:108
  29.4 1.8 %fusion.17 = f32[1024,256]{1,0:T(8,128)S(1)} fusion(bf16[256,1024]{1,0:T(8,128)(2,1)} %copy-done.3, bf16[1,1024,1024]{2,1,0:T(8,128)(2,1)S(1)} %copy-done), kind=kOutput, calls=%fused_computation.63 | convolution fusion | flops 536870912 | bytes 3670016 | tf_op jit(solution)/shard_map/aq,bq->ab/dot_general | solution.py:121
  35.4 1.3 collective-permute-start.6
  36.7 17.3 %collective-permute-done.5 = bf16[256,1024]{1,0:T(8,128)(2,1)} collective-permute-done((bf16[256,1024]{1,0:T(8,128)(2,1)}, bf16[256,1024]{1,0:T(8,128)(2,1)}, u32[]{:S(2)}, u32[]{:S(2)}) %collective-permute-start.5) | collective-permute-done | bytes 524320 | tf_op jit(solution)/shard_map/ppermute | solution.py:13
  63.9 3.5 %collective-permute-start.7 = (f32[512,512]{0,1:T(8,128)}, f32[512,512]{0,1:T(8,128)}, u32[]{:S(2)}, u32[]{:S(2)}) collective-permute-start(f32[512,512]{0,1:T(8,128)} %dynamic-slice_bitcast_fusion.2), channel_id=1, source_target_pairs={{0,2},{2,0},{4,6},{6,4},{1,3},{3,1},{5,7},{7,5},{8,10},{10,8},{12,... | collective-permute-start | bytes 3145736 | tf_op jit(solution)/shard_map/ppermute | solution.py:68
  67.5 2.7 %collective-permute-start.4 = (bf16[512,256]{1,0:T(8,128)(2,1)S(1)}, bf16[512,256]{1,0:T(8,128)(2,1)S(1)}, u32[]{:S(2)}, u32[]{:S(2)}) collective-permute-start(bf16[512,256]{1,0:T(8,128)(2,1)S(1)} %maximum_select_fusion.11), channel_id=1, source_target_pairs={{0,2},{2,0},{4,6},{6,4},{1,3},{3,1},{5,7},{7,5},{8,10},{10,8},{12,... | collective-permute-start | bytes 786440 | tf_op jit(solution)/shard_map/ppermute | solution.py:80
  70.2 10.8 %collective-permute-done.11 = bf16[256,1024]{1,0:T(8,128)(2,1)} collective-permute-done((bf16[256,1024]{1,0:T(8,128)(2,1)}, bf16[256,1024]{1,0:T(8,128)(2,1)}, u32[]{:S(2)}, u32[]{:S(2)}) %collective-permute-start.11) | collective-permute-done | bytes 524320 | tf_op jit(solution)/shard_map/ppermute | solution.py:13
  83.3 1.3 fusion.13
  86.4 1.4 bitcast_add_fusion.2
  89.2 16.6 %collective-permute-done.17 = bf16[256,1024]{1,0:T(8,128)(2,1)S(1)} collective-permute-done((bf16[256,1024]{1,0:T(8,128)(2,1)S(1)}, bf16[256,1024]{1,0:T(8,128)(2,1)S(1)}, u32[]{:S(2)}, u32[]{:S(2)}) %collective-permute-start.17) | collective-permute-done | bytes 524320 | tf_op jit(solution)/shard_map/ppermute | solution.py:13
  105.9 1.3 fusion.11
  108.8 1.3 collective-permute-start.9
  110.7 5.7 %collective-permute-done.9 = bf16[256,512]{0,1:T(8,128)(2,1)S(1)} collective-permute-done((bf16[256,512]{0,1:T(8,128)(2,1)S(1)}, bf16[256,512]{0,1:T(8,128)(2,1)S(1)}, u32[]{:S(2)}, u32[]{:S(2)}) %collective-permute-start.9) | collective-permute-done | bytes 262176 | tf_op jit(solution)/shard_map/ppermute | solution.py:80
  116.6 2.0 %collective-permute-start.10 = (bf16[512,512]{0,1:T(8,128)(2,1)S(1)}, bf16[512,512]{0,1:T(8,128)(2,1)S(1)}, u32[]{:S(2)}, u32[]{:S(2)}) collective-permute-start(bf16[512,512]{0,1:T(8,128)(2,1)S(1)} %maximum_select_fusion.4), channel_id=1, source_target_pairs={{0,2},{2,0},{4,6},{6,4},{1,3},{3,1},{5,7},{7,5},{8,10},{10,8},{12,... | collective-permute-start | bytes 1572872 | tf_op jit(solution)/shard_map/ppermute | solution.py:80
  118.6 2.8 %collective-permute-done.23 = bf16[256,1024]{1,0:T(8,128)(2,1)S(1)} collective-permute-done((bf16[256,1024]{1,0:T(8,128)(2,1)S(1)}, bf16[256,1024]{1,0:T(8,128)(2,1)S(1)}, u32[]{:S(2)}, u32[]{:S(2)}) %collective-permute-start.23) | collective-permute-done | bytes 524320 | tf_op jit(solution)/shard_map/ppermute | solution.py:13
  123.1 4.6 %collective-permute-done.14 = f32[256,512]{0,1:T(8,128)S(1)} collective-permute-done((f32[256,512]{0,1:T(8,128)S(1)}, f32[256,512]{0,1:T(8,128)S(1)}, u32[]{:S(2)}, u32[]{:S(2)}) %collective-permute-start.14) | collective-permute-done | bytes 524320 | tf_op jit(solution)/shard_map/ppermute | solution.py:68
  128.2 1.3 collective-permute-start.15
  130.1 4.8 %collective-permute-done.15 = bf16[256,512]{0,1:T(8,128)(2,1)S(1)} collective-permute-done((bf16[256,512]{0,1:T(8,128)(2,1)S(1)}, bf16[256,512]{0,1:T(8,128)(2,1)S(1)}, u32[]{:S(2)}, u32[]{:S(2)}) %collective-permute-start.15) | collective-permute-done | bytes 262176 | tf_op jit(solution)/shard_map/ppermute | solution.py:80
  135.1 3.9 %collective-permute-start.16 = (bf16[512,512]{0,1:T(8,128)(2,1)S(1)}, bf16[512,512]{0,1:T(8,128)(2,1)S(1)}, u32[]{:S(2)}, u32[]{:S(2)}) collective-permute-start(bf16[512,512]{0,1:T(8,128)(2,1)S(1)} %maximum_select_fusion.5), channel_id=1, source_target_pairs={{0,2},{2,0},{4,6},{6,4},{1,3},{3,1},{5,7},{7,5},{8,10},{10,8},{12,... | collective-permute-start | bytes 1572872 | tf_op jit(solution)/shard_map/ppermute | solution.py:80
  139.0 1.3 collective-permute-start.25
  140.4 5.8 %collective-permute-done.20 = f32[256,512]{0,1:T(8,128)S(1)} collective-permute-done((f32[256,512]{0,1:T(8,128)S(1)}, f32[256,512]{0,1:T(8,128)S(1)}, u32[]{:S(2)}, u32[]{:S(2)}) %collective-permute-start.20) | collective-permute-done | bytes 524320 | tf_op jit(solution)/shard_map/ppermute | solution.py:68
  146.7 1.3 collective-permute-start.21
  148.8 8.6 %collective-permute-done.21 = bf16[256,512]{0,1:T(8,128)(2,1)S(1)} collective-permute-done((bf16[256,512]{0,1:T(8,128)(2,1)S(1)}, bf16[256,512]{0,1:T(8,128)(2,1)S(1)}, u32[]{:S(2)}, u32[]{:S(2)}) %collective-permute-start.21) | collective-permute-done | bytes 262176 | tf_op jit(solution)/shard_map/ppermute | solution.py:80
  157.5 2.2 %collective-permute-start.22 = (bf16[512,512]{0,1:T(8,128)(2,1)S(1)}, bf16[512,512]{0,1:T(8,128)(2,1)S(1)}, u32[]{:S(2)}, u32[]{:S(2)}) collective-permute-start(bf16[512,512]{0,1:T(8,128)(2,1)S(1)} %maximum_select_fusion.6), channel_id=1, source_target_pairs={{0,2},{2,0},{4,6},{6,4},{1,3},{3,1},{5,7},{7,5},{8,10},{10,8},{12,... | collective-permute-start | bytes 1572872 | tf_op jit(solution)/shard_map/ppermute | solution.py:80
  159.7 1.5 fusion.22
  161.7 1.3 collective-permute-start.26
  163.0 1.3 fusion.23
  164.3 2.2 %collective-permute-done.26 = bf16[256,256]{1,0:T(8,128)(2,1)S(1)} collective-permute-done((bf16[256,256]{1,0:T(8,128)(2,1)S(1)}, bf16[256,256]{1,0:T(8,128)(2,1)S(1)}, u32[]{:S(2)}, u32[]{:S(2)}) %collective-permute-start.26) | collective-permute-done | bytes 131104 | tf_op jit(solution)/shard_map/ppermute | solution.py:80
  167.8 1.3 fusion.24
  169.1 2.6 %fusion = bf16[1,1024,1024]{2,1,0:T(8,128)(2,1)} fusion(f32[1024,1024]{1,0:T(8,128)S(1)} %fusion.24, f32[1024,1024]{1,0:T(8,128)S(1)} %fusion.23, f32[1024,1024]{1,0:T(8,128)S(1)} %fusion.21, f32[1024,1024]{1,0:T(8,128)S(1)} %fusion.22, bf16[256,1024]{1,0:T(8,128)(2,1)S(1)} %collective-permute-done.23, bf16[512,256]{1,0:T(8,128)(2,1)S(1)} %collective-permute-done.27, ...), kind=kOutput, calls=%fused_computation.1 | convolution fusion | flops 545521664 | bytes 19922944 | tf_op jit(solution)/shard_map/dot_general | solution.py:131
  (96 shorter events, 28.0 us)
Async XLA Ops:
  0.0 29.4 %copy-start = (bf16[1,1024,1024]{2,1,0:T(8,128)(2,1)S(1)}, bf16[1,1024,1024]{2,1,0:T(8,128)(2,1)}, u32[]{:S(2)}) copy-start(bf16[1,1024,1024]{2,1,0:T(8,128)(2,1)} %param.3) | copy-start | bytes 6291460
  1.2 26.1 %collective-permute-start = (bf16[256,1024]{1,0:T(8,128)(2,1)S(1)}, bf16[256,1024]{1,0:T(8,128)(2,1)S(1)}, u32[]{:S(2)}, u32[]{:S(2)}) collective-permute-start(bf16[256,1024]{1,0:T(8,128)(2,1)S(1)} %slice_bitcast_fusion), channel_id=1, source_target_pairs={{0,16},{8,24},{16,0},{24,8},{1,17},{9,25},{17,1},{25,9},{2,18},{10... | collective-permute-start | bytes 1572872 | tf_op jit(solution)/shard_map/ppermute | solution.py:13
  29.4 3.9 %copy-start.6 = (f32[4]{0:T(128)S(1)}, f32[4]{0:T(128)}, u32[]{:S(2)}) copy-start(f32[4]{0:T(128)} %param.4) | copy-start | bytes 52
  29.4 5.9 %copy-start.5 = (f32[2048]{0:T(1024)S(1)}, f32[2048]{0:T(1024)}, u32[]{:S(2)}) copy-start(f32[2048]{0:T(1024)} %param.5) | copy-start | bytes 24580
  29.4 24.6 %collective-permute-start.5 = (bf16[256,1024]{1,0:T(8,128)(2,1)}, bf16[256,1024]{1,0:T(8,128)(2,1)}, u32[]{:S(2)}, u32[]{:S(2)}) collective-permute-start(bf16[256,1024]{1,0:T(8,128)(2,1)} %slice.17), channel_id=1, source_target_pairs={{0,16},{8,24},{16,0},{24,8},{1,17},{9,25},{17,1},{25,9},{2,18},{10... | collective-permute-start | bytes 1572872 | tf_op jit(solution)/shard_map/ppermute | solution.py:13
  32.0 22.9 %collective-permute-start.1 = (f32[512,256]{1,0:T(8,128)}, f32[512,256]{1,0:T(8,128)}, u32[]{:S(2)}, u32[]{:S(2)}) collective-permute-start(f32[512,256]{1,0:T(8,128)} %constant_dynamic-slice_fusion.5), channel_id=1, source_target_pairs={{0,2},{2,0},{4,6},{6,4},{1,3},{3,1},{5,7},{7,5},{8,10},{10,8},{12,... | collective-permute-start | bytes 1572872 | tf_op jit(solution)/shard_map/ppermute | solution.py:68
  35.4 23.8 %collective-permute-start.6 = (bf16[256,1024]{1,0:T(8,128)(2,1)}, bf16[256,1024]{1,0:T(8,128)(2,1)}, u32[]{:S(2)}, u32[]{:S(2)}) collective-permute-start(bf16[256,1024]{1,0:T(8,128)(2,1)} %copy-done.3), channel_id=1, source_target_pairs={{0,1},{1,0},{2,3},{3,2},{4,5},{5,4},{6,7},{7,6},{8,9},{9,8},{10,11... | collective-permute-start | bytes 1572872 | tf_op jit(solution)/shard_map/ppermute | solution.py:13
  54.9 26.1 %collective-permute-start.11 = (bf16[256,1024]{1,0:T(8,128)(2,1)}, bf16[256,1024]{1,0:T(8,128)(2,1)}, u32[]{:S(2)}, u32[]{:S(2)}) collective-permute-start(bf16[256,1024]{1,0:T(8,128)(2,1)} %slice.18), channel_id=1, source_target_pairs={{0,16},{8,24},{16,0},{24,8},{1,17},{9,25},{17,1},{25,9},{2,18},{10... | collective-permute-start | bytes 1572872 | tf_op jit(solution)/shard_map/ppermute | solution.py:13
  56.0 5.7 %collective-permute-start.2 = (f32[256,256]{1,0:T(8,128)S(1)}, f32[256,256]{1,0:T(8,128)S(1)}, u32[]{:S(2)}, u32[]{:S(2)}) collective-permute-start(f32[256,256]{1,0:T(8,128)S(1)} %constant_dynamic-slice_fusion.4), channel_id=1, source_target_pairs={{0,4},{2,6},{4,0},{6,2},{1,5},{3,7},{5,1},{7,3},{8,12},{10,14},{12... | collective-permute-start | bytes 786440 | tf_op jit(solution)/shard_map/ppermute | solution.py:68
  56.8 25.4 %collective-permute-start.12 = (bf16[256,1024]{1,0:T(8,128)(2,1)}, bf16[256,1024]{1,0:T(8,128)(2,1)}, u32[]{:S(2)}, u32[]{:S(2)}) collective-permute-start(bf16[256,1024]{1,0:T(8,128)(2,1)} %collective-permute-done.5), channel_id=1, source_target_pairs={{0,1},{1,0},{2,3},{3,2},{4,5},{5,4},{6,7},{7,6},{8,9},{9,8},{10,11... | collective-permute-start | bytes 1572872 | tf_op jit(solution)/shard_map/ppermute | solution.py:13
  61.9 5.5 %collective-permute-start.3 = (bf16[256,256]{1,0:T(8,128)(2,1)S(1)}, bf16[256,256]{1,0:T(8,128)(2,1)S(1)}, u32[]{:S(2)}, u32[]{:S(2)}) collective-permute-start(bf16[256,256]{1,0:T(8,128)(2,1)S(1)} %divide_convert_fusion.4), channel_id=1, source_target_pairs={{0,4},{2,6},{4,0},{6,2},{1,5},{3,7},{5,1},{7,3},{8,12},{10,14},{12... | collective-permute-start | bytes 393224 | tf_op jit(solution)/shard_map/ppermute | solution.py:80
  63.9 22.5 %collective-permute-start.7 = (f32[512,512]{0,1:T(8,128)}, f32[512,512]{0,1:T(8,128)}, u32[]{:S(2)}, u32[]{:S(2)}) collective-permute-start(f32[512,512]{0,1:T(8,128)} %dynamic-slice_bitcast_fusion.2), channel_id=1, source_target_pairs={{0,2},{2,0},{4,6},{6,4},{1,3},{3,1},{5,7},{7,5},{8,10},{10,8},{12,... | collective-permute-start | bytes 3145736 | tf_op jit(solution)/shard_map/ppermute | solution.py:68
  67.5 18.7 %collective-permute-start.4 = (bf16[512,256]{1,0:T(8,128)(2,1)S(1)}, bf16[512,256]{1,0:T(8,128)(2,1)S(1)}, u32[]{:S(2)}, u32[]{:S(2)}) collective-permute-start(bf16[512,256]{1,0:T(8,128)(2,1)S(1)} %maximum_select_fusion.11), channel_id=1, source_target_pairs={{0,2},{2,0},{4,6},{6,4},{1,3},{3,1},{5,7},{7,5},{8,10},{10,8},{12,... | collective-permute-start | bytes 786440 | tf_op jit(solution)/shard_map/ppermute | solution.py:80
  81.0 24.8 %collective-permute-start.17 = (bf16[256,1024]{1,0:T(8,128)(2,1)S(1)}, bf16[256,1024]{1,0:T(8,128)(2,1)S(1)}, u32[]{:S(2)}, u32[]{:S(2)}) collective-permute-start(bf16[256,1024]{1,0:T(8,128)(2,1)S(1)} %slice.19), channel_id=1, source_target_pairs={{0,16},{8,24},{16,0},{24,8},{1,17},{9,25},{17,1},{25,9},{2,18},{10... | collective-permute-start | bytes 1572872 | tf_op jit(solution)/shard_map/ppermute | solution.py:13
  84.7 25.4 %collective-permute-start.13 = (f32[512,512]{0,1:T(8,128)S(1)}, f32[512,512]{0,1:T(8,128)S(1)}, u32[]{:S(2)}, u32[]{:S(2)}) collective-permute-start(f32[512,512]{0,1:T(8,128)S(1)} %dynamic-slice_bitcast_fusion.1), channel_id=1, source_target_pairs={{0,2},{2,0},{4,6},{6,4},{1,3},{3,1},{5,7},{7,5},{8,10},{10,8},{12,... | collective-permute-start | bytes 3145736 | tf_op jit(solution)/shard_map/ppermute | solution.py:68
  85.4 20.4 %collective-permute-start.18 = (bf16[256,1024]{1,0:T(8,128)(2,1)}, bf16[256,1024]{1,0:T(8,128)(2,1)S(1)}, u32[]{:S(2)}, u32[]{:S(2)}) collective-permute-start(bf16[256,1024]{1,0:T(8,128)(2,1)} %collective-permute-done.11), channel_id=1, source_target_pairs={{0,1},{1,0},{2,3},{3,2},{4,5},{5,4},{6,7},{7,6},{8,9},{9,8},{10,11... | collective-permute-start | bytes 1572872 | tf_op jit(solution)/shard_map/ppermute | solution.py:13
  87.9 20.7 %collective-permute-start.8 = (f32[256,512]{0,1:T(8,128)S(1)}, f32[256,512]{0,1:T(8,128)S(1)}, u32[]{:S(2)}, u32[]{:S(2)}) collective-permute-start(f32[256,512]{0,1:T(8,128)S(1)} %constant_dynamic-slice_fusion.3), channel_id=1, source_target_pairs={{0,4},{2,6},{4,0},{6,2},{1,5},{3,7},{5,1},{7,3},{8,12},{10,14},{12... | collective-permute-start | bytes 1572872 | tf_op jit(solution)/shard_map/ppermute | solution.py:68
  107.3 22.3 %collective-permute-start.19 = (f32[512,512]{0,1:T(8,128)S(1)}, f32[512,512]{0,1:T(8,128)S(1)}, u32[]{:S(2)}, u32[]{:S(2)}) collective-permute-start(f32[512,512]{0,1:T(8,128)S(1)} %dynamic-slice_bitcast_fusion), channel_id=1, source_target_pairs={{0,2},{2,0},{4,6},{6,4},{1,3},{3,1},{5,7},{7,5},{8,10},{10,8},{12,... | collective-permute-start | bytes 3145736 | tf_op jit(solution)/shard_map/ppermute | solution.py:68
  107.9 13.5 %collective-permute-start.23 = (bf16[256,1024]{1,0:T(8,128)(2,1)S(1)}, bf16[256,1024]{1,0:T(8,128)(2,1)S(1)}, u32[]{:S(2)}, u32[]{:S(2)}) collective-permute-start(bf16[256,1024]{1,0:T(8,128)(2,1)S(1)} %collective-permute-done.17), channel_id=1, source_target_pairs={{0,1},{1,0},{2,3},{3,2},{4,5},{5,4},{6,7},{7,6},{8,9},{9,8},{10,11... | collective-permute-start | bytes 1572872 | tf_op jit(solution)/shard_map/ppermute | solution.py:13
  108.8 7.6 %collective-permute-start.9 = (bf16[256,512]{0,1:T(8,128)(2,1)S(1)}, bf16[256,512]{0,1:T(8,128)(2,1)S(1)}, u32[]{:S(2)}, u32[]{:S(2)}) collective-permute-start(bf16[256,512]{0,1:T(8,128)(2,1)S(1)} %divide_convert_fusion.2), channel_id=1, source_target_pairs={{0,4},{2,6},{4,0},{6,2},{1,5},{3,7},{5,1},{7,3},{8,12},{10,14},{12... | collective-permute-start | bytes 786440 | tf_op jit(solution)/shard_map/ppermute | solution.py:80
  110.4 17.3 %collective-permute-start.14 = (f32[256,512]{0,1:T(8,128)S(1)}, f32[256,512]{0,1:T(8,128)S(1)}, u32[]{:S(2)}, u32[]{:S(2)}) collective-permute-start(f32[256,512]{0,1:T(8,128)S(1)} %constant_dynamic-slice_fusion.2), channel_id=1, source_target_pairs={{0,4},{2,6},{4,0},{6,2},{1,5},{3,7},{5,1},{7,3},{8,12},{10,14},{12... | collective-permute-start | bytes 1572872 | tf_op jit(solution)/shard_map/ppermute | solution.py:68
  116.6 11.2 %collective-permute-start.10 = (bf16[512,512]{0,1:T(8,128)(2,1)S(1)}, bf16[512,512]{0,1:T(8,128)(2,1)S(1)}, u32[]{:S(2)}, u32[]{:S(2)}) collective-permute-start(bf16[512,512]{0,1:T(8,128)(2,1)S(1)} %maximum_select_fusion.4), channel_id=1, source_target_pairs={{0,2},{2,0},{4,6},{6,4},{1,3},{3,1},{5,7},{7,5},{8,10},{10,8},{12,... | collective-permute-start | bytes 1572872 | tf_op jit(solution)/shard_map/ppermute | solution.py:80
  122.2 16.7 %collective-permute-start.24 = (f32[512,256]{1,0:T(8,128)S(1)}, f32[512,256]{1,0:T(8,128)S(1)}, u32[]{:S(2)}, u32[]{:S(2)}) collective-permute-start(f32[512,256]{1,0:T(8,128)S(1)} %dynamic-slice_bitcast_fusion.3), channel_id=1, source_target_pairs={{0,2},{2,0},{4,6},{6,4},{1,3},{3,1},{5,7},{7,5},{8,10},{10,8},{12,... | collective-permute-start | bytes 1572872 | tf_op jit(solution)/shard_map/ppermute | solution.py:68
  128.2 6.7 %collective-permute-start.15 = (bf16[256,512]{0,1:T(8,128)(2,1)S(1)}, bf16[256,512]{0,1:T(8,128)(2,1)S(1)}, u32[]{:S(2)}, u32[]{:S(2)}) collective-permute-start(bf16[256,512]{0,1:T(8,128)(2,1)S(1)} %divide_convert_fusion.1), channel_id=1, source_target_pairs={{0,4},{2,6},{4,0},{6,2},{1,5},{3,7},{5,1},{7,3},{8,12},{10,14},{12... | collective-permute-start | bytes 786440 | tf_op jit(solution)/shard_map/ppermute | solution.py:80
  129.8 16.3 %collective-permute-start.20 = (f32[256,512]{0,1:T(8,128)S(1)}, f32[256,512]{0,1:T(8,128)S(1)}, u32[]{:S(2)}, u32[]{:S(2)}) collective-permute-start(f32[256,512]{0,1:T(8,128)S(1)} %constant_dynamic-slice_fusion.1), channel_id=1, source_target_pairs={{0,4},{2,6},{4,0},{6,2},{1,5},{3,7},{5,1},{7,3},{8,12},{10,14},{12... | collective-permute-start | bytes 1572872 | tf_op jit(solution)/shard_map/ppermute | solution.py:68
  135.1 11.2 %collective-permute-start.16 = (bf16[512,512]{0,1:T(8,128)(2,1)S(1)}, bf16[512,512]{0,1:T(8,128)(2,1)S(1)}, u32[]{:S(2)}, u32[]{:S(2)}) collective-permute-start(bf16[512,512]{0,1:T(8,128)(2,1)S(1)} %maximum_select_fusion.5), channel_id=1, source_target_pairs={{0,2},{2,0},{4,6},{6,4},{1,3},{3,1},{5,7},{7,5},{8,10},{10,8},{12,... | collective-permute-start | bytes 1572872 | tf_op jit(solution)/shard_map/ppermute | solution.py:80
  139.0 9.0 %copy-start.4 = (bf16[256,1024]{1,0:T(8,128)(2,1)S(1)}, bf16[256,1024]{1,0:T(8,128)(2,1)}, u32[]{:S(2)}) copy-start(bf16[256,1024]{1,0:T(8,128)(2,1)} %copy-done.3) | copy-start | bytes 1572868
  139.0 20.7 %collective-permute-start.25 = (f32[256,256]{1,0:T(8,128)S(1)}, f32[256,256]{1,0:T(8,128)S(1)}, u32[]{:S(2)}, u32[]{:S(2)}) collective-permute-start(f32[256,256]{1,0:T(8,128)S(1)} %constant_dynamic-slice_fusion), channel_id=1, source_target_pairs={{0,4},{2,6},{4,0},{6,2},{1,5},{3,7},{5,1},{7,3},{8,12},{10,14},{12... | collective-permute-start | bytes 786440 | tf_op jit(solution)/shard_map/ppermute | solution.py:68
  146.7 10.7 %collective-permute-start.21 = (bf16[256,512]{0,1:T(8,128)(2,1)S(1)}, bf16[256,512]{0,1:T(8,128)(2,1)S(1)}, u32[]{:S(2)}, u32[]{:S(2)}) collective-permute-start(bf16[256,512]{0,1:T(8,128)(2,1)S(1)} %divide_convert_fusion), channel_id=1, source_target_pairs={{0,4},{2,6},{4,0},{6,2},{1,5},{3,7},{5,1},{7,3},{8,12},{10,14},{12... | collective-permute-start | bytes 786440 | tf_op jit(solution)/shard_map/ppermute | solution.py:80
  157.5 3.7 %collective-permute-start.22 = (bf16[512,512]{0,1:T(8,128)(2,1)S(1)}, bf16[512,512]{0,1:T(8,128)(2,1)S(1)}, u32[]{:S(2)}, u32[]{:S(2)}) collective-permute-start(bf16[512,512]{0,1:T(8,128)(2,1)S(1)} %maximum_select_fusion.6), channel_id=1, source_target_pairs={{0,2},{2,0},{4,6},{6,4},{1,3},{3,1},{5,7},{7,5},{8,10},{10,8},{12,... | collective-permute-start | bytes 1572872 | tf_op jit(solution)/shard_map/ppermute | solution.py:80
  161.7 4.8 %collective-permute-start.26 = (bf16[256,256]{1,0:T(8,128)(2,1)S(1)}, bf16[256,256]{1,0:T(8,128)(2,1)S(1)}, u32[]{:S(2)}, u32[]{:S(2)}) collective-permute-start(bf16[256,256]{1,0:T(8,128)(2,1)S(1)} %divide_convert_fusion.3), channel_id=1, source_target_pairs={{0,4},{2,6},{4,0},{6,2},{1,5},{3,7},{5,1},{7,3},{8,12},{10,14},{12... | collective-permute-start | bytes 393224 | tf_op jit(solution)/shard_map/ppermute | solution.py:80
  166.6 2.6 %collective-permute-start.27 = (bf16[512,256]{1,0:T(8,128)(2,1)S(1)}, bf16[512,256]{1,0:T(8,128)(2,1)S(1)}, u32[]{:S(2)}, u32[]{:S(2)}) collective-permute-start(bf16[512,256]{1,0:T(8,128)(2,1)S(1)} %maximum_select_fusion.12), channel_id=1, source_target_pairs={{0,2},{2,0},{4,6},{6,4},{1,3},{3,1},{5,7},{7,5},{8,10},{10,8},{12,... | collective-permute-start | bytes 786440 | tf_op jit(solution)/shard_map/ppermute | solution.py:80
  (3 other events, 5.2 us)

commit v20 on v18

--- a/solution.py
+++ b/solution.py
@@ -3,7 +3,7 @@
 from jax import lax
 from jax.sharding import PartitionSpec as P
 
-CHUNKS = 4
+CHUNKS = 8
 AUX_BY_PERMUTE = True
 NARROW_FAR = False
 

time: 172 us -> 185 us (1.076)
  matrix products: 13.9 us -> 32.3 us
  starting transfers between devices: 35.5 us -> 48 us
  waiting for transfers between devices: 103 us -> 91.2 us
  local copies, waits for them, and re-layouts: 11.7 us -> 6.08 us
    dot_general x5 -> x9, matrix products: 7.44 us -> 25.7 us  [paired_plan(): term = jnp.dot(rows, block, preferred_element_type=jnp.float32)]
    ppermute x10 -> x18, starting transfers between devices: 10.8 us -> 20.3 us  [aux_reduce_scatter(): x = keep + lax.ppermute(send, 'aux', xor_pairs(count, step))]
    ppermute x10 -> x18, waiting for transfers between devices: 21.4 us -> 17.2 us  [aux_all_gather(): other = lax.ppermute(x, 'aux', xor_pairs(count, step))]
    ppermute x8 -> x16, waiting for transfers between devices: 70.8 us -> 66.8 us  [shifted_2(): lax.ppermute(value, axis, [(i, (i + by) % count) for i in range(count)])]
    ppermute x10 -> x18, waiting for transfers between devices: 10.7 us -> 7.18 us  [aux_reduce_scatter(): x = keep + lax.ppermute(send, 'aux', xor_pairs(count, step))]
    ppermute x8 -> x16, starting transfers between devices: 7.15 us -> 10.5 us  [shifted_2(): lax.ppermute(value, axis, [(i, (i + by) % count) for i in range(count)])]
    unnamed x17 -> x19, local copies, waits for them, and re-layouts: 3.7 us -> 1.1 us
    concatenate x3 -> x7, local copies, waits for them, and re-layouts: 2.19 us -> 0.14 us  [paired_plan(): block = jnp.concatenate(parts) if len(parts) > 1 else parts[0]]
  transfers between devices with their start and end apart: 28 -> 52, of which waited for: 12 -> 20; matrix products, arithmetic and copies ran while one was open for 14% -> 16% of each run, Pallas kernels for 0% -> 0%
where the time goes in v20:
time: 185 us
  waiting for transfers between devices  91.2 us (49%)
  starting transfers between devices  48 us (26%)
  matrix products  32.3 us (17%)
  local copies, waits for them, and re-layouts  6.08 us (3%)
  other arithmetic  5.01 us (3%)
  between operations  2.06 us (1%)
    ppermute x16, waiting for transfers between devices, shifted_2(): lax.ppermute(value, axis, [(i, (i + by) % count) for i in range(count)])  66.8 us
    dot_general x9, matrix products, paired_plan(): term = jnp.dot(rows, block, preferred_element_type=jnp.float32)  25.7 us
    ppermute x18, starting transfers between devices, aux_reduce_scatter(): x = keep + lax.ppermute(send, 'aux', xor_pairs(count, step))  20.3 us
    ppermute x18, starting transfers between devices, aux_all_gather(): other = lax.ppermute(x, 'aux', xor_pairs(count, step))  17.3 us
    ppermute x18, waiting for transfers between devices, aux_all_gather(): other = lax.ppermute(x, 'aux', xor_pairs(count, step))  17.2 us
    ppermute x16, starting transfers between devices, shifted_2(): lax.ppermute(value, axis, [(i, (i + by) % count) for i in range(count)])  10.5 us
    ppermute x18, waiting for transfers between devices, aux_reduce_scatter(): x = keep + lax.ppermute(send, 'aux', xor_pairs(count, step))  7.18 us
    dot_general x9, matrix products, paired_plan(): jnp.einsum('aq,bq->ab', own, block, preferred_element_type=jnp.float32)  6.61 us
  transfers between devices with their start and end apart: 52, of which 20 were waited for; matrix products, arithmetic and copies ran while one was open for 16% of the time, Pallas kernels for 0%

profile of v20, /device:TPU:1, one launch (start us, length us, event | category | flops | bytes accessed | tf_op | source)
XLA Modules:
  0.0 184.6 jit_solution(9300937528661226626)
XLA Ops:
  0.0 2.7 %slice_bitcast_fusion.7 = (bf16[128,1024]{1,0:T(8,128)(2,1)S(1)}, bf16[128,1024]{1,0:T(8,128)(2,1)}, bf16[128,1024]{1,0:T(8,128)(2,1)}, bf16[128,1024]{1,0:T(8,1...) fusion(bf16[1,1024,1024]{2,1,0:T(8,128)(2,1)} %param.3), kind=kLoop, calls=%fused_computation.80 | loop fusion | bytes 4194304 | tf_op jit(solution)/shard_map/slice | solution.py:105
  2.7 3.1 %collective-permute-start = (bf16[128,1024]{1,0:T(8,128)(2,1)S(1)}, bf16[128,1024]{1,0:T(8,128)(2,1)S(1)}, u32[]{:S(2)}, u32[]{:S(2)}) collective-permute-start(bf16[128,1024]{1,0:T(8,128)(2,1)S(1)} %get-tuple-element.35), channel_id=1, source_target_pairs={{0,16},{8,24},{16,0},{24,8},{1,17},{9,25},{17,1},{25,9},{2,18},{10... | collective-permute-start | bytes 786440 | tf_op jit(solution)/shard_map/ppermute | solution.py:13
  8.1 9.4 %collective-permute-done = bf16[128,1024]{1,0:T(8,128)(2,1)S(1)} collective-permute-done((bf16[128,1024]{1,0:T(8,128)(2,1)S(1)}, bf16[128,1024]{1,0:T(8,128)(2,1)S(1)}, u32[]{:S(2)}, u32[]{:S(2)}) %collective-permute-start) | collective-permute-done | bytes 262176 | tf_op jit(solution)/shard_map/ppermute | solution.py:13
  20.3 1.4 collective-permute-start.6
  21.6 9.3 %collective-permute-done.5 = bf16[128,1024]{1,0:T(8,128)(2,1)} collective-permute-done((bf16[128,1024]{1,0:T(8,128)(2,1)}, bf16[128,1024]{1,0:T(8,128)(2,1)}, u32[]{:S(2)}, u32[]{:S(2)}) %collective-permute-start.5) | collective-permute-done | bytes 262176 | tf_op jit(solution)/shard_map/ppermute | solution.py:13
  34.5 1.3 collective-permute-start.12
  36.7 4.2 %collective-permute-start.7 = (f32[512,256]{0,1:T(8,128)S(1)}, f32[512,256]{0,1:T(8,128)S(1)}, u32[]{:S(2)}, u32[]{:S(2)}) collective-permute-start(f32[512,256]{0,1:T(8,128)S(1)} %dynamic-slice_bitcast_fusion.6), channel_id=1, source_target_pairs={{0,2},{2,0},{4,6},{6,4},{1,3},{3,1},{5,7},{7,5},{8,10},{10,8},{12,... | collective-permute-start | bytes 1572872 | tf_op jit(solution)/shard_map/ppermute | solution.py:68
  41.0 2.7 %collective-permute-start.4 = (bf16[512,128]{1,0:T(8,128)(2,1)S(1)}, bf16[512,128]{1,0:T(8,128)(2,1)S(1)}, u32[]{:S(2)}, u32[]{:S(2)}) collective-permute-start(bf16[512,128]{1,0:T(8,128)(2,1)S(1)} %maximum_select_fusion.19), channel_id=1, source_target_pairs={{0,2},{2,0},{4,6},{6,4},{1,3},{3,1},{5,7},{7,5},{8,10},{10,8},{12,... | collective-permute-start | bytes 393224 | tf_op jit(solution)/shard_map/ppermute | solution.py:80
  43.7 2.0 %collective-permute-done.11 = bf16[128,1024]{1,0:T(8,128)(2,1)S(1)} collective-permute-done((bf16[128,1024]{1,0:T(8,128)(2,1)}, bf16[128,1024]{1,0:T(8,128)(2,1)S(1)}, u32[]{:S(2)}, u32[]{:S(2)}) %collective-permute-start.11) | collective-permute-done | bytes 262176 | tf_op jit(solution)/shard_map/ppermute | solution.py:13
  49.0 2.7 %fusion.29 = f32[1024,1024]{1,0:T(8,128)} fusion(bf16[1024,128]{1,0:T(8,128)(2,1)S(1)} %maximum_select_fusion.7, bf16[128,1024]{1,0:T(8,128)(2,1)S(1)} %collective-permute-done), kind=kOutput, calls=%fused_computation.122 | convolution fusion | flops 268435456 | bytes 4718592 | tf_op jit(solution)/shard_map/dot_general | solution.py:130
  51.7 8.1 %collective-permute-done.17 = bf16[128,1024]{1,0:T(8,128)(2,1)S(1)} collective-permute-done((bf16[128,1024]{1,0:T(8,128)(2,1)S(1)}, bf16[128,1024]{1,0:T(8,128)(2,1)S(1)}, u32[]{:S(2)}, u32[]{:S(2)}) %collective-permute-start.17) | collective-permute-done | bytes 262176 | tf_op jit(solution)/shard_map/ppermute | solution.py:13
  63.9 9.6 %collective-permute-done.23 = bf16[128,1024]{1,0:T(8,128)(2,1)S(1)} collective-permute-done((bf16[128,1024]{1,0:T(8,128)(2,1)S(1)}, bf16[128,1024]{1,0:T(8,128)(2,1)S(1)}, u32[]{:S(2)}, u32[]{:S(2)}) %collective-permute-start.23) | collective-permute-done | bytes 262176 | tf_op jit(solution)/shard_map/ppermute | solution.py:13
  74.1 1.3 collective-permute-start.14
  78.8 2.6 %collective-permute-start.10 = (bf16[512,256]{0,1:T(8,128)(2,1)S(1)}, bf16[512,256]{0,1:T(8,128)(2,1)S(1)}, u32[]{:S(2)}, u32[]{:S(2)}) collective-permute-start(bf16[512,256]{0,1:T(8,128)(2,1)S(1)} %maximum_select_fusion.8), channel_id=1, source_target_pairs={{0,2},{2,0},{4,6},{6,4},{1,3},{3,1},{5,7},{7,5},{8,10},{10,8},{12,... | collective-permute-start | bytes 786440 | tf_op jit(solution)/shard_map/ppermute | solution.py:80
  81.5 6.3 %collective-permute-done.29 = bf16[128,1024]{1,0:T(8,128)(2,1)S(1)} collective-permute-done((bf16[128,1024]{1,0:T(8,128)(2,1)S(1)}, bf16[128,1024]{1,0:T(8,128)(2,1)S(1)}, u32[]{:S(2)}, u32[]{:S(2)}) %collective-permute-start.29) | collective-permute-done | bytes 262176 | tf_op jit(solution)/shard_map/ppermute | solution.py:13
  89.1 1.7 collective-permute-start.31
  92.4 2.9 %collective-permute-done.20 = f32[256,256]{0,1:T(8,128)S(1)} collective-permute-done((f32[256,256]{0,1:T(8,128)S(1)}, f32[256,256]{0,1:T(8,128)S(1)}, u32[]{:S(2)}, u32[]{:S(2)}) %collective-permute-start.20) | collective-permute-done | bytes 262176 | tf_op jit(solution)/shard_map/ppermute | solution.py:68
  95.6 6.3 %collective-permute-done.35 = bf16[128,1024]{1,0:T(8,128)(2,1)S(1)} collective-permute-done((bf16[128,1024]{1,0:T(8,128)(2,1)S(1)}, bf16[128,1024]{1,0:T(8,128)(2,1)S(1)}, u32[]{:S(2)}, u32[]{:S(2)}) %collective-permute-start.35) | collective-permute-done | bytes 262176 | tf_op jit(solution)/shard_map/ppermute | solution.py:13
  102.7 1.3 collective-permute-start.26
  107.2 9.1 %collective-permute-done.41 = bf16[128,1024]{1,0:T(8,128)(2,1)S(1)} collective-permute-done((bf16[128,1024]{1,0:T(8,128)(2,1)S(1)}, bf16[128,1024]{1,0:T(8,128)(2,1)S(1)}, u32[]{:S(2)}, u32[]{:S(2)}) %collective-permute-start.41) | collective-permute-done | bytes 262176 | tf_op jit(solution)/shard_map/ppermute | solution.py:13
  121.1 6.6 %collective-permute-done.47 = bf16[128,1024]{1,0:T(8,128)(2,1)S(1)} collective-permute-done((bf16[128,1024]{1,0:T(8,128)(2,1)S(1)}, bf16[128,1024]{1,0:T(8,128)(2,1)S(1)}, u32[]{:S(2)}, u32[]{:S(2)}) %collective-permute-start.47) | collective-permute-done | bytes 262176 | tf_op jit(solution)/shard_map/ppermute | solution.py:13
  131.6 3.4 %collective-permute-done.27 = bf16[256,256]{0,1:T(8,128)(2,1)S(1)} collective-permute-done((bf16[256,256]{0,1:T(8,128)(2,1)S(1)}, bf16[256,256]{0,1:T(8,128)(2,1)S(1)}, u32[]{:S(2)}, u32[]{:S(2)}) %collective-permute-start.27) | collective-permute-done | bytes 131104 | tf_op jit(solution)/shard_map/ppermute | solution.py:80
  135.1 1.3 collective-permute-start.28
  138.3 5.2 %collective-permute-done.33 = bf16[256,256]{0,1:T(8,128)(2,1)S(1)} collective-permute-done((bf16[256,256]{0,1:T(8,128)(2,1)S(1)}, bf16[256,256]{0,1:T(8,128)(2,1)S(1)}, u32[]{:S(2)}, u32[]{:S(2)}) %collective-permute-start.33) | collective-permute-done | bytes 131104 | tf_op jit(solution)/shard_map/ppermute | solution.py:80
  147.6 4.8 %collective-permute-done.39 = bf16[256,256]{0,1:T(8,128)(2,1)S(1)} collective-permute-done((bf16[256,256]{0,1:T(8,128)(2,1)S(1)}, bf16[256,256]{0,1:T(8,128)(2,1)S(1)}, u32[]{:S(2)}, u32[]{:S(2)}) %collective-permute-start.39) | collective-permute-done | bytes 131104 | tf_op jit(solution)/shard_map/ppermute | solution.py:80
  153.9 4.2 %collective-permute-done.44 = f32[256,256]{0,1:T(8,128)S(1)} collective-permute-done((f32[256,256]{0,1:T(8,128)S(1)}, f32[256,256]{0,1:T(8,128)S(1)}, u32[]{:S(2)}, u32[]{:S(2)}) %collective-permute-start.44) | collective-permute-done | bytes 262176 | tf_op jit(solution)/shard_map/ppermute | solution.py:68
  158.8 2.8 %fusion.33 = f32[1024,1024]{1,0:T(8,128)} fusion(bf16[1024,256]{0,1:T(8,128)(2,1)S(1)} %maximum_select_fusion.3, bf16[256,1024]{1,0:T(8,128)(2,1)S(1)} %constant_dynamic-update-slice_fusion.6), kind=kOutput, calls=%fused_computation.126 | convolution fusion | flops 536870912 | bytes 5242880 | tf_op jit(solution)/shard_map/dot_general | solution.py:130
  162.8 1.8 collective-permute-start.46
  164.5 2.7 %fusion.34 = f32[1024,1024]{1,0:T(8,128)} fusion(bf16[1024,256]{0,1:T(8,128)(2,1)S(1)} %maximum_select_fusion.4, bf16[256,1024]{1,0:T(8,128)(2,1)S(1)} %constant_dynamic-update-slice_fusion.8), kind=kOutput, calls=%fused_computation.127 | convolution fusion | flops 536870912 | bytes 5242880 | tf_op jit(solution)/shard_map/dot_general | solution.py:130
  167.9 2.8 %fusion.35 = f32[1024,1024]{1,0:T(8,128)} fusion(bf16[1024,256]{0,1:T(8,128)(2,1)S(1)} %maximum_select_fusion.5, bf16[256,1024]{1,0:T(8,128)(2,1)S(1)} %constant_dynamic-update-slice_fusion.10), kind=kOutput, calls=%fused_computation.128 | convolution fusion | flops 536870912 | bytes 5242880 | tf_op jit(solution)/shard_map/dot_general | solution.py:130
  172.2 2.7 %fusion.36 = f32[1024,1024]{1,0:T(8,128)} fusion(bf16[1024,256]{0,1:T(8,128)(2,1)S(1)} %maximum_select_fusion.6, bf16[256,1024]{1,0:T(8,128)(2,1)S(1)} %constant_dynamic-update-slice_fusion.12), kind=kOutput, calls=%fused_computation.129 | convolution fusion | flops 536870912 | bytes 5242880 | tf_op jit(solution)/shard_map/dot_general | solution.py:130
  174.9 9.7 %fusion.18 = bf16[1,1024,1024]{2,1,0:T(8,128)(2,1)} fusion(f32[1024,1024]{1,0:T(8,128)} %fusion.36, f32[1024,1024]{1,0:T(8,128)} %fusion.35, f32[1024,1024]{1,0:T(8,128)} %fusion.34, f32[1024,1024]{1,0:T(8,128)} %fusion.33, f32[1024,1024]{1,0:T(8,128)S(1)} %fusion.32, f32[1024,1024]{1,0:T(8,128)S(1)} %fusion.31, f32[1024,1024]{1,0:T(8,128)} %fusion.29, ...), kind=kOutput, calls=%fused_computation.19 | convolution fusion | flops 280100864 | bytes 36175872 | tf_op jit(solution)/shard_map/dot_general | solution.py:130
  (188 shorter events, 46.5 us)
Async XLA Ops:
  2.7 14.8 %collective-permute-start = (bf16[128,1024]{1,0:T(8,128)(2,1)S(1)}, bf16[128,1024]{1,0:T(8,128)(2,1)S(1)}, u32[]{:S(2)}, u32[]{:S(2)}) collective-permute-start(bf16[128,1024]{1,0:T(8,128)(2,1)S(1)} %get-tuple-element.35), channel_id=1, source_target_pairs={{0,16},{8,24},{16,0},{24,8},{1,17},{9,25},{17,1},{25,9},{2,18},{10... | collective-permute-start | bytes 786440 | tf_op jit(solution)/shard_map/ppermute | solution.py:13
  17.5 13.4 %collective-permute-start.5 = (bf16[128,1024]{1,0:T(8,128)(2,1)}, bf16[128,1024]{1,0:T(8,128)(2,1)}, u32[]{:S(2)}, u32[]{:S(2)}) collective-permute-start(bf16[128,1024]{1,0:T(8,128)(2,1)} %get-tuple-element.20), channel_id=1, source_target_pairs={{0,16},{8,24},{16,0},{24,8},{1,17},{9,25},{17,1},{25,9},{2,18},{10... | collective-permute-start | bytes 786440 | tf_op jit(solution)/shard_map/ppermute | solution.py:13
  19.0 11.9 %collective-permute-start.1 = (f32[512,128]{1,0:T(8,128)}, f32[512,128]{1,0:T(8,128)}, u32[]{:S(2)}, u32[]{:S(2)}) collective-permute-start(f32[512,128]{1,0:T(8,128)} %constant_dynamic-slice_fusion.9), channel_id=1, source_target_pairs={{0,2},{2,0},{4,6},{6,4},{1,3},{3,1},{5,7},{7,5},{8,10},{10,8},{12,... | collective-permute-start | bytes 786440 | tf_op jit(solution)/shard_map/ppermute | solution.py:68
  20.3 13.4 %collective-permute-start.6 = (bf16[128,1024]{1,0:T(8,128)(2,1)S(1)}, bf16[128,1024]{1,0:T(8,128)(2,1)S(1)}, u32[]{:S(2)}, u32[]{:S(2)}) collective-permute-start(bf16[128,1024]{1,0:T(8,128)(2,1)S(1)} %collective-permute-done), channel_id=1, source_target_pairs={{0,1},{1,0},{2,3},{3,2},{4,5},{5,4},{6,7},{7,6},{8,9},{9,8},{10,11... | collective-permute-start | bytes 786440 | tf_op jit(solution)/shard_map/ppermute | solution.py:13
  30.9 14.8 %collective-permute-start.11 = (bf16[128,1024]{1,0:T(8,128)(2,1)}, bf16[128,1024]{1,0:T(8,128)(2,1)S(1)}, u32[]{:S(2)}, u32[]{:S(2)}) collective-permute-start(bf16[128,1024]{1,0:T(8,128)(2,1)} %get-tuple-element.22), channel_id=1, source_target_pairs={{0,16},{8,24},{16,0},{24,8},{1,17},{9,25},{17,1},{25,9},{2,18},{10... | collective-permute-start | bytes 786440 | tf_op jit(solution)/shard_map/ppermute | solution.py:13
  34.5 11.9 %collective-permute-start.12 = (bf16[128,1024]{1,0:T(8,128)(2,1)}, bf16[128,1024]{1,0:T(8,128)(2,1)S(1)}, u32[]{:S(2)}, u32[]{:S(2)}) collective-permute-start(bf16[128,1024]{1,0:T(8,128)(2,1)} %collective-permute-done.5), channel_id=1, source_target_pairs={{0,1},{1,0},{2,3},{3,2},{4,5},{5,4},{6,7},{7,6},{8,9},{9,8},{10,11... | collective-permute-start | bytes 786440 | tf_op jit(solution)/shard_map/ppermute | solution.py:13
  36.7 23.1 %collective-permute-start.7 = (f32[512,256]{0,1:T(8,128)S(1)}, f32[512,256]{0,1:T(8,128)S(1)}, u32[]{:S(2)}, u32[]{:S(2)}) collective-permute-start(f32[512,256]{0,1:T(8,128)S(1)} %dynamic-slice_bitcast_fusion.6), channel_id=1, source_target_pairs={{0,2},{2,0},{4,6},{6,4},{1,3},{3,1},{5,7},{7,5},{8,10},{10,8},{12,... | collective-permute-start | bytes 1572872 | tf_op jit(solution)/shard_map/ppermute | solution.py:68
  45.7 14.1 %collective-permute-start.17 = (bf16[128,1024]{1,0:T(8,128)(2,1)S(1)}, bf16[128,1024]{1,0:T(8,128)(2,1)S(1)}, u32[]{:S(2)}, u32[]{:S(2)}) collective-permute-start(bf16[128,1024]{1,0:T(8,128)(2,1)S(1)} %copy-done.3), channel_id=1, source_target_pairs={{0,16},{8,24},{16,0},{24,8},{1,17},{9,25},{17,1},{25,9},{2,18},{10... | collective-permute-start | bytes 786440 | tf_op jit(solution)/shard_map/ppermute | solution.py:13
  47.2 26.8 %collective-permute-start.13 = (f32[512,256]{0,1:T(8,128)S(1)}, f32[512,256]{0,1:T(8,128)S(1)}, u32[]{:S(2)}, u32[]{:S(2)}) collective-permute-start(f32[512,256]{0,1:T(8,128)S(1)} %dynamic-slice_bitcast_fusion.5), channel_id=1, source_target_pairs={{0,2},{2,0},{4,6},{6,4},{1,3},{3,1},{5,7},{7,5},{8,10},{10,8},{12,... | collective-permute-start | bytes 1572872 | tf_op jit(solution)/shard_map/ppermute | solution.py:68
  47.6 13.3 %collective-permute-start.18 = (bf16[128,1024]{1,0:T(8,128)(2,1)S(1)}, bf16[128,1024]{1,0:T(8,128)(2,1)S(1)}, u32[]{:S(2)}, u32[]{:S(2)}) collective-permute-start(bf16[128,1024]{1,0:T(8,128)(2,1)S(1)} %collective-permute-done.11), channel_id=1, source_target_pairs={{0,1},{1,0},{2,3},{3,2},{4,5},{5,4},{6,7},{7,6},{8,9},{9,8},{10,11... | collective-permute-start | bytes 786440 | tf_op jit(solution)/shard_map/ppermute | solution.py:13
  59.8 13.7 %collective-permute-start.23 = (bf16[128,1024]{1,0:T(8,128)(2,1)S(1)}, bf16[128,1024]{1,0:T(8,128)(2,1)S(1)}, u32[]{:S(2)}, u32[]{:S(2)}) collective-permute-start(bf16[128,1024]{1,0:T(8,128)(2,1)S(1)} %copy-done.2), channel_id=1, source_target_pairs={{0,16},{8,24},{16,0},{24,8},{1,17},{9,25},{17,1},{25,9},{2,18},{10... | collective-permute-start | bytes 786440 | tf_op jit(solution)/shard_map/ppermute | solution.py:13
  59.9 13.6 %collective-permute-start.8 = (f32[256,256]{0,1:T(8,128)S(1)}, f32[256,256]{0,1:T(8,128)S(1)}, u32[]{:S(2)}, u32[]{:S(2)}) collective-permute-start(f32[256,256]{0,1:T(8,128)S(1)} %constant_dynamic-slice_fusion.7), channel_id=1, source_target_pairs={{0,4},{2,6},{4,0},{6,2},{1,5},{3,7},{5,1},{7,3},{8,12},{10,14},{12... | collective-permute-start | bytes 786440 | tf_op jit(solution)/shard_map/ppermute | solution.py:68
  61.8 16.9 %collective-permute-start.19 = (f32[512,256]{0,1:T(8,128)S(1)}, f32[512,256]{0,1:T(8,128)S(1)}, u32[]{:S(2)}, u32[]{:S(2)}) collective-permute-start(f32[512,256]{0,1:T(8,128)S(1)} %dynamic-slice_bitcast_fusion.4), channel_id=1, source_target_pairs={{0,2},{2,0},{4,6},{6,4},{1,3},{3,1},{5,7},{7,5},{8,10},{10,8},{12,... | collective-permute-start | bytes 1572872 | tf_op jit(solution)/shard_map/ppermute | solution.py:68
  62.7 12.8 %collective-permute-start.24 = (bf16[128,1024]{1,0:T(8,128)(2,1)S(1)}, bf16[128,1024]{1,0:T(8,128)(2,1)S(1)}, u32[]{:S(2)}, u32[]{:S(2)}) collective-permute-start(bf16[128,1024]{1,0:T(8,128)(2,1)S(1)} %collective-permute-done.17), channel_id=1, source_target_pairs={{0,1},{1,0},{2,3},{3,2},{4,5},{5,4},{6,7},{7,6},{8,9},{9,8},{10,11... | collective-permute-start | bytes 786440 | tf_op jit(solution)/shard_map/ppermute | solution.py:13
  73.5 14.3 %collective-permute-start.29 = (bf16[128,1024]{1,0:T(8,128)(2,1)S(1)}, bf16[128,1024]{1,0:T(8,128)(2,1)S(1)}, u32[]{:S(2)}, u32[]{:S(2)}) collective-permute-start(bf16[128,1024]{1,0:T(8,128)(2,1)S(1)} %copy-done.1), channel_id=1, source_target_pairs={{0,16},{8,24},{16,0},{24,8},{1,17},{9,25},{17,1},{25,9},{2,18},{10... | collective-permute-start | bytes 786440 | tf_op jit(solution)/shard_map/ppermute | solution.py:13
  74.1 15.0 %collective-permute-start.14 = (f32[256,256]{0,1:T(8,128)S(1)}, f32[256,256]{0,1:T(8,128)S(1)}, u32[]{:S(2)}, u32[]{:S(2)}) collective-permute-start(f32[256,256]{0,1:T(8,128)S(1)} %constant_dynamic-slice_fusion.6), channel_id=1, source_target_pairs={{0,4},{2,6},{4,0},{6,2},{1,5},{3,7},{5,1},{7,3},{8,12},{10,14},{12... | collective-permute-start | bytes 786440 | tf_op jit(solution)/shard_map/ppermute | solution.py:68
  76.3 26.3 %collective-permute-start.25 = (f32[512,256]{0,1:T(8,128)S(1)}, f32[512,256]{0,1:T(8,128)S(1)}, u32[]{:S(2)}, u32[]{:S(2)}) collective-permute-start(f32[512,256]{0,1:T(8,128)S(1)} %dynamic-slice_bitcast_fusion.3), channel_id=1, source_target_pairs={{0,2},{2,0},{4,6},{6,4},{1,3},{3,1},{5,7},{7,5},{8,10},{10,8},{12,... | collective-permute-start | bytes 1572872 | tf_op jit(solution)/shard_map/ppermute | solution.py:68
  78.3 9.9 %collective-permute-start.30 = (bf16[128,1024]{1,0:T(8,128)(2,1)S(1)}, bf16[128,1024]{1,0:T(8,128)(2,1)S(1)}, u32[]{:S(2)}, u32[]{:S(2)}) collective-permute-start(bf16[128,1024]{1,0:T(8,128)(2,1)S(1)} %collective-permute-done.23), channel_id=1, source_target_pairs={{0,1},{1,0},{2,3},{3,2},{4,5},{5,4},{6,7},{7,6},{8,9},{9,8},{10,11... | collective-permute-start | bytes 786440 | tf_op jit(solution)/shard_map/ppermute | solution.py:13
  78.8 12.1 %collective-permute-start.10 = (bf16[512,256]{0,1:T(8,128)(2,1)S(1)}, bf16[512,256]{0,1:T(8,128)(2,1)S(1)}, u32[]{:S(2)}, u32[]{:S(2)}) collective-permute-start(bf16[512,256]{0,1:T(8,128)(2,1)S(1)} %maximum_select_fusion.8), channel_id=1, source_target_pairs={{0,2},{2,0},{4,6},{6,4},{1,3},{3,1},{5,7},{7,5},{8,10},{10,8},{12,... | collective-permute-start | bytes 786440 | tf_op jit(solution)/shard_map/ppermute | solution.py:80
  88.2 13.7 %collective-permute-start.35 = (bf16[128,1024]{1,0:T(8,128)(2,1)S(1)}, bf16[128,1024]{1,0:T(8,128)(2,1)S(1)}, u32[]{:S(2)}, u32[]{:S(2)}) collective-permute-start(bf16[128,1024]{1,0:T(8,128)(2,1)S(1)} %get-tuple-element.30), channel_id=1, source_target_pairs={{0,16},{8,24},{16,0},{24,8},{1,17},{9,25},{17,1},{25,9},{2,18},{10... | collective-permute-start | bytes 786440 | tf_op jit(solution)/shard_map/ppermute | solution.py:13
  89.1 16.7 %collective-permute-start.31 = (f32[512,256]{0,1:T(8,128)S(1)}, f32[512,256]{0,1:T(8,128)S(1)}, u32[]{:S(2)}, u32[]{:S(2)}) collective-permute-start(f32[512,256]{0,1:T(8,128)S(1)} %dynamic-slice_bitcast_fusion.2), channel_id=1, source_target_pairs={{0,2},{2,0},{4,6},{6,4},{1,3},{3,1},{5,7},{7,5},{8,10},{10,8},{12,... | collective-permute-start | bytes 1572872 | tf_op jit(solution)/shard_map/ppermute | solution.py:68
  90.9 13.1 %collective-permute-start.36 = (bf16[128,1024]{1,0:T(8,128)(2,1)S(1)}, bf16[128,1024]{1,0:T(8,128)(2,1)S(1)}, u32[]{:S(2)}, u32[]{:S(2)}) collective-permute-start(bf16[128,1024]{1,0:T(8,128)(2,1)S(1)} %collective-permute-done.29), channel_id=1, source_target_pairs={{0,1},{1,0},{2,3},{3,2},{4,5},{5,4},{6,7},{7,6},{8,9},{9,8},{10,11... | collective-permute-start | bytes 786440 | tf_op jit(solution)/shard_map/ppermute | solution.py:13
  101.9 14.4 %collective-permute-start.41 = (bf16[128,1024]{1,0:T(8,128)(2,1)S(1)}, bf16[128,1024]{1,0:T(8,128)(2,1)S(1)}, u32[]{:S(2)}, u32[]{:S(2)}) collective-permute-start(bf16[128,1024]{1,0:T(8,128)(2,1)S(1)} %get-tuple-element.32), channel_id=1, source_target_pairs={{0,16},{8,24},{16,0},{24,8},{1,17},{9,25},{17,1},{25,9},{2,18},{10... | collective-permute-start | bytes 786440 | tf_op jit(solution)/shard_map/ppermute | solution.py:13
  102.7 17.2 %collective-permute-start.26 = (f32[256,256]{0,1:T(8,128)S(1)}, f32[256,256]{0,1:T(8,128)S(1)}, u32[]{:S(2)}, u32[]{:S(2)}) collective-permute-start(f32[256,256]{0,1:T(8,128)S(1)} %constant_dynamic-slice_fusion.4), channel_id=1, source_target_pairs={{0,4},{2,6},{4,0},{6,2},{1,5},{3,7},{5,1},{7,3},{8,12},{10,14},{12... | collective-permute-start | bytes 786440 | tf_op jit(solution)/shard_map/ppermute | solution.py:68
  104.9 25.4 %collective-permute-start.37 = (f32[512,256]{0,1:T(8,128)S(1)}, f32[512,256]{0,1:T(8,128)S(1)}, u32[]{:S(2)}, u32[]{:S(2)}) collective-permute-start(f32[512,256]{0,1:T(8,128)S(1)} %dynamic-slice_bitcast_fusion.1), channel_id=1, source_target_pairs={{0,2},{2,0},{4,6},{6,4},{1,3},{3,1},{5,7},{7,5},{8,10},{10,8},{12,... | collective-permute-start | bytes 1572872 | tf_op jit(solution)/shard_map/ppermute | solution.py:68
  105.2 12.2 %collective-permute-start.42 = (bf16[128,1024]{1,0:T(8,128)(2,1)S(1)}, bf16[128,1024]{1,0:T(8,128)(2,1)S(1)}, u32[]{:S(2)}, u32[]{:S(2)}) collective-permute-start(bf16[128,1024]{1,0:T(8,128)(2,1)S(1)} %collective-permute-done.35), channel_id=1, source_target_pairs={{0,1},{1,0},{2,3},{3,2},{4,5},{5,4},{6,7},{7,6},{8,9},{9,8},{10,11... | collective-permute-start | bytes 786440 | tf_op jit(solution)/shard_map/ppermute | solution.py:13
  105.8 14.6 %collective-permute-start.21 = (bf16[256,256]{0,1:T(8,128)(2,1)S(1)}, bf16[256,256]{0,1:T(8,128)(2,1)S(1)}, u32[]{:S(2)}, u32[]{:S(2)}) collective-permute-start(bf16[256,256]{0,1:T(8,128)(2,1)S(1)} %divide_convert_fusion.4), channel_id=1, source_target_pairs={{0,4},{2,6},{4,0},{6,2},{1,5},{3,7},{5,1},{7,3},{8,12},{10,14},{12... | collective-permute-start | bytes 393224 | tf_op jit(solution)/shard_map/ppermute | solution.py:80
  116.3 13.2 %collective-permute-start.32 = (f32[256,256]{0,1:T(8,128)S(1)}, f32[256,256]{0,1:T(8,128)S(1)}, u32[]{:S(2)}, u32[]{:S(2)}) collective-permute-start(f32[256,256]{0,1:T(8,128)S(1)} %constant_dynamic-slice_fusion.3), channel_id=1, source_target_pairs={{0,4},{2,6},{4,0},{6,2},{1,5},{3,7},{5,1},{7,3},{8,12},{10,14},{12... | collective-permute-start | bytes 786440 | tf_op jit(solution)/shard_map/ppermute | solution.py:68
  118.3 28.1 %collective-permute-start.43 = (f32[512,256]{0,1:T(8,128)S(1)}, f32[512,256]{0,1:T(8,128)S(1)}, u32[]{:S(2)}, u32[]{:S(2)}) collective-permute-start(f32[512,256]{0,1:T(8,128)S(1)} %dynamic-slice_bitcast_fusion), channel_id=1, source_target_pairs={{0,2},{2,0},{4,6},{6,4},{1,3},{3,1},{5,7},{7,5},{8,10},{10,8},{12,... | collective-permute-start | bytes 1572872 | tf_op jit(solution)/shard_map/ppermute | solution.py:68
  128.4 9.8 %collective-permute-start.48 = (f32[512,128]{1,0:T(8,128)S(1)}, f32[512,128]{1,0:T(8,128)S(1)}, u32[]{:S(2)}, u32[]{:S(2)}) collective-permute-start(f32[512,128]{1,0:T(8,128)S(1)} %dynamic-slice_bitcast_fusion.7), channel_id=1, source_target_pairs={{0,2},{2,0},{4,6},{6,4},{1,3},{3,1},{5,7},{7,5},{8,10},{10,8},{12,... | collective-permute-start | bytes 786440 | tf_op jit(solution)/shard_map/ppermute | solution.py:68
  130.4 14.5 %collective-permute-start.38 = (f32[256,256]{0,1:T(8,128)S(1)}, f32[256,256]{0,1:T(8,128)S(1)}, u32[]{:S(2)}, u32[]{:S(2)}) collective-permute-start(f32[256,256]{0,1:T(8,128)S(1)} %constant_dynamic-slice_fusion.2), channel_id=1, source_target_pairs={{0,4},{2,6},{4,0},{6,2},{1,5},{3,7},{5,1},{7,3},{8,12},{10,14},{12... | collective-permute-start | bytes 786440 | tf_op jit(solution)/shard_map/ppermute | solution.py:68
  146.5 11.5 %collective-permute-start.44 = (f32[256,256]{0,1:T(8,128)S(1)}, f32[256,256]{0,1:T(8,128)S(1)}, u32[]{:S(2)}, u32[]{:S(2)}) collective-permute-start(f32[256,256]{0,1:T(8,128)S(1)} %constant_dynamic-slice_fusion.1), channel_id=1, source_target_pairs={{0,4},{2,6},{4,0},{6,2},{1,5},{3,7},{5,1},{7,3},{8,12},{10,14},{12... | collective-permute-start | bytes 786440 | tf_op jit(solution)/shard_map/ppermute | solution.py:68
  (26 other events, 200.4 us)

commit v21 on v20

--- a/solution.py
+++ b/solution.py
@@ -3,7 +3,7 @@
 from jax import lax
 from jax.sharding import PartitionSpec as P
 
-CHUNKS = 8
+WIDTHS = (128, 256, 256, 256, 128)
 AUX_BY_PERMUTE = True
 NARROW_FAR = False
 
@@ -93,28 +93,33 @@
     vir_count = lax.axis_size("vir")
     aux_count = lax.axis_size("aux")
     share = vir_rows // aux_count
-    width = vir_rows // CHUNKS
+    widths = [w * (vir_rows // sum(WIDTHS)) for w in WIDTHS]
+    starts = [sum(widths[:c]) for c in range(len(widths))]
 
     total = None
     previous = None
     rows_done = None
     mate = None
-    for t in range(CHUNKS + 1):
+    for t in range(len(widths) + 1):
         parts, levels = [], []
-        if t < CHUNKS:
-            piece = own[t * width:(t + 1) * width]
+        if t < len(widths):
+            piece = own[starts[t]:starts[t] + widths[t]]
             if previous is not None:
                 piece, _ = lax.optimization_barrier((piece, previous))
             arrived = shifted_2(piece, "occ", 2)
             previous = arrived
             parts.append(arrived)
-            levels.append(lax.dynamic_slice_in_dim(vir_energy, vir_pos * vir_rows + t * width, width))
+            levels.append(
+                lax.dynamic_slice_in_dim(vir_energy, vir_pos * vir_rows + starts[t], widths[t])
+            )
         if mate is not None:
             parts.append(mate)
             levels.append(
-                lax.dynamic_slice_in_dim(vir_energy, (1 - vir_pos) * vir_rows + (t - 1) * width, width)
+                lax.dynamic_slice_in_dim(
+                    vir_energy, (1 - vir_pos) * vir_rows + starts[t - 1], widths[t - 1]
+                )
             )
-        mate = shifted_2(arrived, "vir", 1) if t < CHUNKS else None
+        mate = shifted_2(arrived, "vir", 1) if t < len(widths) else None
         block = jnp.concatenate(parts) if len(parts) > 1 else parts[0]
         col_level = jnp.concatenate(levels) if len(levels) > 1 else levels[0]
         partial = jnp.einsum("aq,bq->ab", own, block, preferred_element_type=jnp.float32)
@@ -137,7 +142,7 @@
 def on_device(integrals, occ_energy, vir_energy):
     cycle_size = lax.axis_size("occ")
     pairs_here = integrals.shape[0] == 1 and 4 % cycle_size == 0 and lax.axis_size("vir") == 2
-    if pairs_here and integrals.shape[1] % (CHUNKS * 8) == 0:
+    if pairs_here and integrals.shape[1] % sum(WIDTHS) == 0:
         return paired_plan(integrals, occ_energy, vir_energy)
     return general_plan(integrals, occ_energy, vir_energy)
 

time: 185 us -> 185 us (level)
  waiting for transfers between devices: 91.2 us -> 113 us
  matrix products: 32.3 us -> 16 us
  starting transfers between devices: 48 us -> 38.3 us
  other arithmetic: 5.01 us -> 7.49 us
    dot_general x9 -> x6, matrix products: 25.7 us -> 8.38 us  [paired_plan(): term = jnp.dot(rows, block, preferred_element_type=jnp.float32)]
    ppermute x18 -> x12, waiting for transfers between devices: 7.18 us -> 23.5 us  [aux_reduce_scatter(): x = keep + lax.ppermute(send, 'aux', xor_pairs(count, step))]
    ppermute x18 -> x12, starting transfers between devices: 20.3 us -> 9.58 us  [aux_reduce_scatter(): x = keep + lax.ppermute(send, 'aux', xor_pairs(count, step))]
    ppermute x16 -> x10, waiting for transfers between devices: 66.8 us -> 72.3 us  [shifted_2(): lax.ppermute(value, axis, [(i, (i + by) % count) for i in range(count)])]
    ppermute x18 -> x12, starting transfers between devices: 17.3 us -> 19.2 us  [aux_all_gather(): other = lax.ppermute(x, 'aux', xor_pairs(count, step))]
    ppermute x16 -> x10, starting transfers between devices: 10.5 us -> 9.48 us  [shifted_2(): lax.ppermute(value, axis, [(i, (i + by) % count) for i in range(count)])]
    dot_general x9 -> x6, matrix products: 6.61 us -> 7.6 us  [paired_plan(): jnp.einsum('aq,bq->ab', own, block, preferred_element_type=jnp.float32)]
    ppermute x18 -> x12, waiting for transfers between devices: 17.2 us -> 17.1 us  [aux_all_gather(): other = lax.ppermute(x, 'aux', xor_pairs(count, step))]
  transfers between devices with their start and end apart: 52 -> 34, of which waited for: 20 -> 14; matrix products, arithmetic and copies ran while one was open for 16% -> 13% of each run, Pallas kernels for 0% -> 0%
where the time goes in v21:
time: 185 us; the launch traced here: 184 us
  waiting for transfers between devices  113 us (61%)
  starting transfers between devices  38.3 us (21%)
  matrix products  16 us (9%)
  local copies, waits for them, and re-layouts  7.9 us (4%)
  other arithmetic  7.49 us (4%)
    ppermute x10, waiting for transfers between devices, shifted_2(): lax.ppermute(value, axis, [(i, (i + by) % count) for i in range(count)])  72.3 us
    ppermute x12, waiting for transfers between devices, aux_reduce_scatter(): x = keep + lax.ppermute(send, 'aux', xor_pairs(count, step))  23.5 us
    ppermute x12, starting transfers between devices, aux_all_gather(): other = lax.ppermute(x, 'aux', xor_pairs(count, step))  19.2 us
    ppermute x12, waiting for transfers between devices, aux_all_gather(): other = lax.ppermute(x, 'aux', xor_pairs(count, step))  17.1 us
    ppermute x12, starting transfers between devices, aux_reduce_scatter(): x = keep + lax.ppermute(send, 'aux', xor_pairs(count, step))  9.58 us
    ppermute x10, starting transfers between devices, shifted_2(): lax.ppermute(value, axis, [(i, (i + by) % count) for i in range(count)])  9.48 us
    dot_general x6, matrix products, paired_plan(): term = jnp.dot(rows, block, preferred_element_type=jnp.float32)  8.38 us
    dot_general x6, matrix products, paired_plan(): jnp.einsum('aq,bq->ab', own, block, preferred_element_type=jnp.float32)  7.6 us
  transfers between devices with their start and end apart: 34, of which 14 were waited for; matrix products, arithmetic and copies ran while one was open for 13% of the time, Pallas kernels for 0%

profile of v21, /device:TPU:1, one launch (start us, length us, event | category | flops | bytes accessed | tf_op | source)
XLA Modules:
  0.0 184.4 jit_solution(13261047520273883797)
XLA Ops:
  0.0 1.8 slice_bitcast_fusion.4
  1.8 3.1 %collective-permute-start = (bf16[128,1024]{1,0:T(8,128)(2,1)S(1)}, bf16[128,1024]{1,0:T(8,128)(2,1)S(1)}, u32[]{:S(2)}, u32[]{:S(2)}) collective-permute-start(bf16[128,1024]{1,0:T(8,128)(2,1)S(1)} %get-tuple-element.23), channel_id=1, source_target_pairs={{0,16},{8,24},{16,0},{24,8},{1,17},{9,25},{17,1},{25,9},{2,18},{10... | collective-permute-start | bytes 786440 | tf_op jit(solution)/shard_map/ppermute | solution.py:13
  4.9 1.4 fusion.21
  6.3 1.4 fusion.23
  9.0 1.6 fusion.22
  10.6 5.9 %collective-permute-done = bf16[128,1024]{1,0:T(8,128)(2,1)S(1)} collective-permute-done((bf16[128,1024]{1,0:T(8,128)(2,1)S(1)}, bf16[128,1024]{1,0:T(8,128)(2,1)S(1)}, u32[]{:S(2)}, u32[]{:S(2)}) %collective-permute-start) | collective-permute-done | bytes 262176 | tf_op jit(solution)/shard_map/ppermute | solution.py:13
  16.6 2.3 %fusion.11 = f32[1024,128]{1,0:T(8,128)S(1)} fusion(bf16[128,1024]{1,0:T(8,128)(2,1)S(1)} %collective-permute-done, bf16[1,1024,1024]{2,1,0:T(8,128)(2,1)} %param.3), kind=kOutput, calls=%fused_computation.12 | convolution fusion | flops 268435456 | bytes 2883584 | tf_op jit(solution)/shard_map/aq,bq->ab/dot_general | solution.py:125
  18.9 1.3 collective-permute-start.1
  25.3 1.8 collective-permute-done.2
  28.7 1.3 collective-permute-start.3
  30.7 1.5 collective-permute-done.3
  32.2 2.1 %collective-permute-start.4 = (bf16[512,128]{1,0:T(8,128)(2,1)S(1)}, bf16[512,128]{1,0:T(8,128)(2,1)S(1)}, u32[]{:S(2)}, u32[]{:S(2)}) collective-permute-start(bf16[512,128]{1,0:T(8,128)(2,1)S(1)} %maximum_select_fusion.13), channel_id=1, source_target_pairs={{0,2},{2,0},{4,6},{6,4},{1,3},{3,1},{5,7},{7,5},{8,10},{10,8},{12,... | collective-permute-start | bytes 393224 | tf_op jit(solution)/shard_map/ppermute | solution.py:80
  34.3 14.4 %collective-permute-done.5 = bf16[256,1024]{1,0:T(8,128)(2,1)S(1)} collective-permute-done((bf16[256,1024]{1,0:T(8,128)(2,1)}, bf16[256,1024]{1,0:T(8,128)(2,1)S(1)}, u32[]{:S(2)}, u32[]{:S(2)}) %collective-permute-start.5) | collective-permute-done | bytes 524320 | tf_op jit(solution)/shard_map/ppermute | solution.py:13
  49.9 1.4 collective-permute-start.7
  53.3 20.9 %collective-permute-done.11 = bf16[256,1024]{1,0:T(8,128)(2,1)S(1)} collective-permute-done((bf16[256,1024]{1,0:T(8,128)(2,1)}, bf16[256,1024]{1,0:T(8,128)(2,1)S(1)}, u32[]{:S(2)}, u32[]{:S(2)}) %collective-permute-start.11) | collective-permute-done | bytes 524320 | tf_op jit(solution)/shard_map/ppermute | solution.py:13
  78.4 21.0 %collective-permute-done.17 = bf16[256,1024]{1,0:T(8,128)(2,1)S(1)} collective-permute-done((bf16[256,1024]{1,0:T(8,128)(2,1)S(1)}, bf16[256,1024]{1,0:T(8,128)(2,1)S(1)}, u32[]{:S(2)}, u32[]{:S(2)}) %collective-permute-start.17) | collective-permute-done | bytes 524320 | tf_op jit(solution)/shard_map/ppermute | solution.py:13
  102.2 1.4 collective-permute-start.24
  103.5 10.0 %collective-permute-done.23 = bf16[128,1024]{1,0:T(8,128)(2,1)S(1)} collective-permute-done((bf16[128,1024]{1,0:T(8,128)(2,1)S(1)}, bf16[128,1024]{1,0:T(8,128)(2,1)S(1)}, u32[]{:S(2)}, u32[]{:S(2)}) %collective-permute-start.23) | collective-permute-done | bytes 262176 | tf_op jit(solution)/shard_map/ppermute | solution.py:13
  118.1 11.5 %collective-permute-done.14 = f32[256,512]{0,1:T(8,128)S(1)} collective-permute-done((f32[256,512]{0,1:T(8,128)S(1)}, f32[256,512]{0,1:T(8,128)S(1)}, u32[]{:S(2)}, u32[]{:S(2)}) %collective-permute-start.14) | collective-permute-done | bytes 524320 | tf_op jit(solution)/shard_map/ppermute | solution.py:68
  131.8 5.2 %collective-permute-done.15 = bf16[256,512]{0,1:T(8,128)(2,1)S(1)} collective-permute-done((bf16[256,512]{0,1:T(8,128)(2,1)S(1)}, bf16[256,512]{0,1:T(8,128)(2,1)S(1)}, u32[]{:S(2)}, u32[]{:S(2)}) %collective-permute-start.15) | collective-permute-done | bytes 262176 | tf_op jit(solution)/shard_map/ppermute | solution.py:80
  137.1 3.1 %collective-permute-start.16 = (bf16[512,512]{0,1:T(8,128)(2,1)S(1)}, bf16[512,512]{0,1:T(8,128)(2,1)S(1)}, u32[]{:S(2)}, u32[]{:S(2)}) collective-permute-start(bf16[512,512]{0,1:T(8,128)(2,1)S(1)} %maximum_select_fusion.4), channel_id=1, source_target_pairs={{0,2},{2,0},{4,6},{6,4},{1,3},{3,1},{5,7},{7,5},{8,10},{10,8},{12,... | collective-permute-start | bytes 1572872 | tf_op jit(solution)/shard_map/ppermute | solution.py:80
  141.0 7.2 %collective-permute-done.20 = f32[256,512]{0,1:T(8,128)S(1)} collective-permute-done((f32[256,512]{0,1:T(8,128)S(1)}, f32[256,512]{0,1:T(8,128)S(1)}, u32[]{:S(2)}, u32[]{:S(2)}) %collective-permute-start.20) | collective-permute-done | bytes 524320 | tf_op jit(solution)/shard_map/ppermute | solution.py:68
  150.6 4.4 %collective-permute-done.21 = bf16[256,512]{0,1:T(8,128)(2,1)S(1)} collective-permute-done((bf16[256,512]{0,1:T(8,128)(2,1)S(1)}, bf16[256,512]{0,1:T(8,128)(2,1)S(1)}, u32[]{:S(2)}, u32[]{:S(2)}) %collective-permute-start.21) | collective-permute-done | bytes 262176 | tf_op jit(solution)/shard_map/ppermute | solution.py:80
  155.1 4.9 %collective-permute-start.22 = (bf16[512,512]{0,1:T(8,128)(2,1)S(1)}, bf16[512,512]{0,1:T(8,128)(2,1)S(1)}, u32[]{:S(2)}, u32[]{:S(2)}) collective-permute-start(bf16[512,512]{0,1:T(8,128)(2,1)S(1)} %maximum_select_fusion.5), channel_id=1, source_target_pairs={{0,2},{2,0},{4,6},{6,4},{1,3},{3,1},{5,7},{7,5},{8,10},{10,8},{12,... | collective-permute-start | bytes 1572872 | tf_op jit(solution)/shard_map/ppermute | solution.py:80
  160.4 3.0 %collective-permute-done.26 = f32[256,384]{0,1:T(8,128)S(1)} collective-permute-done((f32[256,384]{0,1:T(8,128)S(1)}, f32[256,384]{0,1:T(8,128)S(1)}, u32[]{:S(2)}, u32[]{:S(2)}) %collective-permute-start.26) | collective-permute-done | bytes 393248 | tf_op jit(solution)/shard_map/ppermute | solution.py:68
  165.7 4.5 %collective-permute-done.27 = bf16[256,384]{0,1:T(8,128)(2,1)S(1)} collective-permute-done((bf16[256,384]{0,1:T(8,128)(2,1)S(1)}, bf16[256,384]{0,1:T(8,128)(2,1)S(1)}, u32[]{:S(2)}, u32[]{:S(2)}) %collective-permute-start.27) | collective-permute-done | bytes 196640 | tf_op jit(solution)/shard_map/ppermute | solution.py:80
  170.3 3.8 %collective-permute-start.28 = (bf16[512,384]{0,1:T(8,128)(2,1)S(1)}, bf16[512,384]{0,1:T(8,128)(2,1)S(1)}, u32[]{:S(2)}, u32[]{:S(2)}) collective-permute-start(bf16[512,384]{0,1:T(8,128)(2,1)S(1)} %maximum_select_fusion.7), channel_id=1, source_target_pairs={{0,2},{2,0},{4,6},{6,4},{1,3},{3,1},{5,7},{7,5},{8,10},{10,8},{12,... | collective-permute-start | bytes 1179656 | tf_op jit(solution)/shard_map/ppermute | solution.py:80
  174.1 1.3 fusion.26
  176.1 1.3 fusion.27
  177.4 1.5 collective-permute-done.32
  179.0 1.6 collective-permute-start.33
  181.9 2.5 %fusion = bf16[1,1024,1024]{2,1,0:T(8,128)(2,1)} fusion(f32[1024,1024]{1,0:T(8,128)S(1)} %fusion.28, f32[1024,1024]{1,0:T(8,128)S(1)} %fusion.27, f32[1024,1024]{1,0:T(8,128)S(1)} %fusion.26, f32[1024,1024]{1,0:T(8,128)S(1)} %fusion.24, f32[1024,1024]{1,0:T(8,128)S(1)} %fusion.25, bf16[128,1024]{1,0:T(8,128)(2,1)S(1)} %collective-permute-done.29, ...), kind=kOutput, calls=%fused_computation.1 | convolution fusion | flops 276955136 | bytes 23592960 | tf_op jit(solution)/shard_map/dot_general | solution.py:135
  (115 shorter events, 32.3 us)
Async XLA Ops:
  1.8 14.8 %collective-permute-start = (bf16[128,1024]{1,0:T(8,128)(2,1)S(1)}, bf16[128,1024]{1,0:T(8,128)(2,1)S(1)}, u32[]{:S(2)}, u32[]{:S(2)}) collective-permute-start(bf16[128,1024]{1,0:T(8,128)(2,1)S(1)} %get-tuple-element.23), channel_id=1, source_target_pairs={{0,16},{8,24},{16,0},{24,8},{1,17},{9,25},{17,1},{25,9},{2,18},{10... | collective-permute-start | bytes 786440 | tf_op jit(solution)/shard_map/ppermute | solution.py:13
  22.1 5.0 %collective-permute-start.2 = (f32[256,128]{1,0:T(8,128)}, f32[256,128]{1,0:T(8,128)S(1)}, u32[]{:S(2)}, u32[]{:S(2)}) collective-permute-start(f32[256,128]{1,0:T(8,128)} %constant_dynamic-slice_fusion.5), channel_id=1, source_target_pairs={{0,4},{2,6},{4,0},{6,2},{1,5},{3,7},{5,1},{7,3},{8,12},{10,14},{12... | collective-permute-start | bytes 393224 | tf_op jit(solution)/shard_map/ppermute | solution.py:68
  23.4 25.3 %collective-permute-start.5 = (bf16[256,1024]{1,0:T(8,128)(2,1)}, bf16[256,1024]{1,0:T(8,128)(2,1)S(1)}, u32[]{:S(2)}, u32[]{:S(2)}) collective-permute-start(bf16[256,1024]{1,0:T(8,128)(2,1)} %get-tuple-element.14), channel_id=1, source_target_pairs={{0,16},{8,24},{16,0},{24,8},{1,17},{9,25},{17,1},{25,9},{2,18},{10... | collective-permute-start | bytes 1572872 | tf_op jit(solution)/shard_map/ppermute | solution.py:13
  24.0 24.7 %collective-permute-start.6 = (bf16[128,1024]{1,0:T(8,128)(2,1)S(1)}, bf16[128,1024]{1,0:T(8,128)(2,1)S(1)}, u32[]{:S(2)}, u32[]{:S(2)}) collective-permute-start(bf16[128,1024]{1,0:T(8,128)(2,1)S(1)} %collective-permute-done), channel_id=1, source_target_pairs={{0,1},{1,0},{2,3},{3,2},{4,5},{5,4},{6,7},{7,6},{8,9},{9,8},{10,11... | collective-permute-start | bytes 786440 | tf_op jit(solution)/shard_map/ppermute | solution.py:13
  28.7 3.5 %collective-permute-start.3 = (bf16[256,128]{1,0:T(8,128)(2,1)S(1)}, bf16[256,128]{1,0:T(8,128)(2,1)S(1)}, u32[]{:S(2)}, u32[]{:S(2)}) collective-permute-start(bf16[256,128]{1,0:T(8,128)(2,1)S(1)} %divide_convert_fusion.5), channel_id=1, source_target_pairs={{0,4},{2,6},{4,0},{6,2},{1,5},{3,7},{5,1},{7,3},{8,12},{10,14},{12... | collective-permute-start | bytes 196616 | tf_op jit(solution)/shard_map/ppermute | solution.py:80
  32.2 20.3 %collective-permute-start.4 = (bf16[512,128]{1,0:T(8,128)(2,1)S(1)}, bf16[512,128]{1,0:T(8,128)(2,1)S(1)}, u32[]{:S(2)}, u32[]{:S(2)}) collective-permute-start(bf16[512,128]{1,0:T(8,128)(2,1)S(1)} %maximum_select_fusion.13), channel_id=1, source_target_pairs={{0,2},{2,0},{4,6},{6,4},{1,3},{3,1},{5,7},{7,5},{8,10},{10,8},{12,... | collective-permute-start | bytes 393224 | tf_op jit(solution)/shard_map/ppermute | solution.py:80
  48.7 25.6 %collective-permute-start.11 = (bf16[256,1024]{1,0:T(8,128)(2,1)}, bf16[256,1024]{1,0:T(8,128)(2,1)S(1)}, u32[]{:S(2)}, u32[]{:S(2)}) collective-permute-start(bf16[256,1024]{1,0:T(8,128)(2,1)} %get-tuple-element.16), channel_id=1, source_target_pairs={{0,16},{8,24},{16,0},{24,8},{1,17},{9,25},{17,1},{25,9},{2,18},{10... | collective-permute-start | bytes 1572872 | tf_op jit(solution)/shard_map/ppermute | solution.py:13
  49.9 28.0 %collective-permute-start.7 = (f32[512,384]{0,1:T(8,128)S(1)}, f32[512,384]{0,1:T(8,128)S(1)}, u32[]{:S(2)}, u32[]{:S(2)}) collective-permute-start(f32[512,384]{0,1:T(8,128)S(1)} %dynamic-slice_bitcast_fusion.3), channel_id=1, source_target_pairs={{0,2},{2,0},{4,6},{6,4},{1,3},{3,1},{5,7},{7,5},{8,10},{10,8},{12,... | collective-permute-start | bytes 2359304 | tf_op jit(solution)/shard_map/ppermute | solution.py:68
  51.3 24.3 %collective-permute-start.12 = (bf16[256,1024]{1,0:T(8,128)(2,1)S(1)}, bf16[256,1024]{1,0:T(8,128)(2,1)S(1)}, u32[]{:S(2)}, u32[]{:S(2)}) collective-permute-start(bf16[256,1024]{1,0:T(8,128)(2,1)S(1)} %collective-permute-done.5), channel_id=1, source_target_pairs={{0,1},{1,0},{2,3},{3,2},{4,5},{5,4},{6,7},{7,6},{8,9},{9,8},{10,11... | collective-permute-start | bytes 1572872 | tf_op jit(solution)/shard_map/ppermute | solution.py:13
  74.3 25.1 %collective-permute-start.17 = (bf16[256,1024]{1,0:T(8,128)(2,1)S(1)}, bf16[256,1024]{1,0:T(8,128)(2,1)S(1)}, u32[]{:S(2)}, u32[]{:S(2)}) collective-permute-start(bf16[256,1024]{1,0:T(8,128)(2,1)S(1)} %copy-done.1), channel_id=1, source_target_pairs={{0,16},{8,24},{16,0},{24,8},{1,17},{9,25},{17,1},{25,9},{2,18},{10... | collective-permute-start | bytes 1572872 | tf_op jit(solution)/shard_map/ppermute | solution.py:13
  74.3 25.2 %collective-permute-start.18 = (bf16[256,1024]{1,0:T(8,128)(2,1)S(1)}, bf16[256,1024]{1,0:T(8,128)(2,1)S(1)}, u32[]{:S(2)}, u32[]{:S(2)}) collective-permute-start(bf16[256,1024]{1,0:T(8,128)(2,1)S(1)} %collective-permute-done.11), channel_id=1, source_target_pairs={{0,1},{1,0},{2,3},{3,2},{4,5},{5,4},{6,7},{7,6},{8,9},{9,8},{10,11... | collective-permute-start | bytes 1572872 | tf_op jit(solution)/shard_map/ppermute | solution.py:13
  77.0 38.8 %collective-permute-start.13 = (f32[512,512]{0,1:T(8,128)S(1)}, f32[512,512]{0,1:T(8,128)S(1)}, u32[]{:S(2)}, u32[]{:S(2)}) collective-permute-start(f32[512,512]{0,1:T(8,128)S(1)} %dynamic-slice_bitcast_fusion.1), channel_id=1, source_target_pairs={{0,2},{2,0},{4,6},{6,4},{1,3},{3,1},{5,7},{7,5},{8,10},{10,8},{12,... | collective-permute-start | bytes 3145736 | tf_op jit(solution)/shard_map/ppermute | solution.py:68
  78.1 22.8 %collective-permute-start.8 = (f32[256,384]{0,1:T(8,128)S(1)}, f32[256,384]{0,1:T(8,128)S(1)}, u32[]{:S(2)}, u32[]{:S(2)}) collective-permute-start(f32[256,384]{0,1:T(8,128)S(1)} %constant_dynamic-slice_fusion.4), channel_id=1, source_target_pairs={{0,4},{2,6},{4,0},{6,2},{1,5},{3,7},{5,1},{7,3},{8,12},{10,14},{12... | collective-permute-start | bytes 1179656 | tf_op jit(solution)/shard_map/ppermute | solution.py:68
  99.4 14.1 %collective-permute-start.23 = (bf16[128,1024]{1,0:T(8,128)(2,1)S(1)}, bf16[128,1024]{1,0:T(8,128)(2,1)S(1)}, u32[]{:S(2)}, u32[]{:S(2)}) collective-permute-start(bf16[128,1024]{1,0:T(8,128)(2,1)S(1)} %copy-done.2), channel_id=1, source_target_pairs={{0,16},{8,24},{16,0},{24,8},{1,17},{9,25},{17,1},{25,9},{2,18},{10... | collective-permute-start | bytes 786440 | tf_op jit(solution)/shard_map/ppermute | solution.py:13
  101.0 13.8 %collective-permute-start.9 = (bf16[256,384]{0,1:T(8,128)(2,1)S(1)}, bf16[256,384]{0,1:T(8,128)(2,1)S(1)}, u32[]{:S(2)}, u32[]{:S(2)}) collective-permute-start(bf16[256,384]{0,1:T(8,128)(2,1)S(1)} %divide_convert_fusion.3), channel_id=1, source_target_pairs={{0,4},{2,6},{4,0},{6,2},{1,5},{3,7},{5,1},{7,3},{8,12},{10,14},{12... | collective-permute-start | bytes 589832 | tf_op jit(solution)/shard_map/ppermute | solution.py:80
  101.4 28.9 %collective-permute-start.19 = (f32[512,512]{0,1:T(8,128)S(1)}, f32[512,512]{0,1:T(8,128)S(1)}, u32[]{:S(2)}, u32[]{:S(2)}) collective-permute-start(f32[512,512]{0,1:T(8,128)S(1)} %dynamic-slice_bitcast_fusion), channel_id=1, source_target_pairs={{0,2},{2,0},{4,6},{6,4},{1,3},{3,1},{5,7},{7,5},{8,10},{10,8},{12,... | collective-permute-start | bytes 3145736 | tf_op jit(solution)/shard_map/ppermute | solution.py:68
  102.2 14.2 %collective-permute-start.24 = (bf16[256,1024]{1,0:T(8,128)(2,1)S(1)}, bf16[256,1024]{1,0:T(8,128)(2,1)S(1)}, u32[]{:S(2)}, u32[]{:S(2)}) collective-permute-start(bf16[256,1024]{1,0:T(8,128)(2,1)S(1)} %collective-permute-done.17), channel_id=1, source_target_pairs={{0,1},{1,0},{2,3},{3,2},{4,5},{5,4},{6,7},{7,6},{8,9},{9,8},{10,11... | collective-permute-start | bytes 1572872 | tf_op jit(solution)/shard_map/ppermute | solution.py:13
  113.6 26.6 %collective-permute-start.29 = (bf16[128,1024]{1,0:T(8,128)(2,1)S(1)}, bf16[128,1024]{1,0:T(8,128)(2,1)S(1)}, u32[]{:S(2)}, u32[]{:S(2)}) collective-permute-start(bf16[128,1024]{1,0:T(8,128)(2,1)S(1)} %collective-permute-done.23), channel_id=1, source_target_pairs={{0,1},{1,0},{2,3},{3,2},{4,5},{5,4},{6,7},{7,6},{8,9},{9,8},{10,11... | collective-permute-start | bytes 786440 | tf_op jit(solution)/shard_map/ppermute | solution.py:13
  114.9 2.9 %collective-permute-start.10 = (bf16[512,384]{0,1:T(8,128)(2,1)S(1)}, bf16[512,384]{0,1:T(8,128)(2,1)S(1)}, u32[]{:S(2)}, u32[]{:S(2)}) collective-permute-start(bf16[512,384]{0,1:T(8,128)(2,1)S(1)} %maximum_select_fusion.6), channel_id=1, source_target_pairs={{0,2},{2,0},{4,6},{6,4},{1,3},{3,1},{5,7},{7,5},{8,10},{10,8},{12,... | collective-permute-start | bytes 1179656 | tf_op jit(solution)/shard_map/ppermute | solution.py:80
  116.1 13.6 %collective-permute-start.14 = (f32[256,512]{0,1:T(8,128)S(1)}, f32[256,512]{0,1:T(8,128)S(1)}, u32[]{:S(2)}, u32[]{:S(2)}) collective-permute-start(f32[256,512]{0,1:T(8,128)S(1)} %constant_dynamic-slice_fusion.3), channel_id=1, source_target_pairs={{0,4},{2,6},{4,0},{6,2},{1,5},{3,7},{5,1},{7,3},{8,12},{10,14},{12... | collective-permute-start | bytes 1572872 | tf_op jit(solution)/shard_map/ppermute | solution.py:68
  117.5 31.6 %collective-permute-start.25 = (f32[512,384]{0,1:T(8,128)S(1)}, f32[512,384]{0,1:T(8,128)S(1)}, u32[]{:S(2)}, u32[]{:S(2)}) collective-permute-start(f32[512,384]{0,1:T(8,128)S(1)} %dynamic-slice_bitcast_fusion.2), channel_id=1, source_target_pairs={{0,2},{2,0},{4,6},{6,4},{1,3},{3,1},{5,7},{7,5},{8,10},{10,8},{12,... | collective-permute-start | bytes 2359304 | tf_op jit(solution)/shard_map/ppermute | solution.py:68
  129.9 7.1 %collective-permute-start.15 = (bf16[256,512]{0,1:T(8,128)(2,1)S(1)}, bf16[256,512]{0,1:T(8,128)(2,1)S(1)}, u32[]{:S(2)}, u32[]{:S(2)}) collective-permute-start(bf16[256,512]{0,1:T(8,128)(2,1)S(1)} %divide_convert_fusion.1), channel_id=1, source_target_pairs={{0,4},{2,6},{4,0},{6,2},{1,5},{3,7},{5,1},{7,3},{8,12},{10,14},{12... | collective-permute-start | bytes 786440 | tf_op jit(solution)/shard_map/ppermute | solution.py:80
  130.5 17.7 %collective-permute-start.20 = (f32[256,512]{0,1:T(8,128)S(1)}, f32[256,512]{0,1:T(8,128)S(1)}, u32[]{:S(2)}, u32[]{:S(2)}) collective-permute-start(f32[256,512]{0,1:T(8,128)S(1)} %constant_dynamic-slice_fusion.2), channel_id=1, source_target_pairs={{0,4},{2,6},{4,0},{6,2},{1,5},{3,7},{5,1},{7,3},{8,12},{10,14},{12... | collective-permute-start | bytes 1572872 | tf_op jit(solution)/shard_map/ppermute | solution.py:68
  137.1 11.2 %collective-permute-start.16 = (bf16[512,512]{0,1:T(8,128)(2,1)S(1)}, bf16[512,512]{0,1:T(8,128)(2,1)S(1)}, u32[]{:S(2)}, u32[]{:S(2)}) collective-permute-start(bf16[512,512]{0,1:T(8,128)(2,1)S(1)} %maximum_select_fusion.4), channel_id=1, source_target_pairs={{0,2},{2,0},{4,6},{6,4},{1,3},{3,1},{5,7},{7,5},{8,10},{10,8},{12,... | collective-permute-start | bytes 1572872 | tf_op jit(solution)/shard_map/ppermute | solution.py:80
  140.9 19.1 %collective-permute-start.30 = (f32[512,128]{1,0:T(8,128)S(1)}, f32[512,128]{1,0:T(8,128)S(1)}, u32[]{:S(2)}, u32[]{:S(2)}) collective-permute-start(f32[512,128]{1,0:T(8,128)S(1)} %dynamic-slice_bitcast_fusion.4), channel_id=1, source_target_pairs={{0,2},{2,0},{4,6},{6,4},{1,3},{3,1},{5,7},{7,5},{8,10},{10,8},{12,... | collective-permute-start | bytes 786440 | tf_op jit(solution)/shard_map/ppermute | solution.py:68
  148.8 6.2 %collective-permute-start.21 = (bf16[256,512]{0,1:T(8,128)(2,1)S(1)}, bf16[256,512]{0,1:T(8,128)(2,1)S(1)}, u32[]{:S(2)}, u32[]{:S(2)}) collective-permute-start(bf16[256,512]{0,1:T(8,128)(2,1)S(1)} %divide_convert_fusion), channel_id=1, source_target_pairs={{0,4},{2,6},{4,0},{6,2},{1,5},{3,7},{5,1},{7,3},{8,12},{10,14},{12... | collective-permute-start | bytes 786440 | tf_op jit(solution)/shard_map/ppermute | solution.py:80
  149.3 14.0 %collective-permute-start.26 = (f32[256,384]{0,1:T(8,128)S(1)}, f32[256,384]{0,1:T(8,128)S(1)}, u32[]{:S(2)}, u32[]{:S(2)}) collective-permute-start(f32[256,384]{0,1:T(8,128)S(1)} %constant_dynamic-slice_fusion.1), channel_id=1, source_target_pairs={{0,4},{2,6},{4,0},{6,2},{1,5},{3,7},{5,1},{7,3},{8,12},{10,14},{12... | collective-permute-start | bytes 1179656 | tf_op jit(solution)/shard_map/ppermute | solution.py:68
  155.1 8.4 %collective-permute-start.22 = (bf16[512,512]{0,1:T(8,128)(2,1)S(1)}, bf16[512,512]{0,1:T(8,128)(2,1)S(1)}, u32[]{:S(2)}, u32[]{:S(2)}) collective-permute-start(bf16[512,512]{0,1:T(8,128)(2,1)S(1)} %maximum_select_fusion.5), channel_id=1, source_target_pairs={{0,2},{2,0},{4,6},{6,4},{1,3},{3,1},{5,7},{7,5},{8,10},{10,8},{12,... | collective-permute-start | bytes 1572872 | tf_op jit(solution)/shard_map/ppermute | solution.py:80
  160.0 14.0 %collective-permute-start.31 = (f32[256,128]{1,0:T(8,128)S(1)}, f32[256,128]{1,0:T(8,128)S(1)}, u32[]{:S(2)}, u32[]{:S(2)}) collective-permute-start(f32[256,128]{1,0:T(8,128)S(1)} %constant_dynamic-slice_fusion), channel_id=1, source_target_pairs={{0,4},{2,6},{4,0},{6,2},{1,5},{3,7},{5,1},{7,3},{8,12},{10,14},{12... | collective-permute-start | bytes 393224 | tf_op jit(solution)/shard_map/ppermute | solution.py:68
  164.1 6.1 %collective-permute-start.27 = (bf16[256,384]{0,1:T(8,128)(2,1)S(1)}, bf16[256,384]{0,1:T(8,128)(2,1)S(1)}, u32[]{:S(2)}, u32[]{:S(2)}) collective-permute-start(bf16[256,384]{0,1:T(8,128)(2,1)S(1)} %divide_convert_fusion.2), channel_id=1, source_target_pairs={{0,4},{2,6},{4,0},{6,2},{1,5},{3,7},{5,1},{7,3},{8,12},{10,14},{12... | collective-permute-start | bytes 589832 | tf_op jit(solution)/shard_map/ppermute | solution.py:80
  170.3 5.1 %collective-permute-start.28 = (bf16[512,384]{0,1:T(8,128)(2,1)S(1)}, bf16[512,384]{0,1:T(8,128)(2,1)S(1)}, u32[]{:S(2)}, u32[]{:S(2)}) collective-permute-start(bf16[512,384]{0,1:T(8,128)(2,1)S(1)} %maximum_select_fusion.7), channel_id=1, source_target_pairs={{0,2},{2,0},{4,6},{6,4},{1,3},{3,1},{5,7},{7,5},{8,10},{10,8},{12,... | collective-permute-start | bytes 1179656 | tf_op jit(solution)/shard_map/ppermute | solution.py:80
  175.8 3.2 %collective-permute-start.32 = (bf16[256,128]{1,0:T(8,128)(2,1)S(1)}, bf16[256,128]{1,0:T(8,128)(2,1)S(1)}, u32[]{:S(2)}, u32[]{:S(2)}) collective-permute-start(bf16[256,128]{1,0:T(8,128)(2,1)S(1)} %divide_convert_fusion.4), channel_id=1, source_target_pairs={{0,4},{2,6},{4,0},{6,2},{1,5},{3,7},{5,1},{7,3},{8,12},{10,14},{12... | collective-permute-start | bytes 196616 | tf_op jit(solution)/shard_map/ppermute | solution.py:80
  (7 other events, 70.1 us)

commit v22 on v18

--- a/solution.py
+++ b/solution.py
@@ -126,7 +126,7 @@
             jnp.bfloat16
         )
         rows = aux_all_gather(amplitudes)
-        rows_done = rows
+        rows_done = amplitudes
         term = jnp.dot(rows, block, preferred_element_type=jnp.float32)
         total = term if total is None else total + term
     gamma_own = total

time: 172 us -> 177 us (1.029)
  waiting for transfers between devices: 103 us -> 118 us
  starting transfers between devices: 35.5 us -> 31.7 us
  local copies, waits for them, and re-layouts: 11.7 us -> 7.96 us
  other arithmetic: 5.85 us -> 3.52 us
    ppermute x8, waiting for transfers between devices: 70.8 us -> 80.4 us  [shifted_2(): lax.ppermute(value, axis, [(i, (i + by) % count) for i in range(count)])]
    ppermute x10, starting transfers between devices: 17.5 us -> 11.7 us  [aux_all_gather(): other = lax.ppermute(x, 'aux', xor_pairs(count, step))]
    ppermute x10, waiting for transfers between devices: 21.4 us -> 25.8 us  [aux_all_gather(): other = lax.ppermute(x, 'aux', xor_pairs(count, step))]
    ppermute x10, starting transfers between devices: 10.8 us -> 12.8 us  [aux_reduce_scatter(): x = keep + lax.ppermute(send, 'aux', xor_pairs(count, step))]
    unnamed x17 -> x15, local copies, waits for them, and re-layouts: 3.7 us -> 1.96 us
  transfers between devices with their start and end apart: 28 -> 28, of which waited for: 12 -> 12; matrix products, arithmetic and copies ran while one was open for 14% -> 11% of each run, Pallas kernels for 0% -> 0%
where the time goes in v22:
time: 177 us
  waiting for transfers between devices  118 us (67%)
  starting transfers between devices  31.7 us (18%)
  matrix products  13.6 us (8%)
  local copies, waits for them, and re-layouts  7.96 us (4%)
  other arithmetic  3.52 us (2%)
    ppermute x8, waiting for transfers between devices, shifted_2(): lax.ppermute(value, axis, [(i, (i + by) % count) for i in range(count)])  80.4 us
    ppermute x10, waiting for transfers between devices, aux_all_gather(): other = lax.ppermute(x, 'aux', xor_pairs(count, step))  25.8 us
    ppermute x10, starting transfers between devices, aux_reduce_scatter(): x = keep + lax.ppermute(send, 'aux', xor_pairs(count, step))  12.8 us
    ppermute x10, waiting for transfers between devices, aux_reduce_scatter(): x = keep + lax.ppermute(send, 'aux', xor_pairs(count, step))  12.2 us
    ppermute x10, starting transfers between devices, aux_all_gather(): other = lax.ppermute(x, 'aux', xor_pairs(count, step))  11.7 us
    dot_general x5, matrix products, paired_plan(): term = jnp.dot(rows, block, preferred_element_type=jnp.float32)  7.22 us
    ppermute x8, starting transfers between devices, shifted_2(): lax.ppermute(value, axis, [(i, (i + by) % count) for i in range(count)])  7.22 us
    dot_general x5, matrix products, paired_plan(): jnp.einsum('aq,bq->ab', own, block, preferred_element_type=jnp.float32)  6.42 us
  transfers between devices with their start and end apart: 28, of which 12 were waited for; matrix products, arithmetic and copies ran while one was open for 11% of the time, Pallas kernels for 0%

profile of v22, /device:TPU:1, one launch (start us, length us, event | category | flops | bytes accessed | tf_op | source)
XLA Modules:
  0.0 176.8 jit_solution(13202172067499078364)
XLA Ops:
  0.0 2.8 %slice_bitcast_fusion.3 = (bf16[256,1024]{1,0:T(8,128)(2,1)S(1)}, bf16[256,1024]{1,0:T(8,128)(2,1)}, bf16[256,1024]{1,0:T(8,128)(2,1)}, bf16[256,1024]{1,0:T(8,128)(2,1)}) fusion(bf16[1,1024,1024]{2,1,0:T(8,128)(2,1)} %param.3), kind=kLoop, calls=%fused_computation.71 | loop fusion | bytes 4194304 | tf_op jit(solution)/shard_map/slice | solution.py:105
  2.8 3.1 %collective-permute-start = (bf16[256,1024]{1,0:T(8,128)(2,1)S(1)}, bf16[256,1024]{1,0:T(8,128)(2,1)S(1)}, u32[]{:S(2)}, u32[]{:S(2)}) collective-permute-start(bf16[256,1024]{1,0:T(8,128)(2,1)S(1)} %get-tuple-element.19), channel_id=1, source_target_pairs={{0,16},{8,24},{16,0},{24,8},{1,17},{9,25},{17,1},{25,9},{2,18},{10... | collective-permute-start | bytes 1572872 | tf_op jit(solution)/shard_map/ppermute | solution.py:13
  6.0 22.9 %collective-permute-done = bf16[256,1024]{1,0:T(8,128)(2,1)S(1)} collective-permute-done((bf16[256,1024]{1,0:T(8,128)(2,1)S(1)}, bf16[256,1024]{1,0:T(8,128)(2,1)S(1)}, u32[]{:S(2)}, u32[]{:S(2)}) %collective-permute-start) | collective-permute-done | bytes 524320 | tf_op jit(solution)/shard_map/ppermute | solution.py:13
  29.7 1.8 %fusion.9 = f32[1024,256]{1,0:T(8,128)S(1)} fusion(bf16[256,1024]{1,0:T(8,128)(2,1)} %copy-done.2, bf16[1,1024,1024]{2,1,0:T(8,128)(2,1)S(1)} %copy-done), kind=kOutput, calls=%fused_computation.10 | convolution fusion | flops 536870912 | bytes 3670016 | tf_op jit(solution)/shard_map/aq,bq->ab/dot_general | solution.py:120
  32.3 1.2 collective-permute-start.1
  35.6 1.4 collective-permute-start.6
  37.0 17.3 %collective-permute-done.5 = bf16[256,1024]{1,0:T(8,128)(2,1)} collective-permute-done((bf16[256,1024]{1,0:T(8,128)(2,1)}, bf16[256,1024]{1,0:T(8,128)(2,1)}, u32[]{:S(2)}, u32[]{:S(2)}) %collective-permute-start.5) | collective-permute-done | bytes 524320 | tf_op jit(solution)/shard_map/ppermute | solution.py:13
  54.3 1.1 dynamic-slice_add_fusion.3
  57.3 1.1 constant_dynamic-update-slice_fusion
  58.4 1.3 fusion.7
  59.7 1.3 collective-permute-start.12
  61.7 4.2 %collective-permute-start.7 = (f32[512,512]{0,1:T(8,128)S(1)}, f32[512,512]{0,1:T(8,128)S(1)}, u32[]{:S(2)}, u32[]{:S(2)}) collective-permute-start(f32[512,512]{0,1:T(8,128)S(1)} %dynamic-slice_bitcast_fusion.2), channel_id=1, source_target_pairs={{0,2},{2,0},{4,6},{6,4},{1,3},{3,1},{5,7},{7,5},{8,10},{10,8},{12,... | collective-permute-start | bytes 3145736 | tf_op jit(solution)/shard_map/ppermute | solution.py:68
  66.0 3.6 %collective-permute-start.4 = (bf16[512,256]{1,0:T(8,128)(2,1)S(1)}, bf16[512,256]{1,0:T(8,128)(2,1)S(1)}, u32[]{:S(2)}, u32[]{:S(2)}) collective-permute-start(bf16[512,256]{1,0:T(8,128)(2,1)S(1)} %maximum_select_fusion.15), channel_id=1, source_target_pairs={{0,2},{2,0},{4,6},{6,4},{1,3},{3,1},{5,7},{7,5},{8,10},{10,8},{12,... | collective-permute-start | bytes 786440 | tf_op jit(solution)/shard_map/ppermute | solution.py:80
  69.6 10.7 %collective-permute-done.11 = bf16[256,1024]{1,0:T(8,128)(2,1)S(1)} collective-permute-done((bf16[256,1024]{1,0:T(8,128)(2,1)}, bf16[256,1024]{1,0:T(8,128)(2,1)S(1)}, u32[]{:S(2)}, u32[]{:S(2)}) %collective-permute-start.11) | collective-permute-done | bytes 524320 | tf_op jit(solution)/shard_map/ppermute | solution.py:13
  80.4 1.3 fusion.5
  84.3 1.3 collective-permute-start.8
  85.6 19.5 %collective-permute-done.17 = bf16[256,1024]{1,0:T(8,128)(2,1)S(1)} collective-permute-done((bf16[256,1024]{1,0:T(8,128)(2,1)S(1)}, bf16[256,1024]{1,0:T(8,128)(2,1)S(1)}, u32[]{:S(2)}, u32[]{:S(2)}) %collective-permute-start.17) | collective-permute-done | bytes 524320 | tf_op jit(solution)/shard_map/ppermute | solution.py:13
  105.8 1.3 fusion.3
  108.1 10.0 %collective-permute-done.23 = bf16[256,1024]{1,0:T(8,128)(2,1)S(1)} collective-permute-done((bf16[256,1024]{1,0:T(8,128)(2,1)S(1)}, bf16[256,1024]{1,0:T(8,128)(2,1)S(1)}, u32[]{:S(2)}, u32[]{:S(2)}) %collective-permute-start.23) | collective-permute-done | bytes 524320 | tf_op jit(solution)/shard_map/ppermute | solution.py:13
  118.8 1.4 collective-permute-start.24
  122.4 6.1 %collective-permute-done.9 = bf16[256,512]{0,1:T(8,128)(2,1)S(1)} collective-permute-done((bf16[256,512]{0,1:T(8,128)(2,1)S(1)}, bf16[256,512]{0,1:T(8,128)(2,1)S(1)}, u32[]{:S(2)}, u32[]{:S(2)}) %collective-permute-start.9) | collective-permute-done | bytes 262176 | tf_op jit(solution)/shard_map/ppermute | solution.py:80
  128.6 1.3 collective-permute-start.10
  130.9 8.8 %collective-permute-done.14 = f32[256,512]{0,1:T(8,128)S(1)} collective-permute-done((f32[256,512]{0,1:T(8,128)S(1)}, f32[256,512]{0,1:T(8,128)S(1)}, u32[]{:S(2)}, u32[]{:S(2)}) %collective-permute-start.14) | collective-permute-done | bytes 524320 | tf_op jit(solution)/shard_map/ppermute | solution.py:68
  141.7 14.9 %collective-permute-done.15 = bf16[256,512]{0,1:T(8,128)(2,1)S(1)} collective-permute-done((bf16[256,512]{0,1:T(8,128)(2,1)S(1)}, bf16[256,512]{0,1:T(8,128)(2,1)S(1)}, u32[]{:S(2)}, u32[]{:S(2)}) %collective-permute-start.15) | collective-permute-done | bytes 262176 | tf_op jit(solution)/shard_map/ppermute | solution.py:80
  156.7 1.3 collective-permute-start.16
  159.0 3.2 %collective-permute-done.25 = f32[256,256]{1,0:T(8,128)S(1)} collective-permute-done((f32[256,256]{1,0:T(8,128)S(1)}, f32[256,256]{1,0:T(8,128)S(1)}, u32[]{:S(2)}, u32[]{:S(2)}) %collective-permute-start.25) | collective-permute-done | bytes 262176 | tf_op jit(solution)/shard_map/ppermute | solution.py:68
  163.1 4.7 %collective-permute-done.21 = bf16[256,512]{0,1:T(8,128)(2,1)S(1)} collective-permute-done((bf16[256,512]{0,1:T(8,128)(2,1)S(1)}, bf16[256,512]{0,1:T(8,128)(2,1)S(1)}, u32[]{:S(2)}, u32[]{:S(2)}) %collective-permute-start.21) | collective-permute-done | bytes 262176 | tf_op jit(solution)/shard_map/ppermute | solution.py:80
  167.9 1.3 collective-permute-start.22
  169.2 1.3 fusion.11
  171.6 1.3 fusion.17
  172.9 1.3 fusion.23
  174.2 2.6 %fusion = bf16[1,1024,1024]{2,1,0:T(8,128)(2,1)} fusion(f32[1024,1024]{1,0:T(8,128)S(1)} %fusion.23, f32[1024,1024]{1,0:T(8,128)S(1)} %fusion.17, f32[1024,1024]{1,0:T(8,128)S(1)} %fusion.32, f32[1024,1024]{1,0:T(8,128)S(1)} %fusion.11, bf16[256,1024]{1,0:T(8,128)(2,1)S(1)} %collective-permute-done.23, bf16[512,256]{1,0:T(8,128)(2,1)S(1)} %collective-permute-done.27, ...), kind=kOutput, calls=%fused_computation.1 | convolution fusion | flops 545521664 | bytes 19922944 | tf_op jit(solution)/shard_map/dot_general | solution.py:130
  (87 shorter events, 18.6 us)
Async XLA Ops:
  0.0 29.7 %copy-start = (bf16[1,1024,1024]{2,1,0:T(8,128)(2,1)S(1)}, bf16[1,1024,1024]{2,1,0:T(8,128)(2,1)}, u32[]{:S(2)}) copy-start(bf16[1,1024,1024]{2,1,0:T(8,128)(2,1)} %param.3) | copy-start | bytes 6291460
  2.8 26.0 %collective-permute-start = (bf16[256,1024]{1,0:T(8,128)(2,1)S(1)}, bf16[256,1024]{1,0:T(8,128)(2,1)S(1)}, u32[]{:S(2)}, u32[]{:S(2)}) collective-permute-start(bf16[256,1024]{1,0:T(8,128)(2,1)S(1)} %get-tuple-element.19), channel_id=1, source_target_pairs={{0,16},{8,24},{16,0},{24,8},{1,17},{9,25},{17,1},{25,9},{2,18},{10... | collective-permute-start | bytes 1572872 | tf_op jit(solution)/shard_map/ppermute | solution.py:13
  29.6 3.9 %copy-start.5 = (f32[4]{0:T(128)S(1)}, f32[4]{0:T(128)}, u32[]{:S(2)}) copy-start(f32[4]{0:T(128)} %param.4) | copy-start | bytes 52
  29.7 5.8 %copy-start.4 = (f32[2048]{0:T(1024)S(1)}, f32[2048]{0:T(1024)}, u32[]{:S(2)}) copy-start(f32[2048]{0:T(1024)} %param.5) | copy-start | bytes 24580
  29.7 24.6 %collective-permute-start.5 = (bf16[256,1024]{1,0:T(8,128)(2,1)}, bf16[256,1024]{1,0:T(8,128)(2,1)}, u32[]{:S(2)}, u32[]{:S(2)}) collective-permute-start(bf16[256,1024]{1,0:T(8,128)(2,1)} %get-tuple-element.12), channel_id=1, source_target_pairs={{0,16},{8,24},{16,0},{24,8},{1,17},{9,25},{17,1},{25,9},{2,18},{10... | collective-permute-start | bytes 1572872 | tf_op jit(solution)/shard_map/ppermute | solution.py:13
  32.3 22.0 %collective-permute-start.1 = (f32[512,256]{1,0:T(8,128)}, f32[512,256]{1,0:T(8,128)}, u32[]{:S(2)}, u32[]{:S(2)}) collective-permute-start(f32[512,256]{1,0:T(8,128)} %constant_dynamic-slice_fusion.5), channel_id=1, source_target_pairs={{0,2},{2,0},{4,6},{6,4},{1,3},{3,1},{5,7},{7,5},{8,10},{10,8},{12,... | collective-permute-start | bytes 1572872 | tf_op jit(solution)/shard_map/ppermute | solution.py:68
  35.6 21.7 %collective-permute-start.6 = (bf16[256,1024]{1,0:T(8,128)(2,1)}, bf16[256,1024]{1,0:T(8,128)(2,1)}, u32[]{:S(2)}, u32[]{:S(2)}) collective-permute-start(bf16[256,1024]{1,0:T(8,128)(2,1)} %copy-done.2), channel_id=1, source_target_pairs={{0,1},{1,0},{2,3},{3,2},{4,5},{5,4},{6,7},{7,6},{8,9},{9,8},{10,11... | collective-permute-start | bytes 1572872 | tf_op jit(solution)/shard_map/ppermute | solution.py:13
  54.3 26.0 %collective-permute-start.11 = (bf16[256,1024]{1,0:T(8,128)(2,1)}, bf16[256,1024]{1,0:T(8,128)(2,1)S(1)}, u32[]{:S(2)}, u32[]{:S(2)}) collective-permute-start(bf16[256,1024]{1,0:T(8,128)(2,1)} %get-tuple-element.14), channel_id=1, source_target_pairs={{0,16},{8,24},{16,0},{24,8},{1,17},{9,25},{17,1},{25,9},{2,18},{10... | collective-permute-start | bytes 1572872 | tf_op jit(solution)/shard_map/ppermute | solution.py:13
  55.5 5.7 %collective-permute-start.2 = (f32[256,256]{1,0:T(8,128)S(1)}, f32[256,256]{1,0:T(8,128)S(1)}, u32[]{:S(2)}, u32[]{:S(2)}) collective-permute-start(f32[256,256]{1,0:T(8,128)S(1)} %constant_dynamic-slice_fusion.4), channel_id=1, source_target_pairs={{0,4},{2,6},{4,0},{6,2},{1,5},{3,7},{5,1},{7,3},{8,12},{10,14},{12... | collective-permute-start | bytes 786440 | tf_op jit(solution)/shard_map/ppermute | solution.py:68
  59.7 20.6 %copy-start.1 = (bf16[256,1024]{1,0:T(8,128)(2,1)S(1)}, bf16[256,1024]{1,0:T(8,128)(2,1)}, u32[]{:S(2)}) copy-start(bf16[256,1024]{1,0:T(8,128)(2,1)} %get-tuple-element.16) | copy-start | bytes 1572868
  59.7 20.7 %collective-permute-start.12 = (bf16[256,1024]{1,0:T(8,128)(2,1)}, bf16[256,1024]{1,0:T(8,128)(2,1)S(1)}, u32[]{:S(2)}, u32[]{:S(2)}) collective-permute-start(bf16[256,1024]{1,0:T(8,128)(2,1)} %collective-permute-done.5), channel_id=1, source_target_pairs={{0,1},{1,0},{2,3},{3,2},{4,5},{5,4},{6,7},{7,6},{8,9},{9,8},{10,11... | collective-permute-start | bytes 1572872 | tf_op jit(solution)/shard_map/ppermute | solution.py:13
  61.3 4.6 %collective-permute-start.3 = (bf16[256,256]{1,0:T(8,128)(2,1)S(1)}, bf16[256,256]{1,0:T(8,128)(2,1)S(1)}, u32[]{:S(2)}, u32[]{:S(2)}) collective-permute-start(bf16[256,256]{1,0:T(8,128)(2,1)S(1)} %divide_convert_fusion.4), channel_id=1, source_target_pairs={{0,4},{2,6},{4,0},{6,2},{1,5},{3,7},{5,1},{7,3},{8,12},{10,14},{12... | collective-permute-start | bytes 393224 | tf_op jit(solution)/shard_map/ppermute | solution.py:80
  61.7 22.3 %collective-permute-start.7 = (f32[512,512]{0,1:T(8,128)S(1)}, f32[512,512]{0,1:T(8,128)S(1)}, u32[]{:S(2)}, u32[]{:S(2)}) collective-permute-start(f32[512,512]{0,1:T(8,128)S(1)} %dynamic-slice_bitcast_fusion.2), channel_id=1, source_target_pairs={{0,2},{2,0},{4,6},{6,4},{1,3},{3,1},{5,7},{7,5},{8,10},{10,8},{12,... | collective-permute-start | bytes 3145736 | tf_op jit(solution)/shard_map/ppermute | solution.py:68
  66.0 17.3 %collective-permute-start.4 = (bf16[512,256]{1,0:T(8,128)(2,1)S(1)}, bf16[512,256]{1,0:T(8,128)(2,1)S(1)}, u32[]{:S(2)}, u32[]{:S(2)}) collective-permute-start(bf16[512,256]{1,0:T(8,128)(2,1)S(1)} %maximum_select_fusion.15), channel_id=1, source_target_pairs={{0,2},{2,0},{4,6},{6,4},{1,3},{3,1},{5,7},{7,5},{8,10},{10,8},{12,... | collective-permute-start | bytes 786440 | tf_op jit(solution)/shard_map/ppermute | solution.py:80
  80.3 24.7 %collective-permute-start.17 = (bf16[256,1024]{1,0:T(8,128)(2,1)S(1)}, bf16[256,1024]{1,0:T(8,128)(2,1)S(1)}, u32[]{:S(2)}, u32[]{:S(2)}) collective-permute-start(bf16[256,1024]{1,0:T(8,128)(2,1)S(1)} %copy-done.1), channel_id=1, source_target_pairs={{0,16},{8,24},{16,0},{24,8},{1,17},{9,25},{17,1},{25,9},{2,18},{10... | collective-permute-start | bytes 1572872 | tf_op jit(solution)/shard_map/ppermute | solution.py:13
  81.8 39.4 %collective-permute-start.13 = (f32[512,512]{0,1:T(8,128)S(1)}, f32[512,512]{0,1:T(8,128)S(1)}, u32[]{:S(2)}, u32[]{:S(2)}) collective-permute-start(f32[512,512]{0,1:T(8,128)S(1)} %dynamic-slice_bitcast_fusion.1), channel_id=1, source_target_pairs={{0,2},{2,0},{4,6},{6,4},{1,3},{3,1},{5,7},{7,5},{8,10},{10,8},{12,... | collective-permute-start | bytes 3145736 | tf_op jit(solution)/shard_map/ppermute | solution.py:68
  82.6 23.2 %collective-permute-start.18 = (bf16[256,1024]{1,0:T(8,128)(2,1)S(1)}, bf16[256,1024]{1,0:T(8,128)(2,1)S(1)}, u32[]{:S(2)}, u32[]{:S(2)}) collective-permute-start(bf16[256,1024]{1,0:T(8,128)(2,1)S(1)} %collective-permute-done.11), channel_id=1, source_target_pairs={{0,1},{1,0},{2,3},{3,2},{4,5},{5,4},{6,7},{7,6},{8,9},{9,8},{10,11... | collective-permute-start | bytes 1572872 | tf_op jit(solution)/shard_map/ppermute | solution.py:13
  84.3 36.0 %collective-permute-start.8 = (f32[256,512]{0,1:T(8,128)S(1)}, f32[256,512]{0,1:T(8,128)S(1)}, u32[]{:S(2)}, u32[]{:S(2)}) collective-permute-start(f32[256,512]{0,1:T(8,128)S(1)} %constant_dynamic-slice_fusion.3), channel_id=1, source_target_pairs={{0,4},{2,6},{4,0},{6,2},{1,5},{3,7},{5,1},{7,3},{8,12},{10,14},{12... | collective-permute-start | bytes 1572872 | tf_op jit(solution)/shard_map/ppermute | solution.py:68
  105.0 13.0 %collective-permute-start.23 = (bf16[256,1024]{1,0:T(8,128)(2,1)S(1)}, bf16[256,1024]{1,0:T(8,128)(2,1)S(1)}, u32[]{:S(2)}, u32[]{:S(2)}) collective-permute-start(bf16[256,1024]{1,0:T(8,128)(2,1)S(1)} %collective-permute-done.17), channel_id=1, source_target_pairs={{0,1},{1,0},{2,3},{3,2},{4,5},{5,4},{6,7},{7,6},{8,9},{9,8},{10,11... | collective-permute-start | bytes 1572872 | tf_op jit(solution)/shard_map/ppermute | solution.py:13
  107.2 22.7 %collective-permute-start.19 = (f32[512,512]{0,1:T(8,128)S(1)}, f32[512,512]{0,1:T(8,128)S(1)}, u32[]{:S(2)}, u32[]{:S(2)}) collective-permute-start(f32[512,512]{0,1:T(8,128)S(1)} %dynamic-slice_bitcast_fusion), channel_id=1, source_target_pairs={{0,2},{2,0},{4,6},{6,4},{1,3},{3,1},{5,7},{7,5},{8,10},{10,8},{12,... | collective-permute-start | bytes 3145736 | tf_op jit(solution)/shard_map/ppermute | solution.py:68
  118.8 21.9 %collective-permute-start.24 = (f32[512,256]{1,0:T(8,128)S(1)}, f32[512,256]{1,0:T(8,128)S(1)}, u32[]{:S(2)}, u32[]{:S(2)}) collective-permute-start(f32[512,256]{1,0:T(8,128)S(1)} %dynamic-slice_bitcast_fusion.3), channel_id=1, source_target_pairs={{0,2},{2,0},{4,6},{6,4},{1,3},{3,1},{5,7},{7,5},{8,10},{10,8},{12,... | collective-permute-start | bytes 1572872 | tf_op jit(solution)/shard_map/ppermute | solution.py:68
  120.5 8.0 %collective-permute-start.9 = (bf16[256,512]{0,1:T(8,128)(2,1)S(1)}, bf16[256,512]{0,1:T(8,128)(2,1)S(1)}, u32[]{:S(2)}, u32[]{:S(2)}) collective-permute-start(bf16[256,512]{0,1:T(8,128)(2,1)S(1)} %divide_convert_fusion.2), channel_id=1, source_target_pairs={{0,4},{2,6},{4,0},{6,2},{1,5},{3,7},{5,1},{7,3},{8,12},{10,14},{12... | collective-permute-start | bytes 786440 | tf_op jit(solution)/shard_map/ppermute | solution.py:80
  121.5 18.2 %collective-permute-start.14 = (f32[256,512]{0,1:T(8,128)S(1)}, f32[256,512]{0,1:T(8,128)S(1)}, u32[]{:S(2)}, u32[]{:S(2)}) collective-permute-start(f32[256,512]{0,1:T(8,128)S(1)} %constant_dynamic-slice_fusion.2), channel_id=1, source_target_pairs={{0,4},{2,6},{4,0},{6,2},{1,5},{3,7},{5,1},{7,3},{8,12},{10,14},{12... | collective-permute-start | bytes 1572872 | tf_op jit(solution)/shard_map/ppermute | solution.py:68
  128.6 40.6 %collective-permute-start.10 = (bf16[512,512]{0,1:T(8,128)(2,1)S(1)}, bf16[512,512]{0,1:T(8,128)(2,1)S(1)}, u32[]{:S(2)}, u32[]{:S(2)}) collective-permute-start(bf16[512,512]{0,1:T(8,128)(2,1)S(1)} %maximum_select_fusion.8), channel_id=1, source_target_pairs={{0,2},{2,0},{4,6},{6,4},{1,3},{3,1},{5,7},{7,5},{8,10},{10,8},{12,... | collective-permute-start | bytes 1572872 | tf_op jit(solution)/shard_map/ppermute | solution.py:80
  130.1 27.8 %collective-permute-start.20 = (f32[256,512]{0,1:T(8,128)S(1)}, f32[256,512]{0,1:T(8,128)S(1)}, u32[]{:S(2)}, u32[]{:S(2)}) collective-permute-start(f32[256,512]{0,1:T(8,128)S(1)} %constant_dynamic-slice_fusion.1), channel_id=1, source_target_pairs={{0,4},{2,6},{4,0},{6,2},{1,5},{3,7},{5,1},{7,3},{8,12},{10,14},{12... | collective-permute-start | bytes 1572872 | tf_op jit(solution)/shard_map/ppermute | solution.py:68
  139.9 16.6 %collective-permute-start.15 = (bf16[256,512]{0,1:T(8,128)(2,1)S(1)}, bf16[256,512]{0,1:T(8,128)(2,1)S(1)}, u32[]{:S(2)}, u32[]{:S(2)}) collective-permute-start(bf16[256,512]{0,1:T(8,128)(2,1)S(1)} %divide_convert_fusion.1), channel_id=1, source_target_pairs={{0,4},{2,6},{4,0},{6,2},{1,5},{3,7},{5,1},{7,3},{8,12},{10,14},{12... | collective-permute-start | bytes 786440 | tf_op jit(solution)/shard_map/ppermute | solution.py:80
  140.8 21.3 %collective-permute-start.25 = (f32[256,256]{1,0:T(8,128)S(1)}, f32[256,256]{1,0:T(8,128)S(1)}, u32[]{:S(2)}, u32[]{:S(2)}) collective-permute-start(f32[256,256]{1,0:T(8,128)S(1)} %constant_dynamic-slice_fusion), channel_id=1, source_target_pairs={{0,4},{2,6},{4,0},{6,2},{1,5},{3,7},{5,1},{7,3},{8,12},{10,14},{12... | collective-permute-start | bytes 786440 | tf_op jit(solution)/shard_map/ppermute | solution.py:68
  156.7 14.9 %collective-permute-start.16 = (bf16[512,512]{0,1:T(8,128)(2,1)S(1)}, bf16[512,512]{0,1:T(8,128)(2,1)S(1)}, u32[]{:S(2)}, u32[]{:S(2)}) collective-permute-start(bf16[512,512]{0,1:T(8,128)(2,1)S(1)} %maximum_select_fusion.9), channel_id=1, source_target_pairs={{0,2},{2,0},{4,6},{6,4},{1,3},{3,1},{5,7},{7,5},{8,10},{10,8},{12,... | collective-permute-start | bytes 1572872 | tf_op jit(solution)/shard_map/ppermute | solution.py:80
  158.3 9.5 %collective-permute-start.21 = (bf16[256,512]{0,1:T(8,128)(2,1)S(1)}, bf16[256,512]{0,1:T(8,128)(2,1)S(1)}, u32[]{:S(2)}, u32[]{:S(2)}) collective-permute-start(bf16[256,512]{0,1:T(8,128)(2,1)S(1)} %divide_convert_fusion), channel_id=1, source_target_pairs={{0,4},{2,6},{4,0},{6,2},{1,5},{3,7},{5,1},{7,3},{8,12},{10,14},{12... | collective-permute-start | bytes 786440 | tf_op jit(solution)/shard_map/ppermute | solution.py:80
  162.3 8.3 %collective-permute-start.26 = (bf16[256,256]{1,0:T(8,128)(2,1)S(1)}, bf16[256,256]{1,0:T(8,128)(2,1)S(1)}, u32[]{:S(2)}, u32[]{:S(2)}) collective-permute-start(bf16[256,256]{1,0:T(8,128)(2,1)S(1)} %divide_convert_fusion.3), channel_id=1, source_target_pairs={{0,4},{2,6},{4,0},{6,2},{1,5},{3,7},{5,1},{7,3},{8,12},{10,14},{12... | collective-permute-start | bytes 393224 | tf_op jit(solution)/shard_map/ppermute | solution.py:80
  167.9 5.0 %collective-permute-start.22 = (bf16[512,512]{0,1:T(8,128)(2,1)S(1)}, bf16[512,512]{0,1:T(8,128)(2,1)S(1)}, u32[]{:S(2)}, u32[]{:S(2)}) collective-permute-start(bf16[512,512]{0,1:T(8,128)(2,1)S(1)} %maximum_select_fusion.10), channel_id=1, source_target_pairs={{0,2},{2,0},{4,6},{6,4},{1,3},{3,1},{5,7},{7,5},{8,10},{10,8},{12,... | collective-permute-start | bytes 1572872 | tf_op jit(solution)/shard_map/ppermute | solution.py:80
  170.7 3.5 %collective-permute-start.27 = (bf16[512,256]{1,0:T(8,128)(2,1)S(1)}, bf16[512,256]{1,0:T(8,128)(2,1)S(1)}, u32[]{:S(2)}, u32[]{:S(2)}) collective-permute-start(bf16[512,256]{1,0:T(8,128)(2,1)S(1)} %maximum_select_fusion.16), channel_id=1, source_target_pairs={{0,2},{2,0},{4,6},{6,4},{1,3},{3,1},{5,7},{7,5},{8,10},{10,8},{12,... | collective-permute-start | bytes 786440 | tf_op jit(solution)/shard_map/ppermute | solution.py:80
  (2 other events, 2.4 us)

commit v23 on v20

--- a/solution.py
+++ b/solution.py
@@ -3,7 +3,7 @@
 from jax import lax
 from jax.sharding import PartitionSpec as P
 
-CHUNKS = 8
+CHUNKS = 2
 AUX_BY_PERMUTE = True
 NARROW_FAR = False
 

time: 185 us -> 201 us (1.086)
  waiting for transfers between devices: 91.2 us -> 141 us
  starting transfers between devices: 48 us -> 21.8 us
  matrix products: 32.3 us -> 17.5 us
  local copies, waits for them, and re-layouts: 6.08 us -> 9.92 us
  other arithmetic: 5.01 us -> 8.3 us
    ppermute x18 -> x6, waiting for transfers between devices: 7.18 us -> 33.1 us  [aux_reduce_scatter(): x = keep + lax.ppermute(send, 'aux', xor_pairs(count, step))]
    ppermute x16 -> x4, waiting for transfers between devices: 66.8 us -> 90.9 us  [shifted_2(): lax.ppermute(value, axis, [(i, (i + by) % count) for i in range(count)])]
    dot_general x9 -> x3, matrix products: 25.7 us -> 8.83 us  [paired_plan(): term = jnp.dot(rows, block, preferred_element_type=jnp.float32)]
    ppermute x18 -> x6, starting transfers between devices: 20.3 us -> 7.57 us  [aux_reduce_scatter(): x = keep + lax.ppermute(send, 'aux', xor_pairs(count, step))]
    ppermute x18 -> x6, starting transfers between devices: 17.3 us -> 8.83 us  [aux_all_gather(): other = lax.ppermute(x, 'aux', xor_pairs(count, step))]
    ppermute x16 -> x4, starting transfers between devices: 10.5 us -> 5.38 us  [shifted_2(): lax.ppermute(value, axis, [(i, (i + by) % count) for i in range(count)])]
    add x17 -> x5, other arithmetic: 1.93 us -> 5.86 us  [aux_reduce_scatter(): x = keep + lax.ppermute(send, 'aux', xor_pairs(count, step))]
    dot_general x9 -> x3, matrix products: 6.61 us -> 8.71 us  [paired_plan(): jnp.einsum('aq,bq->ab', own, block, preferred_element_type=jnp.float32)]
  transfers between devices with their start and end apart: 52 -> 16, of which waited for: 20 -> 9; matrix products, arithmetic and copies ran while one was open for 16% -> 14% of each run, Pallas kernels for 0% -> 0%
where the time goes in v23:
time: 201 us; the launch traced here: 200 us
  waiting for transfers between devices  141 us (70%)
  starting transfers between devices  21.8 us (11%)
  matrix products  17.5 us (9%)
  local copies, waits for them, and re-layouts  9.92 us (5%)
  other arithmetic  8.3 us (4%)
    ppermute x4, waiting for transfers between devices, shifted_2(): lax.ppermute(value, axis, [(i, (i + by) % count) for i in range(count)])  90.9 us
    ppermute x6, waiting for transfers between devices, aux_reduce_scatter(): x = keep + lax.ppermute(send, 'aux', xor_pairs(count, step))  33.1 us
    ppermute x6, waiting for transfers between devices, aux_all_gather(): other = lax.ppermute(x, 'aux', xor_pairs(count, step))  17.2 us
    ppermute x6, starting transfers between devices, aux_all_gather(): other = lax.ppermute(x, 'aux', xor_pairs(count, step))  8.83 us
    dot_general x3, matrix products, paired_plan(): term = jnp.dot(rows, block, preferred_element_type=jnp.float32)  8.83 us
    dot_general x3, matrix products, paired_plan(): jnp.einsum('aq,bq->ab', own, block, preferred_element_type=jnp.float32)  8.71 us
    ppermute x6, starting transfers between devices, aux_reduce_scatter(): x = keep + lax.ppermute(send, 'aux', xor_pairs(count, step))  7.57 us
    add x5, other arithmetic, aux_reduce_scatter(): x = keep + lax.ppermute(send, 'aux', xor_pairs(count, step))  5.86 us
  transfers between devices with their start and end apart: 16, of which 9 were waited for; matrix products, arithmetic and copies ran while one was open for 14% of the time, Pallas kernels for 0%

profile of v23, /device:TPU:1, one launch (start us, length us, event | category | flops | bytes accessed | tf_op | source)
XLA Modules:
  0.0 200.3 jit_solution(16986161504096352190)
XLA Ops:
  0.0 2.7 %slice_bitcast_fusion.1 = (bf16[512,1024]{1,0:T(8,128)(2,1)S(1)}, bf16[512,1024]{1,0:T(8,128)(2,1)}) fusion(bf16[1,1024,1024]{2,1,0:T(8,128)(2,1)} %param.3), kind=kLoop, calls=%fused_computation.25 | loop fusion | bytes 4194304 | tf_op jit(solution)/shard_map/slice | solution.py:105
  2.7 3.1 %collective-permute-start = (bf16[512,1024]{1,0:T(8,128)(2,1)S(1)}, bf16[512,1024]{1,0:T(8,128)(2,1)}, u32[]{:S(2)}, u32[]{:S(2)}) collective-permute-start(bf16[512,1024]{1,0:T(8,128)(2,1)S(1)} %get-tuple-element.11), channel_id=1, source_target_pairs={{0,16},{8,24},{16,0},{24,8},{1,17},{9,25},{17,1},{25,9},{2,18},{10... | collective-permute-start | bytes 3145736 | tf_op jit(solution)/shard_map/ppermute | solution.py:13
  5.8 45.5 %collective-permute-done = bf16[512,1024]{1,0:T(8,128)(2,1)} collective-permute-done((bf16[512,1024]{1,0:T(8,128)(2,1)S(1)}, bf16[512,1024]{1,0:T(8,128)(2,1)}, u32[]{:S(2)}, u32[]{:S(2)}) %collective-permute-start) | collective-permute-done | bytes 1048608 | tf_op jit(solution)/shard_map/ppermute | solution.py:13
  52.3 3.1 %fusion.4 = f32[1024,512]{1,0:T(8,128)S(1)} fusion(bf16[512,1024]{1,0:T(8,128)(2,1)} %collective-permute-done, bf16[1,1024,1024]{2,1,0:T(8,128)(2,1)} %param.3), kind=kOutput, calls=%fused_computation.7 | convolution fusion | flops 1073741824 | bytes 5242880 | tf_op jit(solution)/shard_map/aq,bq->ab/dot_general | solution.py:120
  55.5 1.9 collective-permute-start.1
  57.4 41.0 %collective-permute-done.5 = bf16[512,1024]{1,0:T(8,128)(2,1)} collective-permute-done((bf16[512,1024]{1,0:T(8,128)(2,1)}, bf16[512,1024]{1,0:T(8,128)(2,1)}, u32[]{:S(2)}, u32[]{:S(2)}) %collective-permute-start.5) | collective-permute-done | bytes 1048608 | tf_op jit(solution)/shard_map/ppermute | solution.py:13
  98.4 1.3 constant_dynamic-update-slice_fusion.1
  99.7 1.3 constant_dynamic-update-slice_fusion
  101.0 2.4 %fusion.2 = f32[1024,1024]{1,0:T(8,128)S(1)} fusion(bf16[1024,1024]{1,0:T(8,128)(2,1)S(1)} %constant_dynamic-update-slice_fusion, bf16[1,1024,1024]{2,1,0:T(8,128)(2,1)S(1)} %copy-done.1), kind=kOutput, calls=%fused_computation.5 | convolution fusion | flops 2147483648 | bytes 8388608 | tf_op jit(solution)/shard_map/aq,bq->ab/dot_general | solution.py:120
  103.4 1.7 dynamic-slice_bitcast_fusion
  106.0 2.1 %collective-permute-start.7 = (f32[512,1024]{0,1:T(8,128)}, f32[512,1024]{0,1:T(8,128)}, u32[]{:S(2)}, u32[]{:S(2)}) collective-permute-start(f32[512,1024]{0,1:T(8,128)} %dynamic-slice_bitcast_fusion), channel_id=1, source_target_pairs={{0,2},{2,0},{4,6},{6,4},{1,3},{3,1},{5,7},{7,5},{8,10},{10,8},{12,... | collective-permute-start | bytes 6291464 | tf_op jit(solution)/shard_map/ppermute | solution.py:68
  108.1 1.5 dynamic-slice_add_fusion.1
  109.6 1.0 collective-permute-start.2
  112.8 1.2 collective-permute-start.11
  114.1 9.3 %collective-permute-done.2 = f32[256,512]{1,0:T(8,128)S(1)} collective-permute-done((f32[256,512]{1,0:T(8,128)S(1)}, f32[256,512]{1,0:T(8,128)S(1)}, u32[]{:S(2)}, u32[]{:S(2)}) %collective-permute-start.2) | collective-permute-done | bytes 524320 | tf_op jit(solution)/shard_map/ppermute | solution.py:68
  124.5 2.7 %bitcast_add_fusion = f32[512,1024]{0,1:T(8,128)S(1)} fusion(f32[512,1024]{0,1:T(8,128)} %collective-permute-done.7, f32[1024,1024]{1,0:T(8,128)} %copy-done, s32[]{:T(128)S(6)} %select_n.138), kind=kLoop, calls=%fused_computation.2 | loop fusion | flops 524288 | bytes 6291460 | tf_op jit(solution)/shard_map/add | solution.py:68
  127.3 1.1 constant_dynamic-slice_fusion.1
  128.8 2.0 %collective-permute-done.3 = bf16[256,512]{1,0:T(8,128)(2,1)S(1)} collective-permute-done((bf16[256,512]{1,0:T(8,128)(2,1)S(1)}, bf16[256,512]{1,0:T(8,128)(2,1)S(1)}, u32[]{:S(2)}, u32[]{:S(2)}) %collective-permute-start.3) | collective-permute-done | bytes 262176 | tf_op jit(solution)/shard_map/ppermute | solution.py:80
  131.1 2.1 %collective-permute-start.4 = (bf16[512,512]{1,0:T(8,128)(2,1)S(1)}, bf16[512,512]{1,0:T(8,128)(2,1)S(1)}, u32[]{:S(2)}, u32[]{:S(2)}) collective-permute-start(bf16[512,512]{1,0:T(8,128)(2,1)S(1)} %maximum_select_fusion.5), channel_id=1, source_target_pairs={{0,2},{2,0},{4,6},{6,4},{1,3},{3,1},{5,7},{7,5},{8,10},{10,8},{12,... | collective-permute-start | bytes 1572872 | tf_op jit(solution)/shard_map/ppermute | solution.py:80
  133.2 4.5 %collective-permute-done.11 = bf16[512,1024]{1,0:T(8,128)(2,1)} collective-permute-done((bf16[512,1024]{1,0:T(8,128)(2,1)}, bf16[512,1024]{1,0:T(8,128)(2,1)}, u32[]{:S(2)}, u32[]{:S(2)}) %collective-permute-start.11) | collective-permute-done | bytes 1048608 | tf_op jit(solution)/shard_map/ppermute | solution.py:13
  137.6 3.2 %fusion = f32[512,1024]{0,1:T(8,128)S(1)} fusion(bf16[512,1024]{1,0:T(8,128)(2,1)} %collective-permute-done.11, bf16[1,1024,1024]{2,1,0:T(8,128)(2,1)} %param.3), kind=kOutput, calls=%fused_computation.3 | convolution fusion | flops 1073741824 | bytes 5242880 | tf_op jit(solution)/shard_map/aq,bq->ab/dot_general | solution.py:120
  140.9 1.2 collective-permute-start.12
  142.6 11.1 %collective-permute-done.8 = f32[256,1024]{0,1:T(8,128)} collective-permute-done((f32[256,1024]{0,1:T(8,128)}, f32[256,1024]{0,1:T(8,128)}, u32[]{:S(2)}, u32[]{:S(2)}) %collective-permute-start.8) | collective-permute-done | bytes 1048608 | tf_op jit(solution)/shard_map/ppermute | solution.py:68
  153.7 1.4 dynamic-slice_add_fusion
  156.2 11.4 %collective-permute-done.9 = bf16[256,1024]{0,1:T(8,128)(2,1)S(1)} collective-permute-done((bf16[256,1024]{0,1:T(8,128)(2,1)S(1)}, bf16[256,1024]{0,1:T(8,128)(2,1)S(1)}, u32[]{:S(2)}, u32[]{:S(2)}) %collective-permute-start.9) | collective-permute-done | bytes 524320 | tf_op jit(solution)/shard_map/ppermute | solution.py:80
  167.9 2.2 %collective-permute-start.10 = (bf16[512,1024]{0,1:T(8,128)(2,1)S(1)}, bf16[512,1024]{0,1:T(8,128)(2,1)S(1)}, u32[]{:S(2)}, u32[]{:S(2)}) collective-permute-start(bf16[512,1024]{0,1:T(8,128)(2,1)S(1)} %maximum_select_fusion.2), channel_id=1, source_target_pairs={{0,2},{2,0},{4,6},{6,4},{1,3},{3,1},{5,7},{7,5},{8,10},{10,8},{12,... | collective-permute-start | bytes 3145736 | tf_op jit(solution)/shard_map/ppermute | solution.py:80
  171.2 12.7 %collective-permute-done.13 = f32[256,512]{1,0:T(8,128)S(1)} collective-permute-done((f32[256,512]{1,0:T(8,128)S(1)}, f32[256,512]{1,0:T(8,128)S(1)}, u32[]{:S(2)}, u32[]{:S(2)}) %collective-permute-start.13) | collective-permute-done | bytes 524320 | tf_op jit(solution)/shard_map/ppermute | solution.py:68
  185.7 2.5 %fusion.16 = f32[1024,1024]{1,0:T(8,128)S(1)} fusion(bf16[1024,512]{1,0:T(8,128)(2,1)S(1)} %maximum_select_fusion.1, bf16[512,1024]{1,0:T(8,128)(2,1)} %collective-permute-done), kind=kOutput, calls=%fused_computation.43 | convolution fusion | flops 1073741824 | bytes 6291456 | tf_op jit(solution)/shard_map/dot_general | solution.py:130
  188.2 3.7 %collective-permute-done.14 = bf16[256,512]{1,0:T(8,128)(2,1)S(1)} collective-permute-done((bf16[256,512]{1,0:T(8,128)(2,1)S(1)}, bf16[256,512]{1,0:T(8,128)(2,1)S(1)}, u32[]{:S(2)}, u32[]{:S(2)}) %collective-permute-start.14) | collective-permute-done | bytes 262176 | tf_op jit(solution)/shard_map/ppermute | solution.py:80
  192.2 1.8 collective-permute-start.15
  193.9 2.4 %fusion.17 = f32[1024,1024]{1,0:T(8,128)S(1)} fusion(bf16[1024,1024]{0,1:T(8,128)(2,1)S(1)} %maximum_select_fusion, bf16[1024,1024]{1,0:T(8,128)(2,1)S(1)} %copy-done.3), kind=kOutput, calls=%fused_computation.44 | convolution fusion | flops 2147483648 | bytes 8388608 | tf_op jit(solution)/shard_map/dot_general | solution.py:130
  196.4 3.9 %fusion.6 = bf16[1,1024,1024]{2,1,0:T(8,128)(2,1)} fusion(bf16[512,1024]{1,0:T(8,128)(2,1)} %collective-permute-done.11, f32[1024,1024]{1,0:T(8,128)S(1)} %fusion.16, f32[1024,1024]{1,0:T(8,128)S(1)} %fusion.17, bf16[512,512]{1,0:T(8,128)(2,1)S(1)} %collective-permute-done.15, bf16[512,512]{1,0:T(8,128)(2,1)S(1)} %maximum_select_fusion.6, pred[]{:T(512)S(6)} %eq.24), kind=kOutput, calls=%fused_computation.10 | convolution fusion | flops 1082654720 | bytes 12582913 | tf_op jit(solution)/shard_map/dot_general | solution.py:130
  (44 shorter events, 9.7 us)
Async XLA Ops:
  2.7 48.6 %collective-permute-start = (bf16[512,1024]{1,0:T(8,128)(2,1)S(1)}, bf16[512,1024]{1,0:T(8,128)(2,1)}, u32[]{:S(2)}, u32[]{:S(2)}) collective-permute-start(bf16[512,1024]{1,0:T(8,128)(2,1)S(1)} %get-tuple-element.11), channel_id=1, source_target_pairs={{0,16},{8,24},{16,0},{24,8},{1,17},{9,25},{17,1},{25,9},{2,18},{10... | collective-permute-start | bytes 3145736 | tf_op jit(solution)/shard_map/ppermute | solution.py:13
  51.3 47.1 %collective-permute-start.5 = (bf16[512,1024]{1,0:T(8,128)(2,1)}, bf16[512,1024]{1,0:T(8,128)(2,1)}, u32[]{:S(2)}, u32[]{:S(2)}) collective-permute-start(bf16[512,1024]{1,0:T(8,128)(2,1)} %get-tuple-element.8), channel_id=1, source_target_pairs={{0,16},{8,24},{16,0},{24,8},{1,17},{9,25},{17,1},{25,9},{2,18},{10... | collective-permute-start | bytes 3145736 | tf_op jit(solution)/shard_map/ppermute | solution.py:13
  51.3 48.4 %collective-permute-start.6 = (bf16[512,1024]{1,0:T(8,128)(2,1)}, bf16[512,1024]{1,0:T(8,128)(2,1)}, u32[]{:S(2)}, u32[]{:S(2)}) collective-permute-start(bf16[512,1024]{1,0:T(8,128)(2,1)} %collective-permute-done), channel_id=1, source_target_pairs={{0,1},{1,0},{2,3},{3,2},{4,5},{5,4},{6,7},{7,6},{8,9},{9,8},{10,11... | collective-permute-start | bytes 3145736 | tf_op jit(solution)/shard_map/ppermute | solution.py:13
  55.5 45.5 %copy-start.1 = (bf16[1,1024,1024]{2,1,0:T(8,128)(2,1)S(1)}, bf16[1,1024,1024]{2,1,0:T(8,128)(2,1)}, u32[]{:S(2)}) copy-start(bf16[1,1024,1024]{2,1,0:T(8,128)(2,1)} %param.3) | copy-start | bytes 6291460
  55.5 52.6 %collective-permute-start.1 = (f32[512,512]{1,0:T(8,128)S(1)}, f32[512,512]{1,0:T(8,128)}, u32[]{:S(2)}, u32[]{:S(2)}) collective-permute-start(f32[512,512]{1,0:T(8,128)S(1)} %constant_dynamic-slice_fusion.3), channel_id=1, source_target_pairs={{0,2},{2,0},{4,6},{6,4},{1,3},{3,1},{5,7},{7,5},{8,10},{10,8},{12,... | collective-permute-start | bytes 3145736 | tf_op jit(solution)/shard_map/ppermute | solution.py:68
  101.0 2.4 %copy-start.2 = (bf16[1024,1024]{1,0:T(8,128)(2,1)}, bf16[1024,1024]{1,0:T(8,128)(2,1)S(1)}, u32[]{:S(2)}) copy-start(bf16[1024,1024]{1,0:T(8,128)(2,1)S(1)} %constant_dynamic-update-slice_fusion) | copy-start | bytes 6291460
  103.4 2.6 %copy-start = (f32[1024,1024]{1,0:T(8,128)}, f32[1024,1024]{1,0:T(8,128)S(1)}, u32[]{:S(2)}) copy-start(f32[1024,1024]{1,0:T(8,128)S(1)} %fusion.2) | copy-start | bytes 12582916
  106.0 18.6 %collective-permute-start.7 = (f32[512,1024]{0,1:T(8,128)}, f32[512,1024]{0,1:T(8,128)}, u32[]{:S(2)}, u32[]{:S(2)}) collective-permute-start(f32[512,1024]{0,1:T(8,128)} %dynamic-slice_bitcast_fusion), channel_id=1, source_target_pairs={{0,2},{2,0},{4,6},{6,4},{1,3},{3,1},{5,7},{7,5},{8,10},{10,8},{12,... | collective-permute-start | bytes 6291464 | tf_op jit(solution)/shard_map/ppermute | solution.py:68
  108.1 2.5 %copy-start.5 = (f32[4]{0:T(128)S(1)}, f32[4]{0:T(128)}, u32[]{:S(2)}) copy-start(f32[4]{0:T(128)} %param.4) | copy-start | bytes 52
  108.1 4.5 %copy-start.4 = (f32[2048]{0:T(1024)S(1)}, f32[2048]{0:T(1024)}, u32[]{:S(2)}) copy-start(f32[2048]{0:T(1024)} %param.5) | copy-start | bytes 24580
  109.6 13.7 %collective-permute-start.2 = (f32[256,512]{1,0:T(8,128)S(1)}, f32[256,512]{1,0:T(8,128)S(1)}, u32[]{:S(2)}, u32[]{:S(2)}) collective-permute-start(f32[256,512]{1,0:T(8,128)S(1)} %constant_dynamic-slice_fusion.2), channel_id=1, source_target_pairs={{0,4},{2,6},{4,0},{6,2},{1,5},{3,7},{5,1},{7,3},{8,12},{10,14},{12... | collective-permute-start | bytes 1572872 | tf_op jit(solution)/shard_map/ppermute | solution.py:68
  112.8 24.8 %collective-permute-start.11 = (bf16[512,1024]{1,0:T(8,128)(2,1)}, bf16[512,1024]{1,0:T(8,128)(2,1)}, u32[]{:S(2)}, u32[]{:S(2)}) collective-permute-start(bf16[512,1024]{1,0:T(8,128)(2,1)} %collective-permute-done.5), channel_id=1, source_target_pairs={{0,1},{1,0},{2,3},{3,2},{4,5},{5,4},{6,7},{7,6},{8,9},{9,8},{10,11... | collective-permute-start | bytes 3145736 | tf_op jit(solution)/shard_map/ppermute | solution.py:13
  123.5 7.3 %collective-permute-start.3 = (bf16[256,512]{1,0:T(8,128)(2,1)S(1)}, bf16[256,512]{1,0:T(8,128)(2,1)S(1)}, u32[]{:S(2)}, u32[]{:S(2)}) collective-permute-start(bf16[256,512]{1,0:T(8,128)(2,1)S(1)} %divide_convert_fusion.2), channel_id=1, source_target_pairs={{0,4},{2,6},{4,0},{6,2},{1,5},{3,7},{5,1},{7,3},{8,12},{10,14},{12... | collective-permute-start | bytes 786440 | tf_op jit(solution)/shard_map/ppermute | solution.py:80
  128.3 25.3 %collective-permute-start.8 = (f32[256,1024]{0,1:T(8,128)}, f32[256,1024]{0,1:T(8,128)}, u32[]{:S(2)}, u32[]{:S(2)}) collective-permute-start(f32[256,1024]{0,1:T(8,128)} %constant_dynamic-slice_fusion.1), channel_id=1, source_target_pairs={{0,4},{2,6},{4,0},{6,2},{1,5},{3,7},{5,1},{7,3},{8,12},{10,14},{12... | collective-permute-start | bytes 3145736 | tf_op jit(solution)/shard_map/ppermute | solution.py:68
  131.1 11.0 %collective-permute-start.4 = (bf16[512,512]{1,0:T(8,128)(2,1)S(1)}, bf16[512,512]{1,0:T(8,128)(2,1)S(1)}, u32[]{:S(2)}, u32[]{:S(2)}) collective-permute-start(bf16[512,512]{1,0:T(8,128)(2,1)S(1)} %maximum_select_fusion.5), channel_id=1, source_target_pairs={{0,2},{2,0},{4,6},{6,4},{1,3},{3,1},{5,7},{7,5},{8,10},{10,8},{12,... | collective-permute-start | bytes 1572872 | tf_op jit(solution)/shard_map/ppermute | solution.py:80
  140.9 29.1 %collective-permute-start.12 = (f32[512,512]{1,0:T(8,128)S(1)}, f32[512,512]{1,0:T(8,128)S(1)}, u32[]{:S(2)}, u32[]{:S(2)}) collective-permute-start(f32[512,512]{1,0:T(8,128)S(1)} %dynamic-slice_bitcast_fusion.1), channel_id=1, source_target_pairs={{0,2},{2,0},{4,6},{6,4},{1,3},{3,1},{5,7},{7,5},{8,10},{10,8},{12,... | collective-permute-start | bytes 3145736 | tf_op jit(solution)/shard_map/ppermute | solution.py:68
  155.3 12.3 %collective-permute-start.9 = (bf16[256,1024]{0,1:T(8,128)(2,1)S(1)}, bf16[256,1024]{0,1:T(8,128)(2,1)S(1)}, u32[]{:S(2)}, u32[]{:S(2)}) collective-permute-start(bf16[256,1024]{0,1:T(8,128)(2,1)S(1)} %divide_convert_fusion), channel_id=1, source_target_pairs={{0,4},{2,6},{4,0},{6,2},{1,5},{3,7},{5,1},{7,3},{8,12},{10,14},{12... | collective-permute-start | bytes 1572872 | tf_op jit(solution)/shard_map/ppermute | solution.py:80
  167.9 16.2 %collective-permute-start.10 = (bf16[512,1024]{0,1:T(8,128)(2,1)S(1)}, bf16[512,1024]{0,1:T(8,128)(2,1)S(1)}, u32[]{:S(2)}, u32[]{:S(2)}) collective-permute-start(bf16[512,1024]{0,1:T(8,128)(2,1)S(1)} %maximum_select_fusion.2), channel_id=1, source_target_pairs={{0,2},{2,0},{4,6},{6,4},{1,3},{3,1},{5,7},{7,5},{8,10},{10,8},{12,... | collective-permute-start | bytes 3145736 | tf_op jit(solution)/shard_map/ppermute | solution.py:80
  170.3 13.6 %collective-permute-start.13 = (f32[256,512]{1,0:T(8,128)S(1)}, f32[256,512]{1,0:T(8,128)S(1)}, u32[]{:S(2)}, u32[]{:S(2)}) collective-permute-start(f32[256,512]{1,0:T(8,128)S(1)} %constant_dynamic-slice_fusion), channel_id=1, source_target_pairs={{0,4},{2,6},{4,0},{6,2},{1,5},{3,7},{5,1},{7,3},{8,12},{10,14},{12... | collective-permute-start | bytes 1572872 | tf_op jit(solution)/shard_map/ppermute | solution.py:68
  184.9 9.1 %copy-start.3 = (bf16[1024,1024]{1,0:T(8,128)(2,1)S(1)}, bf16[1024,1024]{1,0:T(8,128)(2,1)}, u32[]{:S(2)}) copy-start(bf16[1024,1024]{1,0:T(8,128)(2,1)} %copy-done.2) | copy-start | bytes 6291460
  184.9 7.1 %collective-permute-start.14 = (bf16[256,512]{1,0:T(8,128)(2,1)S(1)}, bf16[256,512]{1,0:T(8,128)(2,1)S(1)}, u32[]{:S(2)}, u32[]{:S(2)}) collective-permute-start(bf16[256,512]{1,0:T(8,128)(2,1)S(1)} %divide_convert_fusion.1), channel_id=1, source_target_pairs={{0,4},{2,6},{4,0},{6,2},{1,5},{3,7},{5,1},{7,3},{8,12},{10,14},{12... | collective-permute-start | bytes 786440 | tf_op jit(solution)/shard_map/ppermute | solution.py:80
  192.2 4.2 %collective-permute-start.15 = (bf16[512,512]{1,0:T(8,128)(2,1)S(1)}, bf16[512,512]{1,0:T(8,128)(2,1)S(1)}, u32[]{:S(2)}, u32[]{:S(2)}) collective-permute-start(bf16[512,512]{1,0:T(8,128)(2,1)S(1)} %maximum_select_fusion.6), channel_id=1, source_target_pairs={{0,2},{2,0},{4,6},{6,4},{1,3},{3,1},{5,7},{7,5},{8,10},{10,8},{12,... | collective-permute-start | bytes 1572872 | tf_op jit(solution)/shard_map/ppermute | solution.py:80
